TPU v7x, 128 devices: a whole 4x4x4 slice. The times are simulated.
128 devices in a mesh: loop: 8 (over x_hi, z), long: 16 (over y, x_lo, core).
Axes of the slice: x: 4 (x_hi: 2, x_lo: 2; x = x_hi * 2 + x_lo), y: 4, z: 4, core: 2. Of those that a mesh axis runs over, the one named last changes fastest.
Arguments:
- amplitudes: bfloat16 [19200, 8192], P('long', 'loop'), may hold values from -6 to 6
- integrals: bfloat16 [19200, 6400], P('long', 'loop'), may hold values from -0.046875 to 0.046875
- owner: int32 [128], replicated, may hold values from 0 to 15, as said below
Outputs:
- residual: float32 [6400, 8192], P('long', 'loop')
Inputs may be any that keep to these rules, and one draw needn't show every extreme that they name: Each slab of 16 consecutive tiles names every owner exactly once.
All inputs are finite; a program needn't handle non-finite values.
Results may differ from a plain program's by a relative error of at most 0.0003.
Values may be sent and summed in bfloat16 or wider, within the bound.
No kernel may reach another device: no remote copies, remote signals or barrier semaphores. Data moves between devices by JAX's collectives and lax.ppermute only.
A program may use at most 192 MiB of HBM per device.

v0:
```python
import jax
import jax.numpy as jnp
from jax import lax
from jax.sharding import PartitionSpec as P

TB = 50


def contract(slab_piece, operand):
    return lax.dot_general(
        slab_piece, operand, (((0,), (0,)), ((), ())), preferred_element_type=jnp.float32
    )


def local(amplitudes, integrals, owner):
    tile_count = owner.shape[0]
    partial_rows = contract(lax.all_gather(integrals, "loop", axis=1, tiled=True), amplitudes)
    slot_order = jnp.argsort(owner * tile_count + jnp.arange(tile_count, dtype=jnp.int32))
    tile_view = partial_rows.reshape(tile_count, TB, partial_rows.shape[1])
    ordered = jnp.take(tile_view, slot_order, axis=0).reshape(
        tile_count * TB, partial_rows.shape[1]
    )
    return lax.psum_scatter(ordered, "long", scatter_dimension=0, tiled=True)


def solution(mesh):
    placed = (P("long", "loop"), P("long", "loop"), P())
    return jax.shard_map(
        local, mesh=mesh, in_specs=placed, out_specs=P("long", "loop"), check_vma=False
    )
```

profile of v0, /device:TPU:0, one launch (start us, length us, event | category | flops | bytes accessed | tf_op | source)
XLA Modules:
  0.0 585.2 jit_solution(10639289730674058873)
XLA Ops:
  6.5 0.0 copy-start
  6.5 0.0 all-gather.2.cloned.1.call-start
  6.5 0.7 all-gather.2.cloned.1.call-update
  7.3 0.0 reduce-scatter.2.cloned.1.call-start
  7.3 0.7 iota_add_fusion
  8.0 2.5 sort.17
  10.5 0.1 broadcast_in_dim.16
  10.6 0.2 broadcast_in_dim.17
  10.8 180.2 %all-gather.2.cloned.1.call-done = bf16[1200,6400]{0,1:T(8,128)(2,1)} async-done(((bf16[1200,800]{0,1:T(8,128)(2,1)}), bf16[1200,6400]{0,1:T(8,128)(2,1)}) %all-gather.2.cloned.1.call-update) | async-done | bytes 15360016 | tf_op jit(solution)/shard_map/all_gather | solution.py:17
  191.0 0.0 copy-done
  191.0 23.6 %fusion = f32[6400,1024]{1,0:T(8,128)} fusion(bf16[1200,6400]{0,1:T(8,128)(2,1)} %all-gather.2.cloned.1.call-done, bf16[1200,1024]{1,0:T(8,128)(2,1)S(1)} %copy-done), kind=kOutput, calls=%fused_computation.6 | convolution fusion | flops 15728640000 | bytes 44032000 | tf_op jit(solution)/shard_map/dot_general | solution.py:10
  214.6 23.8 %reshape.11 = f32[128,50,1024]{2,1,0:T(8,128)} reshape(f32[6400,1024]{1,0:T(8,128)} %fusion) | data formatting | bytes 52428800 | tf_op jit(solution)/shard_map/reshape | solution.py:19
  238.5 22.0 %gather_fusion = f32[128,50,1024]{2,1,0:T(8,128)} fusion(f32[128,50,1024]{2,1,0:T(8,128)} %reshape.11, s32[1024]{0:T(1024)S(1)} %pad_clamp_fusion), kind=kCustom, calls=%fused_computation | custom fusion | bytes 52429312 | tf_op jit(solution)/shard_map/jit(_take)/gather | solution.py:20
  260.5 24.1 %gather.7 = f32[6400,1024]{1,0:T(8,128)} reshape(f32[128,50,1024]{2,1,0:T(8,128)} %gather_fusion) | data formatting | bytes 52428800 | tf_op jit(solution)/shard_map/jit(_take)/gather | solution.py:20
  284.6 0.0 copy-start.1
  284.6 18.5 %broadcast_select_fusion = f32[6400,1024]{1,0:T(8,128)} fusion(f32[6400,1024]{1,0:T(8,128)} %gather.7, pred[6400]{0:T(1024)(128)(4,1)S(1)} %broadcast_in_dim.17), kind=kLoop, calls=%fused_computation.1 | loop fusion | flops 6553600 | bytes 52435200 | tf_op jit(solution)/shard_map/jit(_take)/select_n | solution.py:20
  303.1 0.0 reduce-scatter.2.cloned.1.call-update
  303.1 275.3 %reduce-scatter.2.cloned.1.call-done = f32[400,1024]{1,0:T(8,128)} async-done(((f32[6400,1024]{1,0:T(8,128)}), f32[400,1024]{1,0:T(8,128)}) %reduce-scatter.2.cloned.1.call-update) | async-done | bytes 1638416 | tf_op jit(solution)/shard_map/reduce_scatter | solution.py:23
  578.4 0.0 copy-done.1
  (4 shorter events, 0.0 us)
Async XLA Ops:
  6.5 184.5 %copy-start = (bf16[1200,1024]{1,0:T(8,128)(2,1)S(1)}, bf16[1200,1024]{1,0:T(8,128)(2,1)}, u32[]{:S(2)}) copy-start(bf16[1200,1024]{1,0:T(8,128)(2,1)} %param.3) | copy-start | bytes 7372804
  6.5 184.5 %all-gather.2.cloned.1.call-start = ((), (), s32[]{:S(2)}) async-start(), calls=%async_computation.1 | async-start | bytes 18432000 | tf_op jit(solution)/shard_map/all_gather | solution.py:17
  7.3 571.1 %reduce-scatter.2.cloned.1.call-start = ((), (), s32[]{:S(2)}) async-start(), calls=%async_computation.2 | async-start | bytes 27852800 | tf_op jit(solution)/shard_map/reduce_scatter | solution.py:23
  284.6 293.8 %copy-start.1 = (bf16[1200,1024]{1,0:T(8,128)(2,1)S(1)}, bf16[1200,1024]{1,0:T(8,128)(2,1)}, u32[]{:S(2)}) copy-start(bf16[1200,1024]{1,0:T(8,128)(2,1)} %param.3) | copy-start | bytes 7372804
Sparse Core Ops, SparseCore 0:
  9.6 181.3 all-gather.1
  303.2 275.0 reduce-scatter.1
where the time goes:
time: 586 us; the launch traced here: 585 us
  waiting for transfers between devices  456 us (78%)
  local copies, waits for them, and re-layouts  70.2 us (12%)
  matrix products  23.6 us (4%)
  other arithmetic  21.7 us (4%)
  between operations  13.4 us (2%)
    reduce_scatter x1, waiting for transfers between devices, local(): return lax.psum_scatter(ordered, 'long', scatter_dimension=0, tiled=True)  275 us
    all_gather x1, waiting for transfers between devices, local(): lax.all_gather(integrals, 'loop', axis=1, tiled=True)  180 us
    gather x2, local copies, waits for them, and re-layouts, local(): jnp.take(tile_view, slot_order, axis=0)  46.2 us
    reshape x1, local copies, waits for them, and re-layouts, local(): tile_view = partial_rows.reshape(tile_count, TB, partial_rows.shape[1])  23.8 us
    dot_general x1, matrix products, contract(): lax.dot_general(slab_piece, operand, (((0,), (0,)), ((), ())), preferred_...  23.6 us
    select_n x2, other arithmetic, local(): jnp.take(tile_view, slot_order, axis=0)  18.5 us
  transfers between devices with their start and end apart: 2, of which 2 were waited for; matrix products, arithmetic and copies ran while one was open for 1% of the time, Pallas kernels for 0%

commit v1 on v0

v1 whole, which is shorter than its diff:
```python
import jax
import jax.numpy as jnp
from jax import lax
from jax.sharding import Mesh
from jax.sharding import PartitionSpec as P

TB = 50
LOOP_AXES = ("xh", "z")
LONG_AXES = ("y", "xl", "c")


def local(amplitudes, integrals, owner):
    nxh = lax.axis_size("xh")
    nz = lax.axis_size("z")
    nc = lax.axis_size("c")
    kc = integrals.shape[0]
    tiles_slab = integrals.shape[1] // TB
    slab = lax.axis_index("xh") * nz + lax.axis_index("z")

    slab_owner = lax.dynamic_slice(owner, (slab * tiles_slab,), (tiles_slab,))
    position = jnp.argsort(slab_owner)
    tiles = integrals.reshape(kc, tiles_slab, TB)
    by_owner = jnp.take(tiles, position, axis=1)
    by_owner = by_owner.reshape(kc, tiles_slab // nc, nc, TB)
    by_owner = jnp.moveaxis(by_owner, 2, 0)

    mine = lax.all_to_all(by_owner, "c", 0, 0, tiled=True)
    mine = mine.reshape(nc * kc, tiles_slab // nc, TB)
    gathered = lax.all_gather(mine, "z", axis=0, tiled=False)

    amp = lax.all_gather(amplitudes, "xh", axis=1, tiled=True)
    amp = lax.all_gather(amp, "c", axis=0, tiled=True)

    partial = jnp.einsum(
        "zqkr,qn->kzrn", gathered, amp, preferred_element_type=jnp.float32
    )
    partial = partial.reshape(-1, partial.shape[-1])
    summed = lax.psum_scatter(partial, ("y", "xl"), scatter_dimension=0, tiled=True)
    summed = summed.reshape(nz, TB, nxh, amplitudes.shape[1])
    out = lax.all_to_all(summed, "xh", 2, 0, tiled=True)
    return out.reshape(nxh * nz * TB, amplitudes.shape[1])


def solution(mesh):
    n_loop, n_long = mesh.devices.shape
    fine = Mesh(
        mesh.devices.reshape(2, n_loop // 2, n_long // 4, 2, 2), LOOP_AXES + LONG_AXES
    )
    placed = P(LONG_AXES, LOOP_AXES)
    return jax.shard_map(
        local,
        mesh=fine,
        in_specs=(placed, placed, P()),
        out_specs=placed,
        check_vma=False,
    )
```

time: 586 us -> 536 us (0.915)
  waiting for transfers between devices: 456 us -> 420 us
  blocking collectives: 0 us -> 30.5 us
  local copies, waits for them, and re-layouts: 70.2 us -> 40.4 us
  other arithmetic: 21.7 us -> 5.11 us
    gather x2 -> x1, local copies, waits for them, and re-layouts: 46.2 us -> 2.1 us  [local(): by_owner = jnp.take(tiles, position, axis=1)]
    all_to_all x0 -> x2, blocking collectives: none -> 30.5 us  [the longest x1 25.1 us: local(): out = lax.all_to_all(summed, 'xh', 2, 0, tiled=True)]
    all_gather x1 -> x3, waiting for transfers between devices: 180 us -> 160 us  [the longest x1 79.1 us: local(): gathered = lax.all_gather(mine, 'z', axis=0, tiled=False)]
    select_n x2 -> x1, other arithmetic: 18.5 us -> 0.01 us  [local(): by_owner = jnp.take(tiles, position, axis=1)]
    reduce_scatter x1, waiting for transfers between devices: 275 us -> 259 us  [local(): lax.psum_scatter(partial, ('y', 'xl'), scatter_dimension=0, tiled=True)]
    transpose x0 -> x2, local copies, waits for them, and re-layouts: none -> 13.3 us  [the longest x1 13.1 us: local(): jnp.einsum('zqkr,qn->kzrn', gathered, amp, preferred_element_type=jnp.flo...]
    reshape x1 -> x5, local copies, waits for them, and re-layouts: 23.8 us -> 20 us  [the longest x1 12.3 us: local(): partial = partial.reshape(-1, partial.shape[-1])]
  transfers between devices with their start and end apart: 2 -> 4, of which waited for: 2 -> 4; matrix products, arithmetic and copies ran while one was open for 1% -> 3% of each run, Pallas kernels for 0% -> 0%
where the time goes in v1:
time: 536 us; the launch traced here: 535 us
  waiting for transfers between devices  420 us (78%)
  local copies, waits for them, and re-layouts  40.4 us (8%)
  blocking collectives  30.5 us (6%)
  matrix products  25.7 us (5%)
  between operations  13.2 us (2%)
    reduce_scatter x1, waiting for transfers between devices, local(): lax.psum_scatter(partial, ('y', 'xl'), scatter_dimension=0, tiled=True)  259 us
    all_gather x1, waiting for transfers between devices, local(): gathered = lax.all_gather(mine, 'z', axis=0, tiled=False)  79.1 us
    all_gather x1, waiting for transfers between devices, local(): amp = lax.all_gather(amplitudes, 'xh', axis=1, tiled=True)  53.5 us
    all_gather x1, waiting for transfers between devices, local(): amp = lax.all_gather(amp, 'c', axis=0, tiled=True)  27.1 us
    dot_general x1, matrix products, local(): jnp.einsum('zqkr,qn->kzrn', gathered, amp, preferred_element_type=jnp.flo...  25.7 us
    all_to_all x1, blocking collectives, local(): out = lax.all_to_all(summed, 'xh', 2, 0, tiled=True)  25.1 us
    transpose x1, local copies, waits for them, and re-layouts, local(): jnp.einsum('zqkr,qn->kzrn', gathered, amp, preferred_element_type=jnp.flo...  13.1 us
    reshape x1, local copies, waits for them, and re-layouts, local(): partial = partial.reshape(-1, partial.shape[-1])  12.3 us
  transfers between devices with their start and end apart: 4, of which 4 were waited for; matrix products, arithmetic and copies ran while one was open for 3% of the time, Pallas kernels for 0%

profile of v1, /device:TPU:0, one launch (start us, length us, event | category | flops | bytes accessed | tf_op | source)
XLA Modules:
  0.0 535.2 jit_solution(9224016009615411015)
XLA Ops:
  6.5 0.0 copy-start
  6.5 0.0 all-gather.6.cloned.1.call-start
  6.5 0.7 all-gather.6.cloned.1.call-update
  7.3 0.0 all-gather.4.cloned.1.call-start
  7.3 0.0 copy-done
  7.3 0.1 dynamic_slice.3
  7.4 1.2 sort.17
  8.7 0.1 broadcast_in_dim.14
  8.7 2.6 reshape.22
  11.4 2.1 gather_fusion
  13.5 3.8 fusion.8
  17.3 0.2 copy.15
  17.5 5.4 all_to_all.20
  22.9 1.6 copy.16
  24.5 2.3 all_gather_reshape.3
  26.8 0.0 all-gather.4.cloned.1.call-update
  26.8 0.0 all-gather.8.cloned.1.call-start
  26.8 53.5 %all-gather.6.cloned.1.call-done = bf16[1200,2048]{1,0:T(8,128)(2,1)} async-done(((bf16[1200,1024]{1,0:T(8,128)(2,1)}), bf16[1200,2048]{1,0:T(8,128)(2,1)}) %all-gather.6.cloned.1.call-update) | async-done | bytes 4915216 | tf_op jit(solution)/shard_map/all_gather | solution.py:31
  80.4 0.0 all-gather.8.cloned.1.call-update
  80.4 0.2 reduce-scatter.2.cloned.1.call-start
  80.6 79.1 %all-gather.4.cloned.1.call-done = bf16[4,2400,8,50]{1,2,3,0:T(8,128)(2,1)} async-done(((bf16[1,2400,8,50]{1,2,3,0:T(8,128)(2,1)}), bf16[4,2400,8,50]{1,2,3,0:T(8,128)(2,1)}) %all-gather.4.cloned.1.call-update) | async-done | bytes 7680016 | tf_op jit(solution)/shard_map/all_gather | solution.py:29
  159.8 27.1 %all-gather.8.cloned.1.call-done = bf16[2400,2048]{1,0:T(8,128)(2,1)} async-done(((bf16[1200,2048]{1,0:T(8,128)(2,1)}), bf16[2400,2048]{1,0:T(8,128)(2,1)}) %all-gather.8.cloned.1.call-update) | async-done | bytes 9830416 | tf_op jit(solution)/shard_map/all_gather | solution.py:32
  186.9 25.7 %fusion.3 = f32[8,4,50,2048]{3,2,0,1:T(8,128)} fusion(bf16[2400,2048]{1,0:T(8,128)(2,1)} %all-gather.8.cloned.1.call-done, bf16[4,2400,8,50]{1,2,3,0:T(8,128)(2,1)} %all-gather.4.cloned.1.call-done), kind=kOutput, calls=%fused_computation.4 | convolution fusion | flops 15728640000 | bytes 30617600 | tf_op jit(solution)/shard_map/zqkr,qn->kzrn/dot_general | solution.py:34
  212.6 13.1 %copy.18 = f32[8,4,50,2048]{3,2,1,0:T(8,128)} copy(f32[8,4,50,2048]{3,2,0,1:T(8,128)} %fusion.3) | data formatting | bytes 26214400 | tf_op jit(solution)/shard_map/zqkr,qn->kzrn/transpose | solution.py:34
  225.7 12.3 %reshape.23 = f32[1600,2048]{1,0:T(8,128)} reshape(f32[8,4,50,2048]{3,2,1,0:T(8,128)} %copy.18) | data formatting | bytes 26214400 | tf_op jit(solution)/shard_map/reshape | solution.py:37
  238.0 0.0 reduce-scatter.2.cloned.1.call-update
  238.0 259.5 %reduce-scatter.2.cloned.1.call-done = f32[200,2048]{1,0:T(8,128)} async-done(((f32[1600,2048]{1,0:T(8,128)}), f32[200,2048]{1,0:T(8,128)}) %reduce-scatter.2.cloned.1.call-update) | async-done | bytes 1638416 | tf_op jit(solution)/shard_map/reduce_scatter | solution.py:38
  497.5 2.7 reshape.24
  500.2 1.1 copy.19
  501.2 25.1 %all_to_all.21 = f32[4,50,2,1024]{3,0,1,2:T(4,128)S(1)} all-to-all(f32[4,50,2,1024]{3,0,1,2:T(4,128)S(1)} %copy.19), channel_id=1, replica_groups=mesh['xh'=2,'z'=4,'y'=4,'xl'=2,'c'=2] {'xh'}, dimensions={2} | all-to-all | bytes 3276800 | tf_op jit(solution)/shard_map/all_to_all | solution.py:40
  526.4 0.9 copy.20
  527.3 1.4 reshape.25
  (4 shorter events, 0.0 us)
Async XLA Ops:
  6.5 0.8 copy-start
  6.5 73.8 %all-gather.6.cloned.1.call-start = ((), (), s32[]{:S(2)}) async-start(), calls=%async_computation.4 | async-start | bytes 7372800 | tf_op jit(solution)/shard_map/all_gather | solution.py:31
  7.3 152.5 %all-gather.4.cloned.1.call-start = ((), (), s32[]{:S(2)}) async-start(), calls=%async_computation.3 | async-start | bytes 9728000 | tf_op jit(solution)/shard_map/all_gather | solution.py:29
  26.8 160.1 %all-gather.8.cloned.1.call-start = ((), (), s32[]{:S(2)}) async-start(), calls=%async_computation.5 | async-start | bytes 14745600 | tf_op jit(solution)/shard_map/all_gather | solution.py:32
  80.4 417.1 %reduce-scatter.2.cloned.1.call-start = ((), (), s32[]{:S(2)}) async-start(), calls=%async_computation.6 | async-start | bytes 14745600 | tf_op jit(solution)/shard_map/reduce_scatter | solution.py:38
Sparse Core Ops, SparseCore 0:
  9.0 71.3 all-gather.5
  82.0 77.6 all-gather.3
  161.4 25.3 all-gather.7
  238.1 259.3 reduce-scatter.1

commit v2 on v1

v2 whole, which is shorter than its diff:
```python
import jax
import jax.numpy as jnp
from jax import lax
from jax.sharding import Mesh
from jax.sharding import PartitionSpec as P

TB = 50
LOOP_AXES = ("xh", "z")
LONG_AXES = ("y", "xl", "c")
SWAP = [(0, 1), (1, 0)]


def local(amplitudes, integrals, owner):
    nz = lax.axis_size("z")
    kc = integrals.shape[0]
    width = amplitudes.shape[1]
    tiles_slab = integrals.shape[1] // TB
    xh = lax.axis_index("xh")
    core = lax.axis_index("c")
    slab = xh * nz + lax.axis_index("z")

    slab_owner = lax.dynamic_slice(owner, (slab * tiles_slab,), (tiles_slab,))
    position = jnp.argsort(slab_owner).reshape(tiles_slab // 2, 2)
    tiles = integrals.reshape(kc, tiles_slab, TB)
    mine = jnp.take(tiles, position[:, core], axis=1)
    theirs = jnp.take(tiles, position[:, 1 - core], axis=1)
    from_sibling = lax.ppermute(theirs, "c", SWAP)
    own_owners = jnp.concatenate([mine, from_sibling], axis=0)
    gathered = lax.all_gather(own_owners, "z", axis=0, tiled=False)
    lhs = jnp.transpose(gathered, (1, 2, 0, 3)).reshape(2 * kc, -1)

    amp = jnp.concatenate([amplitudes, lax.ppermute(amplitudes, "xh", SWAP)], axis=1)
    amp = jnp.concatenate([amp, lax.ppermute(amp, "c", SWAP)], axis=0)

    partial = lax.dot_general(
        lhs, amp, (((0,), (0,)), ((), ())), preferred_element_type=jnp.float32
    )
    summed = lax.psum_scatter(partial, ("y", "xl"), scatter_dimension=0, tiled=True)
    keep = summed[:, :width]
    recv = lax.ppermute(summed[:, width:], "xh", SWAP)
    return jnp.where(
        xh == 0,
        jnp.concatenate([keep, recv], axis=0),
        jnp.concatenate([recv, keep], axis=0),
    )


def solution(mesh):
    n_loop, n_long = mesh.devices.shape
    fine = Mesh(
        mesh.devices.reshape(2, n_loop // 2, n_long // 4, 2, 2), LOOP_AXES + LONG_AXES
    )
    placed = P(LONG_AXES, LOOP_AXES)
    return jax.shard_map(
        local,
        mesh=fine,
        in_specs=(placed, placed, P()),
        out_specs=placed,
        check_vma=False,
    )
```

time: 536 us -> 564 us (1.052)
  waiting for transfers between devices: 420 us -> 452 us
  blocking collectives: 30.5 us -> 0 us
  local copies, waits for them, and re-layouts: 40.4 us -> 63.7 us
    ppermute x0 -> x4, waiting for transfers between devices: none -> 73 us  [the longest x1 52.1 us: local(): lax.ppermute(amplitudes, 'xh', SWAP)]
    all_gather x3 -> x1, waiting for transfers between devices: 160 us -> 121 us  [local(): gathered = lax.all_gather(own_owners, 'z', axis=0, tiled=False)]
    all_to_all x2 -> x0, blocking collectives: 30.5 us -> none  [the longest x1 25.1 us: local(): out = lax.all_to_all(summed, 'xh', 2, 0, tiled=True)]
    all_gather x0 -> x1, local copies, waits for them, and re-layouts: none -> 25.3 us  [local(): gathered = lax.all_gather(own_owners, 'z', axis=0, tiled=False)]
    reshape x4 -> x2, local copies, waits for them, and re-layouts: 17.4 us -> 10.4 us  [the longest x1 10.3 us: local(): lhs = jnp.transpose(gathered, (1, 2, 0, 3)).reshape(2 * kc, -1)]
    concatenate x0 -> x2, local copies, waits for them, and re-layouts: none -> 6.85 us  [the longest x1 5.16 us: local(): own_owners = jnp.concatenate([mine, from_sibling], axis=0)]
    ppermute x0 -> x4, starting transfers between devices: none -> 5.89 us  [the longest x1 3.14 us: local(): lax.ppermute(amplitudes, 'xh', SWAP)]
    transpose x2 -> x1, local copies, waits for them, and re-layouts: 13.3 us -> 9.1 us  [local(): lhs = jnp.transpose(gathered, (1, 2, 0, 3)).reshape(2 * kc, -1)]
  transfers between devices with their start and end apart: 4 -> 6, of which waited for: 4 -> 5; matrix products, arithmetic and copies ran while one was open for 3% -> 9% of each run, Pallas kernels for 0% -> 0%
where the time goes in v2:
time: 564 us; the launch traced here: 563 us
  waiting for transfers between devices  452 us (80%)
  local copies, waits for them, and re-layouts  63.7 us (11%)
  matrix products  23.5 us (4%)
  between operations  13.5 us (2%)
  starting transfers between devices  5.93 us (1%)
    reduce_scatter x1, waiting for transfers between devices, local(): lax.psum_scatter(partial, ('y', 'xl'), scatter_dimension=0, tiled=True)  258 us
    all_gather x1, waiting for transfers between devices, local(): gathered = lax.all_gather(own_owners, 'z', axis=0, tiled=False)  121 us
    ppermute x1, waiting for transfers between devices, local(): lax.ppermute(amplitudes, 'xh', SWAP)  52.1 us
    all_gather x1, local copies, waits for them, and re-layouts, local(): gathered = lax.all_gather(own_owners, 'z', axis=0, tiled=False)  25.3 us
    dot_general x1, matrix products, local(): lax.dot_general(lhs, amp, (((0,), (0,)), ((), ())), preferred_element_typ...  23.5 us
    ppermute x1, waiting for transfers between devices, local(): recv = lax.ppermute(summed[:, width:], 'xh', SWAP)  18.8 us
  transfers between devices with their start and end apart: 6, of which 5 were waited for; matrix products, arithmetic and copies ran while one was open for 9% of the time, Pallas kernels for 0%

profile of v2, /device:TPU:0, one launch (start us, length us, event | category | flops | bytes accessed | tf_op | source)
XLA Modules:
  0.0 562.6 jit_solution(15472970228318618840)
XLA Ops:
  6.5 0.0 all-gather.3.cloned.1.call-start
  6.5 0.7 dynamic_slice.9
  7.3 1.2 sort.17
  8.5 0.1 reshape.15
  8.6 0.2 dynamic-slice_reduce_fusion.1
  8.9 2.6 reshape.14
  11.4 0.6 gather_fusion.1
  12.1 0.2 select_bitcast_fusion
  12.3 1.1 copy.6
  13.4 0.0 collective-permute-start
  13.4 0.6 gather_fusion
  14.0 0.2 select_bitcast_fusion.1
  14.2 2.1 collective-permute-done
  16.3 1.4 copy.7
  17.7 0.6 pad_maximum_fusion
  18.3 5.2 copy.8
  23.5 0.0 copy-start
  23.5 0.0 all-gather.3.cloned.1.call-update
  23.5 0.0 reduce-scatter.2.cloned.1.call-start
  23.6 1.6 copy-done
  25.2 3.1 collective-permute-start.1
  28.3 1.7 constant_dynamic-update-slice_fusion.1
  30.0 52.1 %collective-permute-done.1 = bf16[1200,1024]{1,0:T(8,128)(2,1)S(1)} collective-permute-done((bf16[1200,1024]{1,0:T(8,128)(2,1)S(1)}, bf16[1200,1024]{1,0:T(8,128)(2,1)S(1)}, u32[]{:S(2)}, u32[]{:S(2)}) %collective-permute-start.1) | collective-permute-done | bytes 2457632 | tf_op jit(solution)/shard_map/ppermute | solution.py:32
  82.1 1.7 constant_dynamic-update-slice_fusion
  83.8 0.0 collective-permute-start.2
  83.8 121.4 %all-gather.3.cloned.1.call-done = bf16[9600,8,50]{2,1,0:T(8,128)(2,1)} async-done(((bf16[2400,8,50]{2,1,0:T(8,128)(2,1)}), bf16[9600,8,50]{2,1,0:T(8,128)(2,1)}) %all-gather.3.cloned.1.call-update) | async-done | bytes 7680016 | tf_op jit(solution)/shard_map/all_gather | solution.py:29
  205.2 25.3 %copy.11 = bf16[4,2400,8,50]{1,0,2,3:T(4,128)(2,1)} copy(bf16[4,2400,8,50]{3,2,1,0:T(8,128)(2,1)} %bitcast.12) | data formatting | bytes 15360000 | tf_op jit(solution)/shard_map/all_gather | solution.py:29
  230.5 9.1 %copy.10 = bf16[2400,8,4,50]{0,3,2,1:T(8,128)(2,1)} copy(bf16[2400,8,4,50]{0,2,1,3:T(4,128)(2,1)} %bitcast.11) | data formatting | bytes 15360000 | tf_op jit(solution)/shard_map/transpose | solution.py:30
  239.6 10.3 %reshape.16 = bf16[2400,1600]{0,1:T(8,128)(2,1)} reshape(bf16[2400,8,4,50]{0,3,2,1:T(8,128)(2,1)} %copy.10) | data formatting | bytes 15360000 | tf_op jit(solution)/shard_map/reshape | solution.py:30
  249.9 0.0 collective-permute-done.2
  249.9 23.5 %fusion = f32[1600,2048]{1,0:T(8,128)} fusion(bf16[2400,1600]{0,1:T(8,128)(2,1)} %reshape.16, bf16[1200,2048]{1,0:T(8,128)(2,1)} %collective-permute-done.2, bf16[1200,2048]{1,0:T(8,128)(2,1)} %constant_dynamic-update-slice_fusion), kind=kOutput, calls=%fused_computation.2 | convolution fusion | flops 15748300800 | bytes 30617600 | tf_op jit(solution)/shard_map/dot_general | solution.py:35
  273.4 0.0 reduce-scatter.2.cloned.1.call-update
  273.4 258.1 %reduce-scatter.2.cloned.1.call-done = f32[200,2048]{1,0:T(8,128)} async-done(((f32[1600,2048]{1,0:T(8,128)}), f32[200,2048]{1,0:T(8,128)}) %reduce-scatter.2.cloned.1.call-update) | async-done | bytes 1638416 | tf_op jit(solution)/shard_map/reduce_scatter | solution.py:38
  531.4 1.5 fusion.5
  532.9 2.7 collective-permute-start.3
  535.7 18.8 %collective-permute-done.3 = f32[200,1024]{1,0:T(8,128)S(1)} collective-permute-done((f32[200,1024]{1,0:T(8,128)S(1)}, f32[200,1024]{1,0:T(8,128)S(1)}, u32[]{:S(2)}, u32[]{:S(2)}) %collective-permute-start.3) | collective-permute-done | bytes 819232 | tf_op jit(solution)/shard_map/ppermute | solution.py:40
  554.5 1.3 maximum_select_fusion
  (6 shorter events, 0.0 us)
Async XLA Ops:
  6.5 198.7 %all-gather.3.cloned.1.call-start = ((), (), s32[]{:S(2)}) async-start(), calls=%async_computation.2 | async-start | bytes 24576000 | tf_op jit(solution)/shard_map/all_gather | solution.py:29
  13.4 3.0 collective-permute-start
  23.5 1.7 copy-start
  23.5 507.9 %reduce-scatter.2.cloned.1.call-start = ((), (), s32[]{:S(2)}) async-start(), calls=%async_computation.1 | async-start | bytes 14745600 | tf_op jit(solution)/shard_map/reduce_scatter | solution.py:38
  25.2 56.9 %collective-permute-start.1 = (bf16[1200,1024]{1,0:T(8,128)(2,1)S(1)}, bf16[1200,1024]{1,0:T(8,128)(2,1)S(1)}, u32[]{:S(2)}, u32[]{:S(2)}) collective-permute-start(bf16[1200,1024]{1,0:T(8,128)(2,1)S(1)} %copy-done), channel_id=1, source_target_pairs={{0,64},{64,0},{1,65},{65,1},{2,66},{66,2},{3,67},{67,3},{4,68},{68... | collective-permute-start | bytes 7372808 | tf_op jit(solution)/shard_map/ppermute | solution.py:32
  83.8 166.1 %collective-permute-start.2 = (bf16[1200,2048]{1,0:T(8,128)(2,1)}, bf16[1200,2048]{1,0:T(8,128)(2,1)}, u32[]{:S(2)}, u32[]{:S(2)}) collective-permute-start(bf16[1200,2048]{1,0:T(8,128)(2,1)} %constant_dynamic-update-slice_fusion), channel_id=1, source_target_pairs={{0,1},{1,0},{2,3},{3,2},{4,5},{5,4},{6,7},{7,6},{8,9},{9,8},{10,11... | collective-permute-start | bytes 14745608 | tf_op jit(solution)/shard_map/ppermute | solution.py:33
  532.9 21.5 %collective-permute-start.3 = (f32[200,1024]{1,0:T(8,128)S(1)}, f32[200,1024]{1,0:T(8,128)S(1)}, u32[]{:S(2)}, u32[]{:S(2)}) collective-permute-start(f32[200,1024]{1,0:T(8,128)S(1)} %get-tuple-element.11), channel_id=1, source_target_pairs={{0,64},{64,0},{1,65},{65,1},{2,66},{66,2},{3,67},{67,3},{4,68},{68... | collective-permute-start | bytes 2457608 | tf_op jit(solution)/shard_map/ppermute | solution.py:40
Sparse Core Ops, SparseCore 0:
  23.6 181.5 all-gather.2
  273.5 257.8 reduce-scatter.1

commit v3 on v2

--- a/solution.py
+++ b/solution.py
@@ -21,20 +21,20 @@
 
     slab_owner = lax.dynamic_slice(owner, (slab * tiles_slab,), (tiles_slab,))
     position = jnp.argsort(slab_owner).reshape(tiles_slab // 2, 2)
-    tiles = integrals.reshape(kc, tiles_slab, TB)
-    mine = jnp.take(tiles, position[:, core], axis=1)
-    theirs = jnp.take(tiles, position[:, 1 - core], axis=1)
+    tiles = integrals.T.reshape(tiles_slab, TB, kc)
+    mine = jnp.take(tiles, position[:, core], axis=0)
+    theirs = jnp.take(tiles, position[:, 1 - core], axis=0)
     from_sibling = lax.ppermute(theirs, "c", SWAP)
-    own_owners = jnp.concatenate([mine, from_sibling], axis=0)
-    gathered = lax.all_gather(own_owners, "z", axis=0, tiled=False)
-    lhs = jnp.transpose(gathered, (1, 2, 0, 3)).reshape(2 * kc, -1)
+    own_owners = jnp.stack([mine, from_sibling], axis=2)
+    gathered = lax.all_gather(own_owners, "z", axis=1, tiled=True)
 
     amp = jnp.concatenate([amplitudes, lax.ppermute(amplitudes, "xh", SWAP)], axis=1)
-    amp = jnp.concatenate([amp, lax.ppermute(amp, "c", SWAP)], axis=0)
+    amp = jnp.stack([amp, lax.ppermute(amp, "c", SWAP)], axis=0)
 
     partial = lax.dot_general(
-        lhs, amp, (((0,), (0,)), ((), ())), preferred_element_type=jnp.float32
+        gathered, amp, (((2, 3), (0, 1)), ((), ())), preferred_element_type=jnp.float32
     )
+    partial = partial.reshape(-1, partial.shape[-1])
     summed = lax.psum_scatter(partial, ("y", "xl"), scatter_dimension=0, tiled=True)
     keep = summed[:, :width]
     recv = lax.ppermute(summed[:, width:], "xh", SWAP)

time: 564 us -> 427 us (0.76)
  waiting for transfers between devices: 452 us -> 357 us
  local copies, waits for them, and re-layouts: 63.7 us -> 14.1 us
  matrix products: 23.5 us -> 32.5 us
    all_gather x1, waiting for transfers between devices: 121 us -> 15.8 us  [local(): gathered = lax.all_gather(own_owners, 'z', axis=1, tiled=True)]
    all_gather x1 -> x0, local copies, waits for them, and re-layouts: 25.3 us -> none  [local(): gathered = lax.all_gather(own_owners, 'z', axis=0, tiled=False)]
    reshape x2 -> x1, local copies, waits for them, and re-layouts: 12.9 us -> 2.58 us  [local(): tiles = integrals.T.reshape(tiles_slab, TB, kc)]
    transpose x1 -> x0, local copies, waits for them, and re-layouts: 9.1 us -> none  [local(): lhs = jnp.transpose(gathered, (1, 2, 0, 3)).reshape(2 * kc, -1)]
    dot_general x1, matrix products: 23.5 us -> 32.5 us  [local(): lax.dot_general(gathered, amp, (((2, 3), (0, 1)), ((), ())), preferred_el...]
    ppermute x1, waiting for transfers between devices: 0.01 us -> 8.32 us  [local(): amp = jnp.stack([amp, lax.ppermute(amp, 'c', SWAP)], axis=0)]
  transfers between devices with their start and end apart: 6 -> 6, of which waited for: 5 -> 6; matrix products, arithmetic and copies ran while one was open for 9% -> 0% of each run, Pallas kernels for 0% -> 0%
where the time goes in v3:
time: 427 us
  waiting for transfers between devices  357 us (84%)
  matrix products  32.5 us (8%)
  local copies, waits for them, and re-layouts  14.1 us (3%)
  between operations  13.5 us (3%)
  starting transfers between devices  5.93 us (1%)
    reduce_scatter x1, waiting for transfers between devices, local(): lax.psum_scatter(partial, ('y', 'xl'), scatter_dimension=0, tiled=True)  259 us
    ppermute x1, waiting for transfers between devices, local(): lax.ppermute(amplitudes, 'xh', SWAP)  53.5 us
    dot_general x1, matrix products, local(): lax.dot_general(gathered, amp, (((2, 3), (0, 1)), ((), ())), preferred_el...  32.5 us
    ppermute x1, waiting for transfers between devices, local(): recv = lax.ppermute(summed[:, width:], 'xh', SWAP)  18.8 us
    all_gather x1, waiting for transfers between devices, local(): gathered = lax.all_gather(own_owners, 'z', axis=1, tiled=True)  15.8 us
  transfers between devices with their start and end apart: 6, of which 6 were waited for; matrix products, arithmetic and copies ran while one was open for 0% of the time, Pallas kernels for 0%

profile of v3, /device:TPU:0, one launch (start us, length us, event | category | flops | bytes accessed | tf_op | source)
XLA Modules:
  0.0 426.6 jit_solution(11583945499208415729)
XLA Ops:
  6.5 0.0 all-gather.2.cloned.1.call-start
  6.5 0.7 dynamic_slice.9
  7.3 1.2 sort.17
  8.5 0.1 reshape.15
  8.6 0.2 dynamic-slice_reduce_fusion.1
  8.9 2.6 reshape.14
  11.4 0.6 gather_fusion.1
  12.1 0.2 broadcast_select_fusion
  12.3 1.1 copy.4
  13.4 0.0 collective-permute-start
  13.4 0.6 gather_fusion
  14.0 0.2 select_bitcast_fusion
  14.2 2.1 collective-permute-done
  16.4 1.4 copy.12
  17.7 0.2 pad_maximum_fusion
  18.0 0.0 copy-start
  18.0 1.7 copy.6
  19.7 0.0 all-gather.2.cloned.1.call-update
  19.7 0.0 reduce-scatter.2.cloned.1.call-start
  19.7 0.7 copy-done
  20.4 3.1 collective-permute-start.1
  23.6 0.3 constant_dynamic-update-slice_fusion.1
  23.8 53.5 %collective-permute-done.1 = bf16[1200,1024]{1,0:T(8,128)(2,1)S(1)} collective-permute-done((bf16[1200,1024]{1,0:T(8,128)(2,1)S(1)}, bf16[1200,1024]{1,0:T(8,128)(2,1)S(1)}, u32[]{:S(2)}, u32[]{:S(2)}) %collective-permute-start.1) | collective-permute-done | bytes 2457632 | tf_op jit(solution)/shard_map/ppermute | solution.py:31
  77.3 0.3 constant_dynamic-update-slice_fusion
  77.6 0.0 copy-start.1
  77.6 2.3 copy-done.1
  79.9 0.0 collective-permute-start.2
  79.9 8.3 %collective-permute-done.2 = bf16[1200,2048]{1,0:T(8,128)(2,1)} collective-permute-done((bf16[1200,2048]{1,0:T(8,128)(2,1)S(1)}, bf16[1200,2048]{1,0:T(8,128)(2,1)}, u32[]{:S(2)}, u32[]{:S(2)}) %collective-permute-start.2) | collective-permute-done | bytes 4915232 | tf_op jit(solution)/shard_map/ppermute | solution.py:32
  88.2 15.8 %all-gather.2.cloned.1.call-done = bf16[8,200,2,1200]{3,0,2,1:T(8,128)(2,1)} async-done(((bf16[8,50,2,1200]{3,0,2,1:T(8,128)(2,1)}), bf16[8,200,2,1200]{3,0,2,1:T(8,128)(2,1)}) %all-gather.2.cloned.1.call-update) | async-done | bytes 7680016 | tf_op jit(solution)/shard_map/all_gather | solution.py:29
  104.0 32.5 %fusion = f32[8,200,2048,1]{2,1,3,0:T(8,128)} fusion(bf16[1,1200,2048]{2,1,0:T(8,128)(2,1)} %bitcast.4, bf16[1,1200,2048]{2,1,0:T(8,128)(2,1)} %bitcast.18, bf16[8,200,2,1200]{3,0,2,1:T(8,128)(2,1)} %all-gather.2.cloned.1.call-done), kind=kOutput, calls=%fused_computation.3 | convolution fusion | flops 15733555200 | bytes 30617600 | tf_op jit(solution)/shard_map/dot_general | solution.py:34
  136.5 0.0 reduce-scatter.2.cloned.1.call-update
  136.6 258.9 %reduce-scatter.2.cloned.1.call-done = f32[200,2048]{1,0:T(8,128)} async-done(((f32[1600,2048]{1,0:T(8,128)}), f32[200,2048]{1,0:T(8,128)}) %reduce-scatter.2.cloned.1.call-update) | async-done | bytes 1638416 | tf_op jit(solution)/shard_map/reduce_scatter | solution.py:38
  395.5 1.5 fusion.5
  397.0 2.8 collective-permute-start.3
  399.7 18.8 %collective-permute-done.3 = f32[200,1024]{1,0:T(8,128)S(1)} collective-permute-done((f32[200,1024]{1,0:T(8,128)S(1)}, f32[200,1024]{1,0:T(8,128)S(1)}, u32[]{:S(2)}, u32[]{:S(2)}) %collective-permute-start.3) | collective-permute-done | bytes 819232 | tf_op jit(solution)/shard_map/ppermute | solution.py:40
  418.5 1.3 maximum_select_fusion
  (6 shorter events, 0.0 us)
Async XLA Ops:
  6.5 97.5 %all-gather.2.cloned.1.call-start = ((), (), s32[]{:S(2)}) async-start(), calls=%async_computation.1 | async-start | bytes 10240000 | tf_op jit(solution)/shard_map/all_gather | solution.py:29
  13.4 3.0 collective-permute-start
  18.0 2.4 copy-start
  19.7 375.8 %reduce-scatter.2.cloned.1.call-start = ((), (), s32[]{:S(2)}) async-start(), calls=%async_computation.2 | async-start | bytes 14745600 | tf_op jit(solution)/shard_map/reduce_scatter | solution.py:38
  20.4 56.9 %collective-permute-start.1 = (bf16[1200,1024]{1,0:T(8,128)(2,1)S(1)}, bf16[1200,1024]{1,0:T(8,128)(2,1)S(1)}, u32[]{:S(2)}, u32[]{:S(2)}) collective-permute-start(bf16[1200,1024]{1,0:T(8,128)(2,1)S(1)} %copy-done), channel_id=1, source_target_pairs={{0,64},{64,0},{1,65},{65,1},{2,66},{66,2},{3,67},{67,3},{4,68},{68... | collective-permute-start | bytes 7372808 | tf_op jit(solution)/shard_map/ppermute | solution.py:31
  77.6 2.3 copy-start.1
  79.9 8.3 %collective-permute-start.2 = (bf16[1200,2048]{1,0:T(8,128)(2,1)S(1)}, bf16[1200,2048]{1,0:T(8,128)(2,1)}, u32[]{:S(2)}, u32[]{:S(2)}) collective-permute-start(bf16[1200,2048]{1,0:T(8,128)(2,1)S(1)} %constant_dynamic-update-slice_fusion), channel_id=1, source_target_pairs={{0,1},{1,0},{2,3},{3,2},{4,5},{5,4},{6,7},{7,6},{8,9},{9,8},{10,11... | collective-permute-start | bytes 14745608 | tf_op jit(solution)/shard_map/ppermute | solution.py:32
  397.0 21.5 %collective-permute-start.3 = (f32[200,1024]{1,0:T(8,128)S(1)}, f32[200,1024]{1,0:T(8,128)S(1)}, u32[]{:S(2)}, u32[]{:S(2)}) collective-permute-start(f32[200,1024]{1,0:T(8,128)S(1)} %get-tuple-element.11), channel_id=1, source_target_pairs={{0,64},{64,0},{1,65},{65,1},{2,66},{66,2},{3,67},{67,3},{4,68},{68... | collective-permute-start | bytes 2457608 | tf_op jit(solution)/shard_map/ppermute | solution.py:40
Sparse Core Ops, SparseCore 0:
  19.8 84.1 all-gather.1
  136.7 258.7 reduce-scatter.1

commit v4 on v3

--- a/solution.py
+++ b/solution.py
@@ -8,6 +8,34 @@
 LOOP_AXES = ("xh", "z")
 LONG_AXES = ("y", "xl", "c")
 SWAP = [(0, 1), (1, 0)]
+
+
+def ring_pick(parts, index):
+    return lax.dynamic_index_in_dim(parts, index % parts.shape[0], 0, keepdims=False)
+
+
+def reduce_scatter_y_then_xl(partial):
+    ny = lax.axis_size("y")
+    nxl = lax.axis_size("xl")
+    yi = lax.axis_index("y")
+    xi = lax.axis_index("xl")
+    rows = partial.shape[0] // (ny * nxl)
+    half = rows // 2
+    parts = partial.reshape(ny, nxl, rows, partial.shape[1])
+    ahead, back = parts[:, :, :half], parts[:, :, half:]
+    to_next = [(i, (i + 1) % ny) for i in range(ny)]
+    to_prev = [(i, (i - 1) % ny) for i in range(ny)]
+    acc_ahead = ring_pick(ahead, yi + ny - 1)
+    acc_back = ring_pick(back, yi + 1)
+    for step in range(ny - 1):
+        got_ahead = lax.ppermute(acc_ahead, "y", to_next)
+        got_back = lax.ppermute(acc_back, "y", to_prev)
+        acc_ahead = got_ahead + ring_pick(ahead, yi + 2 * ny - 2 - step)
+        acc_back = got_back + ring_pick(back, yi + 2 + step)
+    done = jnp.concatenate([acc_ahead, acc_back], axis=1)
+    mine = lax.dynamic_index_in_dim(done, xi, 0, keepdims=False)
+    other = lax.dynamic_index_in_dim(done, 1 - xi, 0, keepdims=False)
+    return mine + lax.ppermute(other, "xl", SWAP)
 
 
 def local(amplitudes, integrals, owner):
@@ -35,7 +63,7 @@
         gathered, amp, (((2, 3), (0, 1)), ((), ())), preferred_element_type=jnp.float32
     )
     partial = partial.reshape(-1, partial.shape[-1])
-    summed = lax.psum_scatter(partial, ("y", "xl"), scatter_dimension=0, tiled=True)
+    summed = reduce_scatter_y_then_xl(partial)
     keep = summed[:, :width]
     recv = lax.ppermute(summed[:, width:], "xh", SWAP)
     return jnp.where(

time: 427 us -> 360 us (0.84)
  waiting for transfers between devices: 357 us -> 225 us
  other arithmetic: 3.16 us -> 30.5 us
  local copies, waits for them, and re-layouts: 14.1 us -> 40 us
  starting transfers between devices: 5.93 us -> 18.1 us
    reduce_scatter x1 -> x0, waiting for transfers between devices: 259 us -> none  [local(): lax.psum_scatter(partial, ('y', 'xl'), scatter_dimension=0, tiled=True)]
    ppermute x0 -> x7, waiting for transfers between devices: none -> 131 us  [the longest x3 88.6 us: reduce_scatter_y_then_xl(): got_back = lax.ppermute(acc_back, 'y', to_prev)]
    add x0 -> x7, other arithmetic: none -> 16.2 us  [the longest x3 7.75 us: reduce_scatter_y_then_xl(): acc_ahead = got_ahead + ring_pick(ahead, yi + 2 * ny - 2 - step)]
    dynamic_slice x0 -> x4, local copies, waits for them, and re-layouts: none -> 13.2 us  [ring_pick(): lax.dynamic_index_in_dim(parts, index % parts.shape[0], 0, keepdims=False)]
    slice x0 -> x1, local copies, waits for them, and re-layouts: none -> 12.8 us  [reduce_scatter_y_then_xl(): ahead, back = (parts[:, :, :half], parts[:, :, half:])]
    ppermute x0 -> x7, starting transfers between devices: none -> 11.9 us  [the longest x3 10.2 us: reduce_scatter_y_then_xl(): got_back = lax.ppermute(acc_back, 'y', to_prev)]
    concatenate x0 -> x1, other arithmetic: none -> 11.1 us  [reduce_scatter_y_then_xl(): done = jnp.concatenate([acc_ahead, acc_back], axis=1)]
  transfers between devices with their start and end apart: 6 -> 12, of which waited for: 6 -> 12; matrix products, arithmetic and copies ran while one was open for 0% -> 6% of each run, Pallas kernels for 0% -> 0%
where the time goes in v4:
time: 360 us
  waiting for transfers between devices  225 us (62%)
  local copies, waits for them, and re-layouts  40 us (11%)
  matrix products  32.5 us (9%)
  other arithmetic  30.5 us (8%)
  starting transfers between devices  18.1 us (5%)
  between operations  13.5 us (4%)
    ppermute x3, waiting for transfers between devices, reduce_scatter_y_then_xl(): got_back = lax.ppermute(acc_back, 'y', to_prev)  88.6 us
    ppermute x1, waiting for transfers between devices, local(): lax.ppermute(amplitudes, 'xh', SWAP)  52.1 us
    ppermute x1, waiting for transfers between devices, reduce_scatter_y_then_xl(): return mine + lax.ppermute(other, 'xl', SWAP)  33.1 us
    dot_general x1, matrix products, local(): lax.dot_general(gathered, amp, (((2, 3), (0, 1)), ((), ())), preferred_el...  32.5 us
    all_gather x1, waiting for transfers between devices, local(): gathered = lax.all_gather(own_owners, 'z', axis=1, tiled=True)  16.4 us
    ppermute x1, waiting for transfers between devices, local(): recv = lax.ppermute(summed[:, width:], 'xh', SWAP)  15.7 us
    dynamic_slice x4, local copies, waits for them, and re-layouts, ring_pick(): lax.dynamic_index_in_dim(parts, index % parts.shape[0], 0, keepdims=False)  13.2 us
    slice x1, local copies, waits for them, and re-layouts, reduce_scatter_y_then_xl(): ahead, back = (parts[:, :, :half], parts[:, :, half:])  12.8 us
  transfers between devices with their start and end apart: 12, of which 12 were waited for; matrix products, arithmetic and copies ran while one was open for 6% of the time, Pallas kernels for 0%

profile of v4, /device:TPU:0, one launch (start us, length us, event | category | flops | bytes accessed | tf_op | source)
XLA Modules:
  0.0 360.1 jit_solution(7916616867160049844)
XLA Ops:
  6.5 0.0 all-gather.2.cloned.1.call-start
  6.5 0.7 dynamic_slice.41
  7.3 1.2 sort.17
  8.5 0.1 reshape.12
  8.6 0.2 dynamic-slice_reduce_fusion.1
  8.9 2.6 reshape.11
  11.4 0.6 gather_fusion.1
  12.1 0.2 broadcast_select_fusion
  12.3 1.1 copy.4
  13.4 0.0 collective-permute-start
  13.4 0.6 gather_fusion
  14.0 0.2 select_bitcast_fusion
  14.2 2.1 collective-permute-done
  16.3 1.4 copy.35
  17.7 0.2 pad_maximum_fusion
  18.0 0.0 copy-start.2
  18.0 1.7 copy.6
  19.7 0.0 all-gather.2.cloned.1.call-update
  19.7 0.7 copy-done.2
  20.4 3.1 collective-permute-start.1
  23.6 1.7 constant_dynamic-update-slice_fusion.1
  25.2 52.1 %collective-permute-done.1 = bf16[1200,1024]{1,0:T(8,128)(2,1)S(1)} collective-permute-done((bf16[1200,1024]{1,0:T(8,128)(2,1)S(1)}, bf16[1200,1024]{1,0:T(8,128)(2,1)S(1)}, u32[]{:S(2)}, u32[]{:S(2)}) %collective-permute-start.1) | collective-permute-done | bytes 2457632 | tf_op jit(solution)/shard_map/ppermute | solution.py:59
  77.3 1.8 constant_dynamic-update-slice_fusion
  79.1 0.0 collective-permute-start.2
  79.1 8.5 %collective-permute-done.2 = bf16[1200,2048]{1,0:T(8,128)(2,1)} collective-permute-done((bf16[1200,2048]{1,0:T(8,128)(2,1)}, bf16[1200,2048]{1,0:T(8,128)(2,1)}, u32[]{:S(2)}, u32[]{:S(2)}) %collective-permute-start.2) | collective-permute-done | bytes 4915232 | tf_op jit(solution)/shard_map/ppermute | solution.py:60
  87.6 16.4 %all-gather.2.cloned.1.call-done = bf16[8,200,2,1200]{3,0,2,1:T(8,128)(2,1)} async-done(((bf16[8,50,2,1200]{3,0,2,1:T(8,128)(2,1)}), bf16[8,200,2,1200]{3,0,2,1:T(8,128)(2,1)}) %all-gather.2.cloned.1.call-update) | async-done | bytes 7680016 | tf_op jit(solution)/shard_map/all_gather | solution.py:57
  104.0 32.5 %fusion = f32[8,200,2048,1]{2,1,3,0:T(8,128)} fusion(bf16[1,1200,2048]{2,1,0:T(8,128)(2,1)} %bitcast.4, bf16[1,1200,2048]{2,1,0:T(8,128)(2,1)} %bitcast.3, bf16[8,200,2,1200]{3,0,2,1:T(8,128)(2,1)} %all-gather.2.cloned.1.call-done), kind=kOutput, calls=%fused_computation.3 | convolution fusion | flops 15733555200 | bytes 30617600 | tf_op jit(solution)/shard_map/dot_general | solution.py:62
  136.5 12.8 %fusion.7 = (f32[4,2,100,2048]{3,2,1,0:T(8,128)}, f32[4,2,100,2048]{3,2,1,0:T(8,128)}) fusion(f32[4,2,200,2048]{3,2,1,0:T(8,128)} %bitcast.38), kind=kLoop, calls=%fused_computation.47 | loop fusion | bytes 26214400 | tf_op jit(solution)/shard_map/slice | solution.py:25
  149.3 4.7 %constant_dynamic-slice_fusion = (f32[1,2,100,2048]{3,2,1,0:T(8,128)S(1)}, f32[1,2,100,2048]{3,2,1,0:T(8,128)S(1)}, f32[1,2,100,2048]{3,2,1,0:T(8,128)}, f32[1,2,100,2048]{3,2,1,0:T(8,128)S(1)}) fusion(f32[4,2,100,2048]{3,2,1,0:T(8,128)} %get-tuple-element.10, s32[]{:T(128)S(6)} %select_n.94, s32[]{:T(128)S(6)} %select_n.88, s32[]{:T(128)S(6)} %select_n.98, ...), kind=kLoop, calls=%fused_computation.34 | loop fusion | bytes 13107216 | tf_op jit(solution)/shard_map/jit(dynamic_index_in_dim)/dynamic_slice | solution.py:14
  154.1 2.4 copy.33
  156.5 2.7 collective-permute-start.6
  159.3 4.8 %constant_dynamic-slice_fusion.4 = (f32[1,2,100,2048]{3,2,1,0:T(8,128)}, f32[1,2,100,2048]{3,2,1,0:T(8,128)S(1)}, f32[1,2,100,2048]{3,2,1,0:T(8,128)S(1)}, f32[1,2,100,2048]{3,2,1,0:T(8,128)S(1)}) fusion(f32[4,2,100,2048]{3,2,1,0:T(8,128)} %get-tuple-element.11, s32[]{:T(128)S(6)} %select_n.94, s32[]{:T(128)S(6)} %select_n.92, s32[]{:T(128)S(6)} %select_n.90, ...), kind=kLoop, calls=%fused_computation.38 | loop fusion | bytes 13107216 | tf_op jit(solution)/shard_map/jit(dynamic_index_in_dim)/dynamic_slice | solution.py:14
  164.0 0.0 copy-start
  164.0 1.3 copy.34
  165.3 0.1 collective-permute-start.3
  165.4 29.1 %collective-permute-done.6 = f32[2,100,2048]{2,0,1:T(2,128)} collective-permute-done((f32[2,100,2048]{2,0,1:T(2,128)}, f32[2,100,2048]{2,0,1:T(2,128)}, u32[]{:S(2)}, u32[]{:S(2)}) %collective-permute-start.6) | collective-permute-done | bytes 1638432 | tf_op jit(solution)/shard_map/ppermute | solution.py:32
  194.5 0.0 copy-done
  194.5 3.1 bitcast_add_fusion.3
  197.6 3.8 %collective-permute-start.7 = (f32[2,100,2048]{2,0,1:T(2,128)S(1)}, f32[2,100,2048]{2,0,1:T(2,128)S(1)}, u32[]{:S(2)}, u32[]{:S(2)}) collective-permute-start(f32[2,100,2048]{2,0,1:T(2,128)S(1)} %bitcast_add_fusion.3), channel_id=1, source_target_pairs={{0,12},{4,0},{8,4},{12,8},{1,13},{5,1},{9,5},{13,9},{2,14},{6,2},{... | collective-permute-start | bytes 4915208 | tf_op jit(solution)/shard_map/ppermute | solution.py:32
  201.3 2.3 collective-permute-done.3
  203.7 1.7 bitcast_add_fusion.6
  205.4 0.1 collective-permute-start.4
  205.5 29.9 %collective-permute-done.7 = f32[2,100,2048]{2,0,1:T(2,128)S(1)} collective-permute-done((f32[2,100,2048]{2,0,1:T(2,128)S(1)}, f32[2,100,2048]{2,0,1:T(2,128)S(1)}, u32[]{:S(2)}, u32[]{:S(2)}) %collective-permute-start.7) | collective-permute-done | bytes 1638432 | tf_op jit(solution)/shard_map/ppermute | solution.py:32
  235.4 2.9 bitcast_add_fusion.2
  238.3 3.7 %collective-permute-start.8 = (f32[2,100,2048]{2,0,1:T(2,128)}, f32[2,100,2048]{2,0,1:T(2,128)S(1)}, u32[]{:S(2)}, u32[]{:S(2)}) collective-permute-start(f32[2,100,2048]{2,0,1:T(2,128)} %bitcast_add_fusion.2), channel_id=1, source_target_pairs={{0,12},{4,0},{8,4},{12,8},{1,13},{5,1},{9,5},{13,9},{2,14},{6,2},{... | collective-permute-start | bytes 4915208 | tf_op jit(solution)/shard_map/ppermute | solution.py:32
  242.0 1.0 collective-permute-done.4
  242.9 2.9 bitcast_add_fusion.5
  245.8 0.0 collective-permute-start.5
  245.8 29.6 %collective-permute-done.8 = f32[2,100,2048]{2,0,1:T(2,128)S(1)} collective-permute-done((f32[2,100,2048]{2,0,1:T(2,128)}, f32[2,100,2048]{2,0,1:T(2,128)S(1)}, u32[]{:S(2)}, u32[]{:S(2)}) %collective-permute-start.8) | collective-permute-done | bytes 1638432 | tf_op jit(solution)/shard_map/ppermute | solution.py:32
  275.4 0.0 copy-start.1
  275.5 1.7 bitcast_add_fusion.1
  277.1 5.6 %collective-permute-done.5 = f32[2,100,2048]{2,0,1:T(2,128)} collective-permute-done((f32[2,100,2048]{2,0,1:T(2,128)}, f32[2,100,2048]{2,0,1:T(2,128)}, u32[]{:S(2)}, u32[]{:S(2)}) %collective-permute-start.5) | collective-permute-done | bytes 1638432 | tf_op jit(solution)/shard_map/ppermute | solution.py:31
  282.7 0.0 copy-done.1
  282.7 3.1 bitcast_add_fusion.4
  285.8 11.1 %fusion.5 = (f32[1,200,2048]{2,0,1:T(1,128)S(1)}, f32[1,200,2048]{2,0,1:T(1,128)S(1)}) fusion(s32[]{:T(128)S(6)} %select_n.99, f32[2,100,2048]{2,0,1:T(2,128)S(1)} %bitcast_add_fusion.4, f32[2,100,2048]{2,0,1:T(2,128)S(1)} %bitcast_add_fusion.1, s32[]{:T(128)S(6)} %select_n.100), kind=kLoop, calls=%fused_computation.13 | loop fusion | flops 819200 | bytes 6553608 | tf_op jit(solution)/shard_map/concatenate | solution.py:35
  296.9 0.6 copy.32
  297.6 1.5 collective-permute-start.9
  299.1 33.1 %collective-permute-done.9 = f32[200,2048]{1,0:T(8,128)S(1)} collective-permute-done((f32[200,2048]{1,0:T(8,128)S(1)}, f32[200,2048]{1,0:T(8,128)S(1)}, u32[]{:S(2)}, u32[]{:S(2)}) %collective-permute-start.9) | collective-permute-done | bytes 1638432 | tf_op jit(solution)/shard_map/ppermute | solution.py:38
  332.2 0.8 bitcast_add_fusion
  333.0 0.1 fusion.8
  333.1 3.1 collective-permute-start.10
  336.2 15.7 %collective-permute-done.10 = f32[200,1024]{1,0:T(8,128)S(1)} collective-permute-done((f32[200,1024]{1,0:T(8,128)S(1)}, f32[200,1024]{1,0:T(8,128)S(1)}, u32[]{:S(2)}, u32[]{:S(2)}) %collective-permute-start.10) | collective-permute-done | bytes 819232 | tf_op jit(solution)/shard_map/ppermute | solution.py:68
  351.9 1.3 maximum_select_fusion
  (6 shorter events, 0.0 us)
Async XLA Ops:
  6.5 97.5 %all-gather.2.cloned.1.call-start = ((), (), s32[]{:S(2)}) async-start(), calls=%async_computation | async-start | bytes 10240000 | tf_op jit(solution)/shard_map/all_gather | solution.py:57
  13.4 3.0 collective-permute-start
  18.0 2.4 copy-start.2
  20.4 56.9 %collective-permute-start.1 = (bf16[1200,1024]{1,0:T(8,128)(2,1)S(1)}, bf16[1200,1024]{1,0:T(8,128)(2,1)S(1)}, u32[]{:S(2)}, u32[]{:S(2)}) collective-permute-start(bf16[1200,1024]{1,0:T(8,128)(2,1)S(1)} %copy-done.2), channel_id=1, source_target_pairs={{0,64},{64,0},{1,65},{65,1},{2,66},{66,2},{3,67},{67,3},{4,68},{68... | collective-permute-start | bytes 7372808 | tf_op jit(solution)/shard_map/ppermute | solution.py:59
  79.1 8.5 %collective-permute-start.2 = (bf16[1200,2048]{1,0:T(8,128)(2,1)}, bf16[1200,2048]{1,0:T(8,128)(2,1)}, u32[]{:S(2)}, u32[]{:S(2)}) collective-permute-start(bf16[1200,2048]{1,0:T(8,128)(2,1)} %constant_dynamic-update-slice_fusion), channel_id=1, source_target_pairs={{0,1},{1,0},{2,3},{3,2},{4,5},{5,4},{6,7},{7,6},{8,9},{9,8},{10,11... | collective-permute-start | bytes 14745608 | tf_op jit(solution)/shard_map/ppermute | solution.py:60
  156.5 38.0 %collective-permute-start.6 = (f32[2,100,2048]{2,0,1:T(2,128)}, f32[2,100,2048]{2,0,1:T(2,128)}, u32[]{:S(2)}, u32[]{:S(2)}) collective-permute-start(f32[2,100,2048]{2,0,1:T(2,128)} %bitcast.35), channel_id=1, source_target_pairs={{0,12},{4,0},{8,4},{12,8},{1,13},{5,1},{9,5},{13,9},{2,14},{6,2},{... | collective-permute-start | bytes 4915208 | tf_op jit(solution)/shard_map/ppermute | solution.py:32
  164.0 30.4 %copy-start = (f32[1,2,100,2048]{3,2,1,0:T(8,128)S(1)}, f32[1,2,100,2048]{3,2,1,0:T(8,128)}, u32[]{:S(2)}) copy-start(f32[1,2,100,2048]{3,2,1,0:T(8,128)} %get-tuple-element.14) | copy-start | bytes 4915204
  165.3 38.4 %collective-permute-start.3 = (f32[2,100,2048]{2,0,1:T(2,128)S(1)}, f32[2,100,2048]{2,0,1:T(2,128)S(1)}, u32[]{:S(2)}, u32[]{:S(2)}) collective-permute-start(f32[2,100,2048]{2,0,1:T(2,128)S(1)} %bitcast.41), channel_id=1, source_target_pairs={{0,4},{4,8},{8,12},{12,0},{1,5},{5,9},{9,13},{13,1},{2,6},{6,10},{... | collective-permute-start | bytes 4915208 | tf_op jit(solution)/shard_map/ppermute | solution.py:31
  197.6 37.8 %collective-permute-start.7 = (f32[2,100,2048]{2,0,1:T(2,128)S(1)}, f32[2,100,2048]{2,0,1:T(2,128)S(1)}, u32[]{:S(2)}, u32[]{:S(2)}) collective-permute-start(f32[2,100,2048]{2,0,1:T(2,128)S(1)} %bitcast_add_fusion.3), channel_id=1, source_target_pairs={{0,12},{4,0},{8,4},{12,8},{1,13},{5,1},{9,5},{13,9},{2,14},{6,2},{... | collective-permute-start | bytes 4915208 | tf_op jit(solution)/shard_map/ppermute | solution.py:32
  205.4 37.5 %collective-permute-start.4 = (f32[2,100,2048]{2,0,1:T(2,128)S(1)}, f32[2,100,2048]{2,0,1:T(2,128)S(1)}, u32[]{:S(2)}, u32[]{:S(2)}) collective-permute-start(f32[2,100,2048]{2,0,1:T(2,128)S(1)} %bitcast_add_fusion.6), channel_id=1, source_target_pairs={{0,4},{4,8},{8,12},{12,0},{1,5},{5,9},{9,13},{13,1},{2,6},{6,10},{... | collective-permute-start | bytes 4915208 | tf_op jit(solution)/shard_map/ppermute | solution.py:31
  238.3 37.2 %collective-permute-start.8 = (f32[2,100,2048]{2,0,1:T(2,128)}, f32[2,100,2048]{2,0,1:T(2,128)S(1)}, u32[]{:S(2)}, u32[]{:S(2)}) collective-permute-start(f32[2,100,2048]{2,0,1:T(2,128)} %bitcast_add_fusion.2), channel_id=1, source_target_pairs={{0,12},{4,0},{8,4},{12,8},{1,13},{5,1},{9,5},{13,9},{2,14},{6,2},{... | collective-permute-start | bytes 4915208 | tf_op jit(solution)/shard_map/ppermute | solution.py:32
  245.8 36.9 %collective-permute-start.5 = (f32[2,100,2048]{2,0,1:T(2,128)}, f32[2,100,2048]{2,0,1:T(2,128)}, u32[]{:S(2)}, u32[]{:S(2)}) collective-permute-start(f32[2,100,2048]{2,0,1:T(2,128)} %bitcast_add_fusion.5), channel_id=1, source_target_pairs={{0,4},{4,8},{8,12},{12,0},{1,5},{5,9},{9,13},{13,1},{2,6},{6,10},{... | collective-permute-start | bytes 4915208 | tf_op jit(solution)/shard_map/ppermute | solution.py:31
  275.4 7.3 %copy-start.1 = (f32[1,2,100,2048]{3,2,1,0:T(8,128)S(1)}, f32[1,2,100,2048]{3,2,1,0:T(8,128)}, u32[]{:S(2)}) copy-start(f32[1,2,100,2048]{3,2,1,0:T(8,128)} %get-tuple-element.16) | copy-start | bytes 4915204
  297.6 34.6 %collective-permute-start.9 = (f32[200,2048]{1,0:T(8,128)S(1)}, f32[200,2048]{1,0:T(8,128)S(1)}, u32[]{:S(2)}, u32[]{:S(2)}) collective-permute-start(f32[200,2048]{1,0:T(8,128)S(1)} %bitcast.42), channel_id=1, source_target_pairs={{0,2},{2,0},{1,3},{3,1},{4,6},{6,4},{5,7},{7,5},{8,10},{10,8},{9,1... | collective-permute-start | bytes 4915208 | tf_op jit(solution)/shard_map/ppermute | solution.py:38
  333.1 18.8 %collective-permute-start.10 = (f32[200,1024]{1,0:T(8,128)S(1)}, f32[200,1024]{1,0:T(8,128)S(1)}, u32[]{:S(2)}, u32[]{:S(2)}) collective-permute-start(f32[200,1024]{1,0:T(8,128)S(1)} %get-tuple-element.23), channel_id=1, source_target_pairs={{0,64},{64,0},{1,65},{65,1},{2,66},{66,2},{3,67},{67,3},{4,68},{68... | collective-permute-start | bytes 2457608 | tf_op jit(solution)/shard_map/ppermute | solution.py:68
Sparse Core Ops, SparseCore 0:
  19.8 84.1 all-gather.1

commit v5 on v3

--- a/solution.py
+++ b/solution.py
@@ -12,10 +12,14 @@
 
 def local(amplitudes, integrals, owner):
     nz = lax.axis_size("z")
+    ny = lax.axis_size("y")
+    nxl = lax.axis_size("xl")
     kc = integrals.shape[0]
     width = amplitudes.shape[1]
     tiles_slab = integrals.shape[1] // TB
     xh = lax.axis_index("xh")
+    yi = lax.axis_index("y")
+    xi = lax.axis_index("xl")
     core = lax.axis_index("c")
     slab = xh * nz + lax.axis_index("z")
 
@@ -27,22 +31,40 @@
     from_sibling = lax.ppermute(theirs, "c", SWAP)
     own_owners = jnp.stack([mine, from_sibling], axis=2)
     gathered = lax.all_gather(own_owners, "z", axis=1, tiled=True)
+    rows = gathered.shape[1]
+    half = rows // 2
+    by_y = gathered.reshape(ny, nxl, rows, 2, kc)
 
     amp = jnp.concatenate([amplitudes, lax.ppermute(amplitudes, "xh", SWAP)], axis=1)
     amp = jnp.stack([amp, lax.ppermute(amp, "c", SWAP)], axis=0)
 
-    partial = lax.dot_general(
-        gathered, amp, (((2, 3), (0, 1)), ((), ())), preferred_element_type=jnp.float32
-    )
-    partial = partial.reshape(-1, partial.shape[-1])
-    summed = lax.psum_scatter(partial, ("y", "xl"), scatter_dimension=0, tiled=True)
-    keep = summed[:, :width]
-    recv = lax.ppermute(summed[:, width:], "xh", SWAP)
-    return jnp.where(
-        xh == 0,
-        jnp.concatenate([keep, recv], axis=0),
-        jnp.concatenate([recv, keep], axis=0),
-    )
+    def block(y_owner, part):
+        lhs = lax.dynamic_index_in_dim(by_y, y_owner % ny, 0, keepdims=False)
+        lhs = lhs[:, part * half : (part + 1) * half]
+        return lax.dot_general(
+            lhs, amp, (((2, 3), (0, 1)), ((), ())), preferred_element_type=jnp.float32
+        )
+
+    to_next = [(i, (i + 1) % ny) for i in range(ny)]
+    to_prev = [(i, (i - 1) % ny) for i in range(ny)]
+    acc_ahead = block(yi + ny - 1, 0)
+    acc_back = block(yi + 1, 1)
+    for step in range(ny - 1):
+        got_ahead = lax.ppermute(acc_ahead, "y", to_next)
+        got_back = lax.ppermute(acc_back, "y", to_prev)
+        acc_ahead = got_ahead + block(yi + 2 * ny - 2 - step, 0)
+        acc_back = got_back + block(yi + 2 + step, 1)
+
+    kept, came = [], []
+    for acc in (acc_ahead, acc_back):
+        here = lax.dynamic_index_in_dim(acc, xi, 0, keepdims=False)
+        there = lax.dynamic_index_in_dim(acc, 1 - xi, 0, keepdims=False)
+        summed = here + lax.ppermute(there, "xl", SWAP)
+        kept.append(summed[:, :width])
+        came.append(lax.ppermute(summed[:, width:], "xh", SWAP))
+    first = jnp.concatenate(kept + came, axis=0)
+    second = jnp.concatenate(came + kept, axis=0)
+    return jnp.where(xh == 0, first, second)
 
 
 def solution(mesh):

time: 427 us -> 330 us (0.77)
  waiting for transfers between devices: 357 us -> 195 us
  local copies, waits for them, and re-layouts: 14.1 us -> 41.7 us
  starting transfers between devices: 5.93 us -> 23.5 us
  matrix products: 32.5 us -> 48.9 us
    reduce_scatter x1 -> x0, waiting for transfers between devices: 259 us -> none  [local(): lax.psum_scatter(partial, ('y', 'xl'), scatter_dimension=0, tiled=True)]
    ppermute x1 -> x10, waiting for transfers between devices: 18.8 us -> 116 us  [the longest x3 80.1 us: local(): got_back = lax.ppermute(acc_back, 'y', to_prev)]
    ppermute x1 -> x10, starting transfers between devices: 2.75 us -> 20.3 us  [the longest x3 10.5 us: local(): got_back = lax.ppermute(acc_back, 'y', to_prev)]
    dot_general x1 -> x8, matrix products: 32.5 us -> 48.9 us  [block(): lax.dot_general(lhs, amp, (((2, 3), (0, 1)), ((), ())), preferred_element...]
    all_gather x1, waiting for transfers between devices: 15.8 us -> 25 us  [local(): gathered = lax.all_gather(own_owners, 'z', axis=1, tiled=True)]
    reshape x0 -> x1, local copies, waits for them, and re-layouts: none -> 9.2 us  [local(): by_y = gathered.reshape(ny, nxl, rows, 2, kc)]
    squeeze x0 -> x3, local copies, waits for them, and re-layouts: none -> 8.66 us  [the longest x1 8.54 us: block(): lhs = lax.dynamic_index_in_dim(by_y, y_owner % ny, 0, keepdims=False)]
    ppermute x1, waiting for transfers between devices: 8.32 us -> 0.01 us  [local(): amp = jnp.stack([amp, lax.ppermute(amp, 'c', SWAP)], axis=0)]
  transfers between devices with their start and end apart: 6 -> 14, of which waited for: 6 -> 11; matrix products, arithmetic and copies ran while one was open for 0% -> 23% of each run, Pallas kernels for 0% -> 0%
where the time goes in v5:
time: 330 us; the launch traced here: 329 us
  waiting for transfers between devices  195 us (59%)
  matrix products  48.9 us (15%)
  local copies, waits for them, and re-layouts  41.7 us (13%)
  starting transfers between devices  23.5 us (7%)
  between operations  13.7 us (4%)
  other arithmetic  5.77 us (2%)
    ppermute x3, waiting for transfers between devices, local(): got_back = lax.ppermute(acc_back, 'y', to_prev)  80.1 us
    ppermute x1, waiting for transfers between devices, local(): lax.ppermute(amplitudes, 'xh', SWAP)  52.1 us
    dot_general x8, matrix products, block(): lax.dot_general(lhs, amp, (((2, 3), (0, 1)), ((), ())), preferred_element...  48.9 us
    all_gather x1, waiting for transfers between devices, local(): gathered = lax.all_gather(own_owners, 'z', axis=1, tiled=True)  25 us
    ppermute x2, waiting for transfers between devices, local(): summed = here + lax.ppermute(there, 'xl', SWAP)  21.7 us
    ppermute x2, waiting for transfers between devices, local(): came.append(lax.ppermute(summed[:, width:], 'xh', SWAP))  12 us
    ppermute x3, starting transfers between devices, local(): got_back = lax.ppermute(acc_back, 'y', to_prev)  10.5 us
    reshape x1, local copies, waits for them, and re-layouts, local(): by_y = gathered.reshape(ny, nxl, rows, 2, kc)  9.2 us
  transfers between devices with their start and end apart: 14, of which 11 were waited for; matrix products, arithmetic and copies ran while one was open for 23% of the time, Pallas kernels for 0%

profile of v5, /device:TPU:0, one launch (start us, length us, event | category | flops | bytes accessed | tf_op | source)
XLA Modules:
  0.0 328.9 jit_solution(4308015608589769059)
XLA Ops:
  6.5 2.6 reshape.14
  9.2 0.1 dynamic_slice.43
  9.2 1.2 sort.17
  10.5 0.1 reshape.15
  10.6 0.2 dynamic-slice_reduce_fusion.1
  10.8 0.6 gather_fusion.1
  11.5 0.2 broadcast_select_fusion
  11.6 1.1 copy.11
  12.8 0.0 collective-permute-start
  12.8 0.6 gather_fusion
  13.4 0.2 select_bitcast_fusion
  13.6 2.1 collective-permute-done
  15.7 1.4 copy.48
  17.1 0.2 pad_maximum_fusion
  17.4 0.0 copy-start
  17.4 1.7 copy.13
  19.1 0.0 all-gather.2.cloned.1.call-update
  19.1 0.7 copy-done
  19.8 3.1 collective-permute-start.1
  22.9 1.7 constant_dynamic-update-slice_fusion.1
  24.6 52.1 %collective-permute-done.1 = bf16[1200,1024]{1,0:T(8,128)(2,1)S(1)} collective-permute-done((bf16[1200,1024]{1,0:T(8,128)(2,1)S(1)}, bf16[1200,1024]{1,0:T(8,128)(2,1)S(1)}, u32[]{:S(2)}, u32[]{:S(2)}) %collective-permute-start.1) | collective-permute-done | bytes 2457632 | tf_op jit(solution)/shard_map/ppermute | solution.py:38
  76.7 1.7 constant_dynamic-update-slice_fusion
  78.4 25.0 %all-gather.2.cloned.1.call-done = bf16[8,200,2,1200]{3,0,2,1:T(8,128)(2,1)} async-done(((bf16[8,50,2,1200]{3,0,2,1:T(8,128)(2,1)}), bf16[8,200,2,1200]{3,0,2,1:T(8,128)(2,1)}) %all-gather.2.cloned.1.call-update) | async-done | bytes 7680016 | tf_op jit(solution)/shard_map/all_gather | solution.py:33
  103.4 9.2 %copy.40 = bf16[8,200,2,1200]{3,1,2,0:T(8,128)(2,1)} copy(bf16[8,200,2,1200]{3,0,2,1:T(8,128)(2,1)} %all-gather.2.cloned.1.call-done) | data formatting | bytes 15360000 | tf_op jit(solution)/shard_map/reshape | solution.py:36
  112.6 8.5 %dynamic-slice_bitcast_fusion.3 = (bf16[2,200,2,1200]{3,1,2,0:T(8,128)(2,1)}, bf16[2,200,2,1200]{3,1,2,0:T(8,128)(2,1)}, bf16[2,200,2,1200]{3,1,2,0:T(8,128)(2,1...) fusion(bf16[4,2,200,2,1200]{4,2,3,1,0:T(8,128)(2,1)} %bitcast.75, ...), kind=kLoop, calls=%fused_computation.15 | loop fusion | bytes 23040024 | tf_op jit(solution)/shard_map/jit(dynamic_index_in_dim)/squeeze | solution.py:42
  121.1 5.6 %convolution_bitcast_fusion.3 = f32[2,100,2048]{2,1,0:T(8,128)S(1)} fusion(bf16[2,200,2,1200]{3,1,2,0:T(8,128)(2,1)} %get-tuple-element.12, bf16[1,1200,2048]{2,1,0:T(8,128)(2,1)} %bitcast.5, bf16[1,1200,2048]{2,1,0:T(8,128)(2,1)} %bitcast.4), kind=kOutput, calls=%fused_computation.6 | convolution fusion | flops 1970995200 | bytes 12533760 | tf_op jit(solution)/shard_map/dot_general | solution.py:44
  126.7 1.3 copy.25
  128.0 3.0 collective-permute-start.7
  131.0 5.2 %convolution_bitcast_fusion.7 = f32[2,100,2048]{2,1,0:T(8,128)S(1)} fusion(bf16[2,200,2,1200]{3,1,2,0:T(8,128)(2,1)S(1)} %copy-done.2, bf16[1,1200,2048]{2,1,0:T(8,128)(2,1)} %bitcast.5, bf16[1,1200,2048]{2,1,0:T(8,128)(2,1)} %bitcast.4), kind=kOutput, calls=%fused_computation.10 | convolution fusion | flops 1970995200 | bytes 12533760 | tf_op jit(solution)/shard_map/dot_general | solution.py:44
  136.2 1.3 copy.15
  137.5 0.1 collective-permute-start.3
  137.6 28.3 %collective-permute-done.7 = f32[2,100,2048]{2,0,1:T(2,128)S(1)} collective-permute-done((f32[2,100,2048]{2,0,1:T(2,128)S(1)}, f32[2,100,2048]{2,0,1:T(2,128)S(1)}, u32[]{:S(2)}, u32[]{:S(2)}) %collective-permute-start.7) | collective-permute-done | bytes 1638432 | tf_op jit(solution)/shard_map/ppermute | solution.py:54
  165.9 5.8 %copy_add_fusion.2 = f32[2,100,2048]{2,1,0:T(8,128)S(1)} fusion(f32[2,100,2048]{2,0,1:T(2,128)S(1)} %collective-permute-done.7, bf16[2,200,2,1200]{3,1,2,0:T(8,128)(2,1)S(1)} %copy-done.4, bf16[1,1200,2048]{2,1,0:T(8,128)(2,1)} %bitcast.5, bf16[1,1200,2048]{2,1,0:T(8,128)(2,1)} %bitcast.4), kind=kOutput, calls=%fused_computation.20 | convolution fusion | flops 1971404800 | bytes 14172160 | tf_op jit(solution)/shard_map/dot_general | solution.py:44
  171.7 1.3 copy.28
  173.0 3.8 %collective-permute-start.8 = (f32[2,100,2048]{2,0,1:T(2,128)S(1)}, f32[2,100,2048]{2,0,1:T(2,128)S(1)}, u32[]{:S(2)}, u32[]{:S(2)}) collective-permute-start(f32[2,100,2048]{2,0,1:T(2,128)S(1)} %copy.28), channel_id=1, source_target_pairs={{0,12},{4,0},{8,4},{12,8},{1,13},{5,1},{9,5},{13,9},{2,14},{6,2},{... | collective-permute-start | bytes 4915208 | tf_op jit(solution)/shard_map/ppermute | solution.py:54
  176.8 5.8 %copy_add_fusion.5 = f32[2,100,2048]{2,1,0:T(8,128)S(1)} fusion(f32[2,100,2048]{2,0,1:T(2,128)S(1)} %collective-permute-done.3, bf16[2,200,2,1200]{3,1,2,0:T(8,128)(2,1)S(1)} %copy-done.3, bf16[1,1200,2048]{2,1,0:T(8,128)(2,1)} %bitcast.5, bf16[1,1200,2048]{2,1,0:T(8,128)(2,1)} %bitcast.4), kind=kOutput, calls=%fused_computation.23 | convolution fusion | flops 1971404800 | bytes 14172160 | tf_op jit(solution)/shard_map/dot_general | solution.py:44
  182.6 1.3 copy.18
  183.9 0.3 collective-permute-start.4
  184.2 26.6 %collective-permute-done.8 = f32[2,100,2048]{2,0,1:T(2,128)S(1)} collective-permute-done((f32[2,100,2048]{2,0,1:T(2,128)S(1)}, f32[2,100,2048]{2,0,1:T(2,128)S(1)}, u32[]{:S(2)}, u32[]{:S(2)}) %collective-permute-start.8) | collective-permute-done | bytes 1638432 | tf_op jit(solution)/shard_map/ppermute | solution.py:54
  210.8 5.8 %copy_add_fusion.1 = f32[2,100,2048]{2,1,0:T(8,128)S(1)} fusion(f32[2,100,2048]{2,0,1:T(2,128)S(1)} %collective-permute-done.8, bf16[2,200,2,1200]{3,1,2,0:T(8,128)(2,1)S(1)} %copy-done.2, bf16[1,1200,2048]{2,1,0:T(8,128)(2,1)} %bitcast.5, bf16[1,1200,2048]{2,1,0:T(8,128)(2,1)} %bitcast.4), kind=kOutput, calls=%fused_computation.19 | convolution fusion | flops 1971404800 | bytes 14172160 | tf_op jit(solution)/shard_map/dot_general | solution.py:44
  216.6 2.4 copy.30
  219.1 3.7 %collective-permute-start.9 = (f32[2,100,2048]{2,0,1:T(2,128)}, f32[2,100,2048]{2,0,1:T(2,128)}, u32[]{:S(2)}, u32[]{:S(2)}) collective-permute-start(f32[2,100,2048]{2,0,1:T(2,128)} %copy.30), channel_id=1, source_target_pairs={{0,12},{4,0},{8,4},{12,8},{1,13},{5,1},{9,5},{13,9},{2,14},{6,2},{... | collective-permute-start | bytes 4915208 | tf_op jit(solution)/shard_map/ppermute | solution.py:54
  222.8 5.8 %copy_add_fusion.4 = f32[2,100,2048]{2,1,0:T(8,128)S(1)} fusion(f32[2,100,2048]{2,0,1:T(2,128)S(1)} %collective-permute-done.4, bf16[2,200,2,1200]{3,1,2,0:T(8,128)(2,1)S(1)} %copy-done.1, bf16[1,1200,2048]{2,1,0:T(8,128)(2,1)} %bitcast.5, bf16[1,1200,2048]{2,1,0:T(8,128)(2,1)} %bitcast.4), kind=kOutput, calls=%fused_computation.22 | convolution fusion | flops 1971404800 | bytes 14172160 | tf_op jit(solution)/shard_map/dot_general | solution.py:44
  228.6 2.5 copy.21
  231.1 25.2 %collective-permute-done.9 = f32[2,100,2048]{2,0,1:T(2,128)} collective-permute-done((f32[2,100,2048]{2,0,1:T(2,128)}, f32[2,100,2048]{2,0,1:T(2,128)}, u32[]{:S(2)}, u32[]{:S(2)}) %collective-permute-start.9) | collective-permute-done | bytes 1638432 | tf_op jit(solution)/shard_map/ppermute | solution.py:54
  256.2 7.4 %copy_add_fusion = f32[2,100,2048]{2,1,0:T(8,128)S(1)} fusion(f32[2,100,2048]{2,0,1:T(2,128)} %collective-permute-done.9, bf16[2,200,2,1200]{3,1,2,0:T(8,128)(2,1)S(1)} %get-tuple-element.13, bf16[1,1200,2048]{2,1,0:T(8,128)(2,1)} %bitcast.5, bf16[1,1200,2048]{2,1,0:T(8,128)(2,1)} %bitcast.4), kind=kOutput, calls=%fused_computation.18 | convolution fusion | flops 1971404800 | bytes 14172160 | tf_op jit(solution)/shard_map/dot_general | solution.py:44
  263.7 0.1 dynamic-slice_bitcast_fusion.6
  263.8 1.8 collective-permute-start.10
  265.6 2.4 collective-permute-done.5
  267.9 7.4 %copy_add_fusion.3 = f32[2,100,2048]{2,1,0:T(8,128)S(1)} fusion(f32[2,100,2048]{2,0,1:T(2,128)} %collective-permute-done.5, bf16[2,200,2,1200]{3,1,2,0:T(8,128)(2,1)S(1)} %get-tuple-element.13, bf16[1,1200,2048]{2,1,0:T(8,128)(2,1)} %bitcast.5, bf16[1,1200,2048]{2,1,0:T(8,128)(2,1)} %bitcast.4), kind=kOutput, calls=%fused_computation.21 | convolution fusion | flops 1971404800 | bytes 14172160 | tf_op jit(solution)/shard_map/dot_general | solution.py:44
  275.4 1.2 copy-done.5
  276.6 0.1 dynamic-slice_bitcast_fusion.7
  276.6 1.6 collective-permute-start.6
  278.2 7.8 %collective-permute-done.10 = f32[100,2048]{1,0:T(8,128)} collective-permute-done((f32[100,2048]{1,0:T(8,128)S(1)}, f32[100,2048]{1,0:T(8,128)}, u32[]{:S(2)}, u32[]{:S(2)}) %collective-permute-start.10) | collective-permute-done | bytes 819232 | tf_op jit(solution)/shard_map/ppermute | solution.py:62
  286.0 1.2 bitcast_add_fusion
  287.3 0.1 fusion.21
  287.4 3.1 collective-permute-start.12
  290.4 13.9 %collective-permute-done.6 = f32[100,2048]{1,0:T(8,128)} collective-permute-done((f32[100,2048]{1,0:T(8,128)S(1)}, f32[100,2048]{1,0:T(8,128)}, u32[]{:S(2)}, u32[]{:S(2)}) %collective-permute-start.6) | collective-permute-done | bytes 819232 | tf_op jit(solution)/shard_map/ppermute | solution.py:62
  304.3 1.2 bitcast_add_fusion.1
  305.5 0.1 fusion.20
  305.6 3.1 collective-permute-start.11
  308.7 6.8 %collective-permute-done.12 = f32[100,1024]{1,0:T(8,128)S(1)} collective-permute-done((f32[100,1024]{1,0:T(8,128)S(1)}, f32[100,1024]{1,0:T(8,128)S(1)}, u32[]{:S(2)}, u32[]{:S(2)}) %collective-permute-start.12) | collective-permute-done | bytes 409632 | tf_op jit(solution)/shard_map/ppermute | solution.py:64
  315.4 5.2 %collective-permute-done.11 = f32[100,1024]{1,0:T(8,128)S(1)} collective-permute-done((f32[100,1024]{1,0:T(8,128)S(1)}, f32[100,1024]{1,0:T(8,128)S(1)}, u32[]{:S(2)}, u32[]{:S(2)}) %collective-permute-start.11) | collective-permute-done | bytes 409632 | tf_op jit(solution)/shard_map/ppermute | solution.py:64
  320.7 1.4 maximum_select_fusion
  (29 shorter events, 0.1 us)
Async XLA Ops:
  6.5 96.9 %all-gather.2.cloned.1.call-start = ((), (), s32[]{:S(2)}) async-start(), calls=%async_computation | async-start | bytes 10240000 | tf_op jit(solution)/shard_map/all_gather | solution.py:33
  6.5 2.6 copy-start.9
  12.8 3.0 collective-permute-start
  17.4 2.4 copy-start
  19.8 56.9 %collective-permute-start.1 = (bf16[1200,1024]{1,0:T(8,128)(2,1)S(1)}, bf16[1200,1024]{1,0:T(8,128)(2,1)S(1)}, u32[]{:S(2)}, u32[]{:S(2)}) collective-permute-start(bf16[1200,1024]{1,0:T(8,128)(2,1)S(1)} %copy-done), channel_id=1, source_target_pairs={{0,64},{64,0},{1,65},{65,1},{2,66},{66,2},{3,67},{67,3},{4,68},{68... | collective-permute-start | bytes 7372808 | tf_op jit(solution)/shard_map/ppermute | solution.py:38
  78.4 42.7 %collective-permute-start.2 = (bf16[1200,2048]{1,0:T(8,128)(2,1)}, bf16[1200,2048]{1,0:T(8,128)(2,1)}, u32[]{:S(2)}, u32[]{:S(2)}) collective-permute-start(bf16[1200,2048]{1,0:T(8,128)(2,1)} %constant_dynamic-update-slice_fusion), channel_id=1, source_target_pairs={{0,1},{1,0},{2,3},{3,2},{4,5},{5,4},{6,7},{7,6},{8,9},{9,8},{10,11... | collective-permute-start | bytes 14745608 | tf_op jit(solution)/shard_map/ppermute | solution.py:39
  126.7 4.3 %copy-start.2 = (bf16[2,200,2,1200]{3,1,2,0:T(8,128)(2,1)S(1)}, bf16[2,200,2,1200]{3,1,2,0:T(8,128)(2,1)}, u32[]{:S(2)}) copy-start(bf16[2,200,2,1200]{3,1,2,0:T(8,128)(2,1)} %get-tuple-element.15) | copy-start | bytes 5760004
  128.0 37.9 %collective-permute-start.7 = (f32[2,100,2048]{2,0,1:T(2,128)S(1)}, f32[2,100,2048]{2,0,1:T(2,128)S(1)}, u32[]{:S(2)}, u32[]{:S(2)}) collective-permute-start(f32[2,100,2048]{2,0,1:T(2,128)S(1)} %copy.25), channel_id=1, source_target_pairs={{0,12},{4,0},{8,4},{12,8},{1,13},{5,1},{9,5},{13,9},{2,14},{6,2},{... | collective-permute-start | bytes 4915208 | tf_op jit(solution)/shard_map/ppermute | solution.py:54
  136.2 29.7 %copy-start.4 = (bf16[2,200,2,1200]{3,1,2,0:T(8,128)(2,1)S(1)}, bf16[2,200,2,1200]{3,1,2,0:T(8,128)(2,1)}, u32[]{:S(2)}) copy-start(bf16[2,200,2,1200]{3,1,2,0:T(8,128)(2,1)} %get-tuple-element.11) | copy-start | bytes 5760004
  137.5 39.2 %collective-permute-start.3 = (f32[2,100,2048]{2,0,1:T(2,128)S(1)}, f32[2,100,2048]{2,0,1:T(2,128)S(1)}, u32[]{:S(2)}, u32[]{:S(2)}) collective-permute-start(f32[2,100,2048]{2,0,1:T(2,128)S(1)} %copy.15), channel_id=1, source_target_pairs={{0,4},{4,8},{8,12},{12,0},{1,5},{5,9},{9,13},{13,1},{2,6},{6,10},{... | collective-permute-start | bytes 4915208 | tf_op jit(solution)/shard_map/ppermute | solution.py:53
  171.7 5.0 %copy-start.3 = (bf16[2,200,2,1200]{3,1,2,0:T(8,128)(2,1)S(1)}, bf16[2,200,2,1200]{3,1,2,0:T(8,128)(2,1)}, u32[]{:S(2)}) copy-start(bf16[2,200,2,1200]{3,1,2,0:T(8,128)(2,1)} %get-tuple-element.14) | copy-start | bytes 5760004
  173.0 37.8 %collective-permute-start.8 = (f32[2,100,2048]{2,0,1:T(2,128)S(1)}, f32[2,100,2048]{2,0,1:T(2,128)S(1)}, u32[]{:S(2)}, u32[]{:S(2)}) collective-permute-start(f32[2,100,2048]{2,0,1:T(2,128)S(1)} %copy.28), channel_id=1, source_target_pairs={{0,12},{4,0},{8,4},{12,8},{1,13},{5,1},{9,5},{13,9},{2,14},{6,2},{... | collective-permute-start | bytes 4915208 | tf_op jit(solution)/shard_map/ppermute | solution.py:54
  183.9 38.9 %collective-permute-start.4 = (f32[2,100,2048]{2,0,1:T(2,128)S(1)}, f32[2,100,2048]{2,0,1:T(2,128)S(1)}, u32[]{:S(2)}, u32[]{:S(2)}) collective-permute-start(f32[2,100,2048]{2,0,1:T(2,128)S(1)} %copy.18), channel_id=1, source_target_pairs={{0,4},{4,8},{8,12},{12,0},{1,5},{5,9},{9,13},{13,1},{2,6},{6,10},{... | collective-permute-start | bytes 4915208 | tf_op jit(solution)/shard_map/ppermute | solution.py:53
  216.6 6.1 %copy-start.1 = (bf16[2,200,2,1200]{3,1,2,0:T(8,128)(2,1)S(1)}, bf16[2,200,2,1200]{3,1,2,0:T(8,128)(2,1)}, u32[]{:S(2)}) copy-start(bf16[2,200,2,1200]{3,1,2,0:T(8,128)(2,1)} %get-tuple-element.10) | copy-start | bytes 5760004
  219.1 37.2 %collective-permute-start.9 = (f32[2,100,2048]{2,0,1:T(2,128)}, f32[2,100,2048]{2,0,1:T(2,128)}, u32[]{:S(2)}, u32[]{:S(2)}) collective-permute-start(f32[2,100,2048]{2,0,1:T(2,128)} %copy.30), channel_id=1, source_target_pairs={{0,12},{4,0},{8,4},{12,8},{1,13},{5,1},{9,5},{13,9},{2,14},{6,2},{... | collective-permute-start | bytes 4915208 | tf_op jit(solution)/shard_map/ppermute | solution.py:54
  231.1 36.9 %collective-permute-start.5 = (f32[2,100,2048]{2,0,1:T(2,128)}, f32[2,100,2048]{2,0,1:T(2,128)}, u32[]{:S(2)}, u32[]{:S(2)}) collective-permute-start(f32[2,100,2048]{2,0,1:T(2,128)} %copy.21), channel_id=1, source_target_pairs={{0,4},{4,8},{8,12},{12,0},{1,5},{5,9},{9,13},{13,1},{2,6},{6,10},{... | collective-permute-start | bytes 4915208 | tf_op jit(solution)/shard_map/ppermute | solution.py:53
  263.7 1.9 copy-start.7
  263.8 22.3 %collective-permute-start.10 = (f32[100,2048]{1,0:T(8,128)S(1)}, f32[100,2048]{1,0:T(8,128)}, u32[]{:S(2)}, u32[]{:S(2)}) collective-permute-start(f32[100,2048]{1,0:T(8,128)S(1)} %dynamic-slice_bitcast_fusion.6), channel_id=1, source_target_pairs={{0,2},{2,0},{1,3},{3,1},{4,6},{6,4},{5,7},{7,5},{8,10},{10,8},{9,1... | collective-permute-start | bytes 2457608 | tf_op jit(solution)/shard_map/ppermute | solution.py:62
  275.4 1.2 copy-start.5
  276.6 9.5 %copy-start.8 = (f32[2,100,2048]{2,1,0:T(8,128)S(1)}, f32[2,100,2048]{2,1,0:T(8,128)}, u32[]{:S(2)}) copy-start(f32[2,100,2048]{2,1,0:T(8,128)} %copy-done.7) | copy-start | bytes 4915204
  276.6 27.7 %collective-permute-start.6 = (f32[100,2048]{1,0:T(8,128)S(1)}, f32[100,2048]{1,0:T(8,128)}, u32[]{:S(2)}, u32[]{:S(2)}) collective-permute-start(f32[100,2048]{1,0:T(8,128)S(1)} %dynamic-slice_bitcast_fusion.7), channel_id=1, source_target_pairs={{0,2},{2,0},{1,3},{3,1},{4,6},{6,4},{5,7},{7,5},{8,10},{10,8},{9,1... | collective-permute-start | bytes 2457608 | tf_op jit(solution)/shard_map/ppermute | solution.py:62
  278.2 26.1 %copy-start.6 = (f32[2,100,2048]{2,1,0:T(8,128)S(1)}, f32[2,100,2048]{2,1,0:T(8,128)}, u32[]{:S(2)}) copy-start(f32[2,100,2048]{2,1,0:T(8,128)} %copy-done.5) | copy-start | bytes 4915204
  287.4 28.1 %collective-permute-start.12 = (f32[100,1024]{1,0:T(8,128)S(1)}, f32[100,1024]{1,0:T(8,128)S(1)}, u32[]{:S(2)}, u32[]{:S(2)}) collective-permute-start(f32[100,1024]{1,0:T(8,128)S(1)} %get-tuple-element.19), channel_id=1, source_target_pairs={{0,64},{64,0},{1,65},{65,1},{2,66},{66,2},{3,67},{67,3},{4,68},{68... | collective-permute-start | bytes 1228808 | tf_op jit(solution)/shard_map/ppermute | solution.py:64
  305.6 15.1 %collective-permute-start.11 = (f32[100,1024]{1,0:T(8,128)S(1)}, f32[100,1024]{1,0:T(8,128)S(1)}, u32[]{:S(2)}, u32[]{:S(2)}) collective-permute-start(f32[100,1024]{1,0:T(8,128)S(1)} %get-tuple-element.17), channel_id=1, source_target_pairs={{0,64},{64,0},{1,65},{65,1},{2,66},{66,2},{3,67},{67,3},{4,68},{68... | collective-permute-start | bytes 1228808 | tf_op jit(solution)/shard_map/ppermute | solution.py:64
Sparse Core Ops, SparseCore 0:
  19.2 84.1 all-gather.1

commit v6 on v5

--- a/solution.py
+++ b/solution.py
@@ -41,9 +41,10 @@
     def block(y_owner, part):
         lhs = lax.dynamic_index_in_dim(by_y, y_owner % ny, 0, keepdims=False)
         lhs = lhs[:, part * half : (part + 1) * half]
-        return lax.dot_general(
+        product = lax.dot_general(
             lhs, amp, (((2, 3), (0, 1)), ((), ())), preferred_element_type=jnp.float32
         )
+        return lax.optimization_barrier(product)
 
     to_next = [(i, (i + 1) % ny) for i in range(ny)]
     to_prev = [(i, (i - 1) % ny) for i in range(ny)]

time: 330 us -> 314 us (0.952)
  waiting for transfers between devices: 195 us -> 181 us
  matrix products: 48.9 us -> 42.4 us
  other arithmetic: 5.77 us -> 11.7 us
    ppermute x3, waiting for transfers between devices: 80.1 us -> 50.8 us  [local(): got_back = lax.ppermute(acc_back, 'y', to_prev)]
    ppermute x3, waiting for transfers between devices: 2.36 us -> 14.2 us  [local(): got_ahead = lax.ppermute(acc_ahead, 'y', to_next)]
    dot_general x8, matrix products: 48.9 us -> 42.4 us  [block(): lax.dot_general(lhs, amp, (((2, 3), (0, 1)), ((), ())), preferred_element...]
    add x0 -> x6, other arithmetic: none -> 5.9 us  [the longest x3 2.95 us: local(): acc_back = got_back + block(yi + 2 + step, 1)]
  transfers between devices with their start and end apart: 14 -> 14, of which waited for: 11 -> 13; matrix products, arithmetic and copies ran while one was open for 23% -> 24% of each run, Pallas kernels for 0% -> 0%
where the time goes in v6:
time: 314 us; the launch traced here: 313 us
  waiting for transfers between devices  181 us (58%)
  matrix products  42.4 us (14%)
  local copies, waits for them, and re-layouts  40.9 us (13%)
  starting transfers between devices  23.2 us (7%)
  between operations  13.7 us (4%)
  other arithmetic  11.7 us (4%)
    ppermute x1, waiting for transfers between devices, local(): lax.ppermute(amplitudes, 'xh', SWAP)  52 us
    ppermute x3, waiting for transfers between devices, local(): got_back = lax.ppermute(acc_back, 'y', to_prev)  50.8 us
    dot_general x8, matrix products, block(): lax.dot_general(lhs, amp, (((2, 3), (0, 1)), ((), ())), preferred_element...  42.4 us
    all_gather x1, waiting for transfers between devices, local(): gathered = lax.all_gather(own_owners, 'z', axis=1, tiled=True)  25 us
    ppermute x2, waiting for transfers between devices, local(): summed = here + lax.ppermute(there, 'xl', SWAP)  24.8 us
    ppermute x3, waiting for transfers between devices, local(): got_ahead = lax.ppermute(acc_ahead, 'y', to_next)  14.2 us
    ppermute x2, waiting for transfers between devices, local(): came.append(lax.ppermute(summed[:, width:], 'xh', SWAP))  12 us
    ppermute x3, starting transfers between devices, local(): got_back = lax.ppermute(acc_back, 'y', to_prev)  10.5 us
  transfers between devices with their start and end apart: 14, of which 13 were waited for; matrix products, arithmetic and copies ran while one was open for 24% of the time, Pallas kernels for 0%

profile of v6, /device:TPU:0, one launch (start us, length us, event | category | flops | bytes accessed | tf_op | source)
XLA Modules:
  0.0 312.8 jit_solution(15622687653534027881)
XLA Ops:
  6.5 0.7 dynamic_slice.43
  7.3 1.2 sort.17
  8.6 0.2 dynamic-slice_reduce_fusion.1
  8.9 2.6 reshape.14
  11.4 0.6 gather_fusion.1
  12.1 0.2 broadcast_select_fusion
  12.3 1.1 copy.11
  13.4 0.6 gather_fusion
  14.2 2.1 collective-permute-done
  16.3 1.4 copy.48
  17.7 0.2 pad_maximum_fusion
  18.0 1.7 copy.13
  19.8 0.7 copy-done
  20.4 3.1 %collective-permute-start.1 = (bf16[1200,1024]{1,0:T(8,128)(2,1)S(1)}, bf16[1200,1024]{1,0:T(8,128)(2,1)S(1)}, u32[]{:S(2)}, u32[]{:S(2)}) collective-permute-start(bf16[1200,1024]{1,0:T(8,128)(2,1)S(1)} %copy-done), channel_id=1, source_target_pairs={{0,64},{64,0},{1,65},{65,1},{2,66},{66,2},{3,67},{67,3},{4,68},{68... | collective-permute-start | bytes 7372808 | tf_op jit(solution)/shard_map/ppermute | solution.py:38
  23.6 1.7 constant_dynamic-update-slice_fusion.1
  25.3 52.0 %collective-permute-done.1 = bf16[1200,1024]{1,0:T(8,128)(2,1)S(1)} collective-permute-done((bf16[1200,1024]{1,0:T(8,128)(2,1)S(1)}, bf16[1200,1024]{1,0:T(8,128)(2,1)S(1)}, u32[]{:S(2)}, u32[]{:S(2)}) %collective-permute-start.1) | collective-permute-done | bytes 2457632 | tf_op jit(solution)/shard_map/ppermute | solution.py:38
  77.3 1.7 constant_dynamic-update-slice_fusion
  79.0 25.0 %all-gather.2.cloned.1.call-done = bf16[8,200,2,1200]{3,0,2,1:T(8,128)(2,1)} async-done(((bf16[8,50,2,1200]{3,0,2,1:T(8,128)(2,1)}), bf16[8,200,2,1200]{3,0,2,1:T(8,128)(2,1)}) %all-gather.2.cloned.1.call-update) | async-done | bytes 7680016 | tf_op jit(solution)/shard_map/all_gather | solution.py:33
  104.1 9.2 %copy.40 = bf16[8,200,2,1200]{3,1,2,0:T(8,128)(2,1)} copy(bf16[8,200,2,1200]{3,0,2,1:T(8,128)(2,1)} %all-gather.2.cloned.1.call-done) | data formatting | bytes 15360000 | tf_op jit(solution)/shard_map/reshape | solution.py:36
  113.3 8.5 %dynamic-slice_bitcast_fusion.4 = (bf16[2,200,2,1200]{3,1,2,0:T(8,128)(2,1)}, bf16[2,200,2,1200]{3,1,2,0:T(8,128)(2,1)}, bf16[2,200,2,1200]{3,1,2,0:T(8,128)(2,1...) fusion(bf16[4,2,200,2,1200]{4,2,3,1,0:T(8,128)(2,1)} %bitcast.63, ...), kind=kLoop, calls=%fused_computation.16 | loop fusion | bytes 23040024 | tf_op jit(solution)/shard_map/jit(dynamic_index_in_dim)/squeeze | solution.py:42
  121.8 5.5 %convolution_bitcast_fusion.3 = f32[2,100,2048]{2,1,0:T(8,128)S(1)} fusion(bf16[2,200,2,1200]{3,1,2,0:T(8,128)(2,1)} %get-tuple-element.12, bf16[1,1200,2048]{2,1,0:T(8,128)(2,1)} %bitcast.5, bf16[1,1200,2048]{2,1,0:T(8,128)(2,1)} %bitcast.4), kind=kOutput, calls=%fused_computation.6 | convolution fusion | flops 1970995200 | bytes 12533760 | tf_op jit(solution)/shard_map/dot_general | solution.py:44
  127.4 1.3 copy.25
  128.6 3.0 collective-permute-start.7
  131.6 5.2 %convolution_bitcast_fusion.7 = f32[2,100,2048]{2,1,0:T(8,128)S(1)} fusion(bf16[2,200,2,1200]{3,1,2,0:T(8,128)(2,1)S(1)} %copy-done.1, bf16[1,1200,2048]{2,1,0:T(8,128)(2,1)} %bitcast.5, bf16[1,1200,2048]{2,1,0:T(8,128)(2,1)} %bitcast.4), kind=kOutput, calls=%fused_computation.10 | convolution fusion | flops 1970995200 | bytes 12533760 | tf_op jit(solution)/shard_map/dot_general | solution.py:44
  136.9 1.3 copy.15
  138.2 0.2 copy-done.4
  138.4 5.4 %convolution_bitcast_fusion.2 = f32[2,100,2048]{2,1,0:T(8,128)S(1)} fusion(bf16[2,200,2,1200]{3,1,2,0:T(8,128)(2,1)S(1)} %copy-done.4, bf16[1,1200,2048]{2,1,0:T(8,128)(2,1)} %bitcast.5, bf16[1,1200,2048]{2,1,0:T(8,128)(2,1)} %bitcast.4), kind=kOutput, calls=%fused_computation.5 | convolution fusion | flops 1970995200 | bytes 12533760 | tf_op jit(solution)/shard_map/dot_general | solution.py:44
  143.8 5.2 %convolution_bitcast_fusion.6 = f32[2,100,2048]{2,1,0:T(8,128)S(1)} fusion(bf16[2,200,2,1200]{3,1,2,0:T(8,128)(2,1)S(1)} %copy-done.3, bf16[1,1200,2048]{2,1,0:T(8,128)(2,1)} %bitcast.5, bf16[1,1200,2048]{2,1,0:T(8,128)(2,1)} %bitcast.4), kind=kOutput, calls=%fused_computation.9 | convolution fusion | flops 1970995200 | bytes 12533760 | tf_op jit(solution)/shard_map/dot_general | solution.py:44
  149.1 17.4 %collective-permute-done.7 = f32[2,100,2048]{2,0,1:T(2,128)S(1)} collective-permute-done((f32[2,100,2048]{2,0,1:T(2,128)S(1)}, f32[2,100,2048]{2,0,1:T(2,128)S(1)}, u32[]{:S(2)}, u32[]{:S(2)}) %collective-permute-start.7) | collective-permute-done | bytes 1638432 | tf_op jit(solution)/shard_map/ppermute | solution.py:55
  166.5 1.0 copy_add_fusion.2
  167.5 1.3 copy.28
  168.8 3.8 %collective-permute-start.8 = (f32[2,100,2048]{2,0,1:T(2,128)S(1)}, f32[2,100,2048]{2,0,1:T(2,128)S(1)}, u32[]{:S(2)}, u32[]{:S(2)}) collective-permute-start(f32[2,100,2048]{2,0,1:T(2,128)S(1)} %copy.28), channel_id=1, source_target_pairs={{0,12},{4,0},{8,4},{12,8},{1,13},{5,1},{9,5},{13,9},{2,14},{6,2},{... | collective-permute-start | bytes 4915208 | tf_op jit(solution)/shard_map/ppermute | solution.py:55
  172.5 4.0 %collective-permute-done.3 = f32[2,100,2048]{2,0,1:T(2,128)S(1)} collective-permute-done((f32[2,100,2048]{2,0,1:T(2,128)S(1)}, f32[2,100,2048]{2,0,1:T(2,128)S(1)}, u32[]{:S(2)}, u32[]{:S(2)}) %collective-permute-start.3) | collective-permute-done | bytes 1638432 | tf_op jit(solution)/shard_map/ppermute | solution.py:54
  176.5 1.0 copy_add_fusion.5
  177.5 1.3 copy.18
  178.8 0.3 collective-permute-start.4
  179.1 5.2 %convolution_bitcast_fusion.5 = f32[2,100,2048]{2,1,0:T(8,128)S(1)} fusion(bf16[2,200,2,1200]{3,1,2,0:T(8,128)(2,1)S(1)} %copy-done.2, bf16[1,1200,2048]{2,1,0:T(8,128)(2,1)} %bitcast.5, bf16[1,1200,2048]{2,1,0:T(8,128)(2,1)} %bitcast.4), kind=kOutput, calls=%fused_computation.8 | convolution fusion | flops 1970995200 | bytes 12533760 | tf_op jit(solution)/shard_map/dot_general | solution.py:44
  184.4 5.3 %convolution_bitcast_fusion.1 = f32[2,100,2048]{2,1,0:T(8,128)S(1)} fusion(bf16[2,200,2,1200]{3,1,2,0:T(8,128)(2,1)S(1)} %copy-done.1, bf16[1,1200,2048]{2,1,0:T(8,128)(2,1)} %bitcast.5, bf16[1,1200,2048]{2,1,0:T(8,128)(2,1)} %bitcast.4), kind=kOutput, calls=%fused_computation.4 | convolution fusion | flops 1970995200 | bytes 12533760 | tf_op jit(solution)/shard_map/dot_general | solution.py:44
  189.6 17.0 %collective-permute-done.8 = f32[2,100,2048]{2,0,1:T(2,128)S(1)} collective-permute-done((f32[2,100,2048]{2,0,1:T(2,128)S(1)}, f32[2,100,2048]{2,0,1:T(2,128)S(1)}, u32[]{:S(2)}, u32[]{:S(2)}) %collective-permute-start.8) | collective-permute-done | bytes 1638432 | tf_op jit(solution)/shard_map/ppermute | solution.py:55
  206.6 1.0 copy_add_fusion.1
  207.6 1.3 copy.30
  208.8 3.8 %collective-permute-start.9 = (f32[2,100,2048]{2,0,1:T(2,128)S(1)}, f32[2,100,2048]{2,0,1:T(2,128)S(1)}, u32[]{:S(2)}, u32[]{:S(2)}) collective-permute-start(f32[2,100,2048]{2,0,1:T(2,128)S(1)} %copy.30), channel_id=1, source_target_pairs={{0,12},{4,0},{8,4},{12,8},{1,13},{5,1},{9,5},{13,9},{2,14},{6,2},{... | collective-permute-start | bytes 4915208 | tf_op jit(solution)/shard_map/ppermute | solution.py:55
  212.6 3.9 %collective-permute-done.4 = f32[2,100,2048]{2,0,1:T(2,128)S(1)} collective-permute-done((f32[2,100,2048]{2,0,1:T(2,128)S(1)}, f32[2,100,2048]{2,0,1:T(2,128)S(1)}, u32[]{:S(2)}, u32[]{:S(2)}) %collective-permute-start.4) | collective-permute-done | bytes 1638432 | tf_op jit(solution)/shard_map/ppermute | solution.py:54
  216.5 1.0 copy_add_fusion.4
  217.5 1.3 copy.21
  218.9 5.2 %convolution_bitcast_fusion = f32[2,100,2048]{2,1,0:T(8,128)S(1)} fusion(bf16[2,200,2,1200]{3,1,2,0:T(8,128)(2,1)S(1)} %get-tuple-element.13, bf16[1,1200,2048]{2,1,0:T(8,128)(2,1)} %bitcast.5, bf16[1,1200,2048]{2,1,0:T(8,128)(2,1)} %bitcast.4), kind=kOutput, calls=%fused_computation.3 | convolution fusion | flops 1970995200 | bytes 12533760 | tf_op jit(solution)/shard_map/dot_general | solution.py:44
  224.1 5.2 %convolution_bitcast_fusion.4 = f32[2,100,2048]{2,1,0:T(8,128)S(1)} fusion(bf16[2,200,2,1200]{3,1,2,0:T(8,128)(2,1)S(1)} %get-tuple-element.13, bf16[1,1200,2048]{2,1,0:T(8,128)(2,1)} %bitcast.5, bf16[1,1200,2048]{2,1,0:T(8,128)(2,1)} %bitcast.4), kind=kOutput, calls=%fused_computation.7 | convolution fusion | flops 1970995200 | bytes 12533760 | tf_op jit(solution)/shard_map/dot_general | solution.py:44
  229.3 16.4 %collective-permute-done.9 = f32[2,100,2048]{2,0,1:T(2,128)S(1)} collective-permute-done((f32[2,100,2048]{2,0,1:T(2,128)S(1)}, f32[2,100,2048]{2,0,1:T(2,128)S(1)}, u32[]{:S(2)}, u32[]{:S(2)}) %collective-permute-start.9) | collective-permute-done | bytes 1638432 | tf_op jit(solution)/shard_map/ppermute | solution.py:55
  245.8 1.0 copy_add_fusion
  246.8 1.0 dynamic-slice_bitcast_fusion.6
  247.7 1.5 collective-permute-start.10
  249.2 6.2 %collective-permute-done.5 = f32[2,100,2048]{2,0,1:T(2,128)S(1)} collective-permute-done((f32[2,100,2048]{2,0,1:T(2,128)S(1)}, f32[2,100,2048]{2,0,1:T(2,128)S(1)}, u32[]{:S(2)}, u32[]{:S(2)}) %collective-permute-start.5) | collective-permute-done | bytes 1638432 | tf_op jit(solution)/shard_map/ppermute | solution.py:54
  255.4 1.0 copy_add_fusion.3
  256.4 1.0 dynamic-slice_bitcast_fusion.7
  257.4 1.5 collective-permute-start.6
  258.9 10.9 %collective-permute-done.10 = f32[100,2048]{1,0:T(8,128)} collective-permute-done((f32[100,2048]{1,0:T(8,128)}, f32[100,2048]{1,0:T(8,128)}, u32[]{:S(2)}, u32[]{:S(2)}) %collective-permute-start.10) | collective-permute-done | bytes 819232 | tf_op jit(solution)/shard_map/ppermute | solution.py:63
  269.9 1.2 bitcast_add_fusion
  271.2 3.1 collective-permute-start.12
  274.3 13.9 %collective-permute-done.6 = f32[100,2048]{1,0:T(8,128)} collective-permute-done((f32[100,2048]{1,0:T(8,128)}, f32[100,2048]{1,0:T(8,128)}, u32[]{:S(2)}, u32[]{:S(2)}) %collective-permute-start.6) | collective-permute-done | bytes 819232 | tf_op jit(solution)/shard_map/ppermute | solution.py:63
  288.1 1.2 bitcast_add_fusion.1
  289.5 3.1 collective-permute-start.11
  292.5 6.8 %collective-permute-done.12 = f32[100,1024]{1,0:T(8,128)S(1)} collective-permute-done((f32[100,1024]{1,0:T(8,128)S(1)}, f32[100,1024]{1,0:T(8,128)S(1)}, u32[]{:S(2)}, u32[]{:S(2)}) %collective-permute-start.12) | collective-permute-done | bytes 409632 | tf_op jit(solution)/shard_map/ppermute | solution.py:65
  299.3 5.3 %collective-permute-done.11 = f32[100,1024]{1,0:T(8,128)S(1)} collective-permute-done((f32[100,1024]{1,0:T(8,128)S(1)}, f32[100,1024]{1,0:T(8,128)S(1)}, u32[]{:S(2)}, u32[]{:S(2)}) %collective-permute-start.11) | collective-permute-done | bytes 409632 | tf_op jit(solution)/shard_map/ppermute | solution.py:65
  304.6 1.4 maximum_select_fusion
  (25 shorter events, 0.6 us)
Async XLA Ops:
  6.5 97.5 %all-gather.2.cloned.1.call-start = ((), (), s32[]{:S(2)}) async-start(), calls=%async_computation | async-start | bytes 10240000 | tf_op jit(solution)/shard_map/all_gather | solution.py:33
  13.4 3.0 collective-permute-start
  18.0 2.4 copy-start
  20.4 56.9 %collective-permute-start.1 = (bf16[1200,1024]{1,0:T(8,128)(2,1)S(1)}, bf16[1200,1024]{1,0:T(8,128)(2,1)S(1)}, u32[]{:S(2)}, u32[]{:S(2)}) collective-permute-start(bf16[1200,1024]{1,0:T(8,128)(2,1)S(1)} %copy-done), channel_id=1, source_target_pairs={{0,64},{64,0},{1,65},{65,1},{2,66},{66,2},{3,67},{67,3},{4,68},{68... | collective-permute-start | bytes 7372808 | tf_op jit(solution)/shard_map/ppermute | solution.py:38
  79.0 42.8 %collective-permute-start.2 = (bf16[1200,2048]{1,0:T(8,128)(2,1)}, bf16[1200,2048]{1,0:T(8,128)(2,1)}, u32[]{:S(2)}, u32[]{:S(2)}) collective-permute-start(bf16[1200,2048]{1,0:T(8,128)(2,1)} %constant_dynamic-update-slice_fusion), channel_id=1, source_target_pairs={{0,1},{1,0},{2,3},{3,2},{4,5},{5,4},{6,7},{7,6},{8,9},{9,8},{10,11... | collective-permute-start | bytes 14745608 | tf_op jit(solution)/shard_map/ppermute | solution.py:39
  127.4 4.3 %copy-start.1 = (bf16[2,200,2,1200]{3,1,2,0:T(8,128)(2,1)S(1)}, bf16[2,200,2,1200]{3,1,2,0:T(8,128)(2,1)}, u32[]{:S(2)}) copy-start(bf16[2,200,2,1200]{3,1,2,0:T(8,128)(2,1)} %get-tuple-element.15) | copy-start | bytes 5760004
  128.6 37.9 %collective-permute-start.7 = (f32[2,100,2048]{2,0,1:T(2,128)S(1)}, f32[2,100,2048]{2,0,1:T(2,128)S(1)}, u32[]{:S(2)}, u32[]{:S(2)}) collective-permute-start(f32[2,100,2048]{2,0,1:T(2,128)S(1)} %copy.25), channel_id=1, source_target_pairs={{0,12},{4,0},{8,4},{12,8},{1,13},{5,1},{9,5},{13,9},{2,14},{6,2},{... | collective-permute-start | bytes 4915208 | tf_op jit(solution)/shard_map/ppermute | solution.py:55
  136.9 1.6 copy-start.4
  138.2 38.4 %collective-permute-start.3 = (f32[2,100,2048]{2,0,1:T(2,128)S(1)}, f32[2,100,2048]{2,0,1:T(2,128)S(1)}, u32[]{:S(2)}, u32[]{:S(2)}) collective-permute-start(f32[2,100,2048]{2,0,1:T(2,128)S(1)} %copy.15), channel_id=1, source_target_pairs={{0,4},{4,8},{8,12},{12,0},{1,5},{5,9},{9,13},{13,1},{2,6},{6,10},{... | collective-permute-start | bytes 4915208 | tf_op jit(solution)/shard_map/ppermute | solution.py:54
  138.4 5.4 %copy-start.3 = (bf16[2,200,2,1200]{3,1,2,0:T(8,128)(2,1)S(1)}, bf16[2,200,2,1200]{3,1,2,0:T(8,128)(2,1)}, u32[]{:S(2)}) copy-start(bf16[2,200,2,1200]{3,1,2,0:T(8,128)(2,1)} %get-tuple-element.10) | copy-start | bytes 5760004
  168.8 37.8 %collective-permute-start.8 = (f32[2,100,2048]{2,0,1:T(2,128)S(1)}, f32[2,100,2048]{2,0,1:T(2,128)S(1)}, u32[]{:S(2)}, u32[]{:S(2)}) collective-permute-start(f32[2,100,2048]{2,0,1:T(2,128)S(1)} %copy.28), channel_id=1, source_target_pairs={{0,12},{4,0},{8,4},{12,8},{1,13},{5,1},{9,5},{13,9},{2,14},{6,2},{... | collective-permute-start | bytes 4915208 | tf_op jit(solution)/shard_map/ppermute | solution.py:55
  177.5 1.6 copy-start.2
  178.8 37.7 %collective-permute-start.4 = (f32[2,100,2048]{2,0,1:T(2,128)S(1)}, f32[2,100,2048]{2,0,1:T(2,128)S(1)}, u32[]{:S(2)}, u32[]{:S(2)}) collective-permute-start(f32[2,100,2048]{2,0,1:T(2,128)S(1)} %copy.18), channel_id=1, source_target_pairs={{0,4},{4,8},{8,12},{12,0},{1,5},{5,9},{9,13},{13,1},{2,6},{6,10},{... | collective-permute-start | bytes 4915208 | tf_op jit(solution)/shard_map/ppermute | solution.py:54
  208.8 36.9 %collective-permute-start.9 = (f32[2,100,2048]{2,0,1:T(2,128)S(1)}, f32[2,100,2048]{2,0,1:T(2,128)S(1)}, u32[]{:S(2)}, u32[]{:S(2)}) collective-permute-start(f32[2,100,2048]{2,0,1:T(2,128)S(1)} %copy.30), channel_id=1, source_target_pairs={{0,12},{4,0},{8,4},{12,8},{1,13},{5,1},{9,5},{13,9},{2,14},{6,2},{... | collective-permute-start | bytes 4915208 | tf_op jit(solution)/shard_map/ppermute | solution.py:55
  218.8 36.7 %collective-permute-start.5 = (f32[2,100,2048]{2,0,1:T(2,128)S(1)}, f32[2,100,2048]{2,0,1:T(2,128)S(1)}, u32[]{:S(2)}, u32[]{:S(2)}) collective-permute-start(f32[2,100,2048]{2,0,1:T(2,128)S(1)} %copy.21), channel_id=1, source_target_pairs={{0,4},{4,8},{8,12},{12,0},{1,5},{5,9},{9,13},{13,1},{2,6},{6,10},{... | collective-permute-start | bytes 4915208 | tf_op jit(solution)/shard_map/ppermute | solution.py:54
  247.7 22.1 %collective-permute-start.10 = (f32[100,2048]{1,0:T(8,128)}, f32[100,2048]{1,0:T(8,128)}, u32[]{:S(2)}, u32[]{:S(2)}) collective-permute-start(f32[100,2048]{1,0:T(8,128)} %dynamic-slice_bitcast_fusion.6), channel_id=1, source_target_pairs={{0,2},{2,0},{1,3},{3,1},{4,6},{6,4},{5,7},{7,5},{8,10},{10,8},{9,1... | collective-permute-start | bytes 2457608 | tf_op jit(solution)/shard_map/ppermute | solution.py:63
  257.4 30.7 %collective-permute-start.6 = (f32[100,2048]{1,0:T(8,128)}, f32[100,2048]{1,0:T(8,128)}, u32[]{:S(2)}, u32[]{:S(2)}) collective-permute-start(f32[100,2048]{1,0:T(8,128)} %dynamic-slice_bitcast_fusion.7), channel_id=1, source_target_pairs={{0,2},{2,0},{1,3},{3,1},{4,6},{6,4},{5,7},{7,5},{8,10},{10,8},{9,1... | collective-permute-start | bytes 2457608 | tf_op jit(solution)/shard_map/ppermute | solution.py:63
  271.2 28.1 %collective-permute-start.12 = (f32[100,1024]{1,0:T(8,128)S(1)}, f32[100,1024]{1,0:T(8,128)S(1)}, u32[]{:S(2)}, u32[]{:S(2)}) collective-permute-start(f32[100,1024]{1,0:T(8,128)S(1)} %get-tuple-element.19), channel_id=1, source_target_pairs={{0,64},{64,0},{1,65},{65,1},{2,66},{66,2},{3,67},{67,3},{4,68},{68... | collective-permute-start | bytes 1228808 | tf_op jit(solution)/shard_map/ppermute | solution.py:65
  289.5 15.1 %collective-permute-start.11 = (f32[100,1024]{1,0:T(8,128)S(1)}, f32[100,1024]{1,0:T(8,128)S(1)}, u32[]{:S(2)}, u32[]{:S(2)}) collective-permute-start(f32[100,1024]{1,0:T(8,128)S(1)} %get-tuple-element.17), channel_id=1, source_target_pairs={{0,64},{64,0},{1,65},{65,1},{2,66},{66,2},{3,67},{67,3},{4,68},{68... | collective-permute-start | bytes 1228808 | tf_op jit(solution)/shard_map/ppermute | solution.py:65
Sparse Core Ops, SparseCore 0:
  19.9 84.1 all-gather.1

commit v7 on v6

--- a/solution.py
+++ b/solution.py
@@ -32,37 +32,67 @@
     own_owners = jnp.stack([mine, from_sibling], axis=2)
     gathered = lax.all_gather(own_owners, "z", axis=1, tiled=True)
     rows = gathered.shape[1]
-    half = rows // 2
     by_y = gathered.reshape(ny, nxl, rows, 2, kc)
 
     amp = jnp.concatenate([amplitudes, lax.ppermute(amplitudes, "xh", SWAP)], axis=1)
     amp = jnp.stack([amp, lax.ppermute(amp, "c", SWAP)], axis=0)
 
-    def block(y_owner, part):
+    def block(y_owner, low, high):
         lhs = lax.dynamic_index_in_dim(by_y, y_owner % ny, 0, keepdims=False)
-        lhs = lhs[:, part * half : (part + 1) * half]
         product = lax.dot_general(
-            lhs, amp, (((2, 3), (0, 1)), ((), ())), preferred_element_type=jnp.float32
+            lhs[:, low:high], amp, (((2, 3), (0, 1)), ((), ())),
+            preferred_element_type=jnp.float32,
         )
         return lax.optimization_barrier(product)
 
     to_next = [(i, (i + 1) % ny) for i in range(ny)]
     to_prev = [(i, (i - 1) % ny) for i in range(ny)]
-    acc_ahead = block(yi + ny - 1, 0)
-    acc_back = block(yi + 1, 1)
-    for step in range(ny - 1):
-        got_ahead = lax.ppermute(acc_ahead, "y", to_next)
-        got_back = lax.ppermute(acc_back, "y", to_prev)
-        acc_ahead = got_ahead + block(yi + 2 * ny - 2 - step, 0)
-        acc_back = got_back + block(yi + 2 + step, 1)
 
-    kept, came = [], []
-    for acc in (acc_ahead, acc_back):
+    def ring(first_ahead, first_back, next_ahead, next_back):
+        acc_ahead, acc_back = first_ahead, first_back
+        for step in range(ny - 1):
+            got_ahead = lax.ppermute(acc_ahead, "y", to_next)
+            got_back = lax.ppermute(acc_back, "y", to_prev)
+            acc_ahead = got_ahead + next_ahead(yi + 2 * ny - 2 - step)
+            acc_back = got_back + next_back(yi + 2 + step)
+        return acc_ahead, acc_back
+
+    def pair_sum(acc):
         here = lax.dynamic_index_in_dim(acc, xi, 0, keepdims=False)
         there = lax.dynamic_index_in_dim(acc, 1 - xi, 0, keepdims=False)
-        summed = here + lax.ppermute(there, "xl", SWAP)
-        kept.append(summed[:, :width])
-        came.append(lax.ppermute(summed[:, width:], "xh", SWAP))
+        return here + lax.ppermute(there, "xl", SWAP)
+
+    y_rows = 8 * (rows * 5 // 72)
+    y_half = y_rows // 2
+    x_half = 8 * ((rows - y_rows) // 16)
+    late = lax.dot_general(
+        gathered[:, y_rows:], amp, (((2, 3), (0, 1)), ((), ())),
+        preferred_element_type=jnp.float32,
+    ).reshape(ny, nxl, rows - y_rows, amp.shape[-1])
+    late_here = lax.dynamic_index_in_dim(late, xi, 1, keepdims=False)
+    late_there = lax.dynamic_index_in_dim(late, 1 - xi, 1, keepdims=False)
+    late_sum = late_here + lax.ppermute(late_there, "xl", SWAP)
+    late_ahead, late_back = late_sum[:, :x_half], late_sum[:, x_half:]
+
+    def pick(parts):
+        return lambda y_owner: lax.dynamic_index_in_dim(parts, y_owner % ny, 0, keepdims=False)
+
+    early = ring(
+        block(yi + ny - 1, 0, y_half),
+        block(yi + 1, y_half, y_rows),
+        lambda y_owner: block(y_owner, 0, y_half),
+        lambda y_owner: block(y_owner, y_half, y_rows),
+    )
+    late_done = ring(
+        pick(late_ahead)(yi + ny - 1),
+        pick(late_back)(yi + 1),
+        pick(late_ahead),
+        pick(late_back),
+    )
+    pieces = [pair_sum(early[0]), pair_sum(early[1]), late_done[0], late_done[1]]
+
+    kept = [piece[:, :width] for piece in pieces]
+    came = [lax.ppermute(piece[:, width:], "xh", SWAP) for piece in pieces]
     first = jnp.concatenate(kept + came, axis=0)
     second = jnp.concatenate(came + kept, axis=0)
     return jnp.where(xh == 0, first, second)

time: 314 us -> 308 us (0.981)
  waiting for transfers between devices: 181 us -> 148 us
  starting transfers between devices: 23.2 us -> 37.4 us
  matrix products: 42.4 us -> 54.3 us
  local copies, waits for them, and re-layouts: 40.9 us -> 44.6 us
    ppermute x10 -> x19, waiting for transfers between devices: 102 us -> 67.9 us  [the longest x6 52.1 us: ring(): got_ahead = lax.ppermute(acc_ahead, 'y', to_next)]
    ppermute x10 -> x19, starting transfers between devices: 20 us -> 34.2 us  [the longest x6 20.6 us: ring(): got_back = lax.ppermute(acc_back, 'y', to_prev)]
    dot_general x8 -> x9, matrix products: 42.4 us -> 54.3 us  [the longest x8 40.4 us: block(): lax.dot_general(lhs[:, low:high], amp, (((2, 3), (0, 1)), ((), ())), pref...]
    concatenate x0 -> x2, local copies, waits for them, and re-layouts: none -> 8.2 us  [the longest x1 6.89 us: local(): first = jnp.concatenate(kept + came, axis=0)]
    reshape x1, local copies, waits for them, and re-layouts: 9.22 us -> 6.04 us  [local(): by_y = gathered.reshape(ny, nxl, rows, 2, kc)]
    add x8 -> x15, other arithmetic: 8.4 us -> 6.09 us  [the longest x1 2.51 us: local(): late_sum = late_here + lax.ppermute(late_there, 'xl', SWAP)]
  transfers between devices with their start and end apart: 14 -> 23, of which waited for: 13 -> 14; matrix products, arithmetic and copies ran while one was open for 24% -> 23% of each run, Pallas kernels for 0% -> 0%
where the time goes in v7:
time: 308 us; the launch traced here: 307 us
  waiting for transfers between devices  148 us (48%)
  matrix products  54.3 us (18%)
  local copies, waits for them, and re-layouts  44.6 us (14%)
  starting transfers between devices  37.4 us (12%)
  between operations  14 us (5%)
  other arithmetic  9.39 us (3%)
    ppermute x6, waiting for transfers between devices, ring(): got_ahead = lax.ppermute(acc_ahead, 'y', to_next)  52.1 us
    ppermute x1, waiting for transfers between devices, local(): lax.ppermute(amplitudes, 'xh', SWAP)  52 us
    dot_general x8, matrix products, block(): lax.dot_general(lhs[:, low:high], amp, (((2, 3), (0, 1)), ((), ())), pref...  40.4 us
    all_gather x1, waiting for transfers between devices, local(): gathered = lax.all_gather(own_owners, 'z', axis=1, tiled=True)  25.6 us
    ppermute x6, starting transfers between devices, ring(): got_back = lax.ppermute(acc_back, 'y', to_prev)  20.6 us
    dot_general x1, matrix products, local(): lax.dot_general(gathered[:, y_rows:], amp, (((2, 3), (0, 1)), ((), ())),...  14 us
    ppermute x4, starting transfers between devices, local(): came = [lax.ppermute(piece[:, width:], 'xh', SWAP) for piece in pieces]  10.4 us
    squeeze x1, local copies, waits for them, and re-layouts, block(): lhs = lax.dynamic_index_in_dim(by_y, y_owner % ny, 0, keepdims=False)  9.14 us
  transfers between devices with their start and end apart: 23, of which 14 were waited for; matrix products, arithmetic and copies ran while one was open for 23% of the time, Pallas kernels for 0%

profile of v7, /device:TPU:0, one launch (start us, length us, event | category | flops | bytes accessed | tf_op | source)
XLA Modules:
  0.0 307.5 jit_solution(5278871879375407929)
XLA Ops:
  6.5 0.7 dynamic_slice.75
  7.3 1.2 sort.17
  8.9 2.6 reshape.17
  11.4 0.6 gather_fusion.1
  12.3 1.1 copy.4
  13.4 0.6 gather_fusion
  14.2 2.1 collective-permute-done
  16.3 1.4 copy.43
  18.0 1.7 copy.6
  19.8 3.2 %collective-permute-start.1 = (bf16[1200,1024]{1,0:T(8,128)(2,1)S(1)}, bf16[1200,1024]{1,0:T(8,128)(2,1)S(1)}, u32[]{:S(2)}, u32[]{:S(2)}) collective-permute-start(bf16[1200,1024]{1,0:T(8,128)(2,1)S(1)} %copy-done.2), channel_id=1, source_target_pairs={{0,64},{64,0},{1,65},{65,1},{2,66},{66,2},{3,67},{67,3},{4,68},{68... | collective-permute-start | bytes 7372808 | tf_op jit(solution)/shard_map/ppermute | solution.py:37
  23.0 1.7 constant_dynamic-update-slice_fusion.1
  24.7 52.0 %collective-permute-done.1 = bf16[1200,1024]{1,0:T(8,128)(2,1)S(1)} collective-permute-done((bf16[1200,1024]{1,0:T(8,128)(2,1)S(1)}, bf16[1200,1024]{1,0:T(8,128)(2,1)S(1)}, u32[]{:S(2)}, u32[]{:S(2)}) %collective-permute-start.1) | collective-permute-done | bytes 2457632 | tf_op jit(solution)/shard_map/ppermute | solution.py:37
  76.7 1.7 constant_dynamic-update-slice_fusion
  78.4 25.6 %all-gather.2.cloned.1.call-done = bf16[8,200,2,1200]{3,0,2,1:T(8,128)(2,1)} async-done(((bf16[8,50,2,1200]{3,0,2,1:T(8,128)(2,1)}), bf16[8,200,2,1200]{3,0,2,1:T(8,128)(2,1)}) %all-gather.2.cloned.1.call-update) | async-done | bytes 7680016 | tf_op jit(solution)/shard_map/all_gather | solution.py:33
  104.1 6.0 %copy.35 = bf16[8,200,2,1200]{3,1,2,0:T(8,128)(2,1)S(1)} copy(bf16[8,200,2,1200]{3,0,2,1:T(8,128)(2,1)} %all-gather.2.cloned.1.call-done) | data formatting | bytes 15360000 | tf_op jit(solution)/shard_map/reshape | solution.py:35
  110.1 14.0 %fusion = f32[8,96,2048,1]{2,1,3,0:T(8,128)S(1)} fusion(bf16[8,200,2,1200]{3,1,2,0:T(8,128)(2,1)S(1)} %copy.35, bf16[1,1200,2048]{2,1,0:T(8,128)(2,1)} %bitcast.5, bf16[1,1200,2048]{2,1,0:T(8,128)(2,1)} %bitcast.4), kind=kOutput, calls=%fused_computation.3 | convolution fusion | flops 7554662400 | bytes 20054016 | tf_op jit(solution)/shard_map/dot_general | solution.py:68
  124.1 2.7 copy-done.1
  127.0 1.5 collective-permute-start.11
  128.6 9.1 %dynamic-slice_bitcast_fusion.2 = (bf16[2,200,2,1200]{3,1,2,0:T(8,128)(2,1)}, bf16[2,200,2,1200]{3,1,2,0:T(8,128)(2,1)}, bf16[2,200,2,1200]{3,1,2,0:T(8,128)(2,1...) fusion(bf16[4,2,200,2,1200]{4,2,3,1,0:T(8,128)(2,1)} %bitcast.88, ...), kind=kLoop, calls=%fused_computation.17 | loop fusion | bytes 23040024 | tf_op jit(solution)/shard_map/jit(dynamic_index_in_dim)/squeeze | solution.py:41
  137.7 5.1 %convolution_bitcast_fusion.3 = f32[2,52,2048]{2,1,0:T(8,128)S(1)} fusion(bf16[2,200,2,1200]{3,1,2,0:T(8,128)(2,1)} %get-tuple-element.10, bf16[1,1200,2048]{2,1,0:T(8,128)(2,1)} %bitcast.5, bf16[1,1200,2048]{2,1,0:T(8,128)(2,1)} %bitcast.4), kind=kOutput, calls=%fused_computation.10 | convolution fusion | flops 1027276800 | bytes 11255808 | tf_op jit(solution)/shard_map/dot_general | solution.py:42
  142.8 0.7 copy.18
  143.5 3.0 collective-permute-start.7
  146.5 5.1 %convolution_bitcast_fusion.2 = f32[2,52,2048]{2,1,0:T(8,128)S(1)} fusion(bf16[2,200,2,1200]{3,1,2,0:T(8,128)(2,1)} %get-tuple-element.11, bf16[1,1200,2048]{2,1,0:T(8,128)(2,1)} %bitcast.5, bf16[1,1200,2048]{2,1,0:T(8,128)(2,1)} %bitcast.4), kind=kOutput, calls=%fused_computation.9 | convolution fusion | flops 1027276800 | bytes 11255808 | tf_op jit(solution)/shard_map/dot_general | solution.py:42
  151.5 5.0 %convolution_bitcast_fusion.5 = f32[2,52,2048]{2,1,0:T(8,128)S(1)} fusion(bf16[2,200,2,1200]{3,1,2,0:T(8,128)(2,1)} %get-tuple-element.13, bf16[1,1200,2048]{2,1,0:T(8,128)(2,1)} %bitcast.5, bf16[1,1200,2048]{2,1,0:T(8,128)(2,1)} %bitcast.4), kind=kOutput, calls=%fused_computation.12 | convolution fusion | flops 1027276800 | bytes 11255808 | tf_op jit(solution)/shard_map/dot_general | solution.py:42
  156.6 5.2 %convolution_bitcast_fusion.6 = f32[2,52,2048]{2,1,0:T(8,128)S(1)} fusion(bf16[2,200,2,1200]{3,1,2,0:T(8,128)(2,1)} %get-tuple-element.14, bf16[1,1200,2048]{2,1,0:T(8,128)(2,1)} %bitcast.5, bf16[1,1200,2048]{2,1,0:T(8,128)(2,1)} %bitcast.4), kind=kOutput, calls=%fused_computation.13 | convolution fusion | flops 1027276800 | bytes 11255808 | tf_op jit(solution)/shard_map/dot_general | solution.py:42
  161.8 4.9 %convolution_bitcast_fusion.7 = f32[2,52,2048]{2,1,0:T(8,128)S(1)} fusion(bf16[2,200,2,1200]{3,1,2,0:T(8,128)(2,1)S(1)} %copy-done.5, bf16[1,1200,2048]{2,1,0:T(8,128)(2,1)} %bitcast.5, bf16[1,1200,2048]{2,1,0:T(8,128)(2,1)} %bitcast.4), kind=kOutput, calls=%fused_computation.14 | convolution fusion | flops 1027276800 | bytes 11255808 | tf_op jit(solution)/shard_map/dot_general | solution.py:42
  166.7 0.7 copy.8
  167.4 4.9 %convolution_bitcast_fusion.1 = f32[2,52,2048]{2,1,0:T(8,128)S(1)} fusion(bf16[2,200,2,1200]{3,1,2,0:T(8,128)(2,1)S(1)} %copy-done.5, bf16[1,1200,2048]{2,1,0:T(8,128)(2,1)} %bitcast.5, bf16[1,1200,2048]{2,1,0:T(8,128)(2,1)} %bitcast.4), kind=kOutput, calls=%fused_computation.8 | convolution fusion | flops 1027276800 | bytes 11255808 | tf_op jit(solution)/shard_map/dot_general | solution.py:42
  172.4 0.5 copy_add_fusion.2
  172.9 0.7 copy.21
  173.6 3.3 %collective-permute-start.8 = (f32[2,52,2048]{2,0,1:T(2,128)S(1)}, f32[2,52,2048]{2,0,1:T(2,128)S(1)}, u32[]{:S(2)}, u32[]{:S(2)}) collective-permute-start(f32[2,52,2048]{2,0,1:T(2,128)S(1)} %copy.21), channel_id=1, source_target_pairs={{0,12},{4,0},{8,4},{12,8},{1,13},{5,1},{9,5},{13,9},{2,14},{6,2},{... | collective-permute-start | bytes 2555912 | tf_op jit(solution)/shard_map/ppermute | solution.py:55
  176.9 11.7 %collective-permute-done.3 = f32[2,52,2048]{2,0,1:T(2,128)S(1)} collective-permute-done((f32[2,52,2048]{2,0,1:T(2,128)S(1)}, f32[2,52,2048]{2,0,1:T(2,128)S(1)}, u32[]{:S(2)}, u32[]{:S(2)}) %collective-permute-start.3) | collective-permute-done | bytes 852000 | tf_op jit(solution)/shard_map/ppermute | solution.py:54
  189.1 0.7 copy.11
  189.9 4.9 %convolution_bitcast_fusion = f32[2,52,2048]{2,1,0:T(8,128)S(1)} fusion(bf16[2,200,2,1200]{3,1,2,0:T(8,128)(2,1)S(1)} %copy-done.4, bf16[1,1200,2048]{2,1,0:T(8,128)(2,1)} %bitcast.5, bf16[1,1200,2048]{2,1,0:T(8,128)(2,1)} %bitcast.4), kind=kOutput, calls=%fused_computation.7 | convolution fusion | flops 1027276800 | bytes 11255808 | tf_op jit(solution)/shard_map/dot_general | solution.py:42
  195.4 0.7 copy.23
  196.0 3.5 %collective-permute-start.9 = (f32[2,52,2048]{2,0,1:T(2,128)S(1)}, f32[2,52,2048]{2,0,1:T(2,128)S(1)}, u32[]{:S(2)}, u32[]{:S(2)}) collective-permute-start(f32[2,52,2048]{2,0,1:T(2,128)S(1)} %copy.23), channel_id=1, source_target_pairs={{0,12},{4,0},{8,4},{12,8},{1,13},{5,1},{9,5},{13,9},{2,14},{6,2},{... | collective-permute-start | bytes 2555912 | tf_op jit(solution)/shard_map/ppermute | solution.py:55
  199.5 10.7 %collective-permute-done.4 = f32[2,52,2048]{2,0,1:T(2,128)S(1)} collective-permute-done((f32[2,52,2048]{2,0,1:T(2,128)S(1)}, f32[2,52,2048]{2,0,1:T(2,128)S(1)}, u32[]{:S(2)}, u32[]{:S(2)}) %collective-permute-start.4) | collective-permute-done | bytes 852000 | tf_op jit(solution)/shard_map/ppermute | solution.py:54
  210.7 0.7 copy.14
  211.5 5.2 %convolution_bitcast_fusion.4 = f32[2,52,2048]{2,1,0:T(8,128)S(1)} fusion(bf16[2,200,2,1200]{3,1,2,0:T(8,128)(2,1)S(1)} %copy-done.4, bf16[1,1200,2048]{2,1,0:T(8,128)(2,1)} %bitcast.5, bf16[1,1200,2048]{2,1,0:T(8,128)(2,1)} %bitcast.4), kind=kOutput, calls=%fused_computation.11 | convolution fusion | flops 1027276800 | bytes 11255808 | tf_op jit(solution)/shard_map/dot_general | solution.py:42
  216.7 0.5 copy_add_fusion
  217.3 0.6 collective-permute-start.10
  217.9 13.0 %collective-permute-done.5 = f32[2,52,2048]{2,0,1:T(2,128)S(1)} collective-permute-done((f32[2,52,2048]{2,0,1:T(2,128)S(1)}, f32[2,52,2048]{2,0,1:T(2,128)S(1)}, u32[]{:S(2)}, u32[]{:S(2)}) %collective-permute-start.5) | collective-permute-done | bytes 852000 | tf_op jit(solution)/shard_map/ppermute | solution.py:54
  231.5 0.6 collective-permute-start.6
  232.2 0.7 fusion.13
  232.9 3.0 collective-permute-start.19
  235.9 7.3 %collective-permute-done.6 = f32[52,2048]{1,0:T(8,128)S(1)} collective-permute-done((f32[52,2048]{1,0:T(8,128)S(1)}, f32[52,2048]{1,0:T(8,128)S(1)}, u32[]{:S(2)}, u32[]{:S(2)}) %collective-permute-start.6) | collective-permute-done | bytes 426016 | tf_op jit(solution)/shard_map/ppermute | solution.py:63
  243.3 2.5 bitcast_add_fusion
  246.2 3.7 %collective-permute-start.18 = (f32[52,1024]{1,0:T(8,128)S(1)}, f32[52,1024]{1,0:T(8,128)S(1)}, u32[]{:S(2)}, u32[]{:S(2)}) collective-permute-start(f32[52,1024]{1,0:T(8,128)S(1)} %get-tuple-element.20), channel_id=1, source_target_pairs={{0,64},{64,0},{1,65},{65,1},{2,66},{66,2},{3,67},{67,3},{4,68},{68... | collective-permute-start | bytes 638984 | tf_op jit(solution)/shard_map/ppermute | solution.py:95
  250.0 3.3 %collective-permute-start.15 = (f32[48,2048]{1,0:T(8,128)S(1)}, f32[48,2048]{1,0:T(8,128)S(1)}, u32[]{:S(2)}, u32[]{:S(2)}) collective-permute-start(f32[48,2048]{1,0:T(8,128)S(1)} %dynamic-slice_bitcast_fusion.9), channel_id=1, source_target_pairs={{0,12},{4,0},{8,4},{12,8},{1,13},{5,1},{9,5},{13,9},{2,14},{6,2},{... | collective-permute-start | bytes 1179656 | tf_op jit(solution)/shard_map/ppermute | solution.py:55
  253.3 5.7 %collective-permute-done.12 = f32[48,2048]{1,0:T(8,128)S(1)} collective-permute-done((f32[48,2048]{1,0:T(8,128)S(1)}, f32[48,2048]{1,0:T(8,128)S(1)}, u32[]{:S(2)}, u32[]{:S(2)}) %collective-permute-start.12) | collective-permute-done | bytes 393248 | tf_op jit(solution)/shard_map/ppermute | solution.py:54
  259.1 2.2 collective-permute-done.15
  261.4 3.8 %collective-permute-start.16 = (f32[48,2048]{1,0:T(8,128)S(1)}, f32[48,2048]{1,0:T(8,128)S(1)}, u32[]{:S(2)}, u32[]{:S(2)}) collective-permute-start(f32[48,2048]{1,0:T(8,128)S(1)} %bitcast_add_fusion.5), channel_id=1, source_target_pairs={{0,12},{4,0},{8,4},{12,8},{1,13},{5,1},{9,5},{13,9},{2,14},{6,2},{... | collective-permute-start | bytes 1179656 | tf_op jit(solution)/shard_map/ppermute | solution.py:55
  265.1 6.4 %collective-permute-done.13 = f32[48,2048]{1,0:T(8,128)S(1)} collective-permute-done((f32[48,2048]{1,0:T(8,128)S(1)}, f32[48,2048]{1,0:T(8,128)S(1)}, u32[]{:S(2)}, u32[]{:S(2)}) %collective-permute-start.13) | collective-permute-done | bytes 393248 | tf_op jit(solution)/shard_map/ppermute | solution.py:54
  271.7 0.6 collective-permute-done.16
  272.3 3.8 %collective-permute-start.17 = (f32[48,2048]{1,0:T(8,128)S(1)}, f32[48,2048]{1,0:T(8,128)S(1)}, u32[]{:S(2)}, u32[]{:S(2)}) collective-permute-start(f32[48,2048]{1,0:T(8,128)S(1)} %bitcast_add_fusion.4), channel_id=1, source_target_pairs={{0,12},{4,0},{8,4},{12,8},{1,13},{5,1},{9,5},{13,9},{2,14},{6,2},{... | collective-permute-start | bytes 1179656 | tf_op jit(solution)/shard_map/ppermute | solution.py:55
  276.1 4.6 %collective-permute-done.14 = f32[48,2048]{1,0:T(8,128)S(1)} collective-permute-done((f32[48,2048]{1,0:T(8,128)S(1)}, f32[48,2048]{1,0:T(8,128)S(1)}, u32[]{:S(2)}, u32[]{:S(2)}) %collective-permute-start.14) | collective-permute-done | bytes 393248 | tf_op jit(solution)/shard_map/ppermute | solution.py:54
  280.8 2.2 collective-permute-start.20
  283.0 1.5 collective-permute-start.21
  284.6 3.4 %collective-permute-done.20 = f32[48,1024]{1,0:T(8,128)S(1)} collective-permute-done((f32[48,1024]{1,0:T(8,128)S(1)}, f32[48,1024]{1,0:T(8,128)S(1)}, u32[]{:S(2)}, u32[]{:S(2)}) %collective-permute-start.20) | collective-permute-done | bytes 196640 | tf_op jit(solution)/shard_map/ppermute | solution.py:95
  288.0 2.3 collective-permute-done.21
  290.3 0.7 copy-done.10
  291.0 1.3 concatenate.11
  292.3 6.9 %concatenate.10 = f32[400,1024]{1,0:T(8,128)S(1)} concatenate(f32[52,1024]{1,0:T(8,128)} %copy-done.3, f32[52,1024]{1,0:T(8,128)S(1)} %get-tuple-element.19, f32[48,1024]{1,0:T(8,128)} %copy-done.6, f32[48,1024]{1,0:T(8,128)} %copy-done.7, f32[52,1024]{1,0:T(8,128)} %copy-done.8, f32[52,1024]{1,0:T(8,128)} %collective-permute-done.19, f32[48,1024]{1,0:T(8,128)} %copy-done.9, ...), dimensions={0} | concatenate | bytes 3276800 | tf_op jit(solution)/shard_map/concatenate | solution.py:96
  299.2 1.4 broadcast_select_fusion.1
  (76 shorter events, 4.6 us)
Async XLA Ops:
  6.5 97.5 %all-gather.2.cloned.1.call-start = ((), (), s32[]{:S(2)}) async-start(), calls=%async_computation | async-start | bytes 10240000 | tf_op jit(solution)/shard_map/all_gather | solution.py:33
  13.4 3.0 collective-permute-start
  17.7 2.0 copy-start.2
  19.8 57.0 %collective-permute-start.1 = (bf16[1200,1024]{1,0:T(8,128)(2,1)S(1)}, bf16[1200,1024]{1,0:T(8,128)(2,1)S(1)}, u32[]{:S(2)}, u32[]{:S(2)}) collective-permute-start(bf16[1200,1024]{1,0:T(8,128)(2,1)S(1)} %copy-done.2), channel_id=1, source_target_pairs={{0,64},{64,0},{1,65},{65,1},{2,66},{66,2},{3,67},{67,3},{4,68},{68... | collective-permute-start | bytes 7372808 | tf_op jit(solution)/shard_map/ppermute | solution.py:37
  78.4 31.7 %collective-permute-start.2 = (bf16[1200,2048]{1,0:T(8,128)(2,1)}, bf16[1200,2048]{1,0:T(8,128)(2,1)}, u32[]{:S(2)}, u32[]{:S(2)}) collective-permute-start(bf16[1200,2048]{1,0:T(8,128)(2,1)} %constant_dynamic-update-slice_fusion), channel_id=1, source_target_pairs={{0,1},{1,0},{2,3},{3,2},{4,5},{5,4},{6,7},{7,6},{8,9},{9,8},{10,11... | collective-permute-start | bytes 14745608 | tf_op jit(solution)/shard_map/ppermute | solution.py:38
  110.1 14.0 %copy-start = (bf16[8,200,2,1200]{3,1,2,0:T(8,128)(2,1)}, bf16[8,200,2,1200]{3,1,2,0:T(8,128)(2,1)S(1)}, u32[]{:S(2)}) copy-start(bf16[8,200,2,1200]{3,1,2,0:T(8,128)(2,1)S(1)} %copy.35) | copy-start | bytes 23040004
  124.1 2.7 copy-start.1
  127.0 116.3 %collective-permute-start.11 = (f32[4,96,2048]{2,1,0:T(8,128)S(1)}, f32[4,96,2048]{2,1,0:T(8,128)}, u32[]{:S(2)}, u32[]{:S(2)}) collective-permute-start(f32[4,96,2048]{2,1,0:T(8,128)S(1)} %dynamic-slice_bitcast_fusion), channel_id=1, source_target_pairs={{0,2},{2,0},{1,3},{3,1},{4,6},{6,4},{5,7},{7,5},{8,10},{10,8},{9,1... | collective-permute-start | bytes 9437192 | tf_op jit(solution)/shard_map/ppermute | solution.py:74
  143.5 28.9 %collective-permute-start.7 = (f32[2,52,2048]{2,0,1:T(2,128)S(1)}, f32[2,52,2048]{2,0,1:T(2,128)S(1)}, u32[]{:S(2)}, u32[]{:S(2)}) collective-permute-start(f32[2,52,2048]{2,0,1:T(2,128)S(1)} %copy.18), channel_id=1, source_target_pairs={{0,12},{4,0},{8,4},{12,8},{1,13},{5,1},{9,5},{13,9},{2,14},{6,2},{... | collective-permute-start | bytes 2555912 | tf_op jit(solution)/shard_map/ppermute | solution.py:55
  156.6 5.2 %copy-start.5 = (bf16[2,200,2,1200]{3,1,2,0:T(8,128)(2,1)S(1)}, bf16[2,200,2,1200]{3,1,2,0:T(8,128)(2,1)}, u32[]{:S(2)}) copy-start(bf16[2,200,2,1200]{3,1,2,0:T(8,128)(2,1)} %get-tuple-element.15) | copy-start | bytes 5760004
  167.4 21.2 %collective-permute-start.3 = (f32[2,52,2048]{2,0,1:T(2,128)S(1)}, f32[2,52,2048]{2,0,1:T(2,128)S(1)}, u32[]{:S(2)}, u32[]{:S(2)}) collective-permute-start(f32[2,52,2048]{2,0,1:T(2,128)S(1)} %copy.8), channel_id=1, source_target_pairs={{0,4},{4,8},{8,12},{12,0},{1,5},{5,9},{9,13},{13,1},{2,6},{6,10},{... | collective-permute-start | bytes 2555912 | tf_op jit(solution)/shard_map/ppermute | solution.py:54
  172.4 17.5 %copy-start.4 = (bf16[2,200,2,1200]{3,1,2,0:T(8,128)(2,1)S(1)}, bf16[2,200,2,1200]{3,1,2,0:T(8,128)(2,1)}, u32[]{:S(2)}) copy-start(bf16[2,200,2,1200]{3,1,2,0:T(8,128)(2,1)} %get-tuple-element.12) | copy-start | bytes 5760004
  173.6 21.2 %collective-permute-start.8 = (f32[2,52,2048]{2,0,1:T(2,128)S(1)}, f32[2,52,2048]{2,0,1:T(2,128)S(1)}, u32[]{:S(2)}, u32[]{:S(2)}) collective-permute-start(f32[2,52,2048]{2,0,1:T(2,128)S(1)} %copy.21), channel_id=1, source_target_pairs={{0,12},{4,0},{8,4},{12,8},{1,13},{5,1},{9,5},{13,9},{2,14},{6,2},{... | collective-permute-start | bytes 2555912 | tf_op jit(solution)/shard_map/ppermute | solution.py:55
  189.8 20.4 %collective-permute-start.4 = (f32[2,52,2048]{2,0,1:T(2,128)S(1)}, f32[2,52,2048]{2,0,1:T(2,128)S(1)}, u32[]{:S(2)}, u32[]{:S(2)}) collective-permute-start(f32[2,52,2048]{2,0,1:T(2,128)S(1)} %copy.11), channel_id=1, source_target_pairs={{0,4},{4,8},{8,12},{12,0},{1,5},{5,9},{9,13},{13,1},{2,6},{6,10},{... | collective-permute-start | bytes 2555912 | tf_op jit(solution)/shard_map/ppermute | solution.py:54
  196.0 20.7 %collective-permute-start.9 = (f32[2,52,2048]{2,0,1:T(2,128)S(1)}, f32[2,52,2048]{2,0,1:T(2,128)S(1)}, u32[]{:S(2)}, u32[]{:S(2)}) collective-permute-start(f32[2,52,2048]{2,0,1:T(2,128)S(1)} %copy.23), channel_id=1, source_target_pairs={{0,12},{4,0},{8,4},{12,8},{1,13},{5,1},{9,5},{13,9},{2,14},{6,2},{... | collective-permute-start | bytes 2555912 | tf_op jit(solution)/shard_map/ppermute | solution.py:55
  210.7 32.6 %slice-start = ((s8[6291456]{0:T(1024)(128)(4,1)}), s8[4194304]{0:T(1024)(128)(4,1)S(1)}, s32[]{:S(2)}) async-start(s8[6291456]{0:T(1024)(128)(4,1)} %bitcast.90), calls=%async_computation.1 | async-start | bytes 8388608
  211.4 31.9 %slice-start.1 = ((s8[6291456]{0:T(1024)(128)(4,1)}), s8[2097152]{0:T(1024)(128)(4,1)S(1)}, s32[]{:S(2)}) async-start(s8[6291456]{0:T(1024)(128)(4,1)} %bitcast.90), calls=%async_computation.2 | async-start | bytes 4194304
  211.4 19.5 %collective-permute-start.5 = (f32[2,52,2048]{2,0,1:T(2,128)S(1)}, f32[2,52,2048]{2,0,1:T(2,128)S(1)}, u32[]{:S(2)}, u32[]{:S(2)}) collective-permute-start(f32[2,52,2048]{2,0,1:T(2,128)S(1)} %copy.14), channel_id=1, source_target_pairs={{0,4},{4,8},{8,12},{12,0},{1,5},{5,9},{9,13},{13,1},{2,6},{6,10},{... | collective-permute-start | bytes 2555912 | tf_op jit(solution)/shard_map/ppermute | solution.py:54
  217.3 14.8 %collective-permute-start.10 = (f32[52,2048]{1,0:T(8,128)S(1)}, f32[52,2048]{1,0:T(8,128)S(1)}, u32[]{:S(2)}, u32[]{:S(2)}) collective-permute-start(f32[52,2048]{1,0:T(8,128)S(1)} %dynamic-slice_bitcast_fusion.7), channel_id=1, source_target_pairs={{0,2},{2,0},{1,3},{3,1},{4,6},{6,4},{5,7},{7,5},{8,10},{10,8},{9,1... | collective-permute-start | bytes 1277960 | tf_op jit(solution)/shard_map/ppermute | solution.py:63
  231.5 11.7 %collective-permute-start.6 = (f32[52,2048]{1,0:T(8,128)S(1)}, f32[52,2048]{1,0:T(8,128)S(1)}, u32[]{:S(2)}, u32[]{:S(2)}) collective-permute-start(f32[52,2048]{1,0:T(8,128)S(1)} %dynamic-slice_bitcast_fusion.8), channel_id=1, source_target_pairs={{0,2},{2,0},{1,3},{3,1},{4,6},{6,4},{5,7},{7,5},{8,10},{10,8},{9,1... | collective-permute-start | bytes 1277960 | tf_op jit(solution)/shard_map/ppermute | solution.py:63
  232.9 51.7 %collective-permute-start.19 = (f32[52,1024]{1,0:T(8,128)}, f32[52,1024]{1,0:T(8,128)}, u32[]{:S(2)}, u32[]{:S(2)}) collective-permute-start(f32[52,1024]{1,0:T(8,128)} %get-tuple-element.18), channel_id=1, source_target_pairs={{0,64},{64,0},{1,65},{65,1},{2,66},{66,2},{3,67},{67,3},{4,68},{68... | collective-permute-start | bytes 638984 | tf_op jit(solution)/shard_map/ppermute | solution.py:95
  246.1 12.9 %collective-permute-start.12 = (f32[48,2048]{1,0:T(8,128)S(1)}, f32[48,2048]{1,0:T(8,128)S(1)}, u32[]{:S(2)}, u32[]{:S(2)}) collective-permute-start(f32[48,2048]{1,0:T(8,128)S(1)} %dynamic-slice_bitcast_fusion.10), channel_id=1, source_target_pairs={{0,4},{4,8},{8,12},{12,0},{1,5},{5,9},{9,13},{13,1},{2,6},{6,10},{... | collective-permute-start | bytes 1179656 | tf_op jit(solution)/shard_map/ppermute | solution.py:54
  246.2 44.1 %copy-start.3 = (f32[52,1024]{1,0:T(8,128)}, f32[52,1024]{1,0:T(8,128)S(1)}, u32[]{:S(2)}) copy-start(f32[52,1024]{1,0:T(8,128)S(1)} %get-tuple-element.21) | copy-start | bytes 638980
  246.2 38.3 %collective-permute-start.18 = (f32[52,1024]{1,0:T(8,128)S(1)}, f32[52,1024]{1,0:T(8,128)S(1)}, u32[]{:S(2)}, u32[]{:S(2)}) collective-permute-start(f32[52,1024]{1,0:T(8,128)S(1)} %get-tuple-element.20), channel_id=1, source_target_pairs={{0,64},{64,0},{1,65},{65,1},{2,66},{66,2},{3,67},{67,3},{4,68},{68... | collective-permute-start | bytes 638984 | tf_op jit(solution)/shard_map/ppermute | solution.py:95
  250.0 11.3 %collective-permute-start.15 = (f32[48,2048]{1,0:T(8,128)S(1)}, f32[48,2048]{1,0:T(8,128)S(1)}, u32[]{:S(2)}, u32[]{:S(2)}) collective-permute-start(f32[48,2048]{1,0:T(8,128)S(1)} %dynamic-slice_bitcast_fusion.9), channel_id=1, source_target_pairs={{0,12},{4,0},{8,4},{12,8},{1,13},{5,1},{9,5},{13,9},{2,14},{6,2},{... | collective-permute-start | bytes 1179656 | tf_op jit(solution)/shard_map/ppermute | solution.py:55
  259.0 12.5 %collective-permute-start.13 = (f32[48,2048]{1,0:T(8,128)S(1)}, f32[48,2048]{1,0:T(8,128)S(1)}, u32[]{:S(2)}, u32[]{:S(2)}) collective-permute-start(f32[48,2048]{1,0:T(8,128)S(1)} %bitcast_add_fusion.8), channel_id=1, source_target_pairs={{0,4},{4,8},{8,12},{12,0},{1,5},{5,9},{9,13},{13,1},{2,6},{6,10},{... | collective-permute-start | bytes 1179656 | tf_op jit(solution)/shard_map/ppermute | solution.py:54
  261.4 10.9 %collective-permute-start.16 = (f32[48,2048]{1,0:T(8,128)S(1)}, f32[48,2048]{1,0:T(8,128)S(1)}, u32[]{:S(2)}, u32[]{:S(2)}) collective-permute-start(f32[48,2048]{1,0:T(8,128)S(1)} %bitcast_add_fusion.5), channel_id=1, source_target_pairs={{0,12},{4,0},{8,4},{12,8},{1,13},{5,1},{9,5},{13,9},{2,14},{6,2},{... | collective-permute-start | bytes 1179656 | tf_op jit(solution)/shard_map/ppermute | solution.py:55
  271.6 9.1 %collective-permute-start.14 = (f32[48,2048]{1,0:T(8,128)S(1)}, f32[48,2048]{1,0:T(8,128)S(1)}, u32[]{:S(2)}, u32[]{:S(2)}) collective-permute-start(f32[48,2048]{1,0:T(8,128)S(1)} %bitcast_add_fusion.7), channel_id=1, source_target_pairs={{0,4},{4,8},{8,12},{12,0},{1,5},{5,9},{9,13},{13,1},{2,6},{6,10},{... | collective-permute-start | bytes 1179656 | tf_op jit(solution)/shard_map/ppermute | solution.py:54
  272.3 10.6 %collective-permute-start.17 = (f32[48,2048]{1,0:T(8,128)S(1)}, f32[48,2048]{1,0:T(8,128)S(1)}, u32[]{:S(2)}, u32[]{:S(2)}) collective-permute-start(f32[48,2048]{1,0:T(8,128)S(1)} %bitcast_add_fusion.4), channel_id=1, source_target_pairs={{0,12},{4,0},{8,4},{12,8},{1,13},{5,1},{9,5},{13,9},{2,14},{6,2},{... | collective-permute-start | bytes 1179656 | tf_op jit(solution)/shard_map/ppermute | solution.py:55
  280.8 9.5 %copy-start.6 = (f32[48,1024]{1,0:T(8,128)}, f32[48,1024]{1,0:T(8,128)S(1)}, u32[]{:S(2)}) copy-start(f32[48,1024]{1,0:T(8,128)S(1)} %get-tuple-element.25) | copy-start | bytes 589828
  280.8 7.3 %collective-permute-start.20 = (f32[48,1024]{1,0:T(8,128)S(1)}, f32[48,1024]{1,0:T(8,128)S(1)}, u32[]{:S(2)}, u32[]{:S(2)}) collective-permute-start(f32[48,1024]{1,0:T(8,128)S(1)} %get-tuple-element.24), channel_id=1, source_target_pairs={{0,64},{64,0},{1,65},{65,1},{2,66},{66,2},{3,67},{67,3},{4,68},{68... | collective-permute-start | bytes 589832 | tf_op jit(solution)/shard_map/ppermute | solution.py:95
  283.0 7.3 %copy-start.7 = (f32[48,1024]{1,0:T(8,128)}, f32[48,1024]{1,0:T(8,128)S(1)}, u32[]{:S(2)}) copy-start(f32[48,1024]{1,0:T(8,128)S(1)} %get-tuple-element.23) | copy-start | bytes 589828
  283.0 7.3 %collective-permute-start.21 = (f32[48,1024]{1,0:T(8,128)S(1)}, f32[48,1024]{1,0:T(8,128)S(1)}, u32[]{:S(2)}, u32[]{:S(2)}) collective-permute-start(f32[48,1024]{1,0:T(8,128)S(1)} %get-tuple-element.22), channel_id=1, source_target_pairs={{0,64},{64,0},{1,65},{65,1},{2,66},{66,2},{3,67},{67,3},{4,68},{68... | collective-permute-start | bytes 589832 | tf_op jit(solution)/shard_map/ppermute | solution.py:95
  284.6 5.7 %copy-start.8 = (f32[52,1024]{1,0:T(8,128)}, f32[52,1024]{1,0:T(8,128)S(1)}, u32[]{:S(2)}) copy-start(f32[52,1024]{1,0:T(8,128)S(1)} %collective-permute-done.18) | copy-start | bytes 638980
  288.0 2.3 copy-start.9
  290.3 0.7 copy-start.10
Sparse Core Ops, SparseCore 0:
  19.9 84.1 all-gather.1

commit v8 on v7

--- a/solution.py
+++ b/solution.py
@@ -30,9 +30,11 @@
     theirs = jnp.take(tiles, position[:, 1 - core], axis=0)
     from_sibling = lax.ppermute(theirs, "c", SWAP)
     own_owners = jnp.stack([mine, from_sibling], axis=2)
-    gathered = lax.all_gather(own_owners, "z", axis=1, tiled=True)
-    rows = gathered.shape[1]
-    by_y = gathered.reshape(ny, nxl, rows, 2, kc)
+    y_cut = TB * 13 // 25
+    gathered = lax.all_gather(own_owners[:, :y_cut], "z", axis=1, tiled=True)
+    gathered_late = lax.all_gather(own_owners[:, y_cut:], "z", axis=1, tiled=True)
+    y_rows = gathered.shape[1]
+    by_y = gathered.reshape(ny, nxl, y_rows, 2, kc)
 
     amp = jnp.concatenate([amplitudes, lax.ppermute(amplitudes, "xh", SWAP)], axis=1)
     amp = jnp.stack([amp, lax.ppermute(amp, "c", SWAP)], axis=0)
@@ -62,13 +64,13 @@
         there = lax.dynamic_index_in_dim(acc, 1 - xi, 0, keepdims=False)
         return here + lax.ppermute(there, "xl", SWAP)
 
-    y_rows = 8 * (rows * 5 // 72)
     y_half = y_rows // 2
-    x_half = 8 * ((rows - y_rows) // 16)
+    x_rows = gathered_late.shape[1]
+    x_half = 8 * (x_rows // 16)
     late = lax.dot_general(
-        gathered[:, y_rows:], amp, (((2, 3), (0, 1)), ((), ())),
+        gathered_late, amp, (((2, 3), (0, 1)), ((), ())),
         preferred_element_type=jnp.float32,
-    ).reshape(ny, nxl, rows - y_rows, amp.shape[-1])
+    ).reshape(ny, nxl, x_rows, amp.shape[-1])
     late_here = lax.dynamic_index_in_dim(late, xi, 1, keepdims=False)
     late_there = lax.dynamic_index_in_dim(late, 1 - xi, 1, keepdims=False)
     late_sum = late_here + lax.ppermute(late_there, "xl", SWAP)
@@ -93,8 +95,15 @@
 
     kept = [piece[:, :width] for piece in pieces]
     came = [lax.ppermute(piece[:, width:], "xh", SWAP) for piece in pieces]
-    first = jnp.concatenate(kept + came, axis=0)
-    second = jnp.concatenate(came + kept, axis=0)
+
+    def slab_group(parts):
+        early = jnp.concatenate(parts[:2], axis=0).reshape(nz, y_cut, width)
+        late_rows = jnp.concatenate(parts[2:], axis=0).reshape(nz, TB - y_cut, width)
+        return jnp.concatenate([early, late_rows], axis=1).reshape(nz * TB, width)
+
+    kept, came = slab_group(kept), slab_group(came)
+    first = jnp.concatenate([kept, came], axis=0)
+    second = jnp.concatenate([came, kept], axis=0)
     return jnp.where(xh == 0, first, second)
 
 

time: 308 us -> 297 us (0.964)
  local copies, waits for them, and re-layouts: 44.6 us -> 31.4 us
  other arithmetic: 9.39 us -> 13.6 us
    ppermute x2, waiting for transfers between devices: 7.33 us -> 37.6 us  [pair_sum(): return here + lax.ppermute(there, 'xl', SWAP)]
    ppermute x6, waiting for transfers between devices: 52.1 us -> 31.8 us  [ring(): got_ahead = lax.ppermute(acc_ahead, 'y', to_next)]
    all_gather x1 -> x2, waiting for transfers between devices: 25.6 us -> 7.2 us  [the longest x1 7.18 us: local(): lax.all_gather(own_owners[:, y_cut:], 'z', axis=1, tiled=True)]
    squeeze x1, local copies, waits for them, and re-layouts: 9.14 us -> 0.43 us  [block(): lhs = lax.dynamic_index_in_dim(by_y, y_owner % ny, 0, keepdims=False)]
    concatenate x2 -> x0, local copies, waits for them, and re-layouts: 8.2 us -> none  [the longest x1 6.89 us: local(): first = jnp.concatenate(kept + came, axis=0)]
    ppermute x6, starting transfers between devices: 20.6 us -> 12.9 us  [ring(): got_back = lax.ppermute(acc_back, 'y', to_prev)]
    ppermute x4, waiting for transfers between devices: 5.71 us -> 12.9 us  [local(): came = [lax.ppermute(piece[:, width:], 'xh', SWAP) for piece in pieces]]
    ppermute x6, starting transfers between devices: 0.45 us -> 7.12 us  [ring(): got_ahead = lax.ppermute(acc_ahead, 'y', to_next)]
  transfers between devices with their start and end apart: 23 -> 24, of which waited for: 14 -> 16; matrix products, arithmetic and copies ran while one was open for 23% -> 29% of each run, Pallas kernels for 0% -> 0%
where the time goes in v8:
time: 297 us; the launch traced here: 296 us
  waiting for transfers between devices  148 us (50%)
  matrix products  54.7 us (18%)
  starting transfers between devices  34.5 us (12%)
  local copies, waits for them, and re-layouts  31.4 us (11%)
  between operations  13.9 us (5%)
  other arithmetic  13.6 us (5%)
    ppermute x1, waiting for transfers between devices, local(): lax.ppermute(amplitudes, 'xh', SWAP)  50.5 us
    dot_general x8, matrix products, block(): lax.dot_general(lhs[:, low:high], amp, (((2, 3), (0, 1)), ((), ())), pref...  42.6 us
    ppermute x2, waiting for transfers between devices, pair_sum(): return here + lax.ppermute(there, 'xl', SWAP)  37.6 us
    ppermute x6, waiting for transfers between devices, ring(): got_ahead = lax.ppermute(acc_ahead, 'y', to_next)  31.8 us
    ppermute x4, waiting for transfers between devices, local(): came = [lax.ppermute(piece[:, width:], 'xh', SWAP) for piece in pieces]  12.9 us
    ppermute x6, starting transfers between devices, ring(): got_back = lax.ppermute(acc_back, 'y', to_prev)  12.9 us
    dot_general x1, matrix products, local(): lax.dot_general(gathered_late, amp, (((2, 3), (0, 1)), ((), ())), preferr...  12.1 us
    all_gather x1, waiting for transfers between devices, local(): lax.all_gather(own_owners[:, y_cut:], 'z', axis=1, tiled=True)  7.18 us
  transfers between devices with their start and end apart: 24, of which 16 were waited for; matrix products, arithmetic and copies ran while one was open for 29% of the time, Pallas kernels for 0%

profile of v8, /device:TPU:0, one launch (start us, length us, event | category | flops | bytes accessed | tf_op | source)
XLA Modules:
  0.0 295.8 jit_solution(14932996566640186318)
XLA Ops:
  6.5 0.7 dynamic_slice.75
  7.3 1.2 sort.17
  8.9 2.6 reshape.35
  12.3 1.1 copy.4
  14.2 2.1 collective-permute-done
  16.3 1.4 copy.42
  17.9 1.6 copy.6
  19.5 3.2 %collective-permute-start.1 = (bf16[1200,1024]{1,0:T(8,128)(2,1)}, bf16[1200,1024]{1,0:T(8,128)(2,1)S(1)}, u32[]{:S(2)}, u32[]{:S(2)}) collective-permute-start(bf16[1200,1024]{1,0:T(8,128)(2,1)} %param.5), channel_id=1, source_target_pairs={{0,64},{64,0},{1,65},{65,1},{2,66},{66,2},{3,67},{67,3},{4,68},{68... | collective-permute-start | bytes 7372808 | tf_op jit(solution)/shard_map/ppermute | solution.py:39
  22.7 3.4 %constant_dynamic-update-slice_fusion.1 = bf16[1200,2048]{1,0:T(8,128)(2,1)} fusion(bf16[1200,1024]{1,0:T(8,128)(2,1)} %param.5), kind=kLoop, calls=%fused_computation.66 | loop fusion | bytes 4915200
  26.2 50.5 %collective-permute-done.1 = bf16[1200,1024]{1,0:T(8,128)(2,1)S(1)} collective-permute-done((bf16[1200,1024]{1,0:T(8,128)(2,1)}, bf16[1200,1024]{1,0:T(8,128)(2,1)S(1)}, u32[]{:S(2)}, u32[]{:S(2)}) %collective-permute-start.1) | collective-permute-done | bytes 2457632 | tf_op jit(solution)/shard_map/ppermute | solution.py:39
  76.7 1.7 constant_dynamic-update-slice_fusion
  78.4 1.3 pad_maximum_fusion
  79.9 3.5 %copy.34 = bf16[8,104,2,1200]{3,1,2,0:T(8,128)(2,1)S(1)} copy(bf16[8,104,2,1200]{3,0,2,1:T(8,128)(2,1)} %all-gather.3.cloned.1.call-done) | data formatting | bytes 7987200 | tf_op jit(solution)/shard_map/reshape | solution.py:37
  83.8 3.1 %collective-permute-done.2 = bf16[1200,2048]{1,0:T(8,128)(2,1)} collective-permute-done((bf16[1200,2048]{1,0:T(8,128)(2,1)}, bf16[1200,2048]{1,0:T(8,128)(2,1)}, u32[]{:S(2)}, u32[]{:S(2)}) %collective-permute-start.2) | collective-permute-done | bytes 4915232 | tf_op jit(solution)/shard_map/ppermute | solution.py:40
  87.0 4.9 %convolution_bitcast_fusion.7 = f32[2,52,2048]{2,1,0:T(8,128)S(1)} fusion(bf16[2,104,2,1200]{3,1,2,0:T(8,128)(2,1)S(1)} %get-tuple-element.15, bf16[1,1200,2048]{2,1,0:T(8,128)(2,1)} %bitcast.5, bf16[1,1200,2048]{2,1,0:T(8,128)(2,1)} %bitcast.4), kind=kOutput, calls=%fused_computation.12 | convolution fusion | flops 1027276800 | bytes 11255808 | tf_op jit(solution)/shard_map/dot_general | solution.py:44
  91.8 1.6 copy.8
  93.4 1.7 collective-permute-start.3
  95.1 4.9 %convolution_bitcast_fusion.3 = f32[2,52,2048]{2,1,0:T(8,128)S(1)} fusion(bf16[2,104,2,1200]{3,1,2,0:T(8,128)(2,1)S(1)} %get-tuple-element.12, bf16[1,1200,2048]{2,1,0:T(8,128)(2,1)} %bitcast.5, bf16[1,1200,2048]{2,1,0:T(8,128)(2,1)} %bitcast.4), kind=kOutput, calls=%fused_computation.8 | convolution fusion | flops 1027276800 | bytes 11255808 | tf_op jit(solution)/shard_map/dot_general | solution.py:44
  100.0 1.6 copy.18
  101.6 1.7 collective-permute-start.7
  103.4 6.6 %convolution_bitcast_fusion.6 = f32[2,52,2048]{2,1,0:T(8,128)} fusion(bf16[2,104,2,1200]{3,1,2,0:T(8,128)(2,1)S(1)} %get-tuple-element.10, bf16[1,1200,2048]{2,1,0:T(8,128)(2,1)} %bitcast.5, bf16[1,1200,2048]{2,1,0:T(8,128)(2,1)} %bitcast.4), kind=kOutput, calls=%fused_computation.11 | convolution fusion | flops 1027276800 | bytes 11255808 | tf_op jit(solution)/shard_map/dot_general | solution.py:44
  110.0 5.0 %convolution_bitcast_fusion.1 = f32[2,52,2048]{2,1,0:T(8,128)S(1)} fusion(bf16[2,104,2,1200]{3,1,2,0:T(8,128)(2,1)S(1)} %get-tuple-element.15, bf16[1,1200,2048]{2,1,0:T(8,128)(2,1)} %bitcast.5, bf16[1,1200,2048]{2,1,0:T(8,128)(2,1)} %bitcast.4), kind=kOutput, calls=%fused_computation.6 | convolution fusion | flops 1027276800 | bytes 11255808 | tf_op jit(solution)/shard_map/dot_general | solution.py:44
  115.0 6.6 %convolution_bitcast_fusion.2 = f32[2,52,2048]{2,1,0:T(8,128)} fusion(bf16[2,104,2,1200]{3,1,2,0:T(8,128)(2,1)S(1)} %get-tuple-element.11, bf16[1,1200,2048]{2,1,0:T(8,128)(2,1)} %bitcast.5, bf16[1,1200,2048]{2,1,0:T(8,128)(2,1)} %bitcast.4), kind=kOutput, calls=%fused_computation.7 | convolution fusion | flops 1027276800 | bytes 11255808 | tf_op jit(solution)/shard_map/dot_general | solution.py:44
  121.6 7.2 %all-gather.5.cloned.1.call-done = bf16[8,96,2,1200]{3,1,2,0:T(8,128)(2,1)} async-done(((bf16[8,24,2,1200]{3,1,2,0:T(8,128)(2,1)}), bf16[8,96,2,1200]{3,1,2,0:T(8,128)(2,1)}) %all-gather.5.cloned.1.call-update) | async-done | bytes 3686416 | tf_op jit(solution)/shard_map/all_gather | solution.py:35
  128.8 12.1 %fusion.11 = f32[8,96,2048,1]{2,1,3,0:T(8,128)S(1)} fusion(bf16[8,96,2,1200]{3,1,2,0:T(8,128)(2,1)} %all-gather.5.cloned.1.call-done, bf16[1,1200,2048]{2,1,0:T(8,128)(2,1)} %bitcast.5, bf16[1,1200,2048]{2,1,0:T(8,128)(2,1)} %bitcast.4), kind=kOutput, calls=%fused_computation.71 | convolution fusion | flops 7554662400 | bytes 19808256 | tf_op jit(solution)/shard_map/dot_general | solution.py:70
  140.9 4.9 %convolution_bitcast_fusion.5 = f32[2,52,2048]{2,1,0:T(8,128)S(1)} fusion(bf16[2,104,2,1200]{3,1,2,0:T(8,128)(2,1)S(1)} %get-tuple-element.14, bf16[1,1200,2048]{2,1,0:T(8,128)(2,1)} %bitcast.5, bf16[1,1200,2048]{2,1,0:T(8,128)(2,1)} %bitcast.4), kind=kOutput, calls=%fused_computation.10 | convolution fusion | flops 1027276800 | bytes 11255808 | tf_op jit(solution)/shard_map/dot_general | solution.py:44
  146.0 1.5 collective-permute-start.11
  147.6 1.7 copy_add_fusion.5
  149.9 1.6 collective-permute-start.4
  151.5 1.7 copy_add_fusion.2
  153.8 2.0 collective-permute-start.8
  155.9 4.9 %convolution_bitcast_fusion = f32[2,52,2048]{2,1,0:T(8,128)S(1)} fusion(bf16[2,104,2,1200]{3,1,2,0:T(8,128)(2,1)S(1)} %get-tuple-element.13, bf16[1,1200,2048]{2,1,0:T(8,128)(2,1)} %bitcast.5, bf16[1,1200,2048]{2,1,0:T(8,128)(2,1)} %bitcast.4), kind=kOutput, calls=%fused_computation.5 | convolution fusion | flops 1027276800 | bytes 11255808 | tf_op jit(solution)/shard_map/dot_general | solution.py:44
  160.8 10.7 %collective-permute-done.4 = f32[2,52,2048]{2,0,1:T(2,128)S(1)} collective-permute-done((f32[2,52,2048]{2,0,1:T(2,128)S(1)}, f32[2,52,2048]{2,0,1:T(2,128)S(1)}, u32[]{:S(2)}, u32[]{:S(2)}) %collective-permute-start.4) | collective-permute-done | bytes 852000 | tf_op jit(solution)/shard_map/ppermute | solution.py:56
  173.0 1.1 collective-permute-done.8
  175.3 3.0 %collective-permute-start.9 = (f32[2,52,2048]{2,0,1:T(2,128)S(1)}, f32[2,52,2048]{2,0,1:T(2,128)S(1)}, u32[]{:S(2)}, u32[]{:S(2)}) collective-permute-start(f32[2,52,2048]{2,0,1:T(2,128)S(1)} %copy.23), channel_id=1, source_target_pairs={{0,12},{4,0},{8,4},{12,8},{1,13},{5,1},{9,5},{13,9},{2,14},{6,2},{... | collective-permute-start | bytes 2555912 | tf_op jit(solution)/shard_map/ppermute | solution.py:57
  178.3 4.9 %convolution_bitcast_fusion.4 = f32[2,52,2048]{2,1,0:T(8,128)S(1)} fusion(bf16[2,104,2,1200]{3,1,2,0:T(8,128)(2,1)S(1)} %get-tuple-element.13, bf16[1,1200,2048]{2,1,0:T(8,128)(2,1)} %bitcast.5, bf16[1,1200,2048]{2,1,0:T(8,128)(2,1)} %bitcast.4), kind=kOutput, calls=%fused_computation.9 | convolution fusion | flops 1027276800 | bytes 11255808 | tf_op jit(solution)/shard_map/dot_general | solution.py:44
  183.2 10.1 %collective-permute-done.5 = f32[2,52,2048]{2,0,1:T(2,128)S(1)} collective-permute-done((f32[2,52,2048]{2,0,1:T(2,128)S(1)}, f32[2,52,2048]{2,0,1:T(2,128)S(1)}, u32[]{:S(2)}, u32[]{:S(2)}) %collective-permute-start.5) | collective-permute-done | bytes 852000 | tf_op jit(solution)/shard_map/ppermute | solution.py:56
  193.9 1.5 collective-permute-start.6
  196.0 1.1 collective-permute-start.10
  197.0 29.9 %collective-permute-done.6 = f32[52,2048]{1,0:T(8,128)S(1)} collective-permute-done((f32[52,2048]{1,0:T(8,128)S(1)}, f32[52,2048]{1,0:T(8,128)S(1)}, u32[]{:S(2)}, u32[]{:S(2)}) %collective-permute-start.6) | collective-permute-done | bytes 426016 | tf_op jit(solution)/shard_map/ppermute | solution.py:65
  227.7 7.7 %collective-permute-done.10 = f32[52,2048]{1,0:T(8,128)S(1)} collective-permute-done((f32[52,2048]{1,0:T(8,128)S(1)}, f32[52,2048]{1,0:T(8,128)S(1)}, u32[]{:S(2)}, u32[]{:S(2)}) %collective-permute-start.10) | collective-permute-done | bytes 426016 | tf_op jit(solution)/shard_map/ppermute | solution.py:65
  235.5 0.8 fusion.14
  237.0 0.8 dynamic-slice_bitcast_fusion.10
  237.8 1.5 collective-permute-start.12
  239.3 0.8 pad_maximum_fusion.3
  240.1 1.9 reshape.38
  242.0 3.0 %collective-permute-start.18 = (f32[52,1024]{1,0:T(8,128)}, f32[52,1024]{1,0:T(8,128)S(1)}, u32[]{:S(2)}, u32[]{:S(2)}) collective-permute-start(f32[52,1024]{1,0:T(8,128)} %get-tuple-element.19), channel_id=1, source_target_pairs={{0,64},{64,0},{1,65},{65,1},{2,66},{66,2},{3,67},{67,3},{4,68},{68... | collective-permute-start | bytes 638984 | tf_op jit(solution)/shard_map/ppermute | solution.py:97
  245.5 0.8 dynamic-slice_bitcast_fusion.9
  246.3 1.8 collective-permute-start.15
  248.1 3.9 %collective-permute-done.18 = f32[52,1024]{1,0:T(8,128)S(1)} collective-permute-done((f32[52,1024]{1,0:T(8,128)}, f32[52,1024]{1,0:T(8,128)S(1)}, u32[]{:S(2)}, u32[]{:S(2)}) %collective-permute-start.18) | collective-permute-done | bytes 213024 | tf_op jit(solution)/shard_map/ppermute | solution.py:97
  251.9 2.7 collective-permute-done.19
  254.6 0.8 pad_maximum_fusion.4
  255.4 1.9 reshape.42
  257.3 1.6 collective-permute-start.13
  258.9 1.0 bitcast_add_fusion.5
  259.9 1.8 collective-permute-start.16
  261.7 5.8 %collective-permute-done.13 = f32[48,2048]{1,0:T(8,128)S(1)} collective-permute-done((f32[48,2048]{1,0:T(8,128)S(1)}, f32[48,2048]{1,0:T(8,128)S(1)}, u32[]{:S(2)}, u32[]{:S(2)}) %collective-permute-start.13) | collective-permute-done | bytes 393248 | tf_op jit(solution)/shard_map/ppermute | solution.py:56
  268.1 1.1 collective-permute-done.16
  269.2 2.5 collective-permute-start.17
  271.7 5.2 %collective-permute-done.14 = f32[48,2048]{1,0:T(8,128)S(1)} collective-permute-done((f32[48,2048]{1,0:T(8,128)S(1)}, f32[48,2048]{1,0:T(8,128)S(1)}, u32[]{:S(2)}, u32[]{:S(2)}) %collective-permute-start.14) | collective-permute-done | bytes 393248 | tf_op jit(solution)/shard_map/ppermute | solution.py:56
  277.2 3.0 %collective-permute-start.20 = (f32[48,1024]{1,0:T(8,128)S(1)}, f32[48,1024]{1,0:T(8,128)S(1)}, u32[]{:S(2)}, u32[]{:S(2)}) collective-permute-start(f32[48,1024]{1,0:T(8,128)S(1)} %get-tuple-element.23), channel_id=1, source_target_pairs={{0,64},{64,0},{1,65},{65,1},{2,66},{66,2},{3,67},{67,3},{4,68},{68... | collective-permute-start | bytes 589832 | tf_op jit(solution)/shard_map/ppermute | solution.py:97
  281.0 3.4 %collective-permute-done.20 = f32[48,1024]{1,0:T(8,128)S(1)} collective-permute-done((f32[48,1024]{1,0:T(8,128)S(1)}, f32[48,1024]{1,0:T(8,128)S(1)}, u32[]{:S(2)}, u32[]{:S(2)}) %collective-permute-start.20) | collective-permute-done | bytes 196640 | tf_op jit(solution)/shard_map/ppermute | solution.py:97
  284.4 3.0 collective-permute-done.21
  287.6 1.3 maximum_select_fusion
  (69 shorter events, 12.0 us)
Async XLA Ops:
  6.5 73.3 %all-gather.3.cloned.1.call-start = ((), (), s32[]{:S(2)}) async-start(), calls=%async_computation | async-start | bytes 5324800 | tf_op jit(solution)/shard_map/all_gather | solution.py:34
  13.4 3.0 %collective-permute-start = (bf16[8,50,1200]{2,0,1:T(8,128)(2,1)}, bf16[8,50,1200]{2,0,1:T(8,128)(2,1)}, u32[]{:S(2)}, u32[]{:S(2)}) collective-permute-start(bf16[8,50,1200]{2,0,1:T(8,128)(2,1)} %copy.4), channel_id=1, source_target_pairs={{0,1},{1,0},{2,3},{3,2},{4,5},{5,4},{6,7},{7,6},{8,9},{9,8},{10,11... | collective-permute-start | bytes 2880008 | tf_op jit(solution)/shard_map/ppermute | solution.py:31
  19.5 109.3 %all-gather.5.cloned.1.call-start = ((), (), s32[]{:S(2)}) async-start(), calls=%async_computation.1 | async-start | bytes 4915200 | tf_op jit(solution)/shard_map/all_gather | solution.py:35
  19.5 57.2 %collective-permute-start.1 = (bf16[1200,1024]{1,0:T(8,128)(2,1)}, bf16[1200,1024]{1,0:T(8,128)(2,1)S(1)}, u32[]{:S(2)}, u32[]{:S(2)}) collective-permute-start(bf16[1200,1024]{1,0:T(8,128)(2,1)} %param.5), channel_id=1, source_target_pairs={{0,64},{64,0},{1,65},{65,1},{2,66},{66,2},{3,67},{67,3},{4,68},{68... | collective-permute-start | bytes 7372808 | tf_op jit(solution)/shard_map/ppermute | solution.py:39
  78.4 8.5 %collective-permute-start.2 = (bf16[1200,2048]{1,0:T(8,128)(2,1)}, bf16[1200,2048]{1,0:T(8,128)(2,1)}, u32[]{:S(2)}, u32[]{:S(2)}) collective-permute-start(bf16[1200,2048]{1,0:T(8,128)(2,1)} %constant_dynamic-update-slice_fusion), channel_id=1, source_target_pairs={{0,1},{1,0},{2,3},{3,2},{4,5},{5,4},{6,7},{7,6},{8,9},{9,8},{10,11... | collective-permute-start | bytes 14745608 | tf_op jit(solution)/shard_map/ppermute | solution.py:40
  93.4 54.1 %collective-permute-start.3 = (f32[2,52,2048]{2,0,1:T(2,128)}, f32[2,52,2048]{2,0,1:T(2,128)}, u32[]{:S(2)}, u32[]{:S(2)}) collective-permute-start(f32[2,52,2048]{2,0,1:T(2,128)} %copy.8), channel_id=1, source_target_pairs={{0,4},{4,8},{8,12},{12,0},{1,5},{5,9},{9,13},{13,1},{2,6},{6,10},{... | collective-permute-start | bytes 2555912 | tf_op jit(solution)/shard_map/ppermute | solution.py:56
  101.6 49.9 %collective-permute-start.7 = (f32[2,52,2048]{2,0,1:T(2,128)}, f32[2,52,2048]{2,0,1:T(2,128)}, u32[]{:S(2)}, u32[]{:S(2)}) collective-permute-start(f32[2,52,2048]{2,0,1:T(2,128)} %copy.18), channel_id=1, source_target_pairs={{0,12},{4,0},{8,4},{12,8},{1,13},{5,1},{9,5},{13,9},{2,14},{6,2},{... | collective-permute-start | bytes 2555912 | tf_op jit(solution)/shard_map/ppermute | solution.py:57
  145.8 1.8 copy-start.3
  146.0 5.5 %copy-start.2 = (f32[2,52,2048]{2,1,0:T(8,128)S(1)}, f32[2,52,2048]{2,1,0:T(8,128)}, u32[]{:S(2)}) copy-start(f32[2,52,2048]{2,1,0:T(8,128)} %convolution_bitcast_fusion.2) | copy-start | bytes 2555908
  146.0 90.2 %collective-permute-start.11 = (f32[4,96,2048]{2,1,0:T(8,128)S(1)}, f32[4,96,2048]{2,1,0:T(8,128)S(1)}, u32[]{:S(2)}, u32[]{:S(2)}) collective-permute-start(f32[4,96,2048]{2,1,0:T(8,128)S(1)} %dynamic-slice_bitcast_fusion), channel_id=1, source_target_pairs={{0,2},{2,0},{1,3},{3,1},{4,6},{6,4},{5,7},{7,5},{8,10},{10,8},{9,1... | collective-permute-start | bytes 9437192 | tf_op jit(solution)/shard_map/ppermute | solution.py:76
  149.9 21.5 %collective-permute-start.4 = (f32[2,52,2048]{2,0,1:T(2,128)S(1)}, f32[2,52,2048]{2,0,1:T(2,128)S(1)}, u32[]{:S(2)}, u32[]{:S(2)}) collective-permute-start(f32[2,52,2048]{2,0,1:T(2,128)S(1)} %copy.11), channel_id=1, source_target_pairs={{0,4},{4,8},{8,12},{12,0},{1,5},{5,9},{9,13},{13,1},{2,6},{6,10},{... | collective-permute-start | bytes 2555912 | tf_op jit(solution)/shard_map/ppermute | solution.py:56
  153.8 20.3 %collective-permute-start.8 = (f32[2,52,2048]{2,0,1:T(2,128)S(1)}, f32[2,52,2048]{2,0,1:T(2,128)S(1)}, u32[]{:S(2)}, u32[]{:S(2)}) collective-permute-start(f32[2,52,2048]{2,0,1:T(2,128)S(1)} %copy.21), channel_id=1, source_target_pairs={{0,12},{4,0},{8,4},{12,8},{1,13},{5,1},{9,5},{13,9},{2,14},{6,2},{... | collective-permute-start | bytes 2555912 | tf_op jit(solution)/shard_map/ppermute | solution.py:57
  172.6 20.7 %collective-permute-start.5 = (f32[2,52,2048]{2,0,1:T(2,128)S(1)}, f32[2,52,2048]{2,0,1:T(2,128)S(1)}, u32[]{:S(2)}, u32[]{:S(2)}) collective-permute-start(f32[2,52,2048]{2,0,1:T(2,128)S(1)} %copy.14), channel_id=1, source_target_pairs={{0,4},{4,8},{8,12},{12,0},{1,5},{5,9},{9,13},{13,1},{2,6},{6,10},{... | collective-permute-start | bytes 2555912 | tf_op jit(solution)/shard_map/ppermute | solution.py:56
  175.3 20.1 %collective-permute-start.9 = (f32[2,52,2048]{2,0,1:T(2,128)S(1)}, f32[2,52,2048]{2,0,1:T(2,128)S(1)}, u32[]{:S(2)}, u32[]{:S(2)}) collective-permute-start(f32[2,52,2048]{2,0,1:T(2,128)S(1)} %copy.23), channel_id=1, source_target_pairs={{0,12},{4,0},{8,4},{12,8},{1,13},{5,1},{9,5},{13,9},{2,14},{6,2},{... | collective-permute-start | bytes 2555912 | tf_op jit(solution)/shard_map/ppermute | solution.py:57
  193.9 33.0 %collective-permute-start.6 = (f32[52,2048]{1,0:T(8,128)S(1)}, f32[52,2048]{1,0:T(8,128)S(1)}, u32[]{:S(2)}, u32[]{:S(2)}) collective-permute-start(f32[52,2048]{1,0:T(8,128)S(1)} %dynamic-slice_bitcast_fusion.8), channel_id=1, source_target_pairs={{0,2},{2,0},{1,3},{3,1},{4,6},{6,4},{5,7},{7,5},{8,10},{10,8},{9,1... | collective-permute-start | bytes 1277960 | tf_op jit(solution)/shard_map/ppermute | solution.py:65
  196.0 39.5 %collective-permute-start.10 = (f32[52,2048]{1,0:T(8,128)S(1)}, f32[52,2048]{1,0:T(8,128)S(1)}, u32[]{:S(2)}, u32[]{:S(2)}) collective-permute-start(f32[52,2048]{1,0:T(8,128)S(1)} %dynamic-slice_bitcast_fusion.7), channel_id=1, source_target_pairs={{0,2},{2,0},{1,3},{3,1},{4,6},{6,4},{5,7},{7,5},{8,10},{10,8},{9,1... | collective-permute-start | bytes 1277960 | tf_op jit(solution)/shard_map/ppermute | solution.py:65
  237.8 19.4 %collective-permute-start.12 = (f32[48,2048]{1,0:T(8,128)}, f32[48,2048]{1,0:T(8,128)S(1)}, u32[]{:S(2)}, u32[]{:S(2)}) collective-permute-start(f32[48,2048]{1,0:T(8,128)} %dynamic-slice_bitcast_fusion.10), channel_id=1, source_target_pairs={{0,4},{4,8},{8,12},{12,0},{1,5},{5,9},{9,13},{13,1},{2,6},{6,10},{... | collective-permute-start | bytes 1179656 | tf_op jit(solution)/shard_map/ppermute | solution.py:56
  242.0 9.9 %collective-permute-start.18 = (f32[52,1024]{1,0:T(8,128)}, f32[52,1024]{1,0:T(8,128)S(1)}, u32[]{:S(2)}, u32[]{:S(2)}) collective-permute-start(f32[52,1024]{1,0:T(8,128)} %get-tuple-element.19), channel_id=1, source_target_pairs={{0,64},{64,0},{1,65},{65,1},{2,66},{66,2},{3,67},{67,3},{4,68},{68... | collective-permute-start | bytes 638984 | tf_op jit(solution)/shard_map/ppermute | solution.py:97
  245.0 9.7 %collective-permute-start.19 = (f32[52,1024]{1,0:T(8,128)}, f32[52,1024]{1,0:T(8,128)S(1)}, u32[]{:S(2)}, u32[]{:S(2)}) collective-permute-start(f32[52,1024]{1,0:T(8,128)} %get-tuple-element.21), channel_id=1, source_target_pairs={{0,64},{64,0},{1,65},{65,1},{2,66},{66,2},{3,67},{67,3},{4,68},{68... | collective-permute-start | bytes 638984 | tf_op jit(solution)/shard_map/ppermute | solution.py:97
  246.3 12.6 %collective-permute-start.15 = (f32[48,2048]{1,0:T(8,128)}, f32[48,2048]{1,0:T(8,128)}, u32[]{:S(2)}, u32[]{:S(2)}) collective-permute-start(f32[48,2048]{1,0:T(8,128)} %dynamic-slice_bitcast_fusion.9), channel_id=1, source_target_pairs={{0,12},{4,0},{8,4},{12,8},{1,13},{5,1},{9,5},{13,9},{2,14},{6,2},{... | collective-permute-start | bytes 1179656 | tf_op jit(solution)/shard_map/ppermute | solution.py:57
  257.3 10.2 %collective-permute-start.13 = (f32[48,2048]{1,0:T(8,128)S(1)}, f32[48,2048]{1,0:T(8,128)S(1)}, u32[]{:S(2)}, u32[]{:S(2)}) collective-permute-start(f32[48,2048]{1,0:T(8,128)S(1)} %bitcast_add_fusion.8), channel_id=1, source_target_pairs={{0,4},{4,8},{8,12},{12,0},{1,5},{5,9},{9,13},{13,1},{2,6},{6,10},{... | collective-permute-start | bytes 1179656 | tf_op jit(solution)/shard_map/ppermute | solution.py:56
  259.9 9.2 %collective-permute-start.16 = (f32[48,2048]{1,0:T(8,128)S(1)}, f32[48,2048]{1,0:T(8,128)S(1)}, u32[]{:S(2)}, u32[]{:S(2)}) collective-permute-start(f32[48,2048]{1,0:T(8,128)S(1)} %bitcast_add_fusion.5), channel_id=1, source_target_pairs={{0,12},{4,0},{8,4},{12,8},{1,13},{5,1},{9,5},{13,9},{2,14},{6,2},{... | collective-permute-start | bytes 1179656 | tf_op jit(solution)/shard_map/ppermute | solution.py:57
  267.6 13.2 %copy-start = (f32[4,26,1024]{2,1,0:T(8,128)S(1)}, f32[4,26,1024]{2,1,0:T(8,128)}, u32[]{:S(2)}) copy-start(f32[4,26,1024]{2,1,0:T(8,128)} %reshape.38) | copy-start | bytes 1277956
  267.6 9.4 %collective-permute-start.14 = (f32[48,2048]{1,0:T(8,128)S(1)}, f32[48,2048]{1,0:T(8,128)S(1)}, u32[]{:S(2)}, u32[]{:S(2)}) collective-permute-start(f32[48,2048]{1,0:T(8,128)S(1)} %bitcast_add_fusion.7), channel_id=1, source_target_pairs={{0,4},{4,8},{8,12},{12,0},{1,5},{5,9},{9,13},{13,1},{2,6},{6,10},{... | collective-permute-start | bytes 1179656 | tf_op jit(solution)/shard_map/ppermute | solution.py:56
  269.2 7.8 %collective-permute-start.17 = (f32[48,2048]{1,0:T(8,128)S(1)}, f32[48,2048]{1,0:T(8,128)S(1)}, u32[]{:S(2)}, u32[]{:S(2)}) collective-permute-start(f32[48,2048]{1,0:T(8,128)S(1)} %bitcast_add_fusion.4), channel_id=1, source_target_pairs={{0,12},{4,0},{8,4},{12,8},{1,13},{5,1},{9,5},{13,9},{2,14},{6,2},{... | collective-permute-start | bytes 1179656 | tf_op jit(solution)/shard_map/ppermute | solution.py:57
  277.1 10.3 %copy-start.1 = (f32[4,26,1024]{2,1,0:T(8,128)S(1)}, f32[4,26,1024]{2,1,0:T(8,128)}, u32[]{:S(2)}) copy-start(f32[4,26,1024]{2,1,0:T(8,128)} %reshape.42) | copy-start | bytes 1277956
  277.2 7.3 %collective-permute-start.20 = (f32[48,1024]{1,0:T(8,128)S(1)}, f32[48,1024]{1,0:T(8,128)S(1)}, u32[]{:S(2)}, u32[]{:S(2)}) collective-permute-start(f32[48,1024]{1,0:T(8,128)S(1)} %get-tuple-element.23), channel_id=1, source_target_pairs={{0,64},{64,0},{1,65},{65,1},{2,66},{66,2},{3,67},{67,3},{4,68},{68... | collective-permute-start | bytes 589832 | tf_op jit(solution)/shard_map/ppermute | solution.py:97
  280.2 7.2 %collective-permute-start.21 = (f32[48,1024]{1,0:T(8,128)S(1)}, f32[48,1024]{1,0:T(8,128)S(1)}, u32[]{:S(2)}, u32[]{:S(2)}) collective-permute-start(f32[48,1024]{1,0:T(8,128)S(1)} %get-tuple-element.25), channel_id=1, source_target_pairs={{0,64},{64,0},{1,65},{65,1},{2,66},{66,2},{3,67},{67,3},{4,68},{68... | collective-permute-start | bytes 589832 | tf_op jit(solution)/shard_map/ppermute | solution.py:97
Sparse Core Ops, SparseCore 0:
  19.6 51.4 all-gather.2
  79.9 48.8 all-gather.4

commit v9 on v8

--- a/solution.py
+++ b/solution.py
@@ -30,7 +30,7 @@
     theirs = jnp.take(tiles, position[:, 1 - core], axis=0)
     from_sibling = lax.ppermute(theirs, "c", SWAP)
     own_owners = jnp.stack([mine, from_sibling], axis=2)
-    y_cut = TB * 13 // 25
+    y_cut = TB * 3 // 5
     gathered = lax.all_gather(own_owners[:, :y_cut], "z", axis=1, tiled=True)
     gathered_late = lax.all_gather(own_owners[:, y_cut:], "z", axis=1, tiled=True)
     y_rows = gathered.shape[1]

time: 297 us -> 313 us (1.054)
  waiting for transfers between devices: 148 us -> 171 us
  matrix products: 54.7 us -> 49.7 us
    ppermute x2, waiting for transfers between devices: 37.6 us -> 2.02 us  [pair_sum(): return here + lax.ppermute(there, 'xl', SWAP)]
    all_gather x1, waiting for transfers between devices: 0.02 us -> 34.6 us  [local(): gathered = lax.all_gather(own_owners[:, :y_cut], 'z', axis=1, tiled=True)]
    ppermute x6, waiting for transfers between devices: 2.21 us -> 27.5 us  [ring(): got_back = lax.ppermute(acc_back, 'y', to_prev)]
    ppermute x4, waiting for transfers between devices: 12.9 us -> 22.3 us  [local(): came = [lax.ppermute(piece[:, width:], 'xh', SWAP) for piece in pieces]]
    all_gather x1, waiting for transfers between devices: 7.18 us -> 0.02 us  [local(): lax.all_gather(own_owners[:, y_cut:], 'z', axis=1, tiled=True)]
    ppermute x6, waiting for transfers between devices: 31.8 us -> 25.7 us  [ring(): got_ahead = lax.ppermute(acc_ahead, 'y', to_next)]
    ppermute x6, starting transfers between devices: 7.12 us -> 3.09 us  [ring(): got_ahead = lax.ppermute(acc_ahead, 'y', to_next)]
    dot_general x8, matrix products: 42.6 us -> 38.7 us  [block(): lax.dot_general(lhs[:, low:high], amp, (((2, 3), (0, 1)), ((), ())), pref...]
  transfers between devices with their start and end apart: 24 -> 24, of which waited for: 16 -> 16; matrix products, arithmetic and copies ran while one was open for 29% -> 25% of each run, Pallas kernels for 0% -> 0%
where the time goes in v9:
time: 313 us; the launch traced here: 312 us
  waiting for transfers between devices  171 us (55%)
  matrix products  49.7 us (16%)
  starting transfers between devices  34.4 us (11%)
  local copies, waits for them, and re-layouts  29.9 us (10%)
  between operations  14 us (4%)
  other arithmetic  12.1 us (4%)
    ppermute x1, waiting for transfers between devices, local(): lax.ppermute(amplitudes, 'xh', SWAP)  50.6 us
    dot_general x8, matrix products, block(): lax.dot_general(lhs[:, low:high], amp, (((2, 3), (0, 1)), ((), ())), pref...  38.7 us
    all_gather x1, waiting for transfers between devices, local(): gathered = lax.all_gather(own_owners[:, :y_cut], 'z', axis=1, tiled=True)  34.6 us
    ppermute x6, waiting for transfers between devices, ring(): got_back = lax.ppermute(acc_back, 'y', to_prev)  27.5 us
    ppermute x6, waiting for transfers between devices, ring(): got_ahead = lax.ppermute(acc_ahead, 'y', to_next)  25.7 us
    ppermute x4, waiting for transfers between devices, local(): came = [lax.ppermute(piece[:, width:], 'xh', SWAP) for piece in pieces]  22.3 us
    ppermute x6, starting transfers between devices, ring(): got_back = lax.ppermute(acc_back, 'y', to_prev)  16.2 us
    dot_general x1, matrix products, local(): lax.dot_general(gathered_late, amp, (((2, 3), (0, 1)), ((), ())), preferr...  11 us
  transfers between devices with their start and end apart: 24, of which 16 were waited for; matrix products, arithmetic and copies ran while one was open for 25% of the time, Pallas kernels for 0%

profile of v9, /device:TPU:0, one launch (start us, length us, event | category | flops | bytes accessed | tf_op | source)
XLA Modules:
  0.0 311.6 jit_solution(12851607140648721356)
XLA Ops:
  6.5 0.7 dynamic_slice.75
  7.3 1.2 sort.17
  8.9 2.6 reshape.35
  12.3 1.1 copy.4
  14.2 2.1 collective-permute-done
  16.3 1.4 copy.46
  18.1 1.0 copy.25
  19.2 3.2 %collective-permute-start.1 = (bf16[1200,1024]{1,0:T(8,128)(2,1)}, bf16[1200,1024]{1,0:T(8,128)(2,1)S(1)}, u32[]{:S(2)}, u32[]{:S(2)}) collective-permute-start(bf16[1200,1024]{1,0:T(8,128)(2,1)} %param.5), channel_id=1, source_target_pairs={{0,64},{64,0},{1,65},{65,1},{2,66},{66,2},{3,67},{67,3},{4,68},{68... | collective-permute-start | bytes 7372808 | tf_op jit(solution)/shard_map/ppermute | solution.py:39
  22.4 3.4 %constant_dynamic-update-slice_fusion.1 = bf16[1200,2048]{1,0:T(8,128)(2,1)} fusion(bf16[1200,1024]{1,0:T(8,128)(2,1)} %param.5), kind=kLoop, calls=%fused_computation.68 | loop fusion | bytes 4915200
  25.8 50.6 %collective-permute-done.1 = bf16[1200,1024]{1,0:T(8,128)(2,1)S(1)} collective-permute-done((bf16[1200,1024]{1,0:T(8,128)(2,1)}, bf16[1200,1024]{1,0:T(8,128)(2,1)S(1)}, u32[]{:S(2)}, u32[]{:S(2)}) %collective-permute-start.1) | collective-permute-done | bytes 2457632 | tf_op jit(solution)/shard_map/ppermute | solution.py:39
  76.4 1.7 constant_dynamic-update-slice_fusion
  78.2 1.7 copy.6
  80.0 6.6 %collective-permute-done.2 = bf16[1200,2048]{1,0:T(8,128)(2,1)} collective-permute-done((bf16[1200,2048]{1,0:T(8,128)(2,1)}, bf16[1200,2048]{1,0:T(8,128)(2,1)}, u32[]{:S(2)}, u32[]{:S(2)}) %collective-permute-start.2) | collective-permute-done | bytes 4915232 | tf_op jit(solution)/shard_map/ppermute | solution.py:40
  86.6 11.0 %fusion = f32[8,80,2048,1]{2,1,3,0:T(8,128)S(1)} fusion(bf16[8,80,2,1200]{3,0,2,1:T(8,128)(2,1)} %all-gather.5.cloned.1.call-done, bf16[1,1200,2048]{2,1,0:T(8,128)(2,1)} %bitcast.5, bf16[1,1200,2048]{2,1,0:T(8,128)(2,1)} %bitcast.4), kind=kOutput, calls=%fused_computation.3 | convolution fusion | flops 6296371200 | bytes 18145280 | tf_op jit(solution)/shard_map/dot_general | solution.py:70
  97.6 2.0 dynamic-slice_bitcast_fusion
  99.6 1.3 copy-done
  100.8 1.6 collective-permute-start.11
  102.5 34.6 %all-gather.3.cloned.1.call-done = bf16[8,120,2,1200]{3,0,2,1:T(8,128)(2,1)} async-done(((bf16[8,30,2,1200]{3,0,2,1:T(8,128)(2,1)}), bf16[8,120,2,1200]{3,0,2,1:T(8,128)(2,1)}) %all-gather.3.cloned.1.call-update) | async-done | bytes 4608016 | tf_op jit(solution)/shard_map/all_gather | solution.py:34
  137.1 3.9 %copy.36 = bf16[8,120,2,1200]{3,1,2,0:T(8,128)(2,1)S(1)} copy(bf16[8,120,2,1200]{3,0,2,1:T(8,128)(2,1)} %all-gather.3.cloned.1.call-done) | data formatting | bytes 9216000 | tf_op jit(solution)/shard_map/reshape | solution.py:37
  141.6 4.8 %convolution_bitcast_fusion.7 = f32[2,60,2048]{2,1,0:T(8,128)S(1)} fusion(bf16[2,120,2,1200]{3,1,2,0:T(8,128)(2,1)S(1)} %get-tuple-element.15, bf16[1,1200,2048]{2,1,0:T(8,128)(2,1)} %bitcast.5, bf16[1,1200,2048]{2,1,0:T(8,128)(2,1)} %bitcast.4), kind=kOutput, calls=%fused_computation.14 | convolution fusion | flops 1184563200 | bytes 11468800 | tf_op jit(solution)/shard_map/dot_general | solution.py:44
  146.4 0.8 copy.8
  147.2 1.7 collective-permute-start.3
  148.9 4.8 %convolution_bitcast_fusion.6 = f32[2,60,2048]{2,1,0:T(8,128)S(1)} fusion(bf16[2,120,2,1200]{3,1,2,0:T(8,128)(2,1)S(1)} %get-tuple-element.10, bf16[1,1200,2048]{2,1,0:T(8,128)(2,1)} %bitcast.5, bf16[1,1200,2048]{2,1,0:T(8,128)(2,1)} %bitcast.4), kind=kOutput, calls=%fused_computation.13 | convolution fusion | flops 1184563200 | bytes 11468800 | tf_op jit(solution)/shard_map/dot_general | solution.py:44
  153.8 4.8 %convolution_bitcast_fusion.5 = f32[2,60,2048]{2,1,0:T(8,128)S(1)} fusion(bf16[2,120,2,1200]{3,1,2,0:T(8,128)(2,1)S(1)} %get-tuple-element.14, bf16[1,1200,2048]{2,1,0:T(8,128)(2,1)} %bitcast.5, bf16[1,1200,2048]{2,1,0:T(8,128)(2,1)} %bitcast.4), kind=kOutput, calls=%fused_computation.12 | convolution fusion | flops 1184563200 | bytes 11468800 | tf_op jit(solution)/shard_map/dot_general | solution.py:44
  158.6 4.8 %convolution_bitcast_fusion.4 = f32[2,60,2048]{2,1,0:T(8,128)S(1)} fusion(bf16[2,120,2,1200]{3,1,2,0:T(8,128)(2,1)S(1)} %get-tuple-element.13, bf16[1,1200,2048]{2,1,0:T(8,128)(2,1)} %bitcast.5, bf16[1,1200,2048]{2,1,0:T(8,128)(2,1)} %bitcast.4), kind=kOutput, calls=%fused_computation.11 | convolution fusion | flops 1184563200 | bytes 11468800 | tf_op jit(solution)/shard_map/dot_general | solution.py:44
  163.4 4.9 %convolution_bitcast_fusion.3 = f32[2,60,2048]{2,1,0:T(8,128)S(1)} fusion(bf16[2,120,2,1200]{3,1,2,0:T(8,128)(2,1)S(1)} %get-tuple-element.12, bf16[1,1200,2048]{2,1,0:T(8,128)(2,1)} %bitcast.5, bf16[1,1200,2048]{2,1,0:T(8,128)(2,1)} %bitcast.4), kind=kOutput, calls=%fused_computation.10 | convolution fusion | flops 1184563200 | bytes 11468800 | tf_op jit(solution)/shard_map/dot_general | solution.py:44
  168.3 0.8 copy.18
  169.1 1.8 collective-permute-start.7
  170.9 4.8 %convolution_bitcast_fusion.2 = f32[2,60,2048]{2,1,0:T(8,128)S(1)} fusion(bf16[2,120,2,1200]{3,1,2,0:T(8,128)(2,1)S(1)} %get-tuple-element.11, bf16[1,1200,2048]{2,1,0:T(8,128)(2,1)} %bitcast.5, bf16[1,1200,2048]{2,1,0:T(8,128)(2,1)} %bitcast.4), kind=kOutput, calls=%fused_computation.9 | convolution fusion | flops 1184563200 | bytes 11468800 | tf_op jit(solution)/shard_map/dot_general | solution.py:44
  175.7 4.9 %convolution_bitcast_fusion.1 = f32[2,60,2048]{2,1,0:T(8,128)S(1)} fusion(bf16[2,120,2,1200]{3,1,2,0:T(8,128)(2,1)S(1)} %get-tuple-element.15, bf16[1,1200,2048]{2,1,0:T(8,128)(2,1)} %bitcast.5, bf16[1,1200,2048]{2,1,0:T(8,128)(2,1)} %bitcast.4), kind=kOutput, calls=%fused_computation.8 | convolution fusion | flops 1184563200 | bytes 11468800 | tf_op jit(solution)/shard_map/dot_general | solution.py:44
  181.2 0.8 copy.11
  182.3 4.8 %convolution_bitcast_fusion = f32[2,60,2048]{2,1,0:T(8,128)S(1)} fusion(bf16[2,120,2,1200]{3,1,2,0:T(8,128)(2,1)S(1)} %get-tuple-element.13, bf16[1,1200,2048]{2,1,0:T(8,128)(2,1)} %bitcast.5, bf16[1,1200,2048]{2,1,0:T(8,128)(2,1)} %bitcast.4), kind=kOutput, calls=%fused_computation.7 | convolution fusion | flops 1184563200 | bytes 11468800 | tf_op jit(solution)/shard_map/dot_general | solution.py:44
  187.2 5.0 %collective-permute-done.7 = f32[2,60,2048]{2,0,1:T(2,128)S(1)} collective-permute-done((f32[2,60,2048]{2,0,1:T(2,128)S(1)}, f32[2,60,2048]{2,0,1:T(2,128)S(1)}, u32[]{:S(2)}, u32[]{:S(2)}) %collective-permute-start.7) | collective-permute-done | bytes 983072 | tf_op jit(solution)/shard_map/ppermute | solution.py:57
  192.8 0.8 copy.21
  193.6 3.0 collective-permute-start.8
  196.6 9.5 %collective-permute-done.4 = f32[2,60,2048]{2,0,1:T(2,128)S(1)} collective-permute-done((f32[2,60,2048]{2,0,1:T(2,128)S(1)}, f32[2,60,2048]{2,0,1:T(2,128)S(1)}, u32[]{:S(2)}, u32[]{:S(2)}) %collective-permute-start.4) | collective-permute-done | bytes 983072 | tf_op jit(solution)/shard_map/ppermute | solution.py:56
  206.7 0.8 copy.14
  209.0 7.3 %collective-permute-done.8 = f32[2,60,2048]{2,0,1:T(2,128)S(1)} collective-permute-done((f32[2,60,2048]{2,0,1:T(2,128)S(1)}, f32[2,60,2048]{2,0,1:T(2,128)S(1)}, u32[]{:S(2)}, u32[]{:S(2)}) %collective-permute-start.8) | collective-permute-done | bytes 983072 | tf_op jit(solution)/shard_map/ppermute | solution.py:57
  216.4 0.6 copy_add_fusion.1
  217.0 0.8 copy.23
  217.8 3.8 %collective-permute-start.9 = (f32[2,60,2048]{2,0,1:T(2,128)S(1)}, f32[2,60,2048]{2,0,1:T(2,128)S(1)}, u32[]{:S(2)}, u32[]{:S(2)}) collective-permute-start(f32[2,60,2048]{2,0,1:T(2,128)S(1)} %copy.23), channel_id=1, source_target_pairs={{0,12},{4,0},{8,4},{12,8},{1,13},{5,1},{9,5},{13,9},{2,14},{6,2},{... | collective-permute-start | bytes 2949128 | tf_op jit(solution)/shard_map/ppermute | solution.py:57
  221.6 16.3 %collective-permute-done.12 = f32[40,2048]{1,0:T(8,128)S(1)} collective-permute-done((f32[40,2048]{1,0:T(8,128)S(1)}, f32[40,2048]{1,0:T(8,128)S(1)}, u32[]{:S(2)}, u32[]{:S(2)}) %collective-permute-start.12) | collective-permute-done | bytes 327712 | tf_op jit(solution)/shard_map/ppermute | solution.py:56
  238.0 9.4 %collective-permute-done.15 = f32[40,2048]{1,0:T(8,128)S(1)} collective-permute-done((f32[40,2048]{1,0:T(8,128)S(1)}, f32[40,2048]{1,0:T(8,128)S(1)}, u32[]{:S(2)}, u32[]{:S(2)}) %collective-permute-start.15) | collective-permute-done | bytes 327712 | tf_op jit(solution)/shard_map/ppermute | solution.py:57
  247.5 3.8 %collective-permute-start.16 = (f32[40,2048]{1,0:T(8,128)S(1)}, f32[40,2048]{1,0:T(8,128)S(1)}, u32[]{:S(2)}, u32[]{:S(2)}) collective-permute-start(f32[40,2048]{1,0:T(8,128)S(1)} %bitcast_add_fusion.5), channel_id=1, source_target_pairs={{0,12},{4,0},{8,4},{12,8},{1,13},{5,1},{9,5},{13,9},{2,14},{6,2},{... | collective-permute-start | bytes 983048 | tf_op jit(solution)/shard_map/ppermute | solution.py:57
  251.4 4.8 %collective-permute-done.16 = f32[40,2048]{1,0:T(8,128)S(1)} collective-permute-done((f32[40,2048]{1,0:T(8,128)S(1)}, f32[40,2048]{1,0:T(8,128)S(1)}, u32[]{:S(2)}, u32[]{:S(2)}) %collective-permute-start.16) | collective-permute-done | bytes 327712 | tf_op jit(solution)/shard_map/ppermute | solution.py:57
  256.2 3.8 %collective-permute-start.17 = (f32[40,2048]{1,0:T(8,128)S(1)}, f32[40,2048]{1,0:T(8,128)S(1)}, u32[]{:S(2)}, u32[]{:S(2)}) collective-permute-start(f32[40,2048]{1,0:T(8,128)S(1)} %bitcast_add_fusion.4), channel_id=1, source_target_pairs={{0,12},{4,0},{8,4},{12,8},{1,13},{5,1},{9,5},{13,9},{2,14},{6,2},{... | collective-permute-start | bytes 983048 | tf_op jit(solution)/shard_map/ppermute | solution.py:57
  260.0 0.6 copy_add_fusion.3
  260.6 0.9 dynamic-slice_bitcast_fusion.8
  261.5 1.5 collective-permute-start.6
  263.7 0.9 collective-permute-done.17
  264.7 3.0 collective-permute-start.20
  268.3 0.8 dynamic-slice_bitcast_fusion.7
  269.1 1.5 collective-permute-start.10
  270.7 11.4 %collective-permute-done.20 = f32[40,1024]{1,0:T(8,128)S(1)} collective-permute-done((f32[40,1024]{1,0:T(8,128)S(1)}, f32[40,1024]{1,0:T(8,128)S(1)}, u32[]{:S(2)}, u32[]{:S(2)}) %collective-permute-start.20) | collective-permute-done | bytes 163872 | tf_op jit(solution)/shard_map/ppermute | solution.py:97
  282.1 3.2 %collective-permute-done.21 = f32[40,1024]{1,0:T(8,128)} collective-permute-done((f32[40,1024]{1,0:T(8,128)S(1)}, f32[40,1024]{1,0:T(8,128)}, u32[]{:S(2)}, u32[]{:S(2)}) %collective-permute-start.21) | collective-permute-done | bytes 163872 | tf_op jit(solution)/shard_map/ppermute | solution.py:97
  285.3 0.9 pad_maximum_fusion.6
  286.3 1.1 bitcast_add_fusion.2
  287.5 2.0 collective-permute-done.10
  289.5 1.1 bitcast_add_fusion.1
  290.7 3.5 %collective-permute-start.18 = (f32[60,1024]{1,0:T(8,128)S(1)}, f32[60,1024]{1,0:T(8,128)S(1)}, u32[]{:S(2)}, u32[]{:S(2)}) collective-permute-start(f32[60,1024]{1,0:T(8,128)S(1)} %get-tuple-element.19), channel_id=1, source_target_pairs={{0,64},{64,0},{1,65},{65,1},{2,66},{66,2},{3,67},{67,3},{4,68},{68... | collective-permute-start | bytes 737288 | tf_op jit(solution)/shard_map/ppermute | solution.py:97
  294.6 4.7 %collective-permute-done.18 = f32[60,1024]{1,0:T(8,128)S(1)} collective-permute-done((f32[60,1024]{1,0:T(8,128)S(1)}, f32[60,1024]{1,0:T(8,128)S(1)}, u32[]{:S(2)}, u32[]{:S(2)}) %collective-permute-start.18) | collective-permute-done | bytes 245792 | tf_op jit(solution)/shard_map/ppermute | solution.py:97
  299.3 2.9 collective-permute-done.19
  302.2 1.0 pad_maximum_fusion.4
  303.5 1.3 maximum_select_fusion
  (71 shorter events, 9.4 us)
Async XLA Ops:
  6.5 73.5 %all-gather.5.cloned.1.call-start = ((), (), s32[]{:S(2)}) async-start(), calls=%async_computation.1 | async-start | bytes 4096000 | tf_op jit(solution)/shard_map/all_gather | solution.py:35
  13.4 3.0 collective-permute-start
  19.1 118.0 %all-gather.3.cloned.1.call-start = ((), (), s32[]{:S(2)}) async-start(), calls=%async_computation | async-start | bytes 6144000 | tf_op jit(solution)/shard_map/all_gather | solution.py:34
  19.2 57.2 %collective-permute-start.1 = (bf16[1200,1024]{1,0:T(8,128)(2,1)}, bf16[1200,1024]{1,0:T(8,128)(2,1)S(1)}, u32[]{:S(2)}, u32[]{:S(2)}) collective-permute-start(bf16[1200,1024]{1,0:T(8,128)(2,1)} %param.5), channel_id=1, source_target_pairs={{0,64},{64,0},{1,65},{65,1},{2,66},{66,2},{3,67},{67,3},{4,68},{68... | collective-permute-start | bytes 7372808 | tf_op jit(solution)/shard_map/ppermute | solution.py:39
  78.0 8.5 %collective-permute-start.2 = (bf16[1200,2048]{1,0:T(8,128)(2,1)}, bf16[1200,2048]{1,0:T(8,128)(2,1)}, u32[]{:S(2)}, u32[]{:S(2)}) collective-permute-start(bf16[1200,2048]{1,0:T(8,128)(2,1)} %constant_dynamic-update-slice_fusion), channel_id=1, source_target_pairs={{0,1},{1,0},{2,3},{3,2},{4,5},{5,4},{6,7},{7,6},{8,9},{9,8},{10,11... | collective-permute-start | bytes 14745608 | tf_op jit(solution)/shard_map/ppermute | solution.py:40
  97.6 3.3 %copy-start = (f32[8,80,2048,1]{2,1,3,0:T(8,128)}, f32[8,80,2048,1]{2,1,3,0:T(8,128)S(1)}, u32[]{:S(2)}) copy-start(f32[8,80,2048,1]{2,1,3,0:T(8,128)S(1)} %fusion) | copy-start | bytes 15728644
  100.8 106.9 %collective-permute-start.11 = (f32[4,80,2048]{2,1,0:T(8,128)}, f32[4,80,2048]{2,1,0:T(8,128)S(1)}, u32[]{:S(2)}, u32[]{:S(2)}) collective-permute-start(f32[4,80,2048]{2,1,0:T(8,128)} %dynamic-slice_bitcast_fusion), channel_id=1, source_target_pairs={{0,2},{2,0},{1,3},{3,1},{4,6},{6,4},{5,7},{7,5},{8,10},{10,8},{9,1... | collective-permute-start | bytes 7864328 | tf_op jit(solution)/shard_map/ppermute | solution.py:76
  147.2 33.4 %collective-permute-start.3 = (f32[2,60,2048]{2,0,1:T(2,128)S(1)}, f32[2,60,2048]{2,0,1:T(2,128)S(1)}, u32[]{:S(2)}, u32[]{:S(2)}) collective-permute-start(f32[2,60,2048]{2,0,1:T(2,128)S(1)} %copy.8), channel_id=1, source_target_pairs={{0,4},{4,8},{8,12},{12,0},{1,5},{5,9},{9,13},{13,1},{2,6},{6,10},{... | collective-permute-start | bytes 2949128 | tf_op jit(solution)/shard_map/ppermute | solution.py:56
  169.1 23.1 %collective-permute-start.7 = (f32[2,60,2048]{2,0,1:T(2,128)S(1)}, f32[2,60,2048]{2,0,1:T(2,128)S(1)}, u32[]{:S(2)}, u32[]{:S(2)}) collective-permute-start(f32[2,60,2048]{2,0,1:T(2,128)S(1)} %copy.18), channel_id=1, source_target_pairs={{0,12},{4,0},{8,4},{12,8},{1,13},{5,1},{9,5},{13,9},{2,14},{6,2},{... | collective-permute-start | bytes 2949128 | tf_op jit(solution)/shard_map/ppermute | solution.py:57
  180.6 27.2 %slice-start = ((s8[5242880]{0:T(1024)(128)(4,1)}), s8[4194304]{0:T(1024)(128)(4,1)S(1)}, s32[]{:S(2)}) async-start(s8[5242880]{0:T(1024)(128)(4,1)} %bitcast.92), calls=%async_computation.2 | async-start | bytes 8388608
  182.0 25.8 %slice-start.1 = ((s8[5242880]{0:T(1024)(128)(4,1)}), s8[1048576]{0:T(1024)(128)(4,1)S(1)}, s32[]{:S(2)}) async-start(s8[5242880]{0:T(1024)(128)(4,1)} %bitcast.92), calls=%async_computation.3 | async-start | bytes 2097152
  182.0 24.1 %collective-permute-start.4 = (f32[2,60,2048]{2,0,1:T(2,128)S(1)}, f32[2,60,2048]{2,0,1:T(2,128)S(1)}, u32[]{:S(2)}, u32[]{:S(2)}) collective-permute-start(f32[2,60,2048]{2,0,1:T(2,128)S(1)} %copy.11), channel_id=1, source_target_pairs={{0,4},{4,8},{8,12},{12,0},{1,5},{5,9},{9,13},{13,1},{2,6},{6,10},{... | collective-permute-start | bytes 2949128 | tf_op jit(solution)/shard_map/ppermute | solution.py:56
  193.6 22.8 %collective-permute-start.8 = (f32[2,60,2048]{2,0,1:T(2,128)S(1)}, f32[2,60,2048]{2,0,1:T(2,128)S(1)}, u32[]{:S(2)}, u32[]{:S(2)}) collective-permute-start(f32[2,60,2048]{2,0,1:T(2,128)S(1)} %copy.21), channel_id=1, source_target_pairs={{0,12},{4,0},{8,4},{12,8},{1,13},{5,1},{9,5},{13,9},{2,14},{6,2},{... | collective-permute-start | bytes 2949128 | tf_op jit(solution)/shard_map/ppermute | solution.py:57
  207.4 52.6 %collective-permute-start.5 = (f32[2,60,2048]{2,0,1:T(2,128)S(1)}, f32[2,60,2048]{2,0,1:T(2,128)S(1)}, u32[]{:S(2)}, u32[]{:S(2)}) collective-permute-start(f32[2,60,2048]{2,0,1:T(2,128)S(1)} %copy.14), channel_id=1, source_target_pairs={{0,4},{4,8},{8,12},{12,0},{1,5},{5,9},{9,13},{13,1},{2,6},{6,10},{... | collective-permute-start | bytes 2949128 | tf_op jit(solution)/shard_map/ppermute | solution.py:56
  208.5 29.4 %collective-permute-start.12 = (f32[40,2048]{1,0:T(8,128)S(1)}, f32[40,2048]{1,0:T(8,128)S(1)}, u32[]{:S(2)}, u32[]{:S(2)}) collective-permute-start(f32[40,2048]{1,0:T(8,128)S(1)} %dynamic-slice_bitcast_fusion.10), channel_id=1, source_target_pairs={{0,4},{4,8},{8,12},{12,0},{1,5},{5,9},{9,13},{13,1},{2,6},{6,10},{... | collective-permute-start | bytes 983048 | tf_op jit(solution)/shard_map/ppermute | solution.py:56
  217.8 45.2 %collective-permute-start.9 = (f32[2,60,2048]{2,0,1:T(2,128)S(1)}, f32[2,60,2048]{2,0,1:T(2,128)S(1)}, u32[]{:S(2)}, u32[]{:S(2)}) collective-permute-start(f32[2,60,2048]{2,0,1:T(2,128)S(1)} %copy.23), channel_id=1, source_target_pairs={{0,12},{4,0},{8,4},{12,8},{1,13},{5,1},{9,5},{13,9},{2,14},{6,2},{... | collective-permute-start | bytes 2949128 | tf_op jit(solution)/shard_map/ppermute | solution.py:57
  221.5 25.9 %collective-permute-start.15 = (f32[40,2048]{1,0:T(8,128)S(1)}, f32[40,2048]{1,0:T(8,128)S(1)}, u32[]{:S(2)}, u32[]{:S(2)}) collective-permute-start(f32[40,2048]{1,0:T(8,128)S(1)} %dynamic-slice_bitcast_fusion.9), channel_id=1, source_target_pairs={{0,12},{4,0},{8,4},{12,8},{1,13},{5,1},{9,5},{13,9},{2,14},{6,2},{... | collective-permute-start | bytes 983048 | tf_op jit(solution)/shard_map/ppermute | solution.py:57
  238.0 13.3 %collective-permute-start.13 = (f32[40,2048]{1,0:T(8,128)S(1)}, f32[40,2048]{1,0:T(8,128)S(1)}, u32[]{:S(2)}, u32[]{:S(2)}) collective-permute-start(f32[40,2048]{1,0:T(8,128)S(1)} %bitcast_add_fusion.8), channel_id=1, source_target_pairs={{0,4},{4,8},{8,12},{12,0},{1,5},{5,9},{9,13},{13,1},{2,6},{6,10},{... | collective-permute-start | bytes 983048 | tf_op jit(solution)/shard_map/ppermute | solution.py:56
  247.5 8.7 %collective-permute-start.16 = (f32[40,2048]{1,0:T(8,128)S(1)}, f32[40,2048]{1,0:T(8,128)S(1)}, u32[]{:S(2)}, u32[]{:S(2)}) collective-permute-start(f32[40,2048]{1,0:T(8,128)S(1)} %bitcast_add_fusion.5), channel_id=1, source_target_pairs={{0,12},{4,0},{8,4},{12,8},{1,13},{5,1},{9,5},{13,9},{2,14},{6,2},{... | collective-permute-start | bytes 983048 | tf_op jit(solution)/shard_map/ppermute | solution.py:57
  251.3 12.3 %collective-permute-start.14 = (f32[40,2048]{1,0:T(8,128)S(1)}, f32[40,2048]{1,0:T(8,128)S(1)}, u32[]{:S(2)}, u32[]{:S(2)}) collective-permute-start(f32[40,2048]{1,0:T(8,128)S(1)} %bitcast_add_fusion.7), channel_id=1, source_target_pairs={{0,4},{4,8},{8,12},{12,0},{1,5},{5,9},{9,13},{13,1},{2,6},{6,10},{... | collective-permute-start | bytes 983048 | tf_op jit(solution)/shard_map/ppermute | solution.py:56
  256.2 8.4 %collective-permute-start.17 = (f32[40,2048]{1,0:T(8,128)S(1)}, f32[40,2048]{1,0:T(8,128)S(1)}, u32[]{:S(2)}, u32[]{:S(2)}) collective-permute-start(f32[40,2048]{1,0:T(8,128)S(1)} %bitcast_add_fusion.4), channel_id=1, source_target_pairs={{0,12},{4,0},{8,4},{12,8},{1,13},{5,1},{9,5},{13,9},{2,14},{6,2},{... | collective-permute-start | bytes 983048 | tf_op jit(solution)/shard_map/ppermute | solution.py:57
  261.5 24.8 %collective-permute-start.6 = (f32[60,2048]{1,0:T(8,128)}, f32[60,2048]{1,0:T(8,128)}, u32[]{:S(2)}, u32[]{:S(2)}) collective-permute-start(f32[60,2048]{1,0:T(8,128)} %dynamic-slice_bitcast_fusion.8), channel_id=1, source_target_pairs={{0,2},{2,0},{1,3},{3,1},{4,6},{6,4},{5,7},{7,5},{8,10},{10,8},{9,1... | collective-permute-start | bytes 1474568 | tf_op jit(solution)/shard_map/ppermute | solution.py:65
  264.7 17.4 %collective-permute-start.20 = (f32[40,1024]{1,0:T(8,128)S(1)}, f32[40,1024]{1,0:T(8,128)S(1)}, u32[]{:S(2)}, u32[]{:S(2)}) collective-permute-start(f32[40,1024]{1,0:T(8,128)S(1)} %get-tuple-element.23), channel_id=1, source_target_pairs={{0,64},{64,0},{1,65},{65,1},{2,66},{66,2},{3,67},{67,3},{4,68},{68... | collective-permute-start | bytes 491528 | tf_op jit(solution)/shard_map/ppermute | solution.py:97
  267.7 17.7 %collective-permute-start.21 = (f32[40,1024]{1,0:T(8,128)S(1)}, f32[40,1024]{1,0:T(8,128)}, u32[]{:S(2)}, u32[]{:S(2)}) collective-permute-start(f32[40,1024]{1,0:T(8,128)S(1)} %get-tuple-element.25), channel_id=1, source_target_pairs={{0,64},{64,0},{1,65},{65,1},{2,66},{66,2},{3,67},{67,3},{4,68},{68... | collective-permute-start | bytes 491528 | tf_op jit(solution)/shard_map/ppermute | solution.py:97
  269.1 20.4 %collective-permute-start.10 = (f32[60,2048]{1,0:T(8,128)}, f32[60,2048]{1,0:T(8,128)}, u32[]{:S(2)}, u32[]{:S(2)}) collective-permute-start(f32[60,2048]{1,0:T(8,128)} %dynamic-slice_bitcast_fusion.7), channel_id=1, source_target_pairs={{0,2},{2,0},{1,3},{3,1},{4,6},{6,4},{5,7},{7,5},{8,10},{10,8},{9,1... | collective-permute-start | bytes 1474568 | tf_op jit(solution)/shard_map/ppermute | solution.py:65
  290.7 8.6 %collective-permute-start.18 = (f32[60,1024]{1,0:T(8,128)S(1)}, f32[60,1024]{1,0:T(8,128)S(1)}, u32[]{:S(2)}, u32[]{:S(2)}) collective-permute-start(f32[60,1024]{1,0:T(8,128)S(1)} %get-tuple-element.19), channel_id=1, source_target_pairs={{0,64},{64,0},{1,65},{65,1},{2,66},{66,2},{3,67},{67,3},{4,68},{68... | collective-permute-start | bytes 737288 | tf_op jit(solution)/shard_map/ppermute | solution.py:97
  294.1 8.1 %collective-permute-start.19 = (f32[60,1024]{1,0:T(8,128)S(1)}, f32[60,1024]{1,0:T(8,128)}, u32[]{:S(2)}, u32[]{:S(2)}) collective-permute-start(f32[60,1024]{1,0:T(8,128)S(1)} %get-tuple-element.21), channel_id=1, source_target_pairs={{0,64},{64,0},{1,65},{65,1},{2,66},{66,2},{3,67},{67,3},{4,68},{68... | collective-permute-start | bytes 737288 | tf_op jit(solution)/shard_map/ppermute | solution.py:97
Sparse Core Ops, SparseCore 0:
  19.2 43.2 all-gather.4
  80.0 57.0 all-gather.2

commit v10 on v9

--- a/solution.py
+++ b/solution.py
@@ -32,7 +32,8 @@
     own_owners = jnp.stack([mine, from_sibling], axis=2)
     y_cut = TB * 3 // 5
     gathered = lax.all_gather(own_owners[:, :y_cut], "z", axis=1, tiled=True)
-    gathered_late = lax.all_gather(own_owners[:, y_cut:], "z", axis=1, tiled=True)
+    late_rows, gathered = lax.optimization_barrier((own_owners[:, y_cut:], gathered))
+    gathered_late = lax.all_gather(late_rows, "z", axis=1, tiled=True)
     y_rows = gathered.shape[1]
     by_y = gathered.reshape(ny, nxl, y_rows, 2, kc)
 

time: 313 us -> 328 us (1.048)
  local copies, waits for them, and re-layouts: 29.9 us -> 39.3 us
  matrix products: 49.7 us -> 55.8 us
  starting transfers between devices: 34.4 us -> 28.9 us
  waiting for transfers between devices: 171 us -> 175 us
    ppermute x2, waiting for transfers between devices: 2.02 us -> 69.5 us  [pair_sum(): return here + lax.ppermute(there, 'xl', SWAP)]
    all_gather x1, waiting for transfers between devices: 34.6 us -> 2 us  [local(): gathered = lax.all_gather(own_owners[:, :y_cut], 'z', axis=1, tiled=True)]
    ppermute x6, waiting for transfers between devices: 25.7 us -> 4.73 us  [ring(): got_ahead = lax.ppermute(acc_ahead, 'y', to_next)]
    ppermute x6, waiting for transfers between devices: 27.5 us -> 39.2 us  [ring(): got_back = lax.ppermute(acc_back, 'y', to_prev)]
    ppermute x4, waiting for transfers between devices: 22.3 us -> 12.2 us  [local(): came = [lax.ppermute(piece[:, width:], 'xh', SWAP) for piece in pieces]]
    ppermute x6, starting transfers between devices: 16.2 us -> 9.74 us  [ring(): got_back = lax.ppermute(acc_back, 'y', to_prev)]
    ppermute x1, waiting for transfers between devices: 6.55 us -> 0.24 us  [local(): amp = jnp.stack([amp, lax.ppermute(amp, 'c', SWAP)], axis=0)]
    dot_general x8, matrix products: 38.7 us -> 44.8 us  [block(): lax.dot_general(lhs[:, low:high], amp, (((2, 3), (0, 1)), ((), ())), pref...]
  transfers between devices with their start and end apart: 24 -> 24, of which waited for: 16 -> 17; matrix products, arithmetic and copies ran while one was open for 25% -> 29% of each run, Pallas kernels for 0% -> 0%
where the time goes in v10:
time: 328 us
  waiting for transfers between devices  175 us (53%)
  matrix products  55.8 us (17%)
  local copies, waits for them, and re-layouts  39.3 us (12%)
  starting transfers between devices  28.9 us (9%)
  other arithmetic  15 us (5%)
  between operations  13.8 us (4%)
    ppermute x2, waiting for transfers between devices, pair_sum(): return here + lax.ppermute(there, 'xl', SWAP)  69.5 us
    ppermute x1, waiting for transfers between devices, local(): lax.ppermute(amplitudes, 'xh', SWAP)  46.9 us
    dot_general x8, matrix products, block(): lax.dot_general(lhs[:, low:high], amp, (((2, 3), (0, 1)), ((), ())), pref...  44.8 us
    ppermute x6, waiting for transfers between devices, ring(): got_back = lax.ppermute(acc_back, 'y', to_prev)  39.2 us
    ppermute x4, waiting for transfers between devices, local(): came = [lax.ppermute(piece[:, width:], 'xh', SWAP) for piece in pieces]  12.2 us
    dot_general x1, matrix products, local(): lax.dot_general(gathered_late, amp, (((2, 3), (0, 1)), ((), ())), preferr...  11 us
    ppermute x6, starting transfers between devices, ring(): got_back = lax.ppermute(acc_back, 'y', to_prev)  9.74 us
    ppermute x4, starting transfers between devices, local(): came = [lax.ppermute(piece[:, width:], 'xh', SWAP) for piece in pieces]  7.22 us
  transfers between devices with their start and end apart: 24, of which 17 were waited for; matrix products, arithmetic and copies ran while one was open for 29% of the time, Pallas kernels for 0%

profile of v10, /device:TPU:0, one launch (start us, length us, event | category | flops | bytes accessed | tf_op | source)
XLA Modules:
  0.0 327.7 jit_solution(6931901944073855698)
XLA Ops:
  7.3 1.2 sort.17
  8.9 2.6 reshape.35
  12.3 1.1 copy.4
  13.4 3.1 collective-permute-start.1
  17.4 1.4 copy.46
  18.9 1.7 copy.6
  20.7 3.4 %constant_dynamic-update-slice_fusion.1 = bf16[1200,2048]{1,0:T(8,128)(2,1)} fusion(bf16[1200,1024]{1,0:T(8,128)(2,1)} %param.5), kind=kLoop, calls=%fused_computation.66 | loop fusion | bytes 4915200
  24.1 46.9 %collective-permute-done.1 = bf16[1200,1024]{1,0:T(8,128)(2,1)} collective-permute-done((bf16[1200,1024]{1,0:T(8,128)(2,1)}, bf16[1200,1024]{1,0:T(8,128)(2,1)}, u32[]{:S(2)}, u32[]{:S(2)}) %collective-permute-start.1) | collective-permute-done | bytes 2457632 | tf_op jit(solution)/shard_map/ppermute | solution.py:40
  71.0 3.4 %constant_dynamic-update-slice_fusion = bf16[1200,2048]{1,0:T(8,128)(2,1)} fusion(bf16[1200,2048]{1,0:T(8,128)(2,1)} %constant_dynamic-update-slice_fusion.1, bf16[1200,1024]{1,0:T(8,128)(2,1)} %collective-permute-done.1), kind=kLoop, calls=%fused_computation.65 | loop fusion | bytes 4915200 | tf_op jit(solution)/shard_map/concatenate | solution.py:40
  74.7 2.0 all-gather.3.cloned.1.call-done
  76.7 3.9 %copy.36 = bf16[8,120,2,1200]{3,1,2,0:T(8,128)(2,1)S(1)} copy(bf16[8,120,2,1200]{3,0,2,1:T(8,128)(2,1)} %all-gather.3.cloned.1.call-done) | data formatting | bytes 9216000 | tf_op jit(solution)/shard_map/reshape | solution.py:38
  80.6 2.0 dynamic-slice_bitcast_fusion.5
  82.9 5.0 %convolution_bitcast_fusion.7 = f32[2,60,2048]{2,1,0:T(8,128)S(1)} fusion(bf16[2,120,2,1200]{3,1,2,0:T(8,128)(2,1)S(1)} %get-tuple-element.19, bf16[1,1200,2048]{2,1,0:T(8,128)(2,1)} %bitcast.5, bf16[1,1200,2048]{2,1,0:T(8,128)(2,1)} %bitcast.4), kind=kOutput, calls=%fused_computation.14 | convolution fusion | flops 1184563200 | bytes 11468800 | tf_op jit(solution)/shard_map/dot_general | solution.py:45
  87.9 1.7 copy.8
  89.7 1.5 collective-permute-start.3
  91.2 6.5 %convolution_bitcast_fusion.6 = f32[2,60,2048]{2,1,0:T(8,128)} fusion(bf16[2,120,2,1200]{3,1,2,0:T(8,128)(2,1)S(1)} %get-tuple-element.14, bf16[1,1200,2048]{2,1,0:T(8,128)(2,1)} %bitcast.5, bf16[1,1200,2048]{2,1,0:T(8,128)(2,1)} %bitcast.4), kind=kOutput, calls=%fused_computation.13 | convolution fusion | flops 1184563200 | bytes 11468800 | tf_op jit(solution)/shard_map/dot_general | solution.py:45
  97.7 4.8 %convolution_bitcast_fusion.5 = f32[2,60,2048]{2,1,0:T(8,128)S(1)} fusion(bf16[2,120,2,1200]{3,1,2,0:T(8,128)(2,1)S(1)} %get-tuple-element.18, bf16[1,1200,2048]{2,1,0:T(8,128)(2,1)} %bitcast.5, bf16[1,1200,2048]{2,1,0:T(8,128)(2,1)} %bitcast.4), kind=kOutput, calls=%fused_computation.12 | convolution fusion | flops 1184563200 | bytes 11468800 | tf_op jit(solution)/shard_map/dot_general | solution.py:45
  102.5 6.4 %convolution_bitcast_fusion.4 = f32[2,60,2048]{2,1,0:T(8,128)} fusion(bf16[2,120,2,1200]{3,1,2,0:T(8,128)(2,1)S(1)} %get-tuple-element.17, bf16[1,1200,2048]{2,1,0:T(8,128)(2,1)} %bitcast.5, bf16[1,1200,2048]{2,1,0:T(8,128)(2,1)} %bitcast.4), kind=kOutput, calls=%fused_computation.11 | convolution fusion | flops 1184563200 | bytes 11468800 | tf_op jit(solution)/shard_map/dot_general | solution.py:45
  108.9 1.0 copy.25
  110.0 5.1 %convolution_bitcast_fusion.3 = f32[2,60,2048]{2,1,0:T(8,128)S(1)} fusion(bf16[2,120,2,1200]{3,1,2,0:T(8,128)(2,1)} %get-tuple-element.16, bf16[1,1200,2048]{2,1,0:T(8,128)(2,1)} %bitcast.5, bf16[1,1200,2048]{2,1,0:T(8,128)(2,1)} %bitcast.4), kind=kOutput, calls=%fused_computation.10 | convolution fusion | flops 1184563200 | bytes 11468800 | tf_op jit(solution)/shard_map/dot_general | solution.py:45
  115.1 0.8 copy.18
  115.9 1.8 collective-permute-start.7
  117.7 5.1 %convolution_bitcast_fusion.2 = f32[2,60,2048]{2,1,0:T(8,128)S(1)} fusion(bf16[2,120,2,1200]{3,1,2,0:T(8,128)(2,1)S(1)} %copy-done.4, bf16[1,1200,2048]{2,1,0:T(8,128)(2,1)} %bitcast.5, bf16[1,1200,2048]{2,1,0:T(8,128)(2,1)} %bitcast.4), kind=kOutput, calls=%fused_computation.9 | convolution fusion | flops 1184563200 | bytes 11468800 | tf_op jit(solution)/shard_map/dot_general | solution.py:45
  122.9 5.1 %convolution_bitcast_fusion.1 = f32[2,60,2048]{2,1,0:T(8,128)S(1)} fusion(bf16[2,120,2,1200]{3,1,2,0:T(8,128)(2,1)S(1)} %copy-done.3, bf16[1,1200,2048]{2,1,0:T(8,128)(2,1)} %bitcast.5, bf16[1,1200,2048]{2,1,0:T(8,128)(2,1)} %bitcast.4), kind=kOutput, calls=%fused_computation.8 | convolution fusion | flops 1184563200 | bytes 11468800 | tf_op jit(solution)/shard_map/dot_general | solution.py:45
  128.1 1.8 copy_add_fusion.5
  129.9 0.8 copy.11
  131.1 8.4 %collective-permute-done.7 = f32[2,60,2048]{2,0,1:T(2,128)S(1)} collective-permute-done((f32[2,60,2048]{2,0,1:T(2,128)S(1)}, f32[2,60,2048]{2,0,1:T(2,128)S(1)}, u32[]{:S(2)}, u32[]{:S(2)}) %collective-permute-start.7) | collective-permute-done | bytes 983072 | tf_op jit(solution)/shard_map/ppermute | solution.py:58
  140.1 0.8 copy.21
  140.9 3.2 collective-permute-start.8
  144.1 6.6 %convolution_bitcast_fusion = f32[2,60,2048]{2,1,0:T(8,128)} fusion(bf16[2,120,2,1200]{3,1,2,0:T(8,128)(2,1)S(1)} %get-tuple-element.17, bf16[1,1200,2048]{2,1,0:T(8,128)(2,1)} %bitcast.5, bf16[1,1200,2048]{2,1,0:T(8,128)(2,1)} %bitcast.4), kind=kOutput, calls=%fused_computation.7 | convolution fusion | flops 1184563200 | bytes 11468800 | tf_op jit(solution)/shard_map/dot_general | solution.py:45
  150.6 4.4 %collective-permute-done.4 = f32[2,60,2048]{2,0,1:T(2,128)S(1)} collective-permute-done((f32[2,60,2048]{2,0,1:T(2,128)S(1)}, f32[2,60,2048]{2,0,1:T(2,128)S(1)}, u32[]{:S(2)}, u32[]{:S(2)}) %collective-permute-start.4) | collective-permute-done | bytes 983072 | tf_op jit(solution)/shard_map/ppermute | solution.py:57
  155.7 1.7 copy.14
  157.4 6.9 %collective-permute-done.8 = f32[2,60,2048]{2,0,1:T(2,128)S(1)} collective-permute-done((f32[2,60,2048]{2,0,1:T(2,128)S(1)}, f32[2,60,2048]{2,0,1:T(2,128)S(1)}, u32[]{:S(2)}, u32[]{:S(2)}) %collective-permute-start.8) | collective-permute-done | bytes 983072 | tf_op jit(solution)/shard_map/ppermute | solution.py:58
  164.9 1.7 copy.23
  166.7 3.7 %collective-permute-start.9 = (f32[2,60,2048]{2,0,1:T(2,128)}, f32[2,60,2048]{2,0,1:T(2,128)}, u32[]{:S(2)}, u32[]{:S(2)}) collective-permute-start(f32[2,60,2048]{2,0,1:T(2,128)} %copy.23), channel_id=1, source_target_pairs={{0,12},{4,0},{8,4},{12,8},{1,13},{5,1},{9,5},{13,9},{2,14},{6,2},{... | collective-permute-start | bytes 2949128 | tf_op jit(solution)/shard_map/ppermute | solution.py:58
  170.4 11.0 %fusion = f32[8,80,2048,1]{2,1,3,0:T(8,128)S(1)} fusion(bf16[8,80,2,1200]{3,0,2,1:T(8,128)(2,1)} %all-gather.5.cloned.1.call-done, bf16[1,1200,2048]{2,1,0:T(8,128)(2,1)} %bitcast.5, bf16[1,1200,2048]{2,1,0:T(8,128)(2,1)} %bitcast.4), kind=kOutput, calls=%fused_computation.3 | convolution fusion | flops 6296371200 | bytes 18145280 | tf_op jit(solution)/shard_map/dot_general | solution.py:71
  181.4 1.8 dynamic-slice_bitcast_fusion
  183.2 1.3 copy-done
  184.5 1.6 collective-permute-start.11
  186.1 1.8 copy_add_fusion.3
  188.5 1.6 collective-permute-done.9
  190.1 1.8 copy_add_fusion
  191.9 1.7 collective-permute-start.10
  193.6 62.1 %collective-permute-done.6 = f32[60,2048]{1,0:T(8,128)S(1)} collective-permute-done((f32[60,2048]{1,0:T(8,128)S(1)}, f32[60,2048]{1,0:T(8,128)S(1)}, u32[]{:S(2)}, u32[]{:S(2)}) %collective-permute-start.6) | collective-permute-done | bytes 491552 | tf_op jit(solution)/shard_map/ppermute | solution.py:66
  255.7 0.8 fusion.13
  256.5 7.4 %collective-permute-done.10 = f32[60,2048]{1,0:T(8,128)S(1)} collective-permute-done((f32[60,2048]{1,0:T(8,128)S(1)}, f32[60,2048]{1,0:T(8,128)S(1)}, u32[]{:S(2)}, u32[]{:S(2)}) %collective-permute-start.10) | collective-permute-done | bytes 491552 | tf_op jit(solution)/shard_map/ppermute | solution.py:66
  264.7 0.8 pad_maximum_fusion.4
  265.5 1.1 reshape.38
  266.6 3.2 collective-permute-start.18
  270.3 2.1 bitcast_add_fusion
  272.5 0.8 dynamic-slice_bitcast_fusion.10
  273.3 3.3 collective-permute-done.18
  276.6 2.8 collective-permute-done.19
  279.4 0.8 pad_maximum_fusion.5
  280.2 1.9 reshape.42
  282.8 1.5 collective-permute-start.13
  284.3 7.1 %collective-permute-done.15 = f32[40,2048]{1,0:T(8,128)S(1)} collective-permute-done((f32[40,2048]{1,0:T(8,128)S(1)}, f32[40,2048]{1,0:T(8,128)S(1)}, u32[]{:S(2)}, u32[]{:S(2)}) %collective-permute-start.15) | collective-permute-done | bytes 327712 | tf_op jit(solution)/shard_map/ppermute | solution.py:58
  292.1 1.6 collective-permute-start.14
  293.7 8.2 %collective-permute-done.16 = f32[40,2048]{1,0:T(8,128)S(1)} collective-permute-done((f32[40,2048]{1,0:T(8,128)S(1)}, f32[40,2048]{1,0:T(8,128)S(1)}, u32[]{:S(2)}, u32[]{:S(2)}) %collective-permute-start.16) | collective-permute-done | bytes 327712 | tf_op jit(solution)/shard_map/ppermute | solution.py:58
  302.2 7.0 %collective-permute-done.17 = f32[40,2048]{1,0:T(8,128)S(1)} collective-permute-done((f32[40,2048]{1,0:T(8,128)S(1)}, f32[40,2048]{1,0:T(8,128)S(1)}, u32[]{:S(2)}, u32[]{:S(2)}) %collective-permute-start.17) | collective-permute-done | bytes 327712 | tf_op jit(solution)/shard_map/ppermute | solution.py:58
  309.2 3.2 collective-permute-start.20
  313.1 3.0 collective-permute-done.20
  316.1 3.1 collective-permute-done.21
  319.5 1.3 maximum_select_fusion
  (80 shorter events, 10.4 us)
Async XLA Ops:
  6.5 70.2 %all-gather.3.cloned.1.call-start = ((), (), s32[]{:S(2)}) async-start(), calls=%async_computation | async-start | bytes 6144000 | tf_op jit(solution)/shard_map/all_gather | solution.py:34
  13.4 4.0 %collective-permute-start = (bf16[8,50,1200]{2,0,1:T(8,128)(2,1)}, bf16[8,50,1200]{2,0,1:T(8,128)(2,1)}, u32[]{:S(2)}, u32[]{:S(2)}) collective-permute-start(bf16[8,50,1200]{2,0,1:T(8,128)(2,1)} %copy.4), channel_id=1, source_target_pairs={{0,1},{1,0},{2,3},{3,2},{4,5},{5,4},{6,7},{7,6},{8,9},{9,8},{10,11... | collective-permute-start | bytes 2880008 | tf_op jit(solution)/shard_map/ppermute | solution.py:31
  13.4 57.6 %collective-permute-start.1 = (bf16[1200,1024]{1,0:T(8,128)(2,1)}, bf16[1200,1024]{1,0:T(8,128)(2,1)}, u32[]{:S(2)}, u32[]{:S(2)}) collective-permute-start(bf16[1200,1024]{1,0:T(8,128)(2,1)} %param.5), channel_id=1, source_target_pairs={{0,64},{64,0},{1,65},{65,1},{2,66},{66,2},{3,67},{67,3},{4,68},{68... | collective-permute-start | bytes 7372808 | tf_op jit(solution)/shard_map/ppermute | solution.py:40
  20.6 149.7 %all-gather.5.cloned.1.call-start = ((), (), s32[]{:S(2)}) async-start(), calls=%async_computation.1 | async-start | bytes 4096000 | tf_op jit(solution)/shard_map/all_gather | solution.py:36
  74.4 8.5 %collective-permute-start.2 = (bf16[1200,2048]{1,0:T(8,128)(2,1)}, bf16[1200,2048]{1,0:T(8,128)(2,1)}, u32[]{:S(2)}, u32[]{:S(2)}) collective-permute-start(bf16[1200,2048]{1,0:T(8,128)(2,1)} %constant_dynamic-update-slice_fusion), channel_id=1, source_target_pairs={{0,1},{1,0},{2,3},{3,2},{4,5},{5,4},{6,7},{7,6},{8,9},{9,8},{10,11... | collective-permute-start | bytes 14745608 | tf_op jit(solution)/shard_map/ppermute | solution.py:41
  82.7 5.3 %copy-start.2 = (bf16[2,120,2,1200]{3,1,2,0:T(8,128)(2,1)}, bf16[2,120,2,1200]{3,1,2,0:T(8,128)(2,1)S(1)}, u32[]{:S(2)}) copy-start(bf16[2,120,2,1200]{3,1,2,0:T(8,128)(2,1)S(1)} %get-tuple-element.19) | copy-start | bytes 3456004
  89.7 38.4 %collective-permute-start.3 = (f32[2,60,2048]{2,0,1:T(2,128)}, f32[2,60,2048]{2,0,1:T(2,128)}, u32[]{:S(2)}, u32[]{:S(2)}) collective-permute-start(f32[2,60,2048]{2,0,1:T(2,128)} %copy.8), channel_id=1, source_target_pairs={{0,4},{4,8},{8,12},{12,0},{1,5},{5,9},{9,13},{13,1},{2,6},{6,10},{... | collective-permute-start | bytes 2949128 | tf_op jit(solution)/shard_map/ppermute | solution.py:57
  110.0 7.7 %copy-start.4 = (bf16[2,120,2,1200]{3,1,2,0:T(8,128)(2,1)S(1)}, bf16[2,120,2,1200]{3,1,2,0:T(8,128)(2,1)}, u32[]{:S(2)}) copy-start(bf16[2,120,2,1200]{3,1,2,0:T(8,128)(2,1)} %get-tuple-element.15) | copy-start | bytes 3456004
  115.9 23.6 %collective-permute-start.7 = (f32[2,60,2048]{2,0,1:T(2,128)S(1)}, f32[2,60,2048]{2,0,1:T(2,128)S(1)}, u32[]{:S(2)}, u32[]{:S(2)}) collective-permute-start(f32[2,60,2048]{2,0,1:T(2,128)S(1)} %copy.18), channel_id=1, source_target_pairs={{0,12},{4,0},{8,4},{12,8},{1,13},{5,1},{9,5},{13,9},{2,14},{6,2},{... | collective-permute-start | bytes 2949128 | tf_op jit(solution)/shard_map/ppermute | solution.py:58
  117.7 5.2 %copy-start.3 = (bf16[2,120,2,1200]{3,1,2,0:T(8,128)(2,1)S(1)}, bf16[2,120,2,1200]{3,1,2,0:T(8,128)(2,1)}, u32[]{:S(2)}) copy-start(bf16[2,120,2,1200]{3,1,2,0:T(8,128)(2,1)} %copy-done.2) | copy-start | bytes 3456004
  122.9 5.2 %copy-start.7 = (f32[2,60,2048]{2,1,0:T(8,128)S(1)}, f32[2,60,2048]{2,1,0:T(8,128)}, u32[]{:S(2)}) copy-start(f32[2,60,2048]{2,1,0:T(8,128)} %convolution_bitcast_fusion.6) | copy-start | bytes 2949124
  130.7 24.4 %collective-permute-start.4 = (f32[2,60,2048]{2,0,1:T(2,128)S(1)}, f32[2,60,2048]{2,0,1:T(2,128)S(1)}, u32[]{:S(2)}, u32[]{:S(2)}) collective-permute-start(f32[2,60,2048]{2,0,1:T(2,128)S(1)} %copy.11), channel_id=1, source_target_pairs={{0,4},{4,8},{8,12},{12,0},{1,5},{5,9},{9,13},{13,1},{2,6},{6,10},{... | collective-permute-start | bytes 2949128 | tf_op jit(solution)/shard_map/ppermute | solution.py:57
  140.9 23.5 %collective-permute-start.8 = (f32[2,60,2048]{2,0,1:T(2,128)S(1)}, f32[2,60,2048]{2,0,1:T(2,128)S(1)}, u32[]{:S(2)}, u32[]{:S(2)}) collective-permute-start(f32[2,60,2048]{2,0,1:T(2,128)S(1)} %copy.21), channel_id=1, source_target_pairs={{0,12},{4,0},{8,4},{12,8},{1,13},{5,1},{9,5},{13,9},{2,14},{6,2},{... | collective-permute-start | bytes 2949128 | tf_op jit(solution)/shard_map/ppermute | solution.py:58
  157.4 28.6 %collective-permute-start.5 = (f32[2,60,2048]{2,0,1:T(2,128)}, f32[2,60,2048]{2,0,1:T(2,128)}, u32[]{:S(2)}, u32[]{:S(2)}) collective-permute-start(f32[2,60,2048]{2,0,1:T(2,128)} %copy.14), channel_id=1, source_target_pairs={{0,4},{4,8},{8,12},{12,0},{1,5},{5,9},{9,13},{13,1},{2,6},{6,10},{... | collective-permute-start | bytes 2949128 | tf_op jit(solution)/shard_map/ppermute | solution.py:57
  166.7 23.4 %collective-permute-start.9 = (f32[2,60,2048]{2,0,1:T(2,128)}, f32[2,60,2048]{2,0,1:T(2,128)}, u32[]{:S(2)}, u32[]{:S(2)}) collective-permute-start(f32[2,60,2048]{2,0,1:T(2,128)} %copy.23), channel_id=1, source_target_pairs={{0,12},{4,0},{8,4},{12,8},{1,13},{5,1},{9,5},{13,9},{2,14},{6,2},{... | collective-permute-start | bytes 2949128 | tf_op jit(solution)/shard_map/ppermute | solution.py:58
  181.4 3.1 copy-start
  181.4 4.7 %copy-start.5 = (f32[2,60,2048]{2,1,0:T(8,128)S(1)}, f32[2,60,2048]{2,1,0:T(8,128)}, u32[]{:S(2)}) copy-start(f32[2,60,2048]{2,1,0:T(8,128)} %convolution_bitcast_fusion.4) | copy-start | bytes 2949124
  184.5 5.6 %copy-start.6 = (f32[2,60,2048]{2,1,0:T(8,128)S(1)}, f32[2,60,2048]{2,1,0:T(8,128)}, u32[]{:S(2)}) copy-start(f32[2,60,2048]{2,1,0:T(8,128)} %convolution_bitcast_fusion) | copy-start | bytes 2949124
  184.5 85.8 %collective-permute-start.11 = (f32[4,80,2048]{2,1,0:T(8,128)}, f32[4,80,2048]{2,1,0:T(8,128)S(1)}, u32[]{:S(2)}, u32[]{:S(2)}) collective-permute-start(f32[4,80,2048]{2,1,0:T(8,128)} %dynamic-slice_bitcast_fusion), channel_id=1, source_target_pairs={{0,2},{2,0},{1,3},{3,1},{4,6},{6,4},{5,7},{7,5},{8,10},{10,8},{9,1... | collective-permute-start | bytes 7864328 | tf_op jit(solution)/shard_map/ppermute | solution.py:77
  187.9 67.7 %collective-permute-start.6 = (f32[60,2048]{1,0:T(8,128)S(1)}, f32[60,2048]{1,0:T(8,128)S(1)}, u32[]{:S(2)}, u32[]{:S(2)}) collective-permute-start(f32[60,2048]{1,0:T(8,128)S(1)} %dynamic-slice_bitcast_fusion.8), channel_id=1, source_target_pairs={{0,2},{2,0},{1,3},{3,1},{4,6},{6,4},{5,7},{7,5},{8,10},{10,8},{9,1... | collective-permute-start | bytes 1474568 | tf_op jit(solution)/shard_map/ppermute | solution.py:66
  191.9 72.0 %collective-permute-start.10 = (f32[60,2048]{1,0:T(8,128)S(1)}, f32[60,2048]{1,0:T(8,128)S(1)}, u32[]{:S(2)}, u32[]{:S(2)}) collective-permute-start(f32[60,2048]{1,0:T(8,128)S(1)} %dynamic-slice_bitcast_fusion.7), channel_id=1, source_target_pairs={{0,2},{2,0},{1,3},{3,1},{4,6},{6,4},{5,7},{7,5},{8,10},{10,8},{9,1... | collective-permute-start | bytes 1474568 | tf_op jit(solution)/shard_map/ppermute | solution.py:66
  266.6 9.9 %collective-permute-start.18 = (f32[60,1024]{1,0:T(8,128)}, f32[60,1024]{1,0:T(8,128)S(1)}, u32[]{:S(2)}, u32[]{:S(2)}) collective-permute-start(f32[60,1024]{1,0:T(8,128)} %get-tuple-element.23), channel_id=1, source_target_pairs={{0,64},{64,0},{1,65},{65,1},{2,66},{66,2},{3,67},{67,3},{4,68},{68... | collective-permute-start | bytes 737288 | tf_op jit(solution)/shard_map/ppermute | solution.py:98
  269.8 9.6 %collective-permute-start.19 = (f32[60,1024]{1,0:T(8,128)}, f32[60,1024]{1,0:T(8,128)S(1)}, u32[]{:S(2)}, u32[]{:S(2)}) collective-permute-start(f32[60,1024]{1,0:T(8,128)} %get-tuple-element.25), channel_id=1, source_target_pairs={{0,64},{64,0},{1,65},{65,1},{2,66},{66,2},{3,67},{67,3},{4,68},{68... | collective-permute-start | bytes 737288 | tf_op jit(solution)/shard_map/ppermute | solution.py:98
  273.3 9.5 %collective-permute-start.12 = (f32[40,2048]{1,0:T(8,128)}, f32[40,2048]{1,0:T(8,128)S(1)}, u32[]{:S(2)}, u32[]{:S(2)}) collective-permute-start(f32[40,2048]{1,0:T(8,128)} %dynamic-slice_bitcast_fusion.10), channel_id=1, source_target_pairs={{0,4},{4,8},{8,12},{12,0},{1,5},{5,9},{9,13},{13,1},{2,6},{6,10},{... | collective-permute-start | bytes 983048 | tf_op jit(solution)/shard_map/ppermute | solution.py:57
  282.1 9.3 %collective-permute-start.15 = (f32[40,2048]{1,0:T(8,128)S(1)}, f32[40,2048]{1,0:T(8,128)S(1)}, u32[]{:S(2)}, u32[]{:S(2)}) collective-permute-start(f32[40,2048]{1,0:T(8,128)S(1)} %dynamic-slice_bitcast_fusion.9), channel_id=1, source_target_pairs={{0,12},{4,0},{8,4},{12,8},{1,13},{5,1},{9,5},{13,9},{2,14},{6,2},{... | collective-permute-start | bytes 983048 | tf_op jit(solution)/shard_map/ppermute | solution.py:58
  282.8 9.2 %collective-permute-start.13 = (f32[40,2048]{1,0:T(8,128)S(1)}, f32[40,2048]{1,0:T(8,128)S(1)}, u32[]{:S(2)}, u32[]{:S(2)}) collective-permute-start(f32[40,2048]{1,0:T(8,128)S(1)} %bitcast_add_fusion.8), channel_id=1, source_target_pairs={{0,4},{4,8},{8,12},{12,0},{1,5},{5,9},{9,13},{13,1},{2,6},{6,10},{... | collective-permute-start | bytes 983048 | tf_op jit(solution)/shard_map/ppermute | solution.py:57
  291.5 10.5 %collective-permute-start.16 = (f32[40,2048]{1,0:T(8,128)S(1)}, f32[40,2048]{1,0:T(8,128)S(1)}, u32[]{:S(2)}, u32[]{:S(2)}) collective-permute-start(f32[40,2048]{1,0:T(8,128)S(1)} %bitcast_add_fusion.5), channel_id=1, source_target_pairs={{0,12},{4,0},{8,4},{12,8},{1,13},{5,1},{9,5},{13,9},{2,14},{6,2},{... | collective-permute-start | bytes 983048 | tf_op jit(solution)/shard_map/ppermute | solution.py:58
  292.1 10.0 %collective-permute-start.14 = (f32[40,2048]{1,0:T(8,128)S(1)}, f32[40,2048]{1,0:T(8,128)S(1)}, u32[]{:S(2)}, u32[]{:S(2)}) collective-permute-start(f32[40,2048]{1,0:T(8,128)S(1)} %bitcast_add_fusion.7), channel_id=1, source_target_pairs={{0,4},{4,8},{8,12},{12,0},{1,5},{5,9},{9,13},{13,1},{2,6},{6,10},{... | collective-permute-start | bytes 983048 | tf_op jit(solution)/shard_map/ppermute | solution.py:57
  302.0 7.1 %collective-permute-start.17 = (f32[40,2048]{1,0:T(8,128)S(1)}, f32[40,2048]{1,0:T(8,128)S(1)}, u32[]{:S(2)}, u32[]{:S(2)}) collective-permute-start(f32[40,2048]{1,0:T(8,128)S(1)} %bitcast_add_fusion.4), channel_id=1, source_target_pairs={{0,12},{4,0},{8,4},{12,8},{1,13},{5,1},{9,5},{13,9},{2,14},{6,2},{... | collective-permute-start | bytes 983048 | tf_op jit(solution)/shard_map/ppermute | solution.py:58
  309.2 6.9 %collective-permute-start.20 = (f32[40,1024]{1,0:T(8,128)S(1)}, f32[40,1024]{1,0:T(8,128)S(1)}, u32[]{:S(2)}, u32[]{:S(2)}) collective-permute-start(f32[40,1024]{1,0:T(8,128)S(1)} %get-tuple-element.27), channel_id=1, source_target_pairs={{0,64},{64,0},{1,65},{65,1},{2,66},{66,2},{3,67},{67,3},{4,68},{68... | collective-permute-start | bytes 491528 | tf_op jit(solution)/shard_map/ppermute | solution.py:98
  312.4 6.8 %collective-permute-start.21 = (f32[40,1024]{1,0:T(8,128)S(1)}, f32[40,1024]{1,0:T(8,128)S(1)}, u32[]{:S(2)}, u32[]{:S(2)}) collective-permute-start(f32[40,1024]{1,0:T(8,128)S(1)} %get-tuple-element.29), channel_id=1, source_target_pairs={{0,64},{64,0},{1,65},{65,1},{2,66},{66,2},{3,67},{67,3},{4,68},{68... | collective-permute-start | bytes 491528 | tf_op jit(solution)/shard_map/ppermute | solution.py:98
  312.9 6.4 %copy-start.1 = (f32[4,30,1024]{2,1,0:T(8,128)S(1)}, f32[4,30,1024]{2,1,0:T(8,128)}, u32[]{:S(2)}) copy-start(f32[4,30,1024]{2,1,0:T(8,128)} %reshape.42) | copy-start | bytes 1474564
Sparse Core Ops, SparseCore 0:
  20.8 55.8 all-gather.2
  110.1 42.8 all-gather.4

commit v11 on v9

--- a/solution.py
+++ b/solution.py
@@ -30,13 +30,14 @@
     theirs = jnp.take(tiles, position[:, 1 - core], axis=0)
     from_sibling = lax.ppermute(theirs, "c", SWAP)
     own_owners = jnp.stack([mine, from_sibling], axis=2)
-    y_cut = TB * 3 // 5
+    y_cut = TB * 14 // 25
     gathered = lax.all_gather(own_owners[:, :y_cut], "z", axis=1, tiled=True)
-    gathered_late = lax.all_gather(own_owners[:, y_cut:], "z", axis=1, tiled=True)
     y_rows = gathered.shape[1]
     by_y = gathered.reshape(ny, nxl, y_rows, 2, kc)
 
     amp = jnp.concatenate([amplitudes, lax.ppermute(amplitudes, "xh", SWAP)], axis=1)
+    late_rows, amp = lax.optimization_barrier((own_owners[:, y_cut:], amp))
+    gathered_late = lax.all_gather(late_rows, "z", axis=1, tiled=True)
     amp = jnp.stack([amp, lax.ppermute(amp, "c", SWAP)], axis=0)
 
     def block(y_owner, low, high):
@@ -67,13 +68,17 @@
     y_half = y_rows // 2
     x_rows = gathered_late.shape[1]
     x_half = 8 * (x_rows // 16)
-    late = lax.dot_general(
-        gathered_late, amp, (((2, 3), (0, 1)), ((), ())),
-        preferred_element_type=jnp.float32,
-    ).reshape(ny, nxl, x_rows, amp.shape[-1])
-    late_here = lax.dynamic_index_in_dim(late, xi, 1, keepdims=False)
-    late_there = lax.dynamic_index_in_dim(late, 1 - xi, 1, keepdims=False)
-    late_sum = late_here + lax.ppermute(late_there, "xl", SWAP)
+    late_by_xl = gathered_late.reshape(ny, nxl, x_rows, 2, kc)
+
+    def late_block(x_owner):
+        lhs = lax.dynamic_index_in_dim(late_by_xl, x_owner, 1, keepdims=False)
+        product = lax.dot_general(
+            lhs, amp, (((2, 3), (0, 1)), ((), ())), preferred_element_type=jnp.float32
+        )
+        return lax.optimization_barrier(product)
+
+    late_there = late_block(1 - xi)
+    late_sum = late_block(xi) + lax.ppermute(late_there, "xl", SWAP)
     late_ahead, late_back = late_sum[:, :x_half], late_sum[:, x_half:]
 
     def pick(parts):

time: 313 us -> 271 us (0.87)
  waiting for transfers between devices: 171 us -> 115 us
  matrix products: 49.7 us -> 60.9 us
  other arithmetic: 12.1 us -> 18.3 us
  local copies, waits for them, and re-layouts: 29.9 us -> 25.4 us
    all_gather x1, waiting for transfers between devices: 34.6 us -> 0.02 us  [local(): gathered = lax.all_gather(own_owners[:, :y_cut], 'z', axis=1, tiled=True)]
    ppermute x6, waiting for transfers between devices: 27.5 us -> 0.9 us  [ring(): got_back = lax.ppermute(acc_back, 'y', to_prev)]
    ppermute x4, waiting for transfers between devices: 22.3 us -> 8.05 us  [local(): came = [lax.ppermute(piece[:, width:], 'xh', SWAP) for piece in pieces]]
    ppermute x2, waiting for transfers between devices: 2.02 us -> 12 us  [pair_sum(): return here + lax.ppermute(there, 'xl', SWAP)]
    ppermute x1, waiting for transfers between devices: 0.01 us -> 10 us  [local(): late_sum = late_block(xi) + lax.ppermute(late_there, 'xl', SWAP)]
    dot_general x8, matrix products: 38.7 us -> 47.6 us  [block(): lax.dot_general(lhs[:, low:high], amp, (((2, 3), (0, 1)), ((), ())), pref...]
    ppermute x6, starting transfers between devices: 3.09 us -> 8.12 us  [ring(): got_ahead = lax.ppermute(acc_ahead, 'y', to_next)]
    unnamed x7 -> x10, local copies, waits for them, and re-layouts: 4.7 us -> 0.02 us
  transfers between devices with their start and end apart: 24 -> 24, of which waited for: 16 -> 14; matrix products, arithmetic and copies ran while one was open for 25% -> 34% of each run, Pallas kernels for 0% -> 0%
where the time goes in v11:
time: 271 us; the launch traced here: 270 us
  waiting for transfers between devices  115 us (42%)
  matrix products  60.9 us (22%)
  starting transfers between devices  36.3 us (13%)
  local copies, waits for them, and re-layouts  25.4 us (9%)
  other arithmetic  18.3 us (7%)
  between operations  13.9 us (5%)
    ppermute x1, waiting for transfers between devices, local(): lax.ppermute(amplitudes, 'xh', SWAP)  53.7 us
    dot_general x8, matrix products, block(): lax.dot_general(lhs[:, low:high], amp, (((2, 3), (0, 1)), ((), ())), pref...  47.6 us
    ppermute x6, waiting for transfers between devices, ring(): got_ahead = lax.ppermute(acc_ahead, 'y', to_next)  22.8 us
    dot_general x2, matrix products, late_block(): lax.dot_general(lhs, amp, (((2, 3), (0, 1)), ((), ())), preferred_element...  13.3 us
    ppermute x6, starting transfers between devices, ring(): got_back = lax.ppermute(acc_back, 'y', to_prev)  12.9 us
    ppermute x2, waiting for transfers between devices, pair_sum(): return here + lax.ppermute(there, 'xl', SWAP)  12 us
    ppermute x1, waiting for transfers between devices, local(): late_sum = late_block(xi) + lax.ppermute(late_there, 'xl', SWAP)  10 us
    ppermute x4, starting transfers between devices, local(): came = [lax.ppermute(piece[:, width:], 'xh', SWAP) for piece in pieces]  8.36 us
  transfers between devices with their start and end apart: 24, of which 14 were waited for; matrix products, arithmetic and copies ran while one was open for 34% of the time, Pallas kernels for 0%

profile of v11, /device:TPU:0, one launch (start us, length us, event | category | flops | bytes accessed | tf_op | source)
XLA Modules:
  0.0 270.1 jit_solution(11908670111984141093)
XLA Ops:
  7.3 1.2 sort.17
  8.9 2.6 reshape.35
  12.3 1.1 copy.12
  14.2 2.1 collective-permute-done
  16.3 1.4 copy.35
  17.9 1.6 copy.14
  19.6 3.2 %collective-permute-start.1 = (bf16[1200,1024]{1,0:T(8,128)(2,1)}, bf16[1200,1024]{1,0:T(8,128)(2,1)S(1)}, u32[]{:S(2)}, u32[]{:S(2)}) collective-permute-start(bf16[1200,1024]{1,0:T(8,128)(2,1)} %param.5), channel_id=1, source_target_pairs={{0,64},{64,0},{1,65},{65,1},{2,66},{66,2},{3,67},{67,3},{4,68},{68... | collective-permute-start | bytes 7372808 | tf_op jit(solution)/shard_map/ppermute | solution.py:38
  23.1 53.7 %collective-permute-done.1 = bf16[1200,1024]{1,0:T(8,128)(2,1)S(1)} collective-permute-done((bf16[1200,1024]{1,0:T(8,128)(2,1)}, bf16[1200,1024]{1,0:T(8,128)(2,1)S(1)}, u32[]{:S(2)}, u32[]{:S(2)}) %collective-permute-start.1) | collective-permute-done | bytes 2457632 | tf_op jit(solution)/shard_map/ppermute | solution.py:38
  76.8 2.7 %pad_maximum_fusion = bf16[1200,2048]{1,0:T(8,128)(2,1)} fusion(bf16[1200,1024]{1,0:T(8,128)(2,1)S(1)} %collective-permute-done.1, bf16[1200,1024]{1,0:T(8,128)(2,1)S(1)} %copy-done), kind=kLoop, calls=%fused_computation.3 | loop fusion | flops 9830400 | bytes 9830400 | tf_op jit(solution)/shard_map/concatenate | solution.py:38
  79.5 1.1 copy.21
  80.7 3.8 %copy.33 = bf16[8,112,2,1200]{3,1,2,0:T(8,128)(2,1)S(1)} copy(bf16[8,112,2,1200]{3,0,2,1:T(8,128)(2,1)} %all-gather.3.cloned.1.call-done) | data formatting | bytes 8601600 | tf_op jit(solution)/shard_map/reshape | solution.py:36
  85.1 3.0 %collective-permute-done.2 = bf16[1200,2048]{1,0:T(8,128)(2,1)} collective-permute-done((bf16[1200,2048]{1,0:T(8,128)(2,1)}, bf16[1200,2048]{1,0:T(8,128)(2,1)}, u32[]{:S(2)}, u32[]{:S(2)}) %collective-permute-start.2) | collective-permute-done | bytes 4915232 | tf_op jit(solution)/shard_map/ppermute | solution.py:41
  88.0 6.6 %convolution_bitcast_fusion.9 = f32[2,56,2048]{2,1,0:T(8,128)} fusion(bf16[2,112,2,1200]{3,1,2,0:T(8,128)(2,1)S(1)} %get-tuple-element.19, bf16[1,1200,2048]{2,1,0:T(8,128)(2,1)} %bitcast.5, bf16[1,1200,2048]{2,1,0:T(8,128)(2,1)} %bitcast.4), kind=kOutput, calls=%fused_computation.13 | convolution fusion | flops 1105920000 | bytes 11321344 | tf_op jit(solution)/shard_map/dot_general | solution.py:45
  94.6 1.7 collective-permute-start.3
  96.3 6.5 %convolution_bitcast_fusion.5 = f32[2,56,2048]{2,1,0:T(8,128)} fusion(bf16[2,112,2,1200]{3,1,2,0:T(8,128)(2,1)S(1)} %get-tuple-element.16, bf16[1,1200,2048]{2,1,0:T(8,128)(2,1)} %bitcast.5, bf16[1,1200,2048]{2,1,0:T(8,128)(2,1)} %bitcast.4), kind=kOutput, calls=%fused_computation.9 | convolution fusion | flops 1105920000 | bytes 11321344 | tf_op jit(solution)/shard_map/dot_general | solution.py:45
  102.8 1.6 collective-permute-start.7
  104.4 6.6 %convolution_bitcast_fusion.8 = f32[2,56,2048]{2,1,0:T(8,128)} fusion(bf16[2,112,2,1200]{3,1,2,0:T(8,128)(2,1)S(1)} %get-tuple-element.18, bf16[1,1200,2048]{2,1,0:T(8,128)(2,1)} %bitcast.5, bf16[1,1200,2048]{2,1,0:T(8,128)(2,1)} %bitcast.4), kind=kOutput, calls=%fused_computation.12 | convolution fusion | flops 1105920000 | bytes 11321344 | tf_op jit(solution)/shard_map/dot_general | solution.py:45
  111.0 6.6 %convolution_bitcast_fusion.7 = f32[2,56,2048]{2,1,0:T(8,128)} fusion(bf16[2,112,2,1200]{3,1,2,0:T(8,128)(2,1)S(1)} %get-tuple-element.14, bf16[1,1200,2048]{2,1,0:T(8,128)(2,1)} %bitcast.5, bf16[1,1200,2048]{2,1,0:T(8,128)(2,1)} %bitcast.4), kind=kOutput, calls=%fused_computation.11 | convolution fusion | flops 1105920000 | bytes 11321344 | tf_op jit(solution)/shard_map/dot_general | solution.py:45
  117.6 6.6 %convolution_bitcast_fusion.6 = f32[2,56,2048]{2,1,0:T(8,128)} fusion(bf16[2,112,2,1200]{3,1,2,0:T(8,128)(2,1)S(1)} %get-tuple-element.17, bf16[1,1200,2048]{2,1,0:T(8,128)(2,1)} %bitcast.5, bf16[1,1200,2048]{2,1,0:T(8,128)(2,1)} %bitcast.4), kind=kOutput, calls=%fused_computation.10 | convolution fusion | flops 1105920000 | bytes 11321344 | tf_op jit(solution)/shard_map/dot_general | solution.py:45
  124.2 2.7 %all-gather.5.cloned.1.call-done = bf16[8,88,2,1200]{3,0,2,1:T(8,128)(2,1)} async-done(((bf16[8,22,2,1200]{3,0,2,1:T(8,128)(2,1)}), bf16[8,88,2,1200]{3,0,2,1:T(8,128)(2,1)}) %all-gather.5.cloned.1.call-update) | async-done | bytes 3379216 | tf_op jit(solution)/shard_map/all_gather | solution.py:40
  126.9 3.1 %copy.22 = bf16[8,88,2,1200]{3,1,2,0:T(8,128)(2,1)S(1)} copy(bf16[8,88,2,1200]{3,0,2,1:T(8,128)(2,1)} %all-gather.5.cloned.1.call-done) | data formatting | bytes 6758400 | tf_op jit(solution)/shard_map/all_gather | solution.py:40
  130.1 6.7 %convolution_bitcast_fusion = f32[4,88,2048]{2,1,0:T(8,128)S(1)} fusion(bf16[4,2,88,2,1200]{4,2,3,1,0:T(8,128)(2,1)S(1)} %bitcast.97, s32[]{:T(128)S(6)} %select_n.127, bf16[1,1200,2048]{2,1,0:T(8,128)(2,1)} %bitcast.5, bf16[1,1200,2048]{2,1,0:T(8,128)(2,1)} %bitcast.4), kind=kOutput, calls=%fused_computation.4 | convolution fusion | flops 3465216000 | bytes 14516228 | tf_op jit(solution)/shard_map/dot_general | solution.py:75
  136.7 1.5 collective-permute-start.11
  138.3 4.9 %convolution_bitcast_fusion.4 = f32[2,56,2048]{2,1,0:T(8,128)S(1)} fusion(bf16[2,112,2,1200]{3,1,2,0:T(8,128)(2,1)S(1)} %get-tuple-element.15, bf16[1,1200,2048]{2,1,0:T(8,128)(2,1)} %bitcast.5, bf16[1,1200,2048]{2,1,0:T(8,128)(2,1)} %bitcast.4), kind=kOutput, calls=%fused_computation.8 | convolution fusion | flops 1105920000 | bytes 11321344 | tf_op jit(solution)/shard_map/dot_general | solution.py:45
  143.2 1.3 add.182
  144.5 1.6 collective-permute-start.4
  146.1 1.3 add.198
  147.4 1.8 collective-permute-start.8
  149.2 4.9 %convolution_bitcast_fusion.2 = f32[2,56,2048]{2,1,0:T(8,128)S(1)} fusion(bf16[2,112,2,1200]{3,1,2,0:T(8,128)(2,1)S(1)} %get-tuple-element.17, bf16[1,1200,2048]{2,1,0:T(8,128)(2,1)} %bitcast.5, bf16[1,1200,2048]{2,1,0:T(8,128)(2,1)} %bitcast.4), kind=kOutput, calls=%fused_computation.6 | convolution fusion | flops 1105920000 | bytes 11321344 | tf_op jit(solution)/shard_map/dot_general | solution.py:45
  154.1 4.9 %convolution_bitcast_fusion.3 = f32[2,56,2048]{2,1,0:T(8,128)S(1)} fusion(bf16[2,112,2,1200]{3,1,2,0:T(8,128)(2,1)S(1)} %get-tuple-element.19, bf16[1,1200,2048]{2,1,0:T(8,128)(2,1)} %bitcast.5, bf16[1,1200,2048]{2,1,0:T(8,128)(2,1)} %bitcast.4), kind=kOutput, calls=%fused_computation.7 | convolution fusion | flops 1105920000 | bytes 11321344 | tf_op jit(solution)/shard_map/dot_general | solution.py:45
  159.0 8.4 %collective-permute-done.4 = f32[2,56,2048]{2,1,0:T(8,128)S(1)} collective-permute-done((f32[2,56,2048]{2,1,0:T(8,128)S(1)}, f32[2,56,2048]{2,1,0:T(8,128)S(1)}, u32[]{:S(2)}, u32[]{:S(2)}) %collective-permute-start.4) | collective-permute-done | bytes 917536 | tf_op jit(solution)/shard_map/ppermute | solution.py:57
  167.9 0.9 collective-permute-done.8
  168.9 3.3 %collective-permute-start.9 = (f32[2,56,2048]{2,1,0:T(8,128)S(1)}, f32[2,56,2048]{2,1,0:T(8,128)S(1)}, u32[]{:S(2)}, u32[]{:S(2)}) collective-permute-start(f32[2,56,2048]{2,1,0:T(8,128)S(1)} %add.199), channel_id=1, source_target_pairs={{0,12},{4,0},{8,4},{12,8},{1,13},{5,1},{9,5},{13,9},{2,14},{6,2},{... | collective-permute-start | bytes 2752520 | tf_op jit(solution)/shard_map/ppermute | solution.py:58
  172.2 6.6 %convolution_bitcast_fusion.1 = f32[4,88,2048]{2,1,0:T(8,128)S(1)} fusion(bf16[4,2,88,2,1200]{4,2,3,1,0:T(8,128)(2,1)S(1)} %bitcast.98, s32[]{:T(128)S(6)} %select_n.126, bf16[1,1200,2048]{2,1,0:T(8,128)(2,1)} %bitcast.5, bf16[1,1200,2048]{2,1,0:T(8,128)(2,1)} %bitcast.4), kind=kOutput, calls=%fused_computation.5 | convolution fusion | flops 3465216000 | bytes 14516228 | tf_op jit(solution)/shard_map/dot_general | solution.py:75
  178.8 10.8 %collective-permute-done.5 = f32[2,56,2048]{2,1,0:T(8,128)S(1)} collective-permute-done((f32[2,56,2048]{2,1,0:T(8,128)S(1)}, f32[2,56,2048]{2,1,0:T(8,128)S(1)}, u32[]{:S(2)}, u32[]{:S(2)}) %collective-permute-start.5) | collective-permute-done | bytes 917536 | tf_op jit(solution)/shard_map/ppermute | solution.py:57
  190.6 1.5 collective-permute-start.10
  192.2 10.0 %collective-permute-done.11 = f32[4,88,2048]{2,1,0:T(8,128)S(1)} collective-permute-done((f32[4,88,2048]{2,1,0:T(8,128)S(1)}, f32[4,88,2048]{2,1,0:T(8,128)S(1)}, u32[]{:S(2)}, u32[]{:S(2)}) %collective-permute-start.11) | collective-permute-done | bytes 2883616 | tf_op jit(solution)/shard_map/ppermute | solution.py:81
  202.9 0.7 dynamic-slice_bitcast_fusion.9
  203.7 1.5 collective-permute-start.12
  205.2 0.8 dynamic-slice_bitcast_fusion.8
  205.9 1.8 collective-permute-start.15
  207.7 4.3 %collective-permute-done.6 = f32[56,2048]{1,0:T(8,128)S(1)} collective-permute-done((f32[56,2048]{1,0:T(8,128)S(1)}, f32[56,2048]{1,0:T(8,128)S(1)}, u32[]{:S(2)}, u32[]{:S(2)}) %collective-permute-start.6) | collective-permute-done | bytes 458784 | tf_op jit(solution)/shard_map/ppermute | solution.py:66
  212.8 7.7 %collective-permute-done.10 = f32[56,2048]{1,0:T(8,128)S(1)} collective-permute-done((f32[56,2048]{1,0:T(8,128)S(1)}, f32[56,2048]{1,0:T(8,128)S(1)}, u32[]{:S(2)}, u32[]{:S(2)}) %collective-permute-start.10) | collective-permute-done | bytes 458784 | tf_op jit(solution)/shard_map/ppermute | solution.py:66
  221.3 0.8 pad_maximum_fusion.4
  222.1 1.1 reshape.38
  223.2 3.1 %collective-permute-start.18 = (f32[56,1024]{1,0:T(8,128)}, f32[56,1024]{1,0:T(8,128)S(1)}, u32[]{:S(2)}, u32[]{:S(2)}) collective-permute-start(f32[56,1024]{1,0:T(8,128)} %get-tuple-element.21), channel_id=1, source_target_pairs={{0,64},{64,0},{1,65},{65,1},{2,66},{66,2},{3,67},{67,3},{4,68},{68... | collective-permute-start | bytes 688136 | tf_op jit(solution)/shard_map/ppermute | solution.py:102
  226.8 1.7 bitcast_add_fusion.7
  228.5 1.5 collective-permute-start.13
  230.0 1.8 bitcast_add_fusion.4
  231.8 1.8 collective-permute-start.16
  233.6 2.6 collective-permute-done.19
  236.2 0.8 pad_maximum_fusion.5
  237.0 1.9 reshape.42
  238.9 1.0 bitcast_add_fusion.6
  239.9 1.6 collective-permute-start.14
  241.4 1.0 bitcast_add_fusion.3
  242.5 2.7 %collective-permute-start.17 = (f32[48,2048]{1,0:T(8,128)S(1)}, f32[48,2048]{1,0:T(8,128)S(1)}, u32[]{:S(2)}, u32[]{:S(2)}) collective-permute-start(f32[48,2048]{1,0:T(8,128)S(1)} %bitcast_add_fusion.3), channel_id=1, source_target_pairs={{0,12},{4,0},{8,4},{12,8},{1,13},{5,1},{9,5},{13,9},{2,14},{6,2},{... | collective-permute-start | bytes 1179656 | tf_op jit(solution)/shard_map/ppermute | solution.py:58
  245.2 3.5 %collective-permute-done.14 = f32[40,2048]{1,0:T(8,128)S(1)} collective-permute-done((f32[40,2048]{1,0:T(8,128)S(1)}, f32[40,2048]{1,0:T(8,128)S(1)}, u32[]{:S(2)}, u32[]{:S(2)}) %collective-permute-start.14) | collective-permute-done | bytes 327712 | tf_op jit(solution)/shard_map/ppermute | solution.py:57
  249.5 3.1 %collective-permute-start.20 = (f32[40,1024]{1,0:T(8,128)}, f32[40,1024]{1,0:T(8,128)}, u32[]{:S(2)}, u32[]{:S(2)}) collective-permute-start(f32[40,1024]{1,0:T(8,128)} %get-tuple-element.27), channel_id=1, source_target_pairs={{0,64},{64,0},{1,65},{65,1},{2,66},{66,2},{3,67},{67,3},{4,68},{68... | collective-permute-start | bytes 491528 | tf_op jit(solution)/shard_map/ppermute | solution.py:102
  253.3 1.7 collective-permute-start.21
  255.3 3.1 %collective-permute-done.20 = f32[40,1024]{1,0:T(8,128)} collective-permute-done((f32[40,1024]{1,0:T(8,128)}, f32[40,1024]{1,0:T(8,128)}, u32[]{:S(2)}, u32[]{:S(2)}) %collective-permute-start.20) | collective-permute-done | bytes 163872 | tf_op jit(solution)/shard_map/ppermute | solution.py:102
  258.4 2.4 collective-permute-done.21
  260.7 0.9 pad_maximum_fusion.7
  261.9 1.3 maximum_select_fusion
  (69 shorter events, 10.2 us)
Async XLA Ops:
  6.5 74.2 %all-gather.3.cloned.1.call-start = ((), (), s32[]{:S(2)}) async-start(), calls=%async_computation | async-start | bytes 5734400 | tf_op jit(solution)/shard_map/all_gather | solution.py:34
  13.4 3.0 %collective-permute-start = (bf16[8,50,1200]{2,0,1:T(8,128)(2,1)}, bf16[8,50,1200]{2,0,1:T(8,128)(2,1)}, u32[]{:S(2)}, u32[]{:S(2)}) collective-permute-start(bf16[8,50,1200]{2,0,1:T(8,128)(2,1)} %copy.12), channel_id=1, source_target_pairs={{0,1},{1,0},{2,3},{3,2},{4,5},{5,4},{6,7},{7,6},{8,9},{9,8},{10,11... | collective-permute-start | bytes 2880008 | tf_op jit(solution)/shard_map/ppermute | solution.py:31
  19.5 107.4 %all-gather.5.cloned.1.call-start = ((), (), s32[]{:S(2)}) async-start(), calls=%async_computation.1 | async-start | bytes 4505600 | tf_op jit(solution)/shard_map/all_gather | solution.py:40
  19.6 57.2 %copy-start = (bf16[1200,1024]{1,0:T(8,128)(2,1)S(1)}, bf16[1200,1024]{1,0:T(8,128)(2,1)}, u32[]{:S(2)}) copy-start(bf16[1200,1024]{1,0:T(8,128)(2,1)} %param.5) | copy-start | bytes 7372804
  19.6 57.2 %collective-permute-start.1 = (bf16[1200,1024]{1,0:T(8,128)(2,1)}, bf16[1200,1024]{1,0:T(8,128)(2,1)S(1)}, u32[]{:S(2)}, u32[]{:S(2)}) collective-permute-start(bf16[1200,1024]{1,0:T(8,128)(2,1)} %param.5), channel_id=1, source_target_pairs={{0,64},{64,0},{1,65},{65,1},{2,66},{66,2},{3,67},{67,3},{4,68},{68... | collective-permute-start | bytes 7372808 | tf_op jit(solution)/shard_map/ppermute | solution.py:38
  79.5 8.5 %collective-permute-start.2 = (bf16[1200,2048]{1,0:T(8,128)(2,1)}, bf16[1200,2048]{1,0:T(8,128)(2,1)}, u32[]{:S(2)}, u32[]{:S(2)}) collective-permute-start(bf16[1200,2048]{1,0:T(8,128)(2,1)} %pad_maximum_fusion), channel_id=1, source_target_pairs={{0,1},{1,0},{2,3},{3,2},{4,5},{5,4},{6,7},{7,6},{8,9},{9,8},{10,11... | collective-permute-start | bytes 14745608 | tf_op jit(solution)/shard_map/ppermute | solution.py:41
  94.6 48.6 %collective-permute-start.3 = (f32[2,56,2048]{2,1,0:T(8,128)}, f32[2,56,2048]{2,1,0:T(8,128)}, u32[]{:S(2)}, u32[]{:S(2)}) collective-permute-start(f32[2,56,2048]{2,1,0:T(8,128)} %convolution_bitcast_fusion.9), channel_id=1, source_target_pairs={{0,4},{4,8},{8,12},{12,0},{1,5},{5,9},{9,13},{13,1},{2,6},{6,10},{... | collective-permute-start | bytes 2752520 | tf_op jit(solution)/shard_map/ppermute | solution.py:57
  102.8 43.3 %collective-permute-start.7 = (f32[2,56,2048]{2,1,0:T(8,128)}, f32[2,56,2048]{2,1,0:T(8,128)}, u32[]{:S(2)}, u32[]{:S(2)}) collective-permute-start(f32[2,56,2048]{2,1,0:T(8,128)} %convolution_bitcast_fusion.5), channel_id=1, source_target_pairs={{0,12},{4,0},{8,4},{12,8},{1,13},{5,1},{9,5},{13,9},{2,14},{6,2},{... | collective-permute-start | bytes 2752520 | tf_op jit(solution)/shard_map/ppermute | solution.py:58
  136.7 65.4 %collective-permute-start.11 = (f32[4,88,2048]{2,1,0:T(8,128)S(1)}, f32[4,88,2048]{2,1,0:T(8,128)S(1)}, u32[]{:S(2)}, u32[]{:S(2)}) collective-permute-start(f32[4,88,2048]{2,1,0:T(8,128)S(1)} %convolution_bitcast_fusion), channel_id=1, source_target_pairs={{0,2},{2,0},{1,3},{3,1},{4,6},{6,4},{5,7},{7,5},{8,10},{10,8},{9,1... | collective-permute-start | bytes 8650760 | tf_op jit(solution)/shard_map/ppermute | solution.py:81
  138.3 5.0 %copy-start.4 = (f32[2,56,2048]{2,1,0:T(8,128)S(1)}, f32[2,56,2048]{2,1,0:T(8,128)}, u32[]{:S(2)}) copy-start(f32[2,56,2048]{2,1,0:T(8,128)} %convolution_bitcast_fusion.8) | copy-start | bytes 2752516
  144.5 22.9 %collective-permute-start.4 = (f32[2,56,2048]{2,1,0:T(8,128)S(1)}, f32[2,56,2048]{2,1,0:T(8,128)S(1)}, u32[]{:S(2)}, u32[]{:S(2)}) collective-permute-start(f32[2,56,2048]{2,1,0:T(8,128)S(1)} %add.182), channel_id=1, source_target_pairs={{0,4},{4,8},{8,12},{12,0},{1,5},{5,9},{9,13},{13,1},{2,6},{6,10},{... | collective-permute-start | bytes 2752520 | tf_op jit(solution)/shard_map/ppermute | solution.py:57
  147.4 21.4 %collective-permute-start.8 = (f32[2,56,2048]{2,1,0:T(8,128)S(1)}, f32[2,56,2048]{2,1,0:T(8,128)S(1)}, u32[]{:S(2)}, u32[]{:S(2)}) collective-permute-start(f32[2,56,2048]{2,1,0:T(8,128)S(1)} %add.198), channel_id=1, source_target_pairs={{0,12},{4,0},{8,4},{12,8},{1,13},{5,1},{9,5},{13,9},{2,14},{6,2},{... | collective-permute-start | bytes 2752520 | tf_op jit(solution)/shard_map/ppermute | solution.py:58
  154.1 13.4 %copy-start.3 = (f32[2,56,2048]{2,1,0:T(8,128)S(1)}, f32[2,56,2048]{2,1,0:T(8,128)}, u32[]{:S(2)}) copy-start(f32[2,56,2048]{2,1,0:T(8,128)} %convolution_bitcast_fusion.7) | copy-start | bytes 2752516
  167.6 22.1 %collective-permute-start.5 = (f32[2,56,2048]{2,1,0:T(8,128)S(1)}, f32[2,56,2048]{2,1,0:T(8,128)S(1)}, u32[]{:S(2)}, u32[]{:S(2)}) collective-permute-start(f32[2,56,2048]{2,1,0:T(8,128)S(1)} %add.185), channel_id=1, source_target_pairs={{0,4},{4,8},{8,12},{12,0},{1,5},{5,9},{9,13},{13,1},{2,6},{6,10},{... | collective-permute-start | bytes 2752520 | tf_op jit(solution)/shard_map/ppermute | solution.py:57
  168.9 20.7 %copy-start.2 = (f32[2,56,2048]{2,1,0:T(8,128)S(1)}, f32[2,56,2048]{2,1,0:T(8,128)}, u32[]{:S(2)}) copy-start(f32[2,56,2048]{2,1,0:T(8,128)} %convolution_bitcast_fusion.6) | copy-start | bytes 2752516
  168.9 21.5 %collective-permute-start.9 = (f32[2,56,2048]{2,1,0:T(8,128)S(1)}, f32[2,56,2048]{2,1,0:T(8,128)S(1)}, u32[]{:S(2)}, u32[]{:S(2)}) collective-permute-start(f32[2,56,2048]{2,1,0:T(8,128)S(1)} %add.199), channel_id=1, source_target_pairs={{0,12},{4,0},{8,4},{12,8},{1,13},{5,1},{9,5},{13,9},{2,14},{6,2},{... | collective-permute-start | bytes 2752520 | tf_op jit(solution)/shard_map/ppermute | solution.py:58
  189.8 22.2 %collective-permute-start.6 = (f32[56,2048]{1,0:T(8,128)S(1)}, f32[56,2048]{1,0:T(8,128)S(1)}, u32[]{:S(2)}, u32[]{:S(2)}) collective-permute-start(f32[56,2048]{1,0:T(8,128)S(1)} %dynamic-slice_bitcast_fusion.7), channel_id=1, source_target_pairs={{0,2},{2,0},{1,3},{3,1},{4,6},{6,4},{5,7},{7,5},{8,10},{10,8},{9,1... | collective-permute-start | bytes 1376264 | tf_op jit(solution)/shard_map/ppermute | solution.py:66
  190.6 29.9 %collective-permute-start.10 = (f32[56,2048]{1,0:T(8,128)S(1)}, f32[56,2048]{1,0:T(8,128)S(1)}, u32[]{:S(2)}, u32[]{:S(2)}) collective-permute-start(f32[56,2048]{1,0:T(8,128)S(1)} %dynamic-slice_bitcast_fusion.6), channel_id=1, source_target_pairs={{0,2},{2,0},{1,3},{3,1},{4,6},{6,4},{5,7},{7,5},{8,10},{10,8},{9,1... | collective-permute-start | bytes 1376264 | tf_op jit(solution)/shard_map/ppermute | solution.py:66
  203.7 23.1 %collective-permute-start.12 = (f32[40,2048]{1,0:T(8,128)}, f32[40,2048]{1,0:T(8,128)}, u32[]{:S(2)}, u32[]{:S(2)}) collective-permute-start(f32[40,2048]{1,0:T(8,128)} %dynamic-slice_bitcast_fusion.9), channel_id=1, source_target_pairs={{0,4},{4,8},{8,12},{12,0},{1,5},{5,9},{9,13},{13,1},{2,6},{6,10},{... | collective-permute-start | bytes 983048 | tf_op jit(solution)/shard_map/ppermute | solution.py:57
  205.9 24.1 %collective-permute-start.15 = (f32[48,2048]{1,0:T(8,128)}, f32[48,2048]{1,0:T(8,128)}, u32[]{:S(2)}, u32[]{:S(2)}) collective-permute-start(f32[48,2048]{1,0:T(8,128)} %dynamic-slice_bitcast_fusion.8), channel_id=1, source_target_pairs={{0,12},{4,0},{8,4},{12,8},{1,13},{5,1},{9,5},{13,9},{2,14},{6,2},{... | collective-permute-start | bytes 1179656 | tf_op jit(solution)/shard_map/ppermute | solution.py:58
  223.2 10.4 %collective-permute-start.18 = (f32[56,1024]{1,0:T(8,128)}, f32[56,1024]{1,0:T(8,128)S(1)}, u32[]{:S(2)}, u32[]{:S(2)}) collective-permute-start(f32[56,1024]{1,0:T(8,128)} %get-tuple-element.21), channel_id=1, source_target_pairs={{0,64},{64,0},{1,65},{65,1},{2,66},{66,2},{3,67},{67,3},{4,68},{68... | collective-permute-start | bytes 688136 | tf_op jit(solution)/shard_map/ppermute | solution.py:102
  226.2 10.0 %collective-permute-start.19 = (f32[56,1024]{1,0:T(8,128)}, f32[56,1024]{1,0:T(8,128)S(1)}, u32[]{:S(2)}, u32[]{:S(2)}) collective-permute-start(f32[56,1024]{1,0:T(8,128)} %get-tuple-element.23), channel_id=1, source_target_pairs={{0,64},{64,0},{1,65},{65,1},{2,66},{66,2},{3,67},{67,3},{4,68},{68... | collective-permute-start | bytes 688136 | tf_op jit(solution)/shard_map/ppermute | solution.py:102
  228.5 10.4 %collective-permute-start.13 = (f32[40,2048]{1,0:T(8,128)}, f32[40,2048]{1,0:T(8,128)}, u32[]{:S(2)}, u32[]{:S(2)}) collective-permute-start(f32[40,2048]{1,0:T(8,128)} %bitcast_add_fusion.7), channel_id=1, source_target_pairs={{0,4},{4,8},{8,12},{12,0},{1,5},{5,9},{9,13},{13,1},{2,6},{6,10},{... | collective-permute-start | bytes 983048 | tf_op jit(solution)/shard_map/ppermute | solution.py:57
  231.8 9.6 %collective-permute-start.16 = (f32[48,2048]{1,0:T(8,128)}, f32[48,2048]{1,0:T(8,128)}, u32[]{:S(2)}, u32[]{:S(2)}) collective-permute-start(f32[48,2048]{1,0:T(8,128)} %bitcast_add_fusion.4), channel_id=1, source_target_pairs={{0,12},{4,0},{8,4},{12,8},{1,13},{5,1},{9,5},{13,9},{2,14},{6,2},{... | collective-permute-start | bytes 1179656 | tf_op jit(solution)/shard_map/ppermute | solution.py:58
  239.9 8.8 %collective-permute-start.14 = (f32[40,2048]{1,0:T(8,128)S(1)}, f32[40,2048]{1,0:T(8,128)S(1)}, u32[]{:S(2)}, u32[]{:S(2)}) collective-permute-start(f32[40,2048]{1,0:T(8,128)S(1)} %bitcast_add_fusion.6), channel_id=1, source_target_pairs={{0,4},{4,8},{8,12},{12,0},{1,5},{5,9},{9,13},{13,1},{2,6},{6,10},{... | collective-permute-start | bytes 983048 | tf_op jit(solution)/shard_map/ppermute | solution.py:57
  242.5 10.1 %collective-permute-start.17 = (f32[48,2048]{1,0:T(8,128)S(1)}, f32[48,2048]{1,0:T(8,128)S(1)}, u32[]{:S(2)}, u32[]{:S(2)}) collective-permute-start(f32[48,2048]{1,0:T(8,128)S(1)} %bitcast_add_fusion.3), channel_id=1, source_target_pairs={{0,12},{4,0},{8,4},{12,8},{1,13},{5,1},{9,5},{13,9},{2,14},{6,2},{... | collective-permute-start | bytes 1179656 | tf_op jit(solution)/shard_map/ppermute | solution.py:58
  249.5 8.9 %collective-permute-start.20 = (f32[40,1024]{1,0:T(8,128)}, f32[40,1024]{1,0:T(8,128)}, u32[]{:S(2)}, u32[]{:S(2)}) collective-permute-start(f32[40,1024]{1,0:T(8,128)} %get-tuple-element.27), channel_id=1, source_target_pairs={{0,64},{64,0},{1,65},{65,1},{2,66},{66,2},{3,67},{67,3},{4,68},{68... | collective-permute-start | bytes 491528 | tf_op jit(solution)/shard_map/ppermute | solution.py:102
  252.6 9.1 %copy-start.1 = (f32[4,28,1024]{2,1,0:T(8,128)S(1)}, f32[4,28,1024]{2,1,0:T(8,128)}, u32[]{:S(2)}) copy-start(f32[4,28,1024]{2,1,0:T(8,128)} %reshape.42) | copy-start | bytes 1376260
  253.3 7.4 %collective-permute-start.21 = (f32[48,1024]{1,0:T(8,128)}, f32[48,1024]{1,0:T(8,128)S(1)}, u32[]{:S(2)}, u32[]{:S(2)}) collective-permute-start(f32[48,1024]{1,0:T(8,128)} %get-tuple-element.25), channel_id=1, source_target_pairs={{0,64},{64,0},{1,65},{65,1},{2,66},{66,2},{3,67},{67,3},{4,68},{68... | collective-permute-start | bytes 589832 | tf_op jit(solution)/shard_map/ppermute | solution.py:102
Sparse Core Ops, SparseCore 0:
  19.7 54.1 all-gather.2
  80.7 46.1 all-gather.4

commit v12 on v11

--- a/solution.py
+++ b/solution.py
@@ -67,7 +67,6 @@
 
     y_half = y_rows // 2
     x_rows = gathered_late.shape[1]
-    x_half = 8 * (x_rows // 16)
     late_by_xl = gathered_late.reshape(ny, nxl, x_rows, 2, kc)
 
     def late_block(x_owner):
@@ -79,7 +78,6 @@
 
     late_there = late_block(1 - xi)
     late_sum = late_block(xi) + lax.ppermute(late_there, "xl", SWAP)
-    late_ahead, late_back = late_sum[:, :x_half], late_sum[:, x_half:]
 
     def pick(parts):
         return lambda y_owner: lax.dynamic_index_in_dim(parts, y_owner % ny, 0, keepdims=False)
@@ -90,13 +88,11 @@
         lambda y_owner: block(y_owner, 0, y_half),
         lambda y_owner: block(y_owner, y_half, y_rows),
     )
-    late_done = ring(
-        pick(late_ahead)(yi + ny - 1),
-        pick(late_back)(yi + 1),
-        pick(late_ahead),
-        pick(late_back),
-    )
-    pieces = [pair_sum(early[0]), pair_sum(early[1]), late_done[0], late_done[1]]
+    late_done = pick(late_sum)(yi)
+    for hop in range(1, ny):
+        to_owner = [(i, (i + hop) % ny) for i in range(ny)]
+        late_done = late_done + lax.ppermute(pick(late_sum)(yi + hop), "y", to_owner)
+    pieces = [pair_sum(early[0]), pair_sum(early[1]), late_done]
 
     kept = [piece[:, :width] for piece in pieces]
     came = [lax.ppermute(piece[:, width:], "xh", SWAP) for piece in pieces]

time: 271 us -> 256 us (0.945)
  other arithmetic: 18.3 us -> 10.1 us
  local copies, waits for them, and re-layouts: 25.4 us -> 18.3 us
  waiting for transfers between devices: 115 us -> 120 us
  starting transfers between devices: 36.3 us -> 32.1 us
    ppermute x0 -> x3, waiting for transfers between devices: none -> 11.1 us  [local(): lax.ppermute(pick(late_sum)(yi + hop), 'y', to_owner)]
    ppermute x6 -> x3, starting transfers between devices: 12.9 us -> 6.67 us  [ring(): got_back = lax.ppermute(acc_back, 'y', to_prev)]
    ppermute x0 -> x3, starting transfers between devices: none -> 5.71 us  [local(): lax.ppermute(pick(late_sum)(yi + hop), 'y', to_owner)]
    ppermute x6 -> x3, starting transfers between devices: 8.12 us -> 3.59 us  [ring(): got_ahead = lax.ppermute(acc_ahead, 'y', to_next)]
    ppermute x6 -> x3, waiting for transfers between devices: 22.8 us -> 19.2 us  [ring(): got_ahead = lax.ppermute(acc_ahead, 'y', to_next)]
    add x6 -> x3, other arithmetic: 4.41 us -> 1.51 us  [ring(): acc_back = got_back + next_back(yi + 2 + step)]
    reshape x2, local copies, waits for them, and re-layouts: 2.92 us -> 0.1 us  [slab_group(): early = jnp.concatenate(parts[:2], axis=0).reshape(nz, y_cut, width)]
    add x6 -> x3, other arithmetic: 4.32 us -> 1.53 us  [ring(): acc_ahead = got_ahead + next_ahead(yi + 2 * ny - 2 - step)]
  transfers between devices with their start and end apart: 24 -> 20, of which waited for: 14 -> 12; matrix products, arithmetic and copies ran while one was open for 34% -> 31% of each run, Pallas kernels for 0% -> 0%
where the time goes in v12:
time: 256 us; the launch traced here: 255 us
  waiting for transfers between devices  120 us (47%)
  matrix products  60.9 us (24%)
  starting transfers between devices  32.1 us (13%)
  local copies, waits for them, and re-layouts  18.3 us (7%)
  between operations  13.9 us (5%)
  other arithmetic  10.1 us (4%)
    ppermute x1, waiting for transfers between devices, local(): lax.ppermute(amplitudes, 'xh', SWAP)  53.7 us
    dot_general x8, matrix products, block(): lax.dot_general(lhs[:, low:high], amp, (((2, 3), (0, 1)), ((), ())), pref...  47.7 us
    ppermute x3, waiting for transfers between devices, ring(): got_ahead = lax.ppermute(acc_ahead, 'y', to_next)  19.2 us
    dot_general x2, matrix products, late_block(): lax.dot_general(lhs, amp, (((2, 3), (0, 1)), ((), ())), preferred_element...  13.3 us
    ppermute x3, waiting for transfers between devices, local(): lax.ppermute(pick(late_sum)(yi + hop), 'y', to_owner)  11.1 us
    ppermute x2, waiting for transfers between devices, pair_sum(): return here + lax.ppermute(there, 'xl', SWAP)  10.1 us
    ppermute x1, waiting for transfers between devices, local(): late_sum = late_block(xi) + lax.ppermute(late_there, 'xl', SWAP)  10 us
    ppermute x3, starting transfers between devices, local(): came = [lax.ppermute(piece[:, width:], 'xh', SWAP) for piece in pieces]  9.18 us
  transfers between devices with their start and end apart: 20, of which 12 were waited for; matrix products, arithmetic and copies ran while one was open for 31% of the time, Pallas kernels for 0%

profile of v12, /device:TPU:0, one launch (start us, length us, event | category | flops | bytes accessed | tf_op | source)
XLA Modules:
  0.0 255.2 jit_solution(17095568627446264036)
XLA Ops:
  6.5 0.7 dynamic_slice.63
  7.3 1.2 sort.17
  8.6 0.2 fusion.17
  8.9 2.6 %reshape.35 = bf16[16,50,1200]{2,1,0:T(8,128)(2,1)S(1)} reshape(bf16[800,1200]{1,0:T(8,128)(2,1)} %bitcast.95) | data formatting | bytes 3840000 | tf_op jit(solution)/shard_map/reshape | solution.py:28
  11.4 0.6 gather_fusion.1
  12.1 0.2 broadcast_select_fusion
  12.3 1.1 copy.12
  13.4 0.6 gather_fusion
  14.0 0.2 select_bitcast_fusion
  14.2 2.1 collective-permute-done
  16.3 1.4 copy.35
  17.7 0.1 fusion.4
  17.9 1.6 copy.14
  19.6 3.2 %collective-permute-start.1 = (bf16[1200,1024]{1,0:T(8,128)(2,1)}, bf16[1200,1024]{1,0:T(8,128)(2,1)S(1)}, u32[]{:S(2)}, u32[]{:S(2)}) collective-permute-start(bf16[1200,1024]{1,0:T(8,128)(2,1)} %param.5), channel_id=1, source_target_pairs={{0,64},{64,0},{1,65},{65,1},{2,66},{66,2},{3,67},{67,3},{4,68},{68... | collective-permute-start | bytes 7372808 | tf_op jit(solution)/shard_map/ppermute | solution.py:38
  22.8 0.3 pad_maximum_fusion.1
  23.1 53.7 %collective-permute-done.1 = bf16[1200,1024]{1,0:T(8,128)(2,1)S(1)} collective-permute-done((bf16[1200,1024]{1,0:T(8,128)(2,1)}, bf16[1200,1024]{1,0:T(8,128)(2,1)S(1)}, u32[]{:S(2)}, u32[]{:S(2)}) %collective-permute-start.1) | collective-permute-done | bytes 2457632 | tf_op jit(solution)/shard_map/ppermute | solution.py:38
  76.8 2.7 %pad_maximum_fusion = bf16[1200,2048]{1,0:T(8,128)(2,1)} fusion(bf16[1200,1024]{1,0:T(8,128)(2,1)S(1)} %collective-permute-done.1, bf16[1200,1024]{1,0:T(8,128)(2,1)S(1)} %copy-done), kind=kLoop, calls=%fused_computation.3 | loop fusion | flops 9830400 | bytes 9830400 | tf_op jit(solution)/shard_map/concatenate | solution.py:38
  79.5 1.1 copy.21
  80.7 3.8 %copy.33 = bf16[8,112,2,1200]{3,1,2,0:T(8,128)(2,1)S(1)} copy(bf16[8,112,2,1200]{3,0,2,1:T(8,128)(2,1)} %all-gather.3.cloned.1.call-done) | data formatting | bytes 8601600 | tf_op jit(solution)/shard_map/reshape | solution.py:36
  84.5 0.6 dynamic-slice_bitcast_fusion.3
  85.1 3.0 %collective-permute-done.2 = bf16[1200,2048]{1,0:T(8,128)(2,1)} collective-permute-done((bf16[1200,2048]{1,0:T(8,128)(2,1)}, bf16[1200,2048]{1,0:T(8,128)(2,1)}, u32[]{:S(2)}, u32[]{:S(2)}) %collective-permute-start.2) | collective-permute-done | bytes 4915232 | tf_op jit(solution)/shard_map/ppermute | solution.py:41
  88.0 6.6 %convolution_bitcast_fusion.9 = f32[2,56,2048]{2,1,0:T(8,128)} fusion(bf16[2,112,2,1200]{3,1,2,0:T(8,128)(2,1)S(1)} %get-tuple-element.19, bf16[1,1200,2048]{2,1,0:T(8,128)(2,1)} %bitcast.5, bf16[1,1200,2048]{2,1,0:T(8,128)(2,1)} %bitcast.4), kind=kOutput, calls=%fused_computation.13 | convolution fusion | flops 1105920000 | bytes 11321344 | tf_op jit(solution)/shard_map/dot_general | solution.py:45
  94.6 1.7 collective-permute-start.3
  96.3 6.5 %convolution_bitcast_fusion.5 = f32[2,56,2048]{2,1,0:T(8,128)} fusion(bf16[2,112,2,1200]{3,1,2,0:T(8,128)(2,1)S(1)} %get-tuple-element.16, bf16[1,1200,2048]{2,1,0:T(8,128)(2,1)} %bitcast.5, bf16[1,1200,2048]{2,1,0:T(8,128)(2,1)} %bitcast.4), kind=kOutput, calls=%fused_computation.9 | convolution fusion | flops 1105920000 | bytes 11321344 | tf_op jit(solution)/shard_map/dot_general | solution.py:45
  102.8 1.6 collective-permute-start.7
  104.4 6.6 %convolution_bitcast_fusion.8 = f32[2,56,2048]{2,1,0:T(8,128)} fusion(bf16[2,112,2,1200]{3,1,2,0:T(8,128)(2,1)S(1)} %get-tuple-element.18, bf16[1,1200,2048]{2,1,0:T(8,128)(2,1)} %bitcast.5, bf16[1,1200,2048]{2,1,0:T(8,128)(2,1)} %bitcast.4), kind=kOutput, calls=%fused_computation.12 | convolution fusion | flops 1105920000 | bytes 11321344 | tf_op jit(solution)/shard_map/dot_general | solution.py:45
  111.0 6.6 %convolution_bitcast_fusion.7 = f32[2,56,2048]{2,1,0:T(8,128)} fusion(bf16[2,112,2,1200]{3,1,2,0:T(8,128)(2,1)S(1)} %get-tuple-element.14, bf16[1,1200,2048]{2,1,0:T(8,128)(2,1)} %bitcast.5, bf16[1,1200,2048]{2,1,0:T(8,128)(2,1)} %bitcast.4), kind=kOutput, calls=%fused_computation.11 | convolution fusion | flops 1105920000 | bytes 11321344 | tf_op jit(solution)/shard_map/dot_general | solution.py:45
  117.7 6.6 %convolution_bitcast_fusion.6 = f32[2,56,2048]{2,1,0:T(8,128)} fusion(bf16[2,112,2,1200]{3,1,2,0:T(8,128)(2,1)S(1)} %get-tuple-element.17, bf16[1,1200,2048]{2,1,0:T(8,128)(2,1)} %bitcast.5, bf16[1,1200,2048]{2,1,0:T(8,128)(2,1)} %bitcast.4), kind=kOutput, calls=%fused_computation.10 | convolution fusion | flops 1105920000 | bytes 11321344 | tf_op jit(solution)/shard_map/dot_general | solution.py:45
  124.3 2.7 %all-gather.5.cloned.1.call-done = bf16[8,88,2,1200]{3,0,2,1:T(8,128)(2,1)} async-done(((bf16[8,22,2,1200]{3,0,2,1:T(8,128)(2,1)}), bf16[8,88,2,1200]{3,0,2,1:T(8,128)(2,1)}) %all-gather.5.cloned.1.call-update) | async-done | bytes 3379216 | tf_op jit(solution)/shard_map/all_gather | solution.py:40
  126.9 3.1 %copy.22 = bf16[8,88,2,1200]{3,1,2,0:T(8,128)(2,1)S(1)} copy(bf16[8,88,2,1200]{3,0,2,1:T(8,128)(2,1)} %all-gather.5.cloned.1.call-done) | data formatting | bytes 6758400 | tf_op jit(solution)/shard_map/all_gather | solution.py:40
  130.0 6.7 %convolution_bitcast_fusion = f32[4,88,2048]{2,1,0:T(8,128)S(1)} fusion(bf16[4,2,88,2,1200]{4,2,3,1,0:T(8,128)(2,1)S(1)} %bitcast.93, s32[]{:T(128)S(6)} %select_n.118, bf16[1,1200,2048]{2,1,0:T(8,128)(2,1)} %bitcast.5, bf16[1,1200,2048]{2,1,0:T(8,128)(2,1)} %bitcast.4), kind=kOutput, calls=%fused_computation.4 | convolution fusion | flops 3465216000 | bytes 14516228 | tf_op jit(solution)/shard_map/dot_general | solution.py:74
  136.7 1.5 collective-permute-start.11
  138.3 4.9 %convolution_bitcast_fusion.4 = f32[2,56,2048]{2,1,0:T(8,128)S(1)} fusion(bf16[2,112,2,1200]{3,1,2,0:T(8,128)(2,1)S(1)} %get-tuple-element.15, bf16[1,1200,2048]{2,1,0:T(8,128)(2,1)} %bitcast.5, bf16[1,1200,2048]{2,1,0:T(8,128)(2,1)} %bitcast.4), kind=kOutput, calls=%fused_computation.8 | convolution fusion | flops 1105920000 | bytes 11321344 | tf_op jit(solution)/shard_map/dot_general | solution.py:45
  143.2 1.3 add.161
  144.5 1.6 collective-permute-start.4
  146.1 1.3 add.177
  147.4 1.8 collective-permute-start.8
  149.2 4.9 %convolution_bitcast_fusion.2 = f32[2,56,2048]{2,1,0:T(8,128)S(1)} fusion(bf16[2,112,2,1200]{3,1,2,0:T(8,128)(2,1)S(1)} %get-tuple-element.17, bf16[1,1200,2048]{2,1,0:T(8,128)(2,1)} %bitcast.5, bf16[1,1200,2048]{2,1,0:T(8,128)(2,1)} %bitcast.4), kind=kOutput, calls=%fused_computation.6 | convolution fusion | flops 1105920000 | bytes 11321344 | tf_op jit(solution)/shard_map/dot_general | solution.py:45
  154.1 4.9 %convolution_bitcast_fusion.3 = f32[2,56,2048]{2,1,0:T(8,128)S(1)} fusion(bf16[2,112,2,1200]{3,1,2,0:T(8,128)(2,1)S(1)} %get-tuple-element.19, bf16[1,1200,2048]{2,1,0:T(8,128)(2,1)} %bitcast.5, bf16[1,1200,2048]{2,1,0:T(8,128)(2,1)} %bitcast.4), kind=kOutput, calls=%fused_computation.7 | convolution fusion | flops 1105920000 | bytes 11321344 | tf_op jit(solution)/shard_map/dot_general | solution.py:45
  159.0 8.4 %collective-permute-done.4 = f32[2,56,2048]{2,1,0:T(8,128)S(1)} collective-permute-done((f32[2,56,2048]{2,1,0:T(8,128)S(1)}, f32[2,56,2048]{2,1,0:T(8,128)S(1)}, u32[]{:S(2)}, u32[]{:S(2)}) %collective-permute-start.4) | collective-permute-done | bytes 917536 | tf_op jit(solution)/shard_map/ppermute | solution.py:57
  167.4 0.1 add.164
  167.6 0.3 collective-permute-start.5
  167.9 0.9 collective-permute-done.8
  168.8 0.1 add.178
  168.9 3.3 %collective-permute-start.9 = (f32[2,56,2048]{2,1,0:T(8,128)S(1)}, f32[2,56,2048]{2,1,0:T(8,128)S(1)}, u32[]{:S(2)}, u32[]{:S(2)}) collective-permute-start(f32[2,56,2048]{2,1,0:T(8,128)S(1)} %add.178), channel_id=1, source_target_pairs={{0,12},{4,0},{8,4},{12,8},{1,13},{5,1},{9,5},{13,9},{2,14},{6,2},{... | collective-permute-start | bytes 2752520 | tf_op jit(solution)/shard_map/ppermute | solution.py:58
  172.2 6.6 %convolution_bitcast_fusion.1 = f32[4,88,2048]{2,1,0:T(8,128)S(1)} fusion(bf16[4,2,88,2,1200]{4,2,3,1,0:T(8,128)(2,1)S(1)} %bitcast.94, s32[]{:T(128)S(6)} %select_n.117, bf16[1,1200,2048]{2,1,0:T(8,128)(2,1)} %bitcast.5, bf16[1,1200,2048]{2,1,0:T(8,128)(2,1)} %bitcast.4), kind=kOutput, calls=%fused_computation.5 | convolution fusion | flops 3465216000 | bytes 14516228 | tf_op jit(solution)/shard_map/dot_general | solution.py:74
  178.8 10.8 %collective-permute-done.5 = f32[2,56,2048]{2,1,0:T(8,128)S(1)} collective-permute-done((f32[2,56,2048]{2,1,0:T(8,128)S(1)}, f32[2,56,2048]{2,1,0:T(8,128)S(1)}, u32[]{:S(2)}, u32[]{:S(2)}) %collective-permute-start.5) | collective-permute-done | bytes 917536 | tf_op jit(solution)/shard_map/ppermute | solution.py:57
  189.8 0.6 collective-permute-start.6
  190.6 1.5 collective-permute-start.10
  192.1 10.0 %collective-permute-done.11 = f32[4,88,2048]{2,1,0:T(8,128)S(1)} collective-permute-done((f32[4,88,2048]{2,1,0:T(8,128)S(1)}, f32[4,88,2048]{2,1,0:T(8,128)S(1)}, u32[]{:S(2)}, u32[]{:S(2)}) %collective-permute-start.11) | collective-permute-done | bytes 2883616 | tf_op jit(solution)/shard_map/ppermute | solution.py:80
  202.1 0.4 add.181
  202.6 0.2 dynamic-slice_bitcast_fusion.8
  202.8 1.6 collective-permute-start.12
  204.4 2.7 %collective-permute-start.13 = (f32[88,2048]{1,0:T(8,128)S(1)}, f32[88,2048]{1,0:T(8,128)S(1)}, u32[]{:S(2)}, u32[]{:S(2)}) collective-permute-start(f32[88,2048]{1,0:T(8,128)S(1)} %get-tuple-element.22), channel_id=1, source_target_pairs={{0,8},{4,12},{8,0},{12,4},{1,9},{5,13},{9,1},{13,5},{2,10},{6,14},... | collective-permute-start | bytes 2162696 | tf_op jit(solution)/shard_map/ppermute | solution.py:94
  207.1 1.4 collective-permute-start.14
  208.5 3.4 %collective-permute-done.6 = f32[56,2048]{1,0:T(8,128)S(1)} collective-permute-done((f32[56,2048]{1,0:T(8,128)S(1)}, f32[56,2048]{1,0:T(8,128)S(1)}, u32[]{:S(2)}, u32[]{:S(2)}) %collective-permute-start.6) | collective-permute-done | bytes 458784 | tf_op jit(solution)/shard_map/ppermute | solution.py:66
  212.1 3.1 %collective-permute-start.15 = (f32[56,1024]{1,0:T(8,128)S(1)}, f32[56,1024]{1,0:T(8,128)S(1)}, u32[]{:S(2)}, u32[]{:S(2)}) collective-permute-start(f32[56,1024]{1,0:T(8,128)S(1)} %get-tuple-element.26), channel_id=1, source_target_pairs={{0,64},{64,0},{1,65},{65,1},{2,66},{66,2},{3,67},{67,3},{4,68},{68... | collective-permute-start | bytes 688136 | tf_op jit(solution)/shard_map/ppermute | solution.py:98
  215.1 6.7 %collective-permute-done.10 = f32[56,2048]{1,0:T(8,128)S(1)} collective-permute-done((f32[56,2048]{1,0:T(8,128)S(1)}, f32[56,2048]{1,0:T(8,128)S(1)}, u32[]{:S(2)}, u32[]{:S(2)}) %collective-permute-start.10) | collective-permute-done | bytes 458784 | tf_op jit(solution)/shard_map/ppermute | solution.py:66
  221.9 3.1 %collective-permute-start.16 = (f32[56,1024]{1,0:T(8,128)S(1)}, f32[56,1024]{1,0:T(8,128)S(1)}, u32[]{:S(2)}, u32[]{:S(2)}) collective-permute-start(f32[56,1024]{1,0:T(8,128)S(1)} %get-tuple-element.28), channel_id=1, source_target_pairs={{0,64},{64,0},{1,65},{65,1},{2,66},{66,2},{3,67},{67,3},{4,68},{68... | collective-permute-start | bytes 688136 | tf_op jit(solution)/shard_map/ppermute | solution.py:98
  225.0 11.1 %collective-permute-done.13 = f32[88,2048]{1,0:T(8,128)S(1)} collective-permute-done((f32[88,2048]{1,0:T(8,128)S(1)}, f32[88,2048]{1,0:T(8,128)S(1)}, u32[]{:S(2)}, u32[]{:S(2)}) %collective-permute-start.13) | collective-permute-done | bytes 720928 | tf_op jit(solution)/shard_map/ppermute | solution.py:94
  236.1 0.2 fusion.6
  236.3 3.1 %collective-permute-start.17 = (f32[88,1024]{1,0:T(8,128)S(1)}, f32[88,1024]{1,0:T(8,128)S(1)}, u32[]{:S(2)}, u32[]{:S(2)}) collective-permute-start(f32[88,1024]{1,0:T(8,128)S(1)} %get-tuple-element.24), channel_id=1, source_target_pairs={{0,64},{64,0},{1,65},{65,1},{2,66},{66,2},{3,67},{67,3},{4,68},{68... | collective-permute-start | bytes 1081352 | tf_op jit(solution)/shard_map/ppermute | solution.py:98
  239.8 7.0 %collective-permute-done.17 = f32[88,1024]{1,0:T(8,128)S(1)} collective-permute-done((f32[88,1024]{1,0:T(8,128)S(1)}, f32[88,1024]{1,0:T(8,128)S(1)}, u32[]{:S(2)}, u32[]{:S(2)}) %collective-permute-start.17) | collective-permute-done | bytes 360480 | tf_op jit(solution)/shard_map/ppermute | solution.py:98
  247.1 1.3 maximum_select_fusion
  (48 shorter events, 1.4 us)
Async XLA Ops:
  6.5 74.2 %all-gather.3.cloned.1.call-start = ((), (), s32[]{:S(2)}) async-start(), calls=%async_computation | async-start | bytes 5734400 | tf_op jit(solution)/shard_map/all_gather | solution.py:34
  13.4 3.0 %collective-permute-start = (bf16[8,50,1200]{2,0,1:T(8,128)(2,1)}, bf16[8,50,1200]{2,0,1:T(8,128)(2,1)}, u32[]{:S(2)}, u32[]{:S(2)}) collective-permute-start(bf16[8,50,1200]{2,0,1:T(8,128)(2,1)} %copy.12), channel_id=1, source_target_pairs={{0,1},{1,0},{2,3},{3,2},{4,5},{5,4},{6,7},{7,6},{8,9},{9,8},{10,11... | collective-permute-start | bytes 2880008 | tf_op jit(solution)/shard_map/ppermute | solution.py:31
  19.5 107.4 %all-gather.5.cloned.1.call-start = ((), (), s32[]{:S(2)}) async-start(), calls=%async_computation.1 | async-start | bytes 4505600 | tf_op jit(solution)/shard_map/all_gather | solution.py:40
  19.6 57.2 %copy-start = (bf16[1200,1024]{1,0:T(8,128)(2,1)S(1)}, bf16[1200,1024]{1,0:T(8,128)(2,1)}, u32[]{:S(2)}) copy-start(bf16[1200,1024]{1,0:T(8,128)(2,1)} %param.5) | copy-start | bytes 7372804
  19.6 57.2 %collective-permute-start.1 = (bf16[1200,1024]{1,0:T(8,128)(2,1)}, bf16[1200,1024]{1,0:T(8,128)(2,1)S(1)}, u32[]{:S(2)}, u32[]{:S(2)}) collective-permute-start(bf16[1200,1024]{1,0:T(8,128)(2,1)} %param.5), channel_id=1, source_target_pairs={{0,64},{64,0},{1,65},{65,1},{2,66},{66,2},{3,67},{67,3},{4,68},{68... | collective-permute-start | bytes 7372808 | tf_op jit(solution)/shard_map/ppermute | solution.py:38
  79.5 8.5 %collective-permute-start.2 = (bf16[1200,2048]{1,0:T(8,128)(2,1)}, bf16[1200,2048]{1,0:T(8,128)(2,1)}, u32[]{:S(2)}, u32[]{:S(2)}) collective-permute-start(bf16[1200,2048]{1,0:T(8,128)(2,1)} %pad_maximum_fusion), channel_id=1, source_target_pairs={{0,1},{1,0},{2,3},{3,2},{4,5},{5,4},{6,7},{7,6},{8,9},{9,8},{10,11... | collective-permute-start | bytes 14745608 | tf_op jit(solution)/shard_map/ppermute | solution.py:41
  94.6 48.6 %collective-permute-start.3 = (f32[2,56,2048]{2,1,0:T(8,128)}, f32[2,56,2048]{2,1,0:T(8,128)}, u32[]{:S(2)}, u32[]{:S(2)}) collective-permute-start(f32[2,56,2048]{2,1,0:T(8,128)} %convolution_bitcast_fusion.9), channel_id=1, source_target_pairs={{0,4},{4,8},{8,12},{12,0},{1,5},{5,9},{9,13},{13,1},{2,6},{6,10},{... | collective-permute-start | bytes 2752520 | tf_op jit(solution)/shard_map/ppermute | solution.py:57
  102.8 43.2 %collective-permute-start.7 = (f32[2,56,2048]{2,1,0:T(8,128)}, f32[2,56,2048]{2,1,0:T(8,128)}, u32[]{:S(2)}, u32[]{:S(2)}) collective-permute-start(f32[2,56,2048]{2,1,0:T(8,128)} %convolution_bitcast_fusion.5), channel_id=1, source_target_pairs={{0,12},{4,0},{8,4},{12,8},{1,13},{5,1},{9,5},{13,9},{2,14},{6,2},{... | collective-permute-start | bytes 2752520 | tf_op jit(solution)/shard_map/ppermute | solution.py:58
  136.7 65.4 %collective-permute-start.11 = (f32[4,88,2048]{2,1,0:T(8,128)S(1)}, f32[4,88,2048]{2,1,0:T(8,128)S(1)}, u32[]{:S(2)}, u32[]{:S(2)}) collective-permute-start(f32[4,88,2048]{2,1,0:T(8,128)S(1)} %convolution_bitcast_fusion), channel_id=1, source_target_pairs={{0,2},{2,0},{1,3},{3,1},{4,6},{6,4},{5,7},{7,5},{8,10},{10,8},{9,1... | collective-permute-start | bytes 8650760 | tf_op jit(solution)/shard_map/ppermute | solution.py:80
  138.2 5.0 %copy-start.3 = (f32[2,56,2048]{2,1,0:T(8,128)S(1)}, f32[2,56,2048]{2,1,0:T(8,128)}, u32[]{:S(2)}) copy-start(f32[2,56,2048]{2,1,0:T(8,128)} %convolution_bitcast_fusion.8) | copy-start | bytes 2752516
  144.5 22.9 %collective-permute-start.4 = (f32[2,56,2048]{2,1,0:T(8,128)S(1)}, f32[2,56,2048]{2,1,0:T(8,128)S(1)}, u32[]{:S(2)}, u32[]{:S(2)}) collective-permute-start(f32[2,56,2048]{2,1,0:T(8,128)S(1)} %add.161), channel_id=1, source_target_pairs={{0,4},{4,8},{8,12},{12,0},{1,5},{5,9},{9,13},{13,1},{2,6},{6,10},{... | collective-permute-start | bytes 2752520 | tf_op jit(solution)/shard_map/ppermute | solution.py:57
  147.4 21.4 %collective-permute-start.8 = (f32[2,56,2048]{2,1,0:T(8,128)S(1)}, f32[2,56,2048]{2,1,0:T(8,128)S(1)}, u32[]{:S(2)}, u32[]{:S(2)}) collective-permute-start(f32[2,56,2048]{2,1,0:T(8,128)S(1)} %add.177), channel_id=1, source_target_pairs={{0,12},{4,0},{8,4},{12,8},{1,13},{5,1},{9,5},{13,9},{2,14},{6,2},{... | collective-permute-start | bytes 2752520 | tf_op jit(solution)/shard_map/ppermute | solution.py:58
  154.1 13.4 %copy-start.2 = (f32[2,56,2048]{2,1,0:T(8,128)S(1)}, f32[2,56,2048]{2,1,0:T(8,128)}, u32[]{:S(2)}) copy-start(f32[2,56,2048]{2,1,0:T(8,128)} %convolution_bitcast_fusion.7) | copy-start | bytes 2752516
  167.6 22.1 %collective-permute-start.5 = (f32[2,56,2048]{2,1,0:T(8,128)S(1)}, f32[2,56,2048]{2,1,0:T(8,128)S(1)}, u32[]{:S(2)}, u32[]{:S(2)}) collective-permute-start(f32[2,56,2048]{2,1,0:T(8,128)S(1)} %add.164), channel_id=1, source_target_pairs={{0,4},{4,8},{8,12},{12,0},{1,5},{5,9},{9,13},{13,1},{2,6},{6,10},{... | collective-permute-start | bytes 2752520 | tf_op jit(solution)/shard_map/ppermute | solution.py:57
  168.9 20.7 %copy-start.1 = (f32[2,56,2048]{2,1,0:T(8,128)S(1)}, f32[2,56,2048]{2,1,0:T(8,128)}, u32[]{:S(2)}) copy-start(f32[2,56,2048]{2,1,0:T(8,128)} %convolution_bitcast_fusion.6) | copy-start | bytes 2752516
  168.9 21.5 %collective-permute-start.9 = (f32[2,56,2048]{2,1,0:T(8,128)S(1)}, f32[2,56,2048]{2,1,0:T(8,128)S(1)}, u32[]{:S(2)}, u32[]{:S(2)}) collective-permute-start(f32[2,56,2048]{2,1,0:T(8,128)S(1)} %add.178), channel_id=1, source_target_pairs={{0,12},{4,0},{8,4},{12,8},{1,13},{5,1},{9,5},{13,9},{2,14},{6,2},{... | collective-permute-start | bytes 2752520 | tf_op jit(solution)/shard_map/ppermute | solution.py:58
  189.8 22.2 %collective-permute-start.6 = (f32[56,2048]{1,0:T(8,128)S(1)}, f32[56,2048]{1,0:T(8,128)S(1)}, u32[]{:S(2)}, u32[]{:S(2)}) collective-permute-start(f32[56,2048]{1,0:T(8,128)S(1)} %dynamic-slice_bitcast_fusion.10), channel_id=1, source_target_pairs={{0,2},{2,0},{1,3},{3,1},{4,6},{6,4},{5,7},{7,5},{8,10},{10,8},{9,1... | collective-permute-start | bytes 1376264 | tf_op jit(solution)/shard_map/ppermute | solution.py:66
  190.6 31.2 %collective-permute-start.10 = (f32[56,2048]{1,0:T(8,128)S(1)}, f32[56,2048]{1,0:T(8,128)S(1)}, u32[]{:S(2)}, u32[]{:S(2)}) collective-permute-start(f32[56,2048]{1,0:T(8,128)S(1)} %dynamic-slice_bitcast_fusion.9), channel_id=1, source_target_pairs={{0,2},{2,0},{1,3},{3,1},{4,6},{6,4},{5,7},{7,5},{8,10},{10,8},{9,1... | collective-permute-start | bytes 1376264 | tf_op jit(solution)/shard_map/ppermute | solution.py:66
  202.8 22.2 %collective-permute-start.12 = (f32[88,2048]{1,0:T(8,128)S(1)}, f32[88,2048]{1,0:T(8,128)S(1)}, u32[]{:S(2)}, u32[]{:S(2)}) collective-permute-start(f32[88,2048]{1,0:T(8,128)S(1)} %get-tuple-element.20), channel_id=1, source_target_pairs={{0,4},{4,8},{8,12},{12,0},{1,5},{5,9},{9,13},{13,1},{2,6},{6,10},{... | collective-permute-start | bytes 2162696 | tf_op jit(solution)/shard_map/ppermute | solution.py:94
  204.4 31.7 %collective-permute-start.13 = (f32[88,2048]{1,0:T(8,128)S(1)}, f32[88,2048]{1,0:T(8,128)S(1)}, u32[]{:S(2)}, u32[]{:S(2)}) collective-permute-start(f32[88,2048]{1,0:T(8,128)S(1)} %get-tuple-element.22), channel_id=1, source_target_pairs={{0,8},{4,12},{8,0},{12,4},{1,9},{5,13},{9,1},{13,5},{2,10},{6,14},... | collective-permute-start | bytes 2162696 | tf_op jit(solution)/shard_map/ppermute | solution.py:94
  207.1 29.0 %collective-permute-start.14 = (f32[88,2048]{1,0:T(8,128)S(1)}, f32[88,2048]{1,0:T(8,128)S(1)}, u32[]{:S(2)}, u32[]{:S(2)}) collective-permute-start(f32[88,2048]{1,0:T(8,128)S(1)} %get-tuple-element.21), channel_id=1, source_target_pairs={{0,12},{4,0},{8,4},{12,8},{1,13},{5,1},{9,5},{13,9},{2,14},{6,2},{... | collective-permute-start | bytes 2162696 | tf_op jit(solution)/shard_map/ppermute | solution.py:94
  212.1 27.4 %collective-permute-start.15 = (f32[56,1024]{1,0:T(8,128)S(1)}, f32[56,1024]{1,0:T(8,128)S(1)}, u32[]{:S(2)}, u32[]{:S(2)}) collective-permute-start(f32[56,1024]{1,0:T(8,128)S(1)} %get-tuple-element.26), channel_id=1, source_target_pairs={{0,64},{64,0},{1,65},{65,1},{2,66},{66,2},{3,67},{67,3},{4,68},{68... | collective-permute-start | bytes 688136 | tf_op jit(solution)/shard_map/ppermute | solution.py:98
  221.9 17.6 %collective-permute-start.16 = (f32[56,1024]{1,0:T(8,128)S(1)}, f32[56,1024]{1,0:T(8,128)S(1)}, u32[]{:S(2)}, u32[]{:S(2)}) collective-permute-start(f32[56,1024]{1,0:T(8,128)S(1)} %get-tuple-element.28), channel_id=1, source_target_pairs={{0,64},{64,0},{1,65},{65,1},{2,66},{66,2},{3,67},{67,3},{4,68},{68... | collective-permute-start | bytes 688136 | tf_op jit(solution)/shard_map/ppermute | solution.py:98
  236.3 10.5 %collective-permute-start.17 = (f32[88,1024]{1,0:T(8,128)S(1)}, f32[88,1024]{1,0:T(8,128)S(1)}, u32[]{:S(2)}, u32[]{:S(2)}) collective-permute-start(f32[88,1024]{1,0:T(8,128)S(1)} %get-tuple-element.24), channel_id=1, source_target_pairs={{0,64},{64,0},{1,65},{65,1},{2,66},{66,2},{3,67},{67,3},{4,68},{68... | collective-permute-start | bytes 1081352 | tf_op jit(solution)/shard_map/ppermute | solution.py:98
Sparse Core Ops, SparseCore 0:
  19.7 54.1 all-gather.2
  80.7 46.1 all-gather.4

commit v13 on v12

--- a/solution.py
+++ b/solution.py
@@ -82,24 +82,22 @@
     def pick(parts):
         return lambda y_owner: lax.dynamic_index_in_dim(parts, y_owner % ny, 0, keepdims=False)
 
-    early = ring(
-        block(yi + ny - 1, 0, y_half),
-        block(yi + 1, y_half, y_rows),
-        lambda y_owner: block(y_owner, 0, y_half),
-        lambda y_owner: block(y_owner, y_half, y_rows),
-    )
+    early = block(yi, 0, y_rows)
+    for hop in range(1, ny):
+        to_owner = [(i, (i + hop) % ny) for i in range(ny)]
+        early = early + lax.ppermute(block(yi + hop, 0, y_rows), "y", to_owner)
     late_done = pick(late_sum)(yi)
     for hop in range(1, ny):
         to_owner = [(i, (i + hop) % ny) for i in range(ny)]
         late_done = late_done + lax.ppermute(pick(late_sum)(yi + hop), "y", to_owner)
-    pieces = [pair_sum(early[0]), pair_sum(early[1]), late_done]
+    pieces = [pair_sum(early), late_done]
 
     kept = [piece[:, :width] for piece in pieces]
     came = [lax.ppermute(piece[:, width:], "xh", SWAP) for piece in pieces]
 
     def slab_group(parts):
-        early = jnp.concatenate(parts[:2], axis=0).reshape(nz, y_cut, width)
-        late_rows = jnp.concatenate(parts[2:], axis=0).reshape(nz, TB - y_cut, width)
+        early = parts[0].reshape(nz, y_cut, width)
+        late_rows = parts[1].reshape(nz, TB - y_cut, width)
         return jnp.concatenate([early, late_rows], axis=1).reshape(nz * TB, width)
 
     kept, came = slab_group(kept), slab_group(came)

time: 256 us -> 262 us (1.023)
  waiting for transfers between devices: 120 us -> 153 us
  matrix products: 60.9 us -> 46.3 us
  starting transfers between devices: 32.1 us -> 21.6 us
    ppermute x6 -> x3, waiting for transfers between devices: 20.1 us -> 42 us  [local(): early = early + lax.ppermute(block(yi + hop, 0, y_rows), 'y', to_owner)]
    dot_general x8 -> x4, matrix products: 47.7 us -> 29 us  [block(): lax.dot_general(lhs[:, low:high], amp, (((2, 3), (0, 1)), ((), ())), pref...]
    all_gather x1, waiting for transfers between devices: 2.67 us -> 10.8 us  [local(): gathered_late = lax.all_gather(late_rows, 'z', axis=1, tiled=True)]
    ppermute x6 -> x3, starting transfers between devices: 10.3 us -> 4.68 us  [local(): early = early + lax.ppermute(block(yi + hop, 0, y_rows), 'y', to_owner)]
    ppermute x1, waiting for transfers between devices: 10 us -> 4.92 us  [local(): late_sum = late_block(xi) + lax.ppermute(late_there, 'xl', SWAP)]
    dot_general x2, matrix products: 13.3 us -> 17.3 us  [late_block(): lax.dot_general(lhs, amp, (((2, 3), (0, 1)), ((), ())), preferred_element...]
    ppermute x2 -> x1, waiting for transfers between devices: 10.1 us -> 13.2 us  [pair_sum(): return here + lax.ppermute(there, 'xl', SWAP)]
    ppermute x3 -> x2, starting transfers between devices: 9.18 us -> 6.12 us  [local(): came = [lax.ppermute(piece[:, width:], 'xh', SWAP) for piece in pieces]]
  transfers between devices with their start and end apart: 20 -> 15, of which waited for: 12 -> 11; matrix products, arithmetic and copies ran while one was open for 31% -> 24% of each run, Pallas kernels for 0% -> 0%
where the time goes in v13:
time: 262 us
  waiting for transfers between devices  153 us (58%)
  matrix products  46.3 us (18%)
  starting transfers between devices  21.6 us (8%)
  local copies, waits for them, and re-layouts  17.1 us (7%)
  between operations  13.7 us (5%)
  other arithmetic  10.2 us (4%)
    ppermute x1, waiting for transfers between devices, local(): lax.ppermute(amplitudes, 'xh', SWAP)  53.7 us
    ppermute x3, waiting for transfers between devices, local(): early = early + lax.ppermute(block(yi + hop, 0, y_rows), 'y', to_owner)  42 us
    dot_general x4, matrix products, block(): lax.dot_general(lhs[:, low:high], amp, (((2, 3), (0, 1)), ((), ())), pref...  29 us
    dot_general x2, matrix products, late_block(): lax.dot_general(lhs, amp, (((2, 3), (0, 1)), ((), ())), preferred_element...  17.3 us
    ppermute x3, waiting for transfers between devices, local(): lax.ppermute(pick(late_sum)(yi + hop), 'y', to_owner)  14.1 us
    ppermute x1, waiting for transfers between devices, pair_sum(): return here + lax.ppermute(there, 'xl', SWAP)  13.2 us
    all_gather x1, waiting for transfers between devices, local(): gathered_late = lax.all_gather(late_rows, 'z', axis=1, tiled=True)  10.8 us
    ppermute x2, waiting for transfers between devices, local(): came = [lax.ppermute(piece[:, width:], 'xh', SWAP) for piece in pieces]  8.48 us
  transfers between devices with their start and end apart: 15, of which 11 were waited for; matrix products, arithmetic and copies ran while one was open for 24% of the time, Pallas kernels for 0%

profile of v13, /device:TPU:0, one launch (start us, length us, event | category | flops | bytes accessed | tf_op | source)
XLA Modules:
  0.0 261.9 jit_solution(12696542883005820044)
XLA Ops:
  6.5 2.6 reshape.35
  9.2 0.1 dynamic_slice.49
  9.2 1.2 sort.17
  10.5 0.1 reshape.36
  10.6 0.2 dynamic-slice_reduce_fusion.1
  10.8 0.6 gather_fusion.1
  11.4 0.2 broadcast_select_fusion
  11.6 1.1 copy.10
  12.8 0.6 gather_fusion
  13.4 0.2 select_bitcast_fusion
  13.6 2.1 collective-permute-done
  15.7 1.4 copy.27
  17.1 0.1 fusion.4
  17.3 1.6 copy.12
  18.9 0.0 all-gather.3.cloned.1.call-update
  18.9 0.0 all-gather.5.cloned.1.call-start
  19.0 0.0 copy-start.3
  19.0 3.2 %collective-permute-start.1 = (bf16[1200,1024]{1,0:T(8,128)(2,1)}, bf16[1200,1024]{1,0:T(8,128)(2,1)S(1)}, u32[]{:S(2)}, u32[]{:S(2)}) collective-permute-start(bf16[1200,1024]{1,0:T(8,128)(2,1)} %param.5), channel_id=1, source_target_pairs={{0,64},{64,0},{1,65},{65,1},{2,66},{66,2},{3,67},{67,3},{4,68},{68... | collective-permute-start | bytes 7372808 | tf_op jit(solution)/shard_map/ppermute | solution.py:38
  22.2 0.3 pad_maximum_fusion.1
  22.5 53.7 %collective-permute-done.1 = bf16[1200,1024]{1,0:T(8,128)(2,1)S(1)} collective-permute-done((bf16[1200,1024]{1,0:T(8,128)(2,1)}, bf16[1200,1024]{1,0:T(8,128)(2,1)S(1)}, u32[]{:S(2)}, u32[]{:S(2)}) %collective-permute-start.1) | collective-permute-done | bytes 2457632 | tf_op jit(solution)/shard_map/ppermute | solution.py:38
  76.2 2.7 %pad_maximum_fusion = bf16[1200,2048]{1,0:T(8,128)(2,1)} fusion(bf16[1200,1024]{1,0:T(8,128)(2,1)S(1)} %collective-permute-done.1, bf16[1200,1024]{1,0:T(8,128)(2,1)S(1)} %copy-done.3), kind=kLoop, calls=%fused_computation.3 | loop fusion | flops 9830400 | bytes 9830400 | tf_op jit(solution)/shard_map/concatenate | solution.py:38
  78.9 0.0 collective-permute-start.2
  78.9 1.1 copy.17
  79.9 0.0 all-gather.5.cloned.1.call-update
  80.0 0.0 all-gather.3.cloned.1.call-done
  80.0 3.8 %copy.25 = bf16[8,112,2,1200]{3,1,2,0:T(8,128)(2,1)S(1)} copy(bf16[8,112,2,1200]{3,0,2,1:T(8,128)(2,1)} %all-gather.3.cloned.1.call-done) | data formatting | bytes 8601600 | tf_op jit(solution)/shard_map/reshape | solution.py:36
  83.8 3.6 %collective-permute-done.2 = bf16[1200,2048]{1,0:T(8,128)(2,1)} collective-permute-done((bf16[1200,2048]{1,0:T(8,128)(2,1)}, bf16[1200,2048]{1,0:T(8,128)(2,1)}, u32[]{:S(2)}, u32[]{:S(2)}) %collective-permute-start.2) | collective-permute-done | bytes 4915232 | tf_op jit(solution)/shard_map/ppermute | solution.py:41
  87.4 7.8 %convolution_bitcast_fusion.2 = f32[2,112,2048]{2,1,0:T(8,128)} fusion(bf16[4,2,112,2,1200]{4,2,3,1,0:T(8,128)(2,1)S(1)} %bitcast.72, s32[]{:T(128)S(6)} %select_n.90, bf16[1,1200,2048]{2,1,0:T(8,128)(2,1)} %bitcast.5, bf16[1,1200,2048]{2,1,0:T(8,128)(2,1)} %bitcast.4), kind=kOutput, calls=%fused_computation.6 | convolution fusion | flops 2206924800 | bytes 12812292 | tf_op jit(solution)/shard_map/dot_general | solution.py:45
  95.2 3.2 %collective-permute-start.5 = (f32[2,112,2048]{2,1,0:T(8,128)}, f32[2,112,2048]{2,1,0:T(8,128)}, u32[]{:S(2)}, u32[]{:S(2)}) collective-permute-start(f32[2,112,2048]{2,1,0:T(8,128)} %convolution_bitcast_fusion.2), channel_id=1, source_target_pairs={{0,12},{4,0},{8,4},{12,8},{1,13},{5,1},{9,5},{13,9},{2,14},{6,2},{... | collective-permute-start | bytes 5505032 | tf_op jit(solution)/shard_map/ppermute | solution.py:88
  98.4 7.9 %convolution_bitcast_fusion.3 = f32[2,112,2048]{2,1,0:T(8,128)} fusion(bf16[4,2,112,2,1200]{4,2,3,1,0:T(8,128)(2,1)S(1)} %bitcast.73, s32[]{:T(128)S(6)} %select_n.88, bf16[1,1200,2048]{2,1,0:T(8,128)(2,1)} %bitcast.5, bf16[1,1200,2048]{2,1,0:T(8,128)(2,1)} %bitcast.4), kind=kOutput, calls=%fused_computation.7 | convolution fusion | flops 2206924800 | bytes 12812292 | tf_op jit(solution)/shard_map/dot_general | solution.py:45
  106.3 0.5 collective-permute-start.4
  106.8 7.8 %convolution_bitcast_fusion.4 = f32[2,112,2048]{2,1,0:T(8,128)} fusion(bf16[4,2,112,2,1200]{4,2,3,1,0:T(8,128)(2,1)S(1)} %bitcast.74, s32[]{:T(128)S(6)} %select_n.86, bf16[1,1200,2048]{2,1,0:T(8,128)(2,1)} %bitcast.5, bf16[1,1200,2048]{2,1,0:T(8,128)(2,1)} %bitcast.4), kind=kOutput, calls=%fused_computation.8 | convolution fusion | flops 2206924800 | bytes 12812292 | tf_op jit(solution)/shard_map/dot_general | solution.py:45
  114.5 1.0 collective-permute-start.3
  115.5 10.8 %all-gather.5.cloned.1.call-done = bf16[8,88,2,1200]{3,0,2,1:T(8,128)(2,1)} async-done(((bf16[8,22,2,1200]{3,0,2,1:T(8,128)(2,1)}), bf16[8,88,2,1200]{3,0,2,1:T(8,128)(2,1)}) %all-gather.5.cloned.1.call-update) | async-done | bytes 3379216 | tf_op jit(solution)/shard_map/all_gather | solution.py:40
  126.3 3.1 %copy.18 = bf16[8,88,2,1200]{3,1,2,0:T(8,128)(2,1)S(1)} copy(bf16[8,88,2,1200]{3,0,2,1:T(8,128)(2,1)} %all-gather.5.cloned.1.call-done) | data formatting | bytes 6758400 | tf_op jit(solution)/shard_map/all_gather | solution.py:40
  129.4 10.7 %convolution_bitcast_fusion = f32[4,88,2048]{2,1,0:T(8,128)} fusion(bf16[4,2,88,2,1200]{4,2,3,1,0:T(8,128)(2,1)S(1)} %bitcast.76, s32[]{:T(128)S(6)} %select_n.92, bf16[1,1200,2048]{2,1,0:T(8,128)(2,1)} %bitcast.5, bf16[1,1200,2048]{2,1,0:T(8,128)(2,1)} %bitcast.4), kind=kOutput, calls=%fused_computation.4 | convolution fusion | flops 3465216000 | bytes 14516228 | tf_op jit(solution)/shard_map/dot_general | solution.py:74
  140.1 1.5 collective-permute-start.7
  141.6 5.6 %convolution_bitcast_fusion.5 = f32[2,112,2048]{2,1,0:T(8,128)S(1)} fusion(bf16[4,2,112,2,1200]{4,2,3,1,0:T(8,128)(2,1)} %bitcast.75, s32[]{:T(128)S(6)} %select_n.84, bf16[1,1200,2048]{2,1,0:T(8,128)(2,1)} %bitcast.5, bf16[1,1200,2048]{2,1,0:T(8,128)(2,1)} %bitcast.4), kind=kOutput, calls=%fused_computation.9 | convolution fusion | flops 2206924800 | bytes 12812292 | tf_op jit(solution)/shard_map/dot_general | solution.py:45
  147.2 30.4 %collective-permute-done.5 = f32[2,112,2048]{2,1,0:T(8,128)} collective-permute-done((f32[2,112,2048]{2,1,0:T(8,128)}, f32[2,112,2048]{2,1,0:T(8,128)}, u32[]{:S(2)}, u32[]{:S(2)}) %collective-permute-start.5) | collective-permute-done | bytes 1835040 | tf_op jit(solution)/shard_map/ppermute | solution.py:88
  177.6 11.6 %collective-permute-done.3 = f32[2,112,2048]{2,1,0:T(8,128)} collective-permute-done((f32[2,112,2048]{2,1,0:T(8,128)}, f32[2,112,2048]{2,1,0:T(8,128)}, u32[]{:S(2)}, u32[]{:S(2)}) %collective-permute-start.3) | collective-permute-done | bytes 1835040 | tf_op jit(solution)/shard_map/ppermute | solution.py:88
  189.2 3.3 %add_add_fusion = f32[2,112,2048]{2,1,0:T(8,128)S(1)} fusion(f32[2,112,2048]{2,1,0:T(8,128)} %collective-permute-done.5, f32[2,112,2048]{2,1,0:T(8,128)} %collective-permute-done.4, f32[2,112,2048]{2,1,0:T(8,128)S(1)} %convolution_bitcast_fusion.5, f32[2,112,2048]{2,1,0:T(8,128)} %collective-permute-done.3), kind=kLoop, calls=%fused_computation.12 | loop fusion | flops 1376256 | bytes 9175040 | tf_op jit(solution)/shard_map/add | solution.py:88
  192.4 0.1 dynamic-slice_bitcast_fusion
  192.5 1.6 collective-permute-start.6
  194.1 6.6 %convolution_bitcast_fusion.1 = f32[4,88,2048]{2,1,0:T(8,128)S(1)} fusion(bf16[4,2,88,2,1200]{4,2,3,1,0:T(8,128)(2,1)S(1)} %bitcast.77, s32[]{:T(128)S(6)} %select_n.91, bf16[1,1200,2048]{2,1,0:T(8,128)(2,1)} %bitcast.5, bf16[1,1200,2048]{2,1,0:T(8,128)(2,1)} %bitcast.4), kind=kOutput, calls=%fused_computation.5 | convolution fusion | flops 3465216000 | bytes 14516228 | tf_op jit(solution)/shard_map/dot_general | solution.py:74
  200.7 4.9 %collective-permute-done.7 = f32[4,88,2048]{2,1,0:T(8,128)S(1)} collective-permute-done((f32[4,88,2048]{2,1,0:T(8,128)}, f32[4,88,2048]{2,1,0:T(8,128)S(1)}, u32[]{:S(2)}, u32[]{:S(2)}) %collective-permute-start.7) | collective-permute-done | bytes 2883616 | tf_op jit(solution)/shard_map/ppermute | solution.py:80
  205.7 0.4 add.119
  206.1 0.2 dynamic-slice_bitcast_fusion.3
  206.3 2.8 %collective-permute-start.10 = (f32[88,2048]{1,0:T(8,128)S(1)}, f32[88,2048]{1,0:T(8,128)S(1)}, u32[]{:S(2)}, u32[]{:S(2)}) collective-permute-start(f32[88,2048]{1,0:T(8,128)S(1)} %get-tuple-element.15), channel_id=1, source_target_pairs={{0,12},{4,0},{8,4},{12,8},{1,13},{5,1},{9,5},{13,9},{2,14},{6,2},{... | collective-permute-start | bytes 2162696 | tf_op jit(solution)/shard_map/ppermute | solution.py:92
  209.1 0.8 collective-permute-start.9
  210.0 0.9 collective-permute-start.8
  210.8 13.2 %collective-permute-done.6 = f32[112,2048]{1,0:T(8,128)S(1)} collective-permute-done((f32[112,2048]{1,0:T(8,128)S(1)}, f32[112,2048]{1,0:T(8,128)S(1)}, u32[]{:S(2)}, u32[]{:S(2)}) %collective-permute-start.6) | collective-permute-done | bytes 917536 | tf_op jit(solution)/shard_map/ppermute | solution.py:66
  224.0 0.1 bitcast_add_fusion
  224.1 0.1 fusion.21
  224.2 3.1 %collective-permute-start.11 = (f32[112,1024]{1,0:T(8,128)S(1)}, f32[112,1024]{1,0:T(8,128)S(1)}, u32[]{:S(2)}, u32[]{:S(2)}) collective-permute-start(f32[112,1024]{1,0:T(8,128)S(1)} %get-tuple-element.18), channel_id=1, source_target_pairs={{0,64},{64,0},{1,65},{65,1},{2,66},{66,2},{3,67},{67,3},{4,68},{68... | collective-permute-start | bytes 1376264 | tf_op jit(solution)/shard_map/ppermute | solution.py:96
  227.3 10.4 %collective-permute-done.10 = f32[88,2048]{1,0:T(8,128)S(1)} collective-permute-done((f32[88,2048]{1,0:T(8,128)S(1)}, f32[88,2048]{1,0:T(8,128)S(1)}, u32[]{:S(2)}, u32[]{:S(2)}) %collective-permute-start.10) | collective-permute-done | bytes 720928 | tf_op jit(solution)/shard_map/ppermute | solution.py:92
  237.7 3.7 %collective-permute-done.8 = f32[88,2048]{1,0:T(8,128)S(1)} collective-permute-done((f32[88,2048]{1,0:T(8,128)S(1)}, f32[88,2048]{1,0:T(8,128)S(1)}, u32[]{:S(2)}, u32[]{:S(2)}) %collective-permute-start.8) | collective-permute-done | bytes 720928 | tf_op jit(solution)/shard_map/ppermute | solution.py:92
  241.4 0.1 fusion.14
  241.6 3.1 %collective-permute-start.12 = (f32[88,1024]{1,0:T(8,128)S(1)}, f32[88,1024]{1,0:T(8,128)S(1)}, u32[]{:S(2)}, u32[]{:S(2)}) collective-permute-start(f32[88,1024]{1,0:T(8,128)S(1)} %get-tuple-element.20), channel_id=1, source_target_pairs={{0,64},{64,0},{1,65},{65,1},{2,66},{66,2},{3,67},{67,3},{4,68},{68... | collective-permute-start | bytes 1081352 | tf_op jit(solution)/shard_map/ppermute | solution.py:96
  244.8 0.1 pad_maximum_fusion.2
  244.9 0.1 reshape.41
  245.0 8.5 %collective-permute-done.12 = f32[88,1024]{1,0:T(8,128)S(1)} collective-permute-done((f32[88,1024]{1,0:T(8,128)S(1)}, f32[88,1024]{1,0:T(8,128)S(1)}, u32[]{:S(2)}, u32[]{:S(2)}) %collective-permute-start.12) | collective-permute-done | bytes 360480 | tf_op jit(solution)/shard_map/ppermute | solution.py:96
  253.6 0.1 pad_maximum_fusion.3
  253.7 0.1 reshape.44
  253.8 1.3 maximum_select_fusion
  (25 shorter events, 0.3 us)
Async XLA Ops:
  6.5 2.6 copy-start.4
  6.5 73.5 %all-gather.3.cloned.1.call-start = ((), (), s32[]{:S(2)}) async-start(), calls=%async_computation | async-start | bytes 5734400 | tf_op jit(solution)/shard_map/all_gather | solution.py:34
  12.8 3.0 %collective-permute-start = (bf16[8,50,1200]{2,0,1:T(8,128)(2,1)}, bf16[8,50,1200]{2,0,1:T(8,128)(2,1)}, u32[]{:S(2)}, u32[]{:S(2)}) collective-permute-start(bf16[8,50,1200]{2,0,1:T(8,128)(2,1)} %copy.10), channel_id=1, source_target_pairs={{0,1},{1,0},{2,3},{3,2},{4,5},{5,4},{6,7},{7,6},{8,9},{9,8},{10,11... | collective-permute-start | bytes 2880008 | tf_op jit(solution)/shard_map/ppermute | solution.py:31
  18.9 107.4 %all-gather.5.cloned.1.call-start = ((), (), s32[]{:S(2)}) async-start(), calls=%async_computation.1 | async-start | bytes 4505600 | tf_op jit(solution)/shard_map/all_gather | solution.py:40
  19.0 57.2 %copy-start.3 = (bf16[1200,1024]{1,0:T(8,128)(2,1)S(1)}, bf16[1200,1024]{1,0:T(8,128)(2,1)}, u32[]{:S(2)}) copy-start(bf16[1200,1024]{1,0:T(8,128)(2,1)} %param.5) | copy-start | bytes 7372804
  19.0 57.2 %collective-permute-start.1 = (bf16[1200,1024]{1,0:T(8,128)(2,1)}, bf16[1200,1024]{1,0:T(8,128)(2,1)S(1)}, u32[]{:S(2)}, u32[]{:S(2)}) collective-permute-start(bf16[1200,1024]{1,0:T(8,128)(2,1)} %param.5), channel_id=1, source_target_pairs={{0,64},{64,0},{1,65},{65,1},{2,66},{66,2},{3,67},{67,3},{4,68},{68... | collective-permute-start | bytes 7372808 | tf_op jit(solution)/shard_map/ppermute | solution.py:38
  78.9 8.5 %collective-permute-start.2 = (bf16[1200,2048]{1,0:T(8,128)(2,1)}, bf16[1200,2048]{1,0:T(8,128)(2,1)}, u32[]{:S(2)}, u32[]{:S(2)}) collective-permute-start(bf16[1200,2048]{1,0:T(8,128)(2,1)} %pad_maximum_fusion), channel_id=1, source_target_pairs={{0,1},{1,0},{2,3},{3,2},{4,5},{5,4},{6,7},{7,6},{8,9},{9,8},{10,11... | collective-permute-start | bytes 14745608 | tf_op jit(solution)/shard_map/ppermute | solution.py:41
  83.8 23.0 %copy-start = (bf16[8,112,2,1200]{3,1,2,0:T(8,128)(2,1)}, bf16[8,112,2,1200]{3,1,2,0:T(8,128)(2,1)S(1)}, u32[]{:S(2)}) copy-start(bf16[8,112,2,1200]{3,1,2,0:T(8,128)(2,1)S(1)} %copy.25) | copy-start | bytes 12902404
  95.2 82.4 %collective-permute-start.5 = (f32[2,112,2048]{2,1,0:T(8,128)}, f32[2,112,2048]{2,1,0:T(8,128)}, u32[]{:S(2)}, u32[]{:S(2)}) collective-permute-start(f32[2,112,2048]{2,1,0:T(8,128)} %convolution_bitcast_fusion.2), channel_id=1, source_target_pairs={{0,12},{4,0},{8,4},{12,8},{1,13},{5,1},{9,5},{13,9},{2,14},{6,2},{... | collective-permute-start | bytes 5505032 | tf_op jit(solution)/shard_map/ppermute | solution.py:88
  106.3 71.3 %collective-permute-start.4 = (f32[2,112,2048]{2,1,0:T(8,128)}, f32[2,112,2048]{2,1,0:T(8,128)}, u32[]{:S(2)}, u32[]{:S(2)}) collective-permute-start(f32[2,112,2048]{2,1,0:T(8,128)} %convolution_bitcast_fusion.3), channel_id=1, source_target_pairs={{0,8},{4,12},{8,0},{12,4},{1,9},{5,13},{9,1},{13,5},{2,10},{6,14},... | collective-permute-start | bytes 5505032 | tf_op jit(solution)/shard_map/ppermute | solution.py:88
  114.5 74.6 %collective-permute-start.3 = (f32[2,112,2048]{2,1,0:T(8,128)}, f32[2,112,2048]{2,1,0:T(8,128)}, u32[]{:S(2)}, u32[]{:S(2)}) collective-permute-start(f32[2,112,2048]{2,1,0:T(8,128)} %convolution_bitcast_fusion.4), channel_id=1, source_target_pairs={{0,4},{4,8},{8,12},{12,0},{1,5},{5,9},{9,13},{13,1},{2,6},{6,10},{... | collective-permute-start | bytes 5505032 | tf_op jit(solution)/shard_map/ppermute | solution.py:88
  129.4 10.7 %copy-start.1 = (bf16[8,88,2,1200]{3,1,2,0:T(8,128)(2,1)}, bf16[8,88,2,1200]{3,1,2,0:T(8,128)(2,1)S(1)}, u32[]{:S(2)}) copy-start(bf16[8,88,2,1200]{3,1,2,0:T(8,128)(2,1)S(1)} %copy.18) | copy-start | bytes 10137604
  140.1 65.6 %collective-permute-start.7 = (f32[4,88,2048]{2,1,0:T(8,128)}, f32[4,88,2048]{2,1,0:T(8,128)S(1)}, u32[]{:S(2)}, u32[]{:S(2)}) collective-permute-start(f32[4,88,2048]{2,1,0:T(8,128)} %convolution_bitcast_fusion), channel_id=1, source_target_pairs={{0,2},{2,0},{1,3},{3,1},{4,6},{6,4},{5,7},{7,5},{8,10},{10,8},{9,1... | collective-permute-start | bytes 8650760 | tf_op jit(solution)/shard_map/ppermute | solution.py:80
  147.2 46.9 %copy-start.2 = (bf16[8,88,2,1200]{3,1,2,0:T(8,128)(2,1)S(1)}, bf16[8,88,2,1200]{3,1,2,0:T(8,128)(2,1)}, u32[]{:S(2)}) copy-start(bf16[8,88,2,1200]{3,1,2,0:T(8,128)(2,1)} %copy-done.1) | copy-start | bytes 10137604
  192.5 31.5 %collective-permute-start.6 = (f32[112,2048]{1,0:T(8,128)S(1)}, f32[112,2048]{1,0:T(8,128)S(1)}, u32[]{:S(2)}, u32[]{:S(2)}) collective-permute-start(f32[112,2048]{1,0:T(8,128)S(1)} %dynamic-slice_bitcast_fusion), channel_id=1, source_target_pairs={{0,2},{2,0},{1,3},{3,1},{4,6},{6,4},{5,7},{7,5},{8,10},{10,8},{9,1... | collective-permute-start | bytes 2752520 | tf_op jit(solution)/shard_map/ppermute | solution.py:66
  206.3 31.4 %collective-permute-start.10 = (f32[88,2048]{1,0:T(8,128)S(1)}, f32[88,2048]{1,0:T(8,128)S(1)}, u32[]{:S(2)}, u32[]{:S(2)}) collective-permute-start(f32[88,2048]{1,0:T(8,128)S(1)} %get-tuple-element.15), channel_id=1, source_target_pairs={{0,12},{4,0},{8,4},{12,8},{1,13},{5,1},{9,5},{13,9},{2,14},{6,2},{... | collective-permute-start | bytes 2162696 | tf_op jit(solution)/shard_map/ppermute | solution.py:92
  209.1 28.6 %collective-permute-start.9 = (f32[88,2048]{1,0:T(8,128)S(1)}, f32[88,2048]{1,0:T(8,128)S(1)}, u32[]{:S(2)}, u32[]{:S(2)}) collective-permute-start(f32[88,2048]{1,0:T(8,128)S(1)} %get-tuple-element.16), channel_id=1, source_target_pairs={{0,8},{4,12},{8,0},{12,4},{1,9},{5,13},{9,1},{13,5},{2,10},{6,14},... | collective-permute-start | bytes 2162696 | tf_op jit(solution)/shard_map/ppermute | solution.py:92
  210.0 31.4 %collective-permute-start.8 = (f32[88,2048]{1,0:T(8,128)S(1)}, f32[88,2048]{1,0:T(8,128)S(1)}, u32[]{:S(2)}, u32[]{:S(2)}) collective-permute-start(f32[88,2048]{1,0:T(8,128)S(1)} %get-tuple-element.14), channel_id=1, source_target_pairs={{0,4},{4,8},{8,12},{12,0},{1,5},{5,9},{9,13},{13,1},{2,6},{6,10},{... | collective-permute-start | bytes 2162696 | tf_op jit(solution)/shard_map/ppermute | solution.py:92
  224.2 20.5 %collective-permute-start.11 = (f32[112,1024]{1,0:T(8,128)S(1)}, f32[112,1024]{1,0:T(8,128)S(1)}, u32[]{:S(2)}, u32[]{:S(2)}) collective-permute-start(f32[112,1024]{1,0:T(8,128)S(1)} %get-tuple-element.18), channel_id=1, source_target_pairs={{0,64},{64,0},{1,65},{65,1},{2,66},{66,2},{3,67},{67,3},{4,68},{68... | collective-permute-start | bytes 1376264 | tf_op jit(solution)/shard_map/ppermute | solution.py:96
  241.6 11.9 %collective-permute-start.12 = (f32[88,1024]{1,0:T(8,128)S(1)}, f32[88,1024]{1,0:T(8,128)S(1)}, u32[]{:S(2)}, u32[]{:S(2)}) collective-permute-start(f32[88,1024]{1,0:T(8,128)S(1)} %get-tuple-element.20), channel_id=1, source_target_pairs={{0,64},{64,0},{1,65},{65,1},{2,66},{66,2},{3,67},{67,3},{4,68},{68... | collective-permute-start | bytes 1081352 | tf_op jit(solution)/shard_map/ppermute | solution.py:96
Sparse Core Ops, SparseCore 0:
  19.0 54.1 all-gather.2
  80.1 46.1 all-gather.4

commit v14 on v12

--- a/solution.py
+++ b/solution.py
@@ -30,15 +30,15 @@
     theirs = jnp.take(tiles, position[:, 1 - core], axis=0)
     from_sibling = lax.ppermute(theirs, "c", SWAP)
     own_owners = jnp.stack([mine, from_sibling], axis=2)
-    y_cut = TB * 14 // 25
+    y_cut = TB * 29 // 50
     gathered = lax.all_gather(own_owners[:, :y_cut], "z", axis=1, tiled=True)
     y_rows = gathered.shape[1]
     by_y = gathered.reshape(ny, nxl, y_rows, 2, kc)
 
     amp = jnp.concatenate([amplitudes, lax.ppermute(amplitudes, "xh", SWAP)], axis=1)
+    amp = jnp.stack([amp, lax.ppermute(amp, "c", SWAP)], axis=0)
     late_rows, amp = lax.optimization_barrier((own_owners[:, y_cut:], amp))
     gathered_late = lax.all_gather(late_rows, "z", axis=1, tiled=True)
-    amp = jnp.stack([amp, lax.ppermute(amp, "c", SWAP)], axis=0)
 
     def block(y_owner, low, high):
         lhs = lax.dynamic_index_in_dim(by_y, y_owner % ny, 0, keepdims=False)

time: 256 us -> 323 us (1.26)
  waiting for transfers between devices: 120 us -> 203 us
  matrix products: 60.9 us -> 23.7 us
  local copies, waits for them, and re-layouts: 18.3 us -> 32.9 us
  other arithmetic: 10.1 us -> 17.7 us
  starting transfers between devices: 32.1 us -> 28 us
    ppermute x2, waiting for transfers between devices: 10.1 us -> 69.5 us  [pair_sum(): return here + lax.ppermute(there, 'xl', SWAP)]
    ppermute x3, waiting for transfers between devices: 0.9 us -> 47.4 us  [ring(): got_back = lax.ppermute(acc_back, 'y', to_prev)]
    dot_general x8, matrix products: 47.7 us -> 13.1 us  [block(): lax.dot_general(lhs[:, low:high], amp, (((2, 3), (0, 1)), ((), ())), pref...]
    ppermute x3, waiting for transfers between devices: 19.2 us -> 1.23 us  [ring(): got_ahead = lax.ppermute(acc_ahead, 'y', to_next)]
    ppermute x1, waiting for transfers between devices: 53.7 us -> 37.8 us  [local(): lax.ppermute(amplitudes, 'xh', SWAP)]
    ppermute x3, waiting for transfers between devices: 11.1 us -> 26 us  [local(): lax.ppermute(pick(late_sum)(yi + hop), 'y', to_owner)]
    ppermute x1, waiting for transfers between devices: 10 us -> 0.01 us  [local(): late_sum = late_block(xi) + lax.ppermute(late_there, 'xl', SWAP)]
    another operation x0 -> x1, other arithmetic: none -> 8.54 us  [local(): amp = jnp.stack([amp, lax.ppermute(amp, 'c', SWAP)], axis=0)]
  transfers between devices with their start and end apart: 20 -> 20, of which waited for: 12 -> 12; matrix products, arithmetic and copies ran while one was open for 31% -> 22% of each run, Pallas kernels for 0% -> 0%
where the time goes in v14:
time: 323 us; the launch traced here: 319 us
  waiting for transfers between devices  203 us (63%)
  local copies, waits for them, and re-layouts  32.9 us (10%)
  starting transfers between devices  28 us (9%)
  matrix products  23.7 us (7%)
  other arithmetic  17.7 us (5%)
  between operations  14.3 us (4%)
    ppermute x2, waiting for transfers between devices, pair_sum(): return here + lax.ppermute(there, 'xl', SWAP)  69.5 us
    ppermute x3, waiting for transfers between devices, ring(): got_back = lax.ppermute(acc_back, 'y', to_prev)  47.4 us
    ppermute x1, waiting for transfers between devices, local(): lax.ppermute(amplitudes, 'xh', SWAP)  37.8 us
    ppermute x3, waiting for transfers between devices, local(): lax.ppermute(pick(late_sum)(yi + hop), 'y', to_owner)  26 us
    dot_general x8, matrix products, block(): lax.dot_general(lhs[:, low:high], amp, (((2, 3), (0, 1)), ((), ())), pref...  13.1 us
    ppermute x3, starting transfers between devices, ring(): got_back = lax.ppermute(acc_back, 'y', to_prev)  11.2 us
    dot_general x2, matrix products, late_block(): lax.dot_general(lhs, amp, (((2, 3), (0, 1)), ((), ())), preferred_element...  10.7 us
    ppermute x3, waiting for transfers between devices, local(): came = [lax.ppermute(piece[:, width:], 'xh', SWAP) for piece in pieces]  10.5 us
  transfers between devices with their start and end apart: 20, of which 12 were waited for; matrix products, arithmetic and copies ran while one was open for 22% of the time, Pallas kernels for 0%

profile of v14, /device:TPU:0, one launch (start us, length us, event | category | flops | bytes accessed | tf_op | source)
XLA Modules:
  0.0 319.3 jit_solution(2083223806188525777)
XLA Ops:
  6.5 3.1 collective-permute-start.1
  9.7 2.6 reshape.35
  12.4 1.2 sort.17
  13.9 0.6 gather_fusion.1
  14.8 1.1 copy.12
  15.9 0.6 gather_fusion
  16.7 2.1 collective-permute-done
  18.8 1.4 copy.56
  20.4 1.7 copy.14
  22.1 3.4 %constant_dynamic-update-slice_fusion.1 = bf16[1200,2048]{1,0:T(8,128)(2,1)} fusion(bf16[1200,1024]{1,0:T(8,128)(2,1)} %param.5), kind=kLoop, calls=%fused_computation.89 | loop fusion | bytes 4915200
  25.5 37.8 %collective-permute-done.1 = bf16[1200,1024]{1,0:T(8,128)(2,1)} collective-permute-done((bf16[1200,1024]{1,0:T(8,128)(2,1)}, bf16[1200,1024]{1,0:T(8,128)(2,1)}, u32[]{:S(2)}, u32[]{:S(2)}) %collective-permute-start.1) | collective-permute-done | bytes 2457632 | tf_op jit(solution)/shard_map/ppermute | solution.py:38
  63.3 3.4 %constant_dynamic-update-slice_fusion = bf16[1200,2048]{1,0:T(8,128)(2,1)} fusion(bf16[1200,2048]{1,0:T(8,128)(2,1)} %constant_dynamic-update-slice_fusion.1, bf16[1200,1024]{1,0:T(8,128)(2,1)} %collective-permute-done.1), kind=kLoop, calls=%fused_computation.88 | loop fusion | bytes 4915200 | tf_op jit(solution)/shard_map/concatenate | solution.py:38
  66.8 0.5 collective-permute-start.2
  67.7 8.1 %collective-permute-done.2 = bf16[1200,2048]{1,0:T(8,128)(2,1)} collective-permute-done((bf16[1200,2048]{1,0:T(8,128)(2,1)}, bf16[1200,2048]{1,0:T(8,128)(2,1)}, u32[]{:S(2)}, u32[]{:S(2)}) %collective-permute-start.2) | collective-permute-done | bytes 4915232 | tf_op jit(solution)/shard_map/ppermute | solution.py:39
  75.8 8.5 %pad_maximum_fusion = bf16[2,1200,2048]{2,1,0:T(8,128)(2,1)} fusion(bf16[1,1200,2048]{2,1,0:T(8,128)(2,1)} %bitcast.5, bf16[1,1200,2048]{2,1,0:T(8,128)(2,1)} %bitcast.4), kind=kLoop, calls=%fused_computation.2 | loop fusion | flops 4915200 | bytes 19660800 | tf_op jit(solution)/shard_map/stack | solution.py:39
  84.4 1.1 copy.33
  85.5 4.0 %copy.47 = bf16[8,116,2,1200]{3,1,2,0:T(8,128)(2,1)S(1)} copy(bf16[8,116,2,1200]{3,0,2,1:T(8,128)(2,1)} %all-gather.3.cloned.1.call-done) | data formatting | bytes 8908800 | tf_op jit(solution)/shard_map/reshape | solution.py:36
  89.5 0.5 dynamic-slice_bitcast_fusion.4
  90.4 0.7 slice-done.2
  91.1 1.7 fusion.47
  92.8 1.6 fusion.35
  94.4 1.7 fusion.44
  96.1 1.7 fusion.38
  97.8 0.7 copy.26
  98.6 3.5 %collective-permute-start.7 = (f32[2,58,2048]{2,0,1:T(2,128)S(1)}, f32[2,58,2048]{2,0,1:T(2,128)S(1)}, u32[]{:S(2)}, u32[]{:S(2)}) collective-permute-start(f32[2,58,2048]{2,0,1:T(2,128)S(1)} %copy.26), channel_id=1, source_target_pairs={{0,12},{4,0},{8,4},{12,8},{1,13},{5,1},{9,5},{13,9},{2,14},{6,2},{... | collective-permute-start | bytes 2850824 | tf_op jit(solution)/shard_map/ppermute | solution.py:58
  102.0 1.7 fusion.41
  103.8 1.6 fusion.26
  105.3 0.7 copy.16
  106.1 16.5 %collective-permute-done.7 = f32[2,58,2048]{2,0,1:T(2,128)S(1)} collective-permute-done((f32[2,58,2048]{2,0,1:T(2,128)S(1)}, f32[2,58,2048]{2,0,1:T(2,128)S(1)}, u32[]{:S(2)}, u32[]{:S(2)}) %collective-permute-start.7) | collective-permute-done | bytes 950304 | tf_op jit(solution)/shard_map/ppermute | solution.py:58
  122.7 0.6 copy_add_fusion.3
  123.2 0.7 copy.29
  124.0 3.8 %collective-permute-start.8 = (f32[2,58,2048]{2,0,1:T(2,128)S(1)}, f32[2,58,2048]{2,0,1:T(2,128)S(1)}, u32[]{:S(2)}, u32[]{:S(2)}) collective-permute-start(f32[2,58,2048]{2,0,1:T(2,128)S(1)} %copy.29), channel_id=1, source_target_pairs={{0,12},{4,0},{8,4},{12,8},{1,13},{5,1},{9,5},{13,9},{2,14},{6,2},{... | collective-permute-start | bytes 2850824 | tf_op jit(solution)/shard_map/ppermute | solution.py:58
  127.7 1.5 fusion.29
  129.3 0.9 collective-permute-done.3
  130.2 0.6 copy_add_fusion.6
  130.7 0.7 copy.19
  131.6 16.0 %collective-permute-done.8 = f32[2,58,2048]{2,0,1:T(2,128)S(1)} collective-permute-done((f32[2,58,2048]{2,0,1:T(2,128)S(1)}, f32[2,58,2048]{2,0,1:T(2,128)S(1)}, u32[]{:S(2)}, u32[]{:S(2)}) %collective-permute-start.8) | collective-permute-done | bytes 950304 | tf_op jit(solution)/shard_map/ppermute | solution.py:58
  147.6 0.6 copy_add_fusion.2
  148.2 0.7 copy.31
  148.9 4.0 %collective-permute-start.9 = (f32[2,58,2048]{2,0,1:T(2,128)S(1)}, f32[2,58,2048]{2,0,1:T(2,128)S(1)}, u32[]{:S(2)}, u32[]{:S(2)}) collective-permute-start(f32[2,58,2048]{2,0,1:T(2,128)S(1)} %copy.31), channel_id=1, source_target_pairs={{0,12},{4,0},{8,4},{12,8},{1,13},{5,1},{9,5},{13,9},{2,14},{6,2},{... | collective-permute-start | bytes 2850824 | tf_op jit(solution)/shard_map/ppermute | solution.py:58
  152.9 1.5 fusion.32
  154.8 0.6 copy_add_fusion.5
  155.4 1.7 copy.22
  157.1 14.8 %collective-permute-done.9 = f32[2,58,2048]{2,0,1:T(2,128)S(1)} collective-permute-done((f32[2,58,2048]{2,0,1:T(2,128)S(1)}, f32[2,58,2048]{2,0,1:T(2,128)S(1)}, u32[]{:S(2)}, u32[]{:S(2)}) %collective-permute-start.9) | collective-permute-done | bytes 950304 | tf_op jit(solution)/shard_map/ppermute | solution.py:58
  171.9 0.6 copy_add_fusion.1
  172.6 3.1 copy.34
  175.7 6.8 %fusion.23 = f32[4,84,2048]{2,1,0:T(8,128)S(1)} fusion(bf16[2,1200,2048]{2,1,0:T(8,128)(2,1)} %pad_maximum_fusion, bf16[4,2,84,2,1200]{4,2,3,1,0:T(8,128)(2,1)S(1)} %bitcast.126, s32[]{:T(128)S(6)} %select_n.118), kind=kOutput, calls=%fused_computation.24 | convolution fusion | flops 3303014400 | bytes 14385156 | tf_op jit(solution)/shard_map/dot_general | solution.py:74
  182.5 1.8 copy.35
  184.3 1.5 collective-permute-start.11
  185.8 0.7 collective-permute-start.10
  186.5 0.6 copy_add_fusion.4
  187.2 1.5 collective-permute-start.6
  188.6 69.5 %collective-permute-done.10 = f32[58,2048]{1,0:T(8,128)S(1)} collective-permute-done((f32[58,2048]{1,0:T(8,128)S(1)}, f32[58,2048]{1,0:T(8,128)S(1)}, u32[]{:S(2)}, u32[]{:S(2)}) %collective-permute-start.10) | collective-permute-done | bytes 475168 | tf_op jit(solution)/shard_map/ppermute | solution.py:66
  258.3 3.3 %collective-permute-start.16 = (f32[58,1024]{1,0:T(8,128)S(1)}, f32[58,1024]{1,0:T(8,128)S(1)}, u32[]{:S(2)}, u32[]{:S(2)}) collective-permute-start(f32[58,1024]{1,0:T(8,128)S(1)} %get-tuple-element.28), channel_id=1, source_target_pairs={{0,64},{64,0},{1,65},{65,1},{2,66},{66,2},{3,67},{67,3},{4,68},{68... | collective-permute-start | bytes 712712 | tf_op jit(solution)/shard_map/ppermute | solution.py:98
  261.6 3.9 %fusion.20 = f32[4,84,2048]{2,1,0:T(8,128)S(1)} fusion(bf16[2,1200,2048]{2,1,0:T(8,128)(2,1)S(1)} %bitcast.122, bf16[4,2,84,2,1200]{4,2,3,1,0:T(8,128)(2,1)S(1)} %bitcast.127, s32[]{:T(128)S(6)} %select_n.117), kind=kOutput, calls=%fused_computation.23 | convolution fusion | flops 3303014400 | bytes 14385156 | tf_op jit(solution)/shard_map/dot_general | solution.py:74
  265.5 1.7 copy_add_fusion
  267.3 3.8 %collective-permute-start.14 = (f32[84,2048]{1,0:T(8,128)S(1)}, f32[84,2048]{1,0:T(8,128)S(1)}, u32[]{:S(2)}, u32[]{:S(2)}) collective-permute-start(f32[84,2048]{1,0:T(8,128)S(1)} %get-tuple-element.21), channel_id=1, source_target_pairs={{0,12},{4,0},{8,4},{12,8},{1,13},{5,1},{9,5},{13,9},{2,14},{6,2},{... | collective-permute-start | bytes 2064392 | tf_op jit(solution)/shard_map/ppermute | solution.py:94
  271.1 0.9 collective-permute-start.12
  272.2 0.6 collective-permute-start.15
  272.8 22.6 %collective-permute-done.14 = f32[84,2048]{1,0:T(8,128)S(1)} collective-permute-done((f32[84,2048]{1,0:T(8,128)S(1)}, f32[84,2048]{1,0:T(8,128)S(1)}, u32[]{:S(2)}, u32[]{:S(2)}) %collective-permute-start.14) | collective-permute-done | bytes 688160 | tf_op jit(solution)/shard_map/ppermute | solution.py:94
  295.4 3.4 %collective-permute-done.12 = f32[84,2048]{1,0:T(8,128)S(1)} collective-permute-done((f32[84,2048]{1,0:T(8,128)S(1)}, f32[84,2048]{1,0:T(8,128)S(1)}, u32[]{:S(2)}, u32[]{:S(2)}) %collective-permute-start.12) | collective-permute-done | bytes 688160 | tf_op jit(solution)/shard_map/ppermute | solution.py:94
  299.0 0.6 collective-permute-start.17
  300.1 10.5 %collective-permute-done.17 = f32[84,1024]{1,0:T(8,128)S(1)} collective-permute-done((f32[84,1024]{1,0:T(8,128)S(1)}, f32[84,1024]{1,0:T(8,128)S(1)}, u32[]{:S(2)}, u32[]{:S(2)}) %collective-permute-start.17) | collective-permute-done | bytes 344096 | tf_op jit(solution)/shard_map/ppermute | solution.py:98
  310.9 1.3 maximum_select_fusion
  (65 shorter events, 3.5 us)
Async XLA Ops:
  6.5 5.7 %copy-start = (s32[128]{0:T(128)S(1)}, s32[128]{0:T(128)}, u32[]{:S(2)}) copy-start(s32[128]{0:T(128)} %param.7) | copy-start | bytes 1540
  6.5 78.9 %all-gather.3.cloned.1.call-start = ((), (), s32[]{:S(2)}) async-start(), calls=%async_computation | async-start | bytes 5939200 | tf_op jit(solution)/shard_map/all_gather | solution.py:34
  6.5 56.8 %collective-permute-start.1 = (bf16[1200,1024]{1,0:T(8,128)(2,1)}, bf16[1200,1024]{1,0:T(8,128)(2,1)}, u32[]{:S(2)}, u32[]{:S(2)}) collective-permute-start(bf16[1200,1024]{1,0:T(8,128)(2,1)} %param.5), channel_id=1, source_target_pairs={{0,64},{64,0},{1,65},{65,1},{2,66},{66,2},{3,67},{67,3},{4,68},{68... | collective-permute-start | bytes 7372808 | tf_op jit(solution)/shard_map/ppermute | solution.py:38
  15.9 3.0 collective-permute-start
  22.1 150.4 %all-gather.5.cloned.1.call-start = ((), (), s32[]{:S(2)}) async-start(), calls=%async_computation.1 | async-start | bytes 4300800 | tf_op jit(solution)/shard_map/all_gather | solution.py:41
  66.8 9.0 %collective-permute-start.2 = (bf16[1200,2048]{1,0:T(8,128)(2,1)}, bf16[1200,2048]{1,0:T(8,128)(2,1)}, u32[]{:S(2)}, u32[]{:S(2)}) collective-permute-start(bf16[1200,2048]{1,0:T(8,128)(2,1)} %constant_dynamic-update-slice_fusion), channel_id=1, source_target_pairs={{0,1},{1,0},{2,3},{3,2},{4,5},{5,4},{6,7},{7,6},{8,9},{9,8},{10,11... | collective-permute-start | bytes 14745608 | tf_op jit(solution)/shard_map/ppermute | solution.py:39
  85.5 4.6 %slice-start = ((s8[9830400]{0:T(1024)(128)(4,1)}), s8[4194304]{0:T(1024)(128)(4,1)S(1)}, s32[]{:S(2)}) async-start(s8[9830400]{0:T(1024)(128)(4,1)} %bitcast.119), calls=%async_computation.2 | async-start | bytes 8388608
  85.5 4.9 %slice-start.1 = ((s8[9830400]{0:T(1024)(128)(4,1)}), s8[4194304]{0:T(1024)(128)(4,1)S(1)}, s32[]{:S(2)}) async-start(s8[9830400]{0:T(1024)(128)(4,1)} %bitcast.119), calls=%async_computation.3 | async-start | bytes 8388608
  89.5 1.6 slice-start.2
  98.6 24.1 %collective-permute-start.7 = (f32[2,58,2048]{2,0,1:T(2,128)S(1)}, f32[2,58,2048]{2,0,1:T(2,128)S(1)}, u32[]{:S(2)}, u32[]{:S(2)}) collective-permute-start(f32[2,58,2048]{2,0,1:T(2,128)S(1)} %copy.26), channel_id=1, source_target_pairs={{0,12},{4,0},{8,4},{12,8},{1,13},{5,1},{9,5},{13,9},{2,14},{6,2},{... | collective-permute-start | bytes 2850824 | tf_op jit(solution)/shard_map/ppermute | solution.py:58
  106.1 24.1 %collective-permute-start.3 = (f32[2,58,2048]{2,0,1:T(2,128)S(1)}, f32[2,58,2048]{2,0,1:T(2,128)S(1)}, u32[]{:S(2)}, u32[]{:S(2)}) collective-permute-start(f32[2,58,2048]{2,0,1:T(2,128)S(1)} %copy.16), channel_id=1, source_target_pairs={{0,4},{4,8},{8,12},{12,0},{1,5},{5,9},{9,13},{13,1},{2,6},{6,10},{... | collective-permute-start | bytes 2850824 | tf_op jit(solution)/shard_map/ppermute | solution.py:57
  124.0 23.6 %collective-permute-start.8 = (f32[2,58,2048]{2,0,1:T(2,128)S(1)}, f32[2,58,2048]{2,0,1:T(2,128)S(1)}, u32[]{:S(2)}, u32[]{:S(2)}) collective-permute-start(f32[2,58,2048]{2,0,1:T(2,128)S(1)} %copy.29), channel_id=1, source_target_pairs={{0,12},{4,0},{8,4},{12,8},{1,13},{5,1},{9,5},{13,9},{2,14},{6,2},{... | collective-permute-start | bytes 2850824 | tf_op jit(solution)/shard_map/ppermute | solution.py:58
  131.5 23.3 %collective-permute-start.4 = (f32[2,58,2048]{2,0,1:T(2,128)S(1)}, f32[2,58,2048]{2,0,1:T(2,128)S(1)}, u32[]{:S(2)}, u32[]{:S(2)}) collective-permute-start(f32[2,58,2048]{2,0,1:T(2,128)S(1)} %copy.19), channel_id=1, source_target_pairs={{0,4},{4,8},{8,12},{12,0},{1,5},{5,9},{9,13},{13,1},{2,6},{6,10},{... | collective-permute-start | bytes 2850824 | tf_op jit(solution)/shard_map/ppermute | solution.py:57
  148.9 23.0 %collective-permute-start.9 = (f32[2,58,2048]{2,0,1:T(2,128)S(1)}, f32[2,58,2048]{2,0,1:T(2,128)S(1)}, u32[]{:S(2)}, u32[]{:S(2)}) collective-permute-start(f32[2,58,2048]{2,0,1:T(2,128)S(1)} %copy.31), channel_id=1, source_target_pairs={{0,12},{4,0},{8,4},{12,8},{1,13},{5,1},{9,5},{13,9},{2,14},{6,2},{... | collective-permute-start | bytes 2850824 | tf_op jit(solution)/shard_map/ppermute | solution.py:58
  157.1 29.4 %collective-permute-start.5 = (f32[2,58,2048]{2,0,1:T(2,128)}, f32[2,58,2048]{2,0,1:T(2,128)S(1)}, u32[]{:S(2)}, u32[]{:S(2)}) collective-permute-start(f32[2,58,2048]{2,0,1:T(2,128)} %copy.22), channel_id=1, source_target_pairs={{0,4},{4,8},{8,12},{12,0},{1,5},{5,9},{9,13},{13,1},{2,6},{6,10},{... | collective-permute-start | bytes 2850824 | tf_op jit(solution)/shard_map/ppermute | solution.py:57
  172.6 89.0 %slice-start.3 = ((s8[9830400]{0:T(1024)(128)(4,1)}), s8[1441792]{0:T(1024)(128)(4,1)S(1)}, s32[]{:S(2)}) async-start(s8[9830400]{0:T(1024)(128)(4,1)} %bitcast.121), calls=%async_computation.5 | async-start | bytes 2883584
  175.7 85.9 %slice-start.4 = ((s8[9830400]{0:T(1024)(128)(4,1)}), s8[4194304]{0:T(1024)(128)(4,1)S(1)}, s32[]{:S(2)}) async-start(s8[9830400]{0:T(1024)(128)(4,1)} %bitcast.121), calls=%async_computation.6 | async-start | bytes 8388608
  175.7 85.9 %slice-start.5 = ((s8[9830400]{0:T(1024)(128)(4,1)}), s8[4194304]{0:T(1024)(128)(4,1)S(1)}, s32[]{:S(2)}) async-start(s8[9830400]{0:T(1024)(128)(4,1)} %bitcast.121), calls=%async_computation.7 | async-start | bytes 8388608
  184.3 81.2 %collective-permute-start.11 = (f32[4,84,2048]{2,0,1:T(4,128)S(1)}, f32[4,84,2048]{2,0,1:T(4,128)S(1)}, u32[]{:S(2)}, u32[]{:S(2)}) collective-permute-start(f32[4,84,2048]{2,0,1:T(4,128)S(1)} %copy.35), channel_id=1, source_target_pairs={{0,2},{2,0},{1,3},{3,1},{4,6},{6,4},{5,7},{7,5},{8,10},{10,8},{9,1... | collective-permute-start | bytes 8257544 | tf_op jit(solution)/shard_map/ppermute | solution.py:80
  185.8 72.3 %collective-permute-start.10 = (f32[58,2048]{1,0:T(8,128)S(1)}, f32[58,2048]{1,0:T(8,128)S(1)}, u32[]{:S(2)}, u32[]{:S(2)}) collective-permute-start(f32[58,2048]{1,0:T(8,128)S(1)} %dynamic-slice_bitcast_fusion.9), channel_id=1, source_target_pairs={{0,2},{2,0},{1,3},{3,1},{4,6},{6,4},{5,7},{7,5},{8,10},{10,8},{9,1... | collective-permute-start | bytes 1425416 | tf_op jit(solution)/shard_map/ppermute | solution.py:66
  187.2 84.9 %collective-permute-start.6 = (f32[58,2048]{1,0:T(8,128)S(1)}, f32[58,2048]{1,0:T(8,128)S(1)}, u32[]{:S(2)}, u32[]{:S(2)}) collective-permute-start(f32[58,2048]{1,0:T(8,128)S(1)} %dynamic-slice_bitcast_fusion.10), channel_id=1, source_target_pairs={{0,2},{2,0},{1,3},{3,1},{4,6},{6,4},{5,7},{7,5},{8,10},{10,8},{9,1... | collective-permute-start | bytes 1425416 | tf_op jit(solution)/shard_map/ppermute | solution.py:66
  258.3 41.5 %collective-permute-start.16 = (f32[58,1024]{1,0:T(8,128)S(1)}, f32[58,1024]{1,0:T(8,128)S(1)}, u32[]{:S(2)}, u32[]{:S(2)}) collective-permute-start(f32[58,1024]{1,0:T(8,128)S(1)} %get-tuple-element.28), channel_id=1, source_target_pairs={{0,64},{64,0},{1,65},{65,1},{2,66},{66,2},{3,67},{67,3},{4,68},{68... | collective-permute-start | bytes 712712 | tf_op jit(solution)/shard_map/ppermute | solution.py:98
  267.3 28.0 %collective-permute-start.14 = (f32[84,2048]{1,0:T(8,128)S(1)}, f32[84,2048]{1,0:T(8,128)S(1)}, u32[]{:S(2)}, u32[]{:S(2)}) collective-permute-start(f32[84,2048]{1,0:T(8,128)S(1)} %get-tuple-element.21), channel_id=1, source_target_pairs={{0,12},{4,0},{8,4},{12,8},{1,13},{5,1},{9,5},{13,9},{2,14},{6,2},{... | collective-permute-start | bytes 2064392 | tf_op jit(solution)/shard_map/ppermute | solution.py:94
  271.1 24.2 %collective-permute-start.13 = (f32[84,2048]{1,0:T(8,128)S(1)}, f32[84,2048]{1,0:T(8,128)S(1)}, u32[]{:S(2)}, u32[]{:S(2)}) collective-permute-start(f32[84,2048]{1,0:T(8,128)S(1)} %get-tuple-element.22), channel_id=1, source_target_pairs={{0,8},{4,12},{8,0},{12,4},{1,9},{5,13},{9,1},{13,5},{2,10},{6,14},... | collective-permute-start | bytes 2064392 | tf_op jit(solution)/shard_map/ppermute | solution.py:94
  271.1 27.7 %collective-permute-start.12 = (f32[84,2048]{1,0:T(8,128)S(1)}, f32[84,2048]{1,0:T(8,128)S(1)}, u32[]{:S(2)}, u32[]{:S(2)}) collective-permute-start(f32[84,2048]{1,0:T(8,128)S(1)} %get-tuple-element.20), channel_id=1, source_target_pairs={{0,4},{4,8},{8,12},{12,0},{1,5},{5,9},{9,13},{13,1},{2,6},{6,10},{... | collective-permute-start | bytes 2064392 | tf_op jit(solution)/shard_map/ppermute | solution.py:94
  272.2 27.6 %collective-permute-start.15 = (f32[58,1024]{1,0:T(8,128)S(1)}, f32[58,1024]{1,0:T(8,128)S(1)}, u32[]{:S(2)}, u32[]{:S(2)}) collective-permute-start(f32[58,1024]{1,0:T(8,128)S(1)} %get-tuple-element.26), channel_id=1, source_target_pairs={{0,64},{64,0},{1,65},{65,1},{2,66},{66,2},{3,67},{67,3},{4,68},{68... | collective-permute-start | bytes 712712 | tf_op jit(solution)/shard_map/ppermute | solution.py:98
  299.0 11.6 %collective-permute-start.17 = (f32[84,1024]{1,0:T(8,128)S(1)}, f32[84,1024]{1,0:T(8,128)S(1)}, u32[]{:S(2)}, u32[]{:S(2)}) collective-permute-start(f32[84,1024]{1,0:T(8,128)S(1)} %get-tuple-element.24), channel_id=1, source_target_pairs={{0,64},{64,0},{1,65},{65,1},{2,66},{66,2},{3,67},{67,3},{4,68},{68... | collective-permute-start | bytes 1032200 | tf_op jit(solution)/shard_map/ppermute | solution.py:98
Sparse Core Ops, SparseCore 0:
  22.2 53.5 all-gather.2
  85.6 44.7 all-gather.4

commit v15 on v12

--- a/solution.py
+++ b/solution.py
@@ -88,14 +88,24 @@
         lambda y_owner: block(y_owner, 0, y_half),
         lambda y_owner: block(y_owner, y_half, y_rows),
     )
-    late_done = pick(late_sum)(yi)
+    nxh = lax.axis_size("xh")
+    own_block = pick(late_sum)(yi)
+    late_kept = own_block[:, :width]
+    late_came = lax.ppermute(own_block[:, width:], "xh", SWAP)
     for hop in range(1, ny):
         to_owner = [(i, (i + hop) % ny) for i in range(ny)]
-        late_done = late_done + lax.ppermute(pick(late_sum)(yi + hop), "y", to_owner)
-    pieces = [pair_sum(early[0]), pair_sum(early[1]), late_done]
+        to_partner = [
+            (h * ny + i, (nxh - 1 - h) * ny + (i + hop) % ny)
+            for h in range(nxh)
+            for i in range(ny)
+        ]
+        block_out = pick(late_sum)(yi + hop)
+        late_kept = late_kept + lax.ppermute(block_out[:, :width], "y", to_owner)
+        late_came = late_came + lax.ppermute(block_out[:, width:], ("xh", "y"), to_partner)
+    pieces = [pair_sum(early[0]), pair_sum(early[1])]
 
-    kept = [piece[:, :width] for piece in pieces]
-    came = [lax.ppermute(piece[:, width:], "xh", SWAP) for piece in pieces]
+    kept = [piece[:, :width] for piece in pieces] + [late_kept]
+    came = [lax.ppermute(piece[:, width:], "xh", SWAP) for piece in pieces] + [late_came]
 
     def slab_group(parts):
         early = jnp.concatenate(parts[:2], axis=0).reshape(nz, y_cut, width)

time: 256 us -> 274 us (1.070)
  waiting for transfers between devices: 120 us -> 128 us
  starting transfers between devices: 32.1 us -> 37.8 us
    ppermute x6 -> x9, waiting for transfers between devices: 18.1 us -> 29.7 us  [the longest x2 24.4 us: local(): lax.ppermute(piece[:, width:], 'xh', SWAP)]
    ppermute x6 -> x9, starting transfers between devices: 14.9 us -> 20.6 us  [the longest x3 10.5 us: local(): lax.ppermute(block_out[:, width:], ('xh', 'y'), to_partner)]
    ppermute x2, waiting for transfers between devices: 10.1 us -> 6.75 us  [pair_sum(): return here + lax.ppermute(there, 'xl', SWAP)]
  transfers between devices with their start and end apart: 20 -> 23, of which waited for: 12 -> 13; matrix products, arithmetic and copies ran while one was open for 31% -> 30% of each run, Pallas kernels for 0% -> 0%
where the time goes in v15:
time: 274 us
  waiting for transfers between devices  128 us (47%)
  matrix products  60.9 us (22%)
  starting transfers between devices  37.8 us (14%)
  local copies, waits for them, and re-layouts  20.8 us (8%)
  between operations  13.9 us (5%)
  other arithmetic  12.4 us (5%)
    ppermute x1, waiting for transfers between devices, local(): lax.ppermute(amplitudes, 'xh', SWAP)  53.7 us
    dot_general x8, matrix products, block(): lax.dot_general(lhs[:, low:high], amp, (((2, 3), (0, 1)), ((), ())), pref...  47.6 us
    ppermute x2, waiting for transfers between devices, local(): lax.ppermute(piece[:, width:], 'xh', SWAP)  24.4 us
    ppermute x3, waiting for transfers between devices, ring(): got_ahead = lax.ppermute(acc_ahead, 'y', to_next)  19.2 us
    dot_general x2, matrix products, late_block(): lax.dot_general(lhs, amp, (((2, 3), (0, 1)), ((), ())), preferred_element...  13.3 us
    ppermute x3, starting transfers between devices, local(): lax.ppermute(block_out[:, width:], ('xh', 'y'), to_partner)  10.5 us
    ppermute x1, waiting for transfers between devices, local(): late_sum = late_block(xi) + lax.ppermute(late_there, 'xl', SWAP)  10 us
    ppermute x2, waiting for transfers between devices, pair_sum(): return here + lax.ppermute(there, 'xl', SWAP)  6.75 us
  transfers between devices with their start and end apart: 23, of which 13 were waited for; matrix products, arithmetic and copies ran while one was open for 30% of the time, Pallas kernels for 0%

profile of v15, /device:TPU:0, one launch (start us, length us, event | category | flops | bytes accessed | tf_op | source)
XLA Modules:
  0.0 273.9 jit_solution(10142154365944701608)
XLA Ops:
  6.5 0.7 dynamic_slice.63
  7.3 1.2 sort.17
  8.9 2.6 reshape.35
  11.4 0.6 gather_fusion.1
  12.3 1.1 copy.12
  13.4 0.6 gather_fusion
  14.2 2.1 collective-permute-done
  16.3 1.4 copy.35
  17.9 1.6 copy.14
  19.6 3.2 %collective-permute-start.1 = (bf16[1200,1024]{1,0:T(8,128)(2,1)}, bf16[1200,1024]{1,0:T(8,128)(2,1)S(1)}, u32[]{:S(2)}, u32[]{:S(2)}) collective-permute-start(bf16[1200,1024]{1,0:T(8,128)(2,1)} %param.5), channel_id=1, source_target_pairs={{0,64},{64,0},{1,65},{65,1},{2,66},{66,2},{3,67},{67,3},{4,68},{68... | collective-permute-start | bytes 7372808 | tf_op jit(solution)/shard_map/ppermute | solution.py:38
  23.1 53.7 %collective-permute-done.1 = bf16[1200,1024]{1,0:T(8,128)(2,1)S(1)} collective-permute-done((bf16[1200,1024]{1,0:T(8,128)(2,1)}, bf16[1200,1024]{1,0:T(8,128)(2,1)S(1)}, u32[]{:S(2)}, u32[]{:S(2)}) %collective-permute-start.1) | collective-permute-done | bytes 2457632 | tf_op jit(solution)/shard_map/ppermute | solution.py:38
  76.8 2.7 pad_maximum_fusion
  79.5 1.1 copy.21
  80.8 3.8 %copy.33 = bf16[8,112,2,1200]{3,1,2,0:T(8,128)(2,1)S(1)} copy(bf16[8,112,2,1200]{3,0,2,1:T(8,128)(2,1)} %all-gather.3.cloned.1.call-done) | data formatting | bytes 8601600 | tf_op jit(solution)/shard_map/reshape | solution.py:36
  84.5 0.6 dynamic-slice_bitcast_fusion.3
  85.1 2.9 %collective-permute-done.2 = bf16[1200,2048]{1,0:T(8,128)(2,1)} collective-permute-done((bf16[1200,2048]{1,0:T(8,128)(2,1)}, bf16[1200,2048]{1,0:T(8,128)(2,1)}, u32[]{:S(2)}, u32[]{:S(2)}) %collective-permute-start.2) | collective-permute-done | bytes 4915232 | tf_op jit(solution)/shard_map/ppermute | solution.py:41
  88.0 6.6 %convolution_bitcast_fusion.9 = f32[2,56,2048]{2,1,0:T(8,128)} fusion(bf16[2,112,2,1200]{3,1,2,0:T(8,128)(2,1)S(1)} %get-tuple-element.19, bf16[1,1200,2048]{2,1,0:T(8,128)(2,1)} %bitcast.5, bf16[1,1200,2048]{2,1,0:T(8,128)(2,1)} %bitcast.4), kind=kOutput, calls=%fused_computation.13 | convolution fusion | flops 1105920000 | bytes 11321344 | tf_op jit(solution)/shard_map/dot_general | solution.py:45
  94.6 1.7 collective-permute-start.3
  96.3 6.5 %convolution_bitcast_fusion.5 = f32[2,56,2048]{2,1,0:T(8,128)} fusion(bf16[2,112,2,1200]{3,1,2,0:T(8,128)(2,1)S(1)} %get-tuple-element.16, bf16[1,1200,2048]{2,1,0:T(8,128)(2,1)} %bitcast.5, bf16[1,1200,2048]{2,1,0:T(8,128)(2,1)} %bitcast.4), kind=kOutput, calls=%fused_computation.9 | convolution fusion | flops 1105920000 | bytes 11321344 | tf_op jit(solution)/shard_map/dot_general | solution.py:45
  102.8 1.6 collective-permute-start.7
  104.4 6.6 %convolution_bitcast_fusion.8 = f32[2,56,2048]{2,1,0:T(8,128)} fusion(bf16[2,112,2,1200]{3,1,2,0:T(8,128)(2,1)S(1)} %get-tuple-element.18, bf16[1,1200,2048]{2,1,0:T(8,128)(2,1)} %bitcast.5, bf16[1,1200,2048]{2,1,0:T(8,128)(2,1)} %bitcast.4), kind=kOutput, calls=%fused_computation.12 | convolution fusion | flops 1105920000 | bytes 11321344 | tf_op jit(solution)/shard_map/dot_general | solution.py:45
  111.0 6.6 %convolution_bitcast_fusion.7 = f32[2,56,2048]{2,1,0:T(8,128)} fusion(bf16[2,112,2,1200]{3,1,2,0:T(8,128)(2,1)S(1)} %get-tuple-element.14, bf16[1,1200,2048]{2,1,0:T(8,128)(2,1)} %bitcast.5, bf16[1,1200,2048]{2,1,0:T(8,128)(2,1)} %bitcast.4), kind=kOutput, calls=%fused_computation.11 | convolution fusion | flops 1105920000 | bytes 11321344 | tf_op jit(solution)/shard_map/dot_general | solution.py:45
  117.6 6.6 %convolution_bitcast_fusion.6 = f32[2,56,2048]{2,1,0:T(8,128)} fusion(bf16[2,112,2,1200]{3,1,2,0:T(8,128)(2,1)S(1)} %get-tuple-element.17, bf16[1,1200,2048]{2,1,0:T(8,128)(2,1)} %bitcast.5, bf16[1,1200,2048]{2,1,0:T(8,128)(2,1)} %bitcast.4), kind=kOutput, calls=%fused_computation.10 | convolution fusion | flops 1105920000 | bytes 11321344 | tf_op jit(solution)/shard_map/dot_general | solution.py:45
  124.2 2.7 all-gather.5.cloned.1.call-done
  126.9 3.1 %copy.22 = bf16[8,88,2,1200]{3,1,2,0:T(8,128)(2,1)S(1)} copy(bf16[8,88,2,1200]{3,0,2,1:T(8,128)(2,1)} %all-gather.5.cloned.1.call-done) | data formatting | bytes 6758400 | tf_op jit(solution)/shard_map/all_gather | solution.py:40
  130.1 6.6 %convolution_bitcast_fusion = f32[4,88,2048]{2,1,0:T(8,128)S(1)} fusion(bf16[4,2,88,2,1200]{4,2,3,1,0:T(8,128)(2,1)S(1)} %bitcast.89, s32[]{:T(128)S(6)} %select_n.118, bf16[1,1200,2048]{2,1,0:T(8,128)(2,1)} %bitcast.5, bf16[1,1200,2048]{2,1,0:T(8,128)(2,1)} %bitcast.4), kind=kOutput, calls=%fused_computation.4 | convolution fusion | flops 3465216000 | bytes 14516228 | tf_op jit(solution)/shard_map/dot_general | solution.py:74
  136.7 1.5 collective-permute-start.11
  138.3 4.9 %convolution_bitcast_fusion.4 = f32[2,56,2048]{2,1,0:T(8,128)S(1)} fusion(bf16[2,112,2,1200]{3,1,2,0:T(8,128)(2,1)S(1)} %get-tuple-element.15, bf16[1,1200,2048]{2,1,0:T(8,128)(2,1)} %bitcast.5, bf16[1,1200,2048]{2,1,0:T(8,128)(2,1)} %bitcast.4), kind=kOutput, calls=%fused_computation.8 | convolution fusion | flops 1105920000 | bytes 11321344 | tf_op jit(solution)/shard_map/dot_general | solution.py:45
  143.2 1.3 add.170
  144.5 1.6 collective-permute-start.4
  146.1 1.3 add.186
  147.4 1.8 collective-permute-start.8
  149.2 4.9 %convolution_bitcast_fusion.2 = f32[2,56,2048]{2,1,0:T(8,128)S(1)} fusion(bf16[2,112,2,1200]{3,1,2,0:T(8,128)(2,1)S(1)} %get-tuple-element.17, bf16[1,1200,2048]{2,1,0:T(8,128)(2,1)} %bitcast.5, bf16[1,1200,2048]{2,1,0:T(8,128)(2,1)} %bitcast.4), kind=kOutput, calls=%fused_computation.6 | convolution fusion | flops 1105920000 | bytes 11321344 | tf_op jit(solution)/shard_map/dot_general | solution.py:45
  154.1 4.9 %convolution_bitcast_fusion.3 = f32[2,56,2048]{2,1,0:T(8,128)S(1)} fusion(bf16[2,112,2,1200]{3,1,2,0:T(8,128)(2,1)S(1)} %get-tuple-element.19, bf16[1,1200,2048]{2,1,0:T(8,128)(2,1)} %bitcast.5, bf16[1,1200,2048]{2,1,0:T(8,128)(2,1)} %bitcast.4), kind=kOutput, calls=%fused_computation.7 | convolution fusion | flops 1105920000 | bytes 11321344 | tf_op jit(solution)/shard_map/dot_general | solution.py:45
  159.0 8.4 %collective-permute-done.4 = f32[2,56,2048]{2,1,0:T(8,128)S(1)} collective-permute-done((f32[2,56,2048]{2,1,0:T(8,128)S(1)}, f32[2,56,2048]{2,1,0:T(8,128)S(1)}, u32[]{:S(2)}, u32[]{:S(2)}) %collective-permute-start.4) | collective-permute-done | bytes 917536 | tf_op jit(solution)/shard_map/ppermute | solution.py:57
  167.6 0.3 collective-permute-start.5
  167.9 0.9 collective-permute-done.8
  168.9 3.3 %collective-permute-start.9 = (f32[2,56,2048]{2,1,0:T(8,128)S(1)}, f32[2,56,2048]{2,1,0:T(8,128)S(1)}, u32[]{:S(2)}, u32[]{:S(2)}) collective-permute-start(f32[2,56,2048]{2,1,0:T(8,128)S(1)} %add.187), channel_id=1, source_target_pairs={{0,12},{4,0},{8,4},{12,8},{1,13},{5,1},{9,5},{13,9},{2,14},{6,2},{... | collective-permute-start | bytes 2752520 | tf_op jit(solution)/shard_map/ppermute | solution.py:58
  172.2 6.6 %convolution_bitcast_fusion.1 = f32[4,88,2048]{2,1,0:T(8,128)S(1)} fusion(bf16[4,2,88,2,1200]{4,2,3,1,0:T(8,128)(2,1)S(1)} %bitcast.90, s32[]{:T(128)S(6)} %select_n.117, bf16[1,1200,2048]{2,1,0:T(8,128)(2,1)} %bitcast.5, bf16[1,1200,2048]{2,1,0:T(8,128)(2,1)} %bitcast.4), kind=kOutput, calls=%fused_computation.5 | convolution fusion | flops 3465216000 | bytes 14516228 | tf_op jit(solution)/shard_map/dot_general | solution.py:74
  178.8 10.8 %collective-permute-done.5 = f32[2,56,2048]{2,1,0:T(8,128)S(1)} collective-permute-done((f32[2,56,2048]{2,1,0:T(8,128)S(1)}, f32[2,56,2048]{2,1,0:T(8,128)S(1)}, u32[]{:S(2)}, u32[]{:S(2)}) %collective-permute-start.5) | collective-permute-done | bytes 917536 | tf_op jit(solution)/shard_map/ppermute | solution.py:57
  189.8 0.7 collective-permute-start.6
  190.6 1.5 collective-permute-start.10
  192.2 10.0 %collective-permute-done.11 = f32[4,88,2048]{2,1,0:T(8,128)S(1)} collective-permute-done((f32[4,88,2048]{2,1,0:T(8,128)S(1)}, f32[4,88,2048]{2,1,0:T(8,128)S(1)}, u32[]{:S(2)}, u32[]{:S(2)}) %collective-permute-start.11) | collective-permute-done | bytes 2883616 | tf_op jit(solution)/shard_map/ppermute | solution.py:80
  202.2 0.6 add.190
  203.1 0.8 fusion.19
  203.9 1.5 collective-permute-start.12
  205.4 0.8 fusion.20
  206.2 2.7 collective-permute-start.13
  208.9 0.8 fusion.21
  209.7 1.4 collective-permute-start.14
  211.1 0.9 collective-permute-done.6
  212.0 3.9 %collective-permute-start.18 = (f32[88,1024]{1,0:T(8,128)}, f32[88,1024]{1,0:T(8,128)S(1)}, u32[]{:S(2)}, u32[]{:S(2)}) collective-permute-start(f32[88,1024]{1,0:T(8,128)} %get-tuple-element.27), channel_id=1, source_target_pairs={{0,68},{4,72},{8,76},{12,64},{64,4},{68,8},{72,12},{76,0},{1,69},{... | collective-permute-start | bytes 1081352 | tf_op jit(solution)/shard_map/ppermute | solution.py:104
  216.0 5.9 %collective-permute-done.10 = f32[56,2048]{1,0:T(8,128)S(1)} collective-permute-done((f32[56,2048]{1,0:T(8,128)S(1)}, f32[56,2048]{1,0:T(8,128)S(1)}, u32[]{:S(2)}, u32[]{:S(2)}) %collective-permute-start.10) | collective-permute-done | bytes 458784 | tf_op jit(solution)/shard_map/ppermute | solution.py:66
  221.8 5.4 %collective-permute-start.19 = (f32[88,1024]{1,0:T(8,128)}, f32[88,1024]{1,0:T(8,128)S(1)}, u32[]{:S(2)}, u32[]{:S(2)}) collective-permute-start(f32[88,1024]{1,0:T(8,128)} %get-tuple-element.29), channel_id=1, source_target_pairs={{0,72},{4,76},{8,64},{12,68},{64,8},{68,12},{72,0},{76,4},{1,73},{... | collective-permute-start | bytes 1081352 | tf_op jit(solution)/shard_map/ppermute | solution.py:104
  227.4 1.2 collective-permute-start.20
  228.6 3.0 %collective-permute-start.15 = (f32[56,1024]{1,0:T(8,128)S(1)}, f32[56,1024]{1,0:T(8,128)S(1)}, u32[]{:S(2)}, u32[]{:S(2)}) collective-permute-start(f32[56,1024]{1,0:T(8,128)S(1)} %get-tuple-element.33), channel_id=1, source_target_pairs={{0,64},{64,0},{1,65},{65,1},{2,66},{66,2},{3,67},{67,3},{4,68},{68... | collective-permute-start | bytes 688136 | tf_op jit(solution)/shard_map/ppermute | solution.py:108
  231.6 0.6 collective-permute-start.16
  232.2 20.6 %collective-permute-done.15 = f32[56,1024]{1,0:T(8,128)S(1)} collective-permute-done((f32[56,1024]{1,0:T(8,128)S(1)}, f32[56,1024]{1,0:T(8,128)S(1)}, u32[]{:S(2)}, u32[]{:S(2)}) %collective-permute-start.15) | collective-permute-done | bytes 229408 | tf_op jit(solution)/shard_map/ppermute | solution.py:108
  252.9 0.9 collective-permute-start.17
  254.1 3.8 %collective-permute-done.16 = f32[56,1024]{1,0:T(8,128)} collective-permute-done((f32[56,1024]{1,0:T(8,128)S(1)}, f32[56,1024]{1,0:T(8,128)}, u32[]{:S(2)}, u32[]{:S(2)}) %collective-permute-start.16) | collective-permute-done | bytes 229408 | tf_op jit(solution)/shard_map/ppermute | solution.py:108
  257.9 1.1 pad_maximum_fusion.5
  259.1 5.3 %collective-permute-done.17 = f32[88,1024]{1,0:T(8,128)} collective-permute-done((f32[88,1024]{1,0:T(8,128)S(1)}, f32[88,1024]{1,0:T(8,128)}, u32[]{:S(2)}, u32[]{:S(2)}) %collective-permute-start.17) | collective-permute-done | bytes 360480 | tf_op jit(solution)/shard_map/ppermute | solution.py:94
  264.3 1.2 add_add_fusion
  265.8 1.3 maximum_select_fusion
  (59 shorter events, 3.0 us)
Async XLA Ops:
  6.5 74.2 %all-gather.3.cloned.1.call-start = ((), (), s32[]{:S(2)}) async-start(), calls=%async_computation | async-start | bytes 5734400 | tf_op jit(solution)/shard_map/all_gather | solution.py:34
  13.4 3.0 %collective-permute-start = (bf16[8,50,1200]{2,0,1:T(8,128)(2,1)}, bf16[8,50,1200]{2,0,1:T(8,128)(2,1)}, u32[]{:S(2)}, u32[]{:S(2)}) collective-permute-start(bf16[8,50,1200]{2,0,1:T(8,128)(2,1)} %copy.12), channel_id=1, source_target_pairs={{0,1},{1,0},{2,3},{3,2},{4,5},{5,4},{6,7},{7,6},{8,9},{9,8},{10,11... | collective-permute-start | bytes 2880008 | tf_op jit(solution)/shard_map/ppermute | solution.py:31
  19.5 107.4 %all-gather.5.cloned.1.call-start = ((), (), s32[]{:S(2)}) async-start(), calls=%async_computation.1 | async-start | bytes 4505600 | tf_op jit(solution)/shard_map/all_gather | solution.py:40
  19.6 57.2 %copy-start = (bf16[1200,1024]{1,0:T(8,128)(2,1)S(1)}, bf16[1200,1024]{1,0:T(8,128)(2,1)}, u32[]{:S(2)}) copy-start(bf16[1200,1024]{1,0:T(8,128)(2,1)} %param.5) | copy-start | bytes 7372804
  19.6 57.2 %collective-permute-start.1 = (bf16[1200,1024]{1,0:T(8,128)(2,1)}, bf16[1200,1024]{1,0:T(8,128)(2,1)S(1)}, u32[]{:S(2)}, u32[]{:S(2)}) collective-permute-start(bf16[1200,1024]{1,0:T(8,128)(2,1)} %param.5), channel_id=1, source_target_pairs={{0,64},{64,0},{1,65},{65,1},{2,66},{66,2},{3,67},{67,3},{4,68},{68... | collective-permute-start | bytes 7372808 | tf_op jit(solution)/shard_map/ppermute | solution.py:38
  79.5 8.5 %collective-permute-start.2 = (bf16[1200,2048]{1,0:T(8,128)(2,1)}, bf16[1200,2048]{1,0:T(8,128)(2,1)}, u32[]{:S(2)}, u32[]{:S(2)}) collective-permute-start(bf16[1200,2048]{1,0:T(8,128)(2,1)} %pad_maximum_fusion), channel_id=1, source_target_pairs={{0,1},{1,0},{2,3},{3,2},{4,5},{5,4},{6,7},{7,6},{8,9},{9,8},{10,11... | collective-permute-start | bytes 14745608 | tf_op jit(solution)/shard_map/ppermute | solution.py:41
  94.6 48.6 %collective-permute-start.3 = (f32[2,56,2048]{2,1,0:T(8,128)}, f32[2,56,2048]{2,1,0:T(8,128)}, u32[]{:S(2)}, u32[]{:S(2)}) collective-permute-start(f32[2,56,2048]{2,1,0:T(8,128)} %convolution_bitcast_fusion.9), channel_id=1, source_target_pairs={{0,4},{4,8},{8,12},{12,0},{1,5},{5,9},{9,13},{13,1},{2,6},{6,10},{... | collective-permute-start | bytes 2752520 | tf_op jit(solution)/shard_map/ppermute | solution.py:57
  102.8 43.3 %collective-permute-start.7 = (f32[2,56,2048]{2,1,0:T(8,128)}, f32[2,56,2048]{2,1,0:T(8,128)}, u32[]{:S(2)}, u32[]{:S(2)}) collective-permute-start(f32[2,56,2048]{2,1,0:T(8,128)} %convolution_bitcast_fusion.5), channel_id=1, source_target_pairs={{0,12},{4,0},{8,4},{12,8},{1,13},{5,1},{9,5},{13,9},{2,14},{6,2},{... | collective-permute-start | bytes 2752520 | tf_op jit(solution)/shard_map/ppermute | solution.py:58
  136.7 65.4 %collective-permute-start.11 = (f32[4,88,2048]{2,1,0:T(8,128)S(1)}, f32[4,88,2048]{2,1,0:T(8,128)S(1)}, u32[]{:S(2)}, u32[]{:S(2)}) collective-permute-start(f32[4,88,2048]{2,1,0:T(8,128)S(1)} %convolution_bitcast_fusion), channel_id=1, source_target_pairs={{0,2},{2,0},{1,3},{3,1},{4,6},{6,4},{5,7},{7,5},{8,10},{10,8},{9,1... | collective-permute-start | bytes 8650760 | tf_op jit(solution)/shard_map/ppermute | solution.py:80
  138.3 5.0 %copy-start.3 = (f32[2,56,2048]{2,1,0:T(8,128)S(1)}, f32[2,56,2048]{2,1,0:T(8,128)}, u32[]{:S(2)}) copy-start(f32[2,56,2048]{2,1,0:T(8,128)} %convolution_bitcast_fusion.8) | copy-start | bytes 2752516
  144.5 22.9 %collective-permute-start.4 = (f32[2,56,2048]{2,1,0:T(8,128)S(1)}, f32[2,56,2048]{2,1,0:T(8,128)S(1)}, u32[]{:S(2)}, u32[]{:S(2)}) collective-permute-start(f32[2,56,2048]{2,1,0:T(8,128)S(1)} %add.170), channel_id=1, source_target_pairs={{0,4},{4,8},{8,12},{12,0},{1,5},{5,9},{9,13},{13,1},{2,6},{6,10},{... | collective-permute-start | bytes 2752520 | tf_op jit(solution)/shard_map/ppermute | solution.py:57
  147.4 21.4 %collective-permute-start.8 = (f32[2,56,2048]{2,1,0:T(8,128)S(1)}, f32[2,56,2048]{2,1,0:T(8,128)S(1)}, u32[]{:S(2)}, u32[]{:S(2)}) collective-permute-start(f32[2,56,2048]{2,1,0:T(8,128)S(1)} %add.186), channel_id=1, source_target_pairs={{0,12},{4,0},{8,4},{12,8},{1,13},{5,1},{9,5},{13,9},{2,14},{6,2},{... | collective-permute-start | bytes 2752520 | tf_op jit(solution)/shard_map/ppermute | solution.py:58
  154.1 13.4 %copy-start.2 = (f32[2,56,2048]{2,1,0:T(8,128)S(1)}, f32[2,56,2048]{2,1,0:T(8,128)}, u32[]{:S(2)}) copy-start(f32[2,56,2048]{2,1,0:T(8,128)} %convolution_bitcast_fusion.7) | copy-start | bytes 2752516
  167.6 22.1 %collective-permute-start.5 = (f32[2,56,2048]{2,1,0:T(8,128)S(1)}, f32[2,56,2048]{2,1,0:T(8,128)S(1)}, u32[]{:S(2)}, u32[]{:S(2)}) collective-permute-start(f32[2,56,2048]{2,1,0:T(8,128)S(1)} %add.173), channel_id=1, source_target_pairs={{0,4},{4,8},{8,12},{12,0},{1,5},{5,9},{9,13},{13,1},{2,6},{6,10},{... | collective-permute-start | bytes 2752520 | tf_op jit(solution)/shard_map/ppermute | solution.py:57
  168.9 20.7 %copy-start.1 = (f32[2,56,2048]{2,1,0:T(8,128)S(1)}, f32[2,56,2048]{2,1,0:T(8,128)}, u32[]{:S(2)}) copy-start(f32[2,56,2048]{2,1,0:T(8,128)} %convolution_bitcast_fusion.6) | copy-start | bytes 2752516
  168.9 21.5 %collective-permute-start.9 = (f32[2,56,2048]{2,1,0:T(8,128)S(1)}, f32[2,56,2048]{2,1,0:T(8,128)S(1)}, u32[]{:S(2)}, u32[]{:S(2)}) collective-permute-start(f32[2,56,2048]{2,1,0:T(8,128)S(1)} %add.187), channel_id=1, source_target_pairs={{0,12},{4,0},{8,4},{12,8},{1,13},{5,1},{9,5},{13,9},{2,14},{6,2},{... | collective-permute-start | bytes 2752520 | tf_op jit(solution)/shard_map/ppermute | solution.py:58
  189.8 22.2 %collective-permute-start.6 = (f32[56,2048]{1,0:T(8,128)S(1)}, f32[56,2048]{1,0:T(8,128)S(1)}, u32[]{:S(2)}, u32[]{:S(2)}) collective-permute-start(f32[56,2048]{1,0:T(8,128)S(1)} %dynamic-slice_bitcast_fusion.11), channel_id=1, source_target_pairs={{0,2},{2,0},{1,3},{3,1},{4,6},{6,4},{5,7},{7,5},{8,10},{10,8},{9,1... | collective-permute-start | bytes 1376264 | tf_op jit(solution)/shard_map/ppermute | solution.py:66
  190.6 31.2 %collective-permute-start.10 = (f32[56,2048]{1,0:T(8,128)S(1)}, f32[56,2048]{1,0:T(8,128)S(1)}, u32[]{:S(2)}, u32[]{:S(2)}) collective-permute-start(f32[56,2048]{1,0:T(8,128)S(1)} %dynamic-slice_bitcast_fusion.10), channel_id=1, source_target_pairs={{0,2},{2,0},{1,3},{3,1},{4,6},{6,4},{5,7},{7,5},{8,10},{10,8},{9,1... | collective-permute-start | bytes 1376264 | tf_op jit(solution)/shard_map/ppermute | solution.py:66
  203.9 23.5 %collective-permute-start.12 = (f32[88,1024]{1,0:T(8,128)S(1)}, f32[88,1024]{1,0:T(8,128)S(1)}, u32[]{:S(2)}, u32[]{:S(2)}) collective-permute-start(f32[88,1024]{1,0:T(8,128)S(1)} %get-tuple-element.26), channel_id=1, source_target_pairs={{0,4},{4,8},{8,12},{12,0},{1,5},{5,9},{9,13},{13,1},{2,6},{6,10},{... | collective-permute-start | bytes 1081352 | tf_op jit(solution)/shard_map/ppermute | solution.py:103
  206.2 22.4 %collective-permute-start.13 = (f32[88,1024]{1,0:T(8,128)S(1)}, f32[88,1024]{1,0:T(8,128)S(1)}, u32[]{:S(2)}, u32[]{:S(2)}) collective-permute-start(f32[88,1024]{1,0:T(8,128)S(1)} %get-tuple-element.28), channel_id=1, source_target_pairs={{0,8},{4,12},{8,0},{12,4},{1,9},{5,13},{9,1},{13,5},{2,10},{6,14},... | collective-permute-start | bytes 1081352 | tf_op jit(solution)/shard_map/ppermute | solution.py:103
  209.7 21.9 %collective-permute-start.14 = (f32[88,1024]{1,0:T(8,128)S(1)}, f32[88,1024]{1,0:T(8,128)S(1)}, u32[]{:S(2)}, u32[]{:S(2)}) collective-permute-start(f32[88,1024]{1,0:T(8,128)S(1)} %get-tuple-element.30), channel_id=1, source_target_pairs={{0,12},{4,0},{8,4},{12,8},{1,13},{5,1},{9,5},{13,9},{2,14},{6,2},{... | collective-permute-start | bytes 1081352 | tf_op jit(solution)/shard_map/ppermute | solution.py:103
  212.0 47.1 %collective-permute-start.18 = (f32[88,1024]{1,0:T(8,128)}, f32[88,1024]{1,0:T(8,128)S(1)}, u32[]{:S(2)}, u32[]{:S(2)}) collective-permute-start(f32[88,1024]{1,0:T(8,128)} %get-tuple-element.27), channel_id=1, source_target_pairs={{0,68},{4,72},{8,76},{12,64},{64,4},{68,8},{72,12},{76,0},{1,69},{... | collective-permute-start | bytes 1081352 | tf_op jit(solution)/shard_map/ppermute | solution.py:104
  221.8 37.2 %collective-permute-start.19 = (f32[88,1024]{1,0:T(8,128)}, f32[88,1024]{1,0:T(8,128)S(1)}, u32[]{:S(2)}, u32[]{:S(2)}) collective-permute-start(f32[88,1024]{1,0:T(8,128)} %get-tuple-element.29), channel_id=1, source_target_pairs={{0,72},{4,76},{8,64},{12,68},{64,8},{68,12},{72,0},{76,4},{1,73},{... | collective-permute-start | bytes 1081352 | tf_op jit(solution)/shard_map/ppermute | solution.py:104
  227.4 31.7 %collective-permute-start.20 = (f32[88,1024]{1,0:T(8,128)}, f32[88,1024]{1,0:T(8,128)}, u32[]{:S(2)}, u32[]{:S(2)}) collective-permute-start(f32[88,1024]{1,0:T(8,128)} %get-tuple-element.31), channel_id=1, source_target_pairs={{0,76},{4,64},{8,68},{12,72},{64,12},{68,0},{72,4},{76,8},{1,77},{... | collective-permute-start | bytes 1081352 | tf_op jit(solution)/shard_map/ppermute | solution.py:104
  228.6 24.3 %collective-permute-start.15 = (f32[56,1024]{1,0:T(8,128)S(1)}, f32[56,1024]{1,0:T(8,128)S(1)}, u32[]{:S(2)}, u32[]{:S(2)}) collective-permute-start(f32[56,1024]{1,0:T(8,128)S(1)} %get-tuple-element.33), channel_id=1, source_target_pairs={{0,64},{64,0},{1,65},{65,1},{2,66},{66,2},{3,67},{67,3},{4,68},{68... | collective-permute-start | bytes 688136 | tf_op jit(solution)/shard_map/ppermute | solution.py:108
  231.6 26.3 %collective-permute-start.16 = (f32[56,1024]{1,0:T(8,128)S(1)}, f32[56,1024]{1,0:T(8,128)}, u32[]{:S(2)}, u32[]{:S(2)}) collective-permute-start(f32[56,1024]{1,0:T(8,128)S(1)} %get-tuple-element.35), channel_id=1, source_target_pairs={{0,64},{64,0},{1,65},{65,1},{2,66},{66,2},{3,67},{67,3},{4,68},{68... | collective-permute-start | bytes 688136 | tf_op jit(solution)/shard_map/ppermute | solution.py:108
  252.9 0.9 copy-start.4
  252.9 11.4 %collective-permute-start.17 = (f32[88,1024]{1,0:T(8,128)S(1)}, f32[88,1024]{1,0:T(8,128)}, u32[]{:S(2)}, u32[]{:S(2)}) collective-permute-start(f32[88,1024]{1,0:T(8,128)S(1)} %get-tuple-element.25), channel_id=1, source_target_pairs={{0,64},{64,0},{1,65},{65,1},{2,66},{66,2},{3,67},{67,3},{4,68},{68... | collective-permute-start | bytes 1081352 | tf_op jit(solution)/shard_map/ppermute | solution.py:94
Sparse Core Ops, SparseCore 0:
  19.7 54.1 all-gather.2
  80.7 46.1 all-gather.4

commit v16 on v12

--- a/solution.py
+++ b/solution.py
@@ -77,7 +77,12 @@
         return lax.optimization_barrier(product)
 
     late_there = late_block(1 - xi)
-    late_sum = late_block(xi) + lax.ppermute(late_there, "xl", SWAP)
+    late_here = late_block(xi)
+    cut_rows = 8 * (x_rows // 16)
+    late_parts = [
+        late_here[:, rows] + lax.ppermute(late_there[:, rows], "xl", SWAP)
+        for rows in (slice(0, cut_rows), slice(cut_rows, x_rows))
+    ]
 
     def pick(parts):
         return lambda y_owner: lax.dynamic_index_in_dim(parts, y_owner % ny, 0, keepdims=False)
@@ -88,11 +93,13 @@
         lambda y_owner: block(y_owner, 0, y_half),
         lambda y_owner: block(y_owner, y_half, y_rows),
     )
-    late_done = pick(late_sum)(yi)
-    for hop in range(1, ny):
-        to_owner = [(i, (i + hop) % ny) for i in range(ny)]
-        late_done = late_done + lax.ppermute(pick(late_sum)(yi + hop), "y", to_owner)
-    pieces = [pair_sum(early[0]), pair_sum(early[1]), late_done]
+    pieces = [pair_sum(early[0]), pair_sum(early[1])]
+    for late_sum in late_parts:
+        late_done = pick(late_sum)(yi)
+        for hop in range(1, ny):
+            to_owner = [(i, (i + hop) % ny) for i in range(ny)]
+            late_done = late_done + lax.ppermute(pick(late_sum)(yi + hop), "y", to_owner)
+        pieces.append(late_done)
 
     kept = [piece[:, :width] for piece in pieces]
     came = [lax.ppermute(piece[:, width:], "xh", SWAP) for piece in pieces]

time: 256 us -> 287 us (1.12)
  waiting for transfers between devices: 120 us -> 134 us
  starting transfers between devices: 32.1 us -> 40.6 us
  other arithmetic: 10.1 us -> 16.7 us
    ppermute x1 -> x2, waiting for transfers between devices: 10 us -> 29.3 us  [local(): lax.ppermute(late_there[:, rows], 'xl', SWAP)]
    ppermute x3, waiting for transfers between devices: 0.9 us -> 11.6 us  [ring(): got_back = lax.ppermute(acc_back, 'y', to_prev)]
    ppermute x3, waiting for transfers between devices: 19.2 us -> 8.58 us  [ring(): got_ahead = lax.ppermute(acc_ahead, 'y', to_next)]
    ppermute x3 -> x6, starting transfers between devices: 5.71 us -> 12.4 us  [local(): lax.ppermute(pick(late_sum)(yi + hop), 'y', to_owner)]
    ppermute x1, waiting for transfers between devices: 53.7 us -> 50.1 us  [local(): lax.ppermute(amplitudes, 'xh', SWAP)]
    ppermute x3 -> x4, waiting for transfers between devices: 6.97 us -> 8.01 us  [local(): came = [lax.ppermute(piece[:, width:], 'xh', SWAP) for piece in pieces]]
    ppermute x3 -> x6, waiting for transfers between devices: 11.1 us -> 12.1 us  [local(): lax.ppermute(pick(late_sum)(yi + hop), 'y', to_owner)]
    ppermute x3 -> x4, starting transfers between devices: 9.18 us -> 9.22 us  [local(): came = [lax.ppermute(piece[:, width:], 'xh', SWAP) for piece in pieces]]
  transfers between devices with their start and end apart: 20 -> 25, of which waited for: 12 -> 13; matrix products, arithmetic and copies ran while one was open for 31% -> 31% of each run, Pallas kernels for 0% -> 0%
where the time goes in v16:
time: 287 us; the launch traced here: 286 us
  waiting for transfers between devices  134 us (47%)
  matrix products  60.8 us (21%)
  starting transfers between devices  40.6 us (14%)
  local copies, waits for them, and re-layouts  19.9 us (7%)
  other arithmetic  16.7 us (6%)
  between operations  13.9 us (5%)
    ppermute x1, waiting for transfers between devices, local(): lax.ppermute(amplitudes, 'xh', SWAP)  50.1 us
    dot_general x8, matrix products, block(): lax.dot_general(lhs[:, low:high], amp, (((2, 3), (0, 1)), ((), ())), pref...  47.5 us
    ppermute x2, waiting for transfers between devices, local(): lax.ppermute(late_there[:, rows], 'xl', SWAP)  29.3 us
    dot_general x2, matrix products, late_block(): lax.dot_general(lhs, amp, (((2, 3), (0, 1)), ((), ())), preferred_element...  13.3 us
    ppermute x6, starting transfers between devices, local(): lax.ppermute(pick(late_sum)(yi + hop), 'y', to_owner)  12.4 us
    ppermute x6, waiting for transfers between devices, local(): lax.ppermute(pick(late_sum)(yi + hop), 'y', to_owner)  12.1 us
    ppermute x2, waiting for transfers between devices, pair_sum(): return here + lax.ppermute(there, 'xl', SWAP)  11.6 us
    ppermute x3, waiting for transfers between devices, ring(): got_back = lax.ppermute(acc_back, 'y', to_prev)  11.6 us
  transfers between devices with their start and end apart: 25, of which 13 were waited for; matrix products, arithmetic and copies ran while one was open for 31% of the time, Pallas kernels for 0%

profile of v16, /device:TPU:0, one launch (start us, length us, event | category | flops | bytes accessed | tf_op | source)
XLA Modules:
  0.0 286.1 jit_solution(971659888989905016)
XLA Ops:
  6.5 0.7 dynamic_slice.76
  7.3 1.2 sort.17
  8.9 2.6 reshape.35
  11.4 0.6 gather_fusion.1
  12.3 1.1 copy.12
  13.4 3.1 %collective-permute-start.1 = (bf16[1200,1024]{1,0:T(8,128)(2,1)}, bf16[1200,1024]{1,0:T(8,128)(2,1)}, u32[]{:S(2)}, u32[]{:S(2)}) collective-permute-start(bf16[1200,1024]{1,0:T(8,128)(2,1)} %param.5), channel_id=1, source_target_pairs={{0,64},{64,0},{1,65},{65,1},{2,66},{66,2},{3,67},{67,3},{4,68},{68... | collective-permute-start | bytes 7372808 | tf_op jit(solution)/shard_map/ppermute | solution.py:38
  16.5 0.6 gather_fusion
  17.4 1.4 copy.35
  18.9 1.6 copy.14
  20.6 0.3 pad_maximum_fusion.1
  20.9 50.1 %collective-permute-done.1 = bf16[1200,1024]{1,0:T(8,128)(2,1)} collective-permute-done((bf16[1200,1024]{1,0:T(8,128)(2,1)}, bf16[1200,1024]{1,0:T(8,128)(2,1)}, u32[]{:S(2)}, u32[]{:S(2)}) %collective-permute-start.1) | collective-permute-done | bytes 2457632 | tf_op jit(solution)/shard_map/ppermute | solution.py:38
  71.0 5.3 %pad_maximum_fusion = bf16[1200,2048]{1,0:T(8,128)(2,1)} fusion(bf16[1200,1024]{1,0:T(8,128)(2,1)} %collective-permute-done.1, bf16[1200,1024]{1,0:T(8,128)(2,1)} %param.5), kind=kLoop, calls=%fused_computation.3 | loop fusion | flops 9830400 | bytes 9830400 | tf_op jit(solution)/shard_map/concatenate | solution.py:38
  76.3 1.1 copy.21
  77.5 3.8 %copy.33 = bf16[8,112,2,1200]{3,1,2,0:T(8,128)(2,1)S(1)} copy(bf16[8,112,2,1200]{3,0,2,1:T(8,128)(2,1)} %all-gather.3.cloned.1.call-done) | data formatting | bytes 8601600 | tf_op jit(solution)/shard_map/reshape | solution.py:36
  81.3 0.6 dynamic-slice_bitcast_fusion.3
  81.8 3.0 %collective-permute-done.2 = bf16[1200,2048]{1,0:T(8,128)(2,1)} collective-permute-done((bf16[1200,2048]{1,0:T(8,128)(2,1)}, bf16[1200,2048]{1,0:T(8,128)(2,1)}, u32[]{:S(2)}, u32[]{:S(2)}) %collective-permute-start.2) | collective-permute-done | bytes 4915232 | tf_op jit(solution)/shard_map/ppermute | solution.py:41
  84.8 6.5 %convolution_bitcast_fusion.9 = f32[2,56,2048]{2,1,0:T(8,128)} fusion(bf16[2,112,2,1200]{3,1,2,0:T(8,128)(2,1)S(1)} %get-tuple-element.19, bf16[1,1200,2048]{2,1,0:T(8,128)(2,1)} %bitcast.5, bf16[1,1200,2048]{2,1,0:T(8,128)(2,1)} %bitcast.4), kind=kOutput, calls=%fused_computation.13 | convolution fusion | flops 1105920000 | bytes 11321344 | tf_op jit(solution)/shard_map/dot_general | solution.py:45
  91.4 1.7 collective-permute-start.3
  93.1 6.5 %convolution_bitcast_fusion.8 = f32[2,56,2048]{2,1,0:T(8,128)} fusion(bf16[2,112,2,1200]{3,1,2,0:T(8,128)(2,1)S(1)} %get-tuple-element.18, bf16[1,1200,2048]{2,1,0:T(8,128)(2,1)} %bitcast.5, bf16[1,1200,2048]{2,1,0:T(8,128)(2,1)} %bitcast.4), kind=kOutput, calls=%fused_computation.12 | convolution fusion | flops 1105920000 | bytes 11321344 | tf_op jit(solution)/shard_map/dot_general | solution.py:45
  99.6 6.6 %convolution_bitcast_fusion.7 = f32[2,56,2048]{2,1,0:T(8,128)} fusion(bf16[2,112,2,1200]{3,1,2,0:T(8,128)(2,1)S(1)} %get-tuple-element.14, bf16[1,1200,2048]{2,1,0:T(8,128)(2,1)} %bitcast.5, bf16[1,1200,2048]{2,1,0:T(8,128)(2,1)} %bitcast.4), kind=kOutput, calls=%fused_computation.11 | convolution fusion | flops 1105920000 | bytes 11321344 | tf_op jit(solution)/shard_map/dot_general | solution.py:45
  106.2 6.6 %convolution_bitcast_fusion.6 = f32[2,56,2048]{2,1,0:T(8,128)} fusion(bf16[2,112,2,1200]{3,1,2,0:T(8,128)(2,1)S(1)} %get-tuple-element.17, bf16[1,1200,2048]{2,1,0:T(8,128)(2,1)} %bitcast.5, bf16[1,1200,2048]{2,1,0:T(8,128)(2,1)} %bitcast.4), kind=kOutput, calls=%fused_computation.10 | convolution fusion | flops 1105920000 | bytes 11321344 | tf_op jit(solution)/shard_map/dot_general | solution.py:45
  112.8 5.0 %convolution_bitcast_fusion.2 = f32[2,56,2048]{2,1,0:T(8,128)S(1)} fusion(bf16[2,112,2,1200]{3,1,2,0:T(8,128)(2,1)S(1)} %get-tuple-element.17, bf16[1,1200,2048]{2,1,0:T(8,128)(2,1)} %bitcast.5, bf16[1,1200,2048]{2,1,0:T(8,128)(2,1)} %bitcast.4), kind=kOutput, calls=%fused_computation.6 | convolution fusion | flops 1105920000 | bytes 11321344 | tf_op jit(solution)/shard_map/dot_general | solution.py:45
  117.8 4.9 %convolution_bitcast_fusion.3 = f32[2,56,2048]{2,1,0:T(8,128)S(1)} fusion(bf16[2,112,2,1200]{3,1,2,0:T(8,128)(2,1)S(1)} %get-tuple-element.19, bf16[1,1200,2048]{2,1,0:T(8,128)(2,1)} %bitcast.5, bf16[1,1200,2048]{2,1,0:T(8,128)(2,1)} %bitcast.4), kind=kOutput, calls=%fused_computation.7 | convolution fusion | flops 1105920000 | bytes 11321344 | tf_op jit(solution)/shard_map/dot_general | solution.py:45
  122.7 6.5 %convolution_bitcast_fusion.4 = f32[2,56,2048]{2,1,0:T(8,128)} fusion(bf16[2,112,2,1200]{3,1,2,0:T(8,128)(2,1)S(1)} %get-tuple-element.15, bf16[1,1200,2048]{2,1,0:T(8,128)(2,1)} %bitcast.5, bf16[1,1200,2048]{2,1,0:T(8,128)(2,1)} %bitcast.4), kind=kOutput, calls=%fused_computation.8 | convolution fusion | flops 1105920000 | bytes 11321344 | tf_op jit(solution)/shard_map/dot_general | solution.py:45
  129.2 3.1 %copy.22 = bf16[8,88,2,1200]{3,1,2,0:T(8,128)(2,1)S(1)} copy(bf16[8,88,2,1200]{3,0,2,1:T(8,128)(2,1)} %all-gather.5.cloned.1.call-done) | data formatting | bytes 6758400 | tf_op jit(solution)/shard_map/all_gather | solution.py:40
  132.3 6.7 %convolution_bitcast_fusion = f32[4,88,2048]{2,1,0:T(8,128)S(1)} fusion(bf16[4,2,88,2,1200]{4,2,3,1,0:T(8,128)(2,1)S(1)} %bitcast.105, s32[]{:T(128)S(6)} %select_n.131, bf16[1,1200,2048]{2,1,0:T(8,128)(2,1)} %bitcast.5, bf16[1,1200,2048]{2,1,0:T(8,128)(2,1)} %bitcast.4), kind=kOutput, calls=%fused_computation.4 | convolution fusion | flops 3465216000 | bytes 14516228 | tf_op jit(solution)/shard_map/dot_general | solution.py:74
  139.1 1.6 collective-permute-start.11
  140.6 4.9 %convolution_bitcast_fusion.5 = f32[2,56,2048]{2,1,0:T(8,128)S(1)} fusion(bf16[2,112,2,1200]{3,1,2,0:T(8,128)(2,1)S(1)} %get-tuple-element.16, bf16[1,1200,2048]{2,1,0:T(8,128)(2,1)} %bitcast.5, bf16[1,1200,2048]{2,1,0:T(8,128)(2,1)} %bitcast.4), kind=kOutput, calls=%fused_computation.9 | convolution fusion | flops 1105920000 | bytes 11321344 | tf_op jit(solution)/shard_map/dot_general | solution.py:45
  145.5 1.8 collective-permute-start.7
  147.4 0.8 collective-permute-start.15
  148.2 6.6 %convolution_bitcast_fusion.1 = f32[4,88,2048]{2,1,0:T(8,128)S(1)} fusion(bf16[4,2,88,2,1200]{4,2,3,1,0:T(8,128)(2,1)S(1)} %bitcast.106, s32[]{:T(128)S(6)} %select_n.130, bf16[1,1200,2048]{2,1,0:T(8,128)(2,1)} %bitcast.5, bf16[1,1200,2048]{2,1,0:T(8,128)(2,1)} %bitcast.4), kind=kOutput, calls=%fused_computation.5 | convolution fusion | flops 3465216000 | bytes 14516228 | tf_op jit(solution)/shard_map/dot_general | solution.py:74
  154.9 1.4 add.185
  156.3 0.5 collective-permute-start.4
  156.7 10.7 %collective-permute-done.7 = f32[2,56,2048]{2,1,0:T(8,128)S(1)} collective-permute-done((f32[2,56,2048]{2,1,0:T(8,128)S(1)}, f32[2,56,2048]{2,1,0:T(8,128)S(1)}, u32[]{:S(2)}, u32[]{:S(2)}) %collective-permute-start.7) | collective-permute-done | bytes 917536 | tf_op jit(solution)/shard_map/ppermute | solution.py:58
  167.5 3.1 %collective-permute-start.8 = (f32[2,56,2048]{2,1,0:T(8,128)S(1)}, f32[2,56,2048]{2,1,0:T(8,128)S(1)}, u32[]{:S(2)}, u32[]{:S(2)}) collective-permute-start(f32[2,56,2048]{2,1,0:T(8,128)S(1)} %add.201), channel_id=1, source_target_pairs={{0,12},{4,0},{8,4},{12,8},{1,13},{5,1},{9,5},{13,9},{2,14},{6,2},{... | collective-permute-start | bytes 2752520 | tf_op jit(solution)/shard_map/ppermute | solution.py:58
  171.1 1.7 collective-permute-start.12
  172.7 1.5 collective-permute-start.13
  174.2 29.2 %collective-permute-done.15 = f32[4,48,2048]{2,1,0:T(8,128)S(1)} collective-permute-done((f32[4,48,2048]{2,1,0:T(8,128)S(1)}, f32[4,48,2048]{2,1,0:T(8,128)S(1)}, u32[]{:S(2)}, u32[]{:S(2)}) %collective-permute-start.15) | collective-permute-done | bytes 1572896 | tf_op jit(solution)/shard_map/ppermute | solution.py:83
  203.4 1.9 collective-permute-start.14
  205.6 0.2 collective-permute-start.16
  205.8 3.0 %collective-permute-start.17 = (f32[48,2048]{1,0:T(8,128)S(1)}, f32[48,2048]{1,0:T(8,128)S(1)}, u32[]{:S(2)}, u32[]{:S(2)}) collective-permute-start(f32[48,2048]{1,0:T(8,128)S(1)} %get-tuple-element.22), channel_id=1, source_target_pairs={{0,8},{4,12},{8,0},{12,4},{1,9},{5,13},{9,1},{13,5},{2,10},{6,14},... | collective-permute-start | bytes 1179656 | tf_op jit(solution)/shard_map/ppermute | solution.py:101
  208.8 10.4 %collective-permute-done.14 = f32[40,2048]{1,0:T(8,128)S(1)} collective-permute-done((f32[40,2048]{1,0:T(8,128)S(1)}, f32[40,2048]{1,0:T(8,128)S(1)}, u32[]{:S(2)}, u32[]{:S(2)}) %collective-permute-start.14) | collective-permute-done | bytes 327712 | tf_op jit(solution)/shard_map/ppermute | solution.py:101
  219.2 4.2 %collective-permute-start.18 = (f32[48,2048]{1,0:T(8,128)S(1)}, f32[48,2048]{1,0:T(8,128)S(1)}, u32[]{:S(2)}, u32[]{:S(2)}) collective-permute-start(f32[48,2048]{1,0:T(8,128)S(1)} %get-tuple-element.21), channel_id=1, source_target_pairs={{0,12},{4,0},{8,4},{12,8},{1,13},{5,1},{9,5},{13,9},{2,14},{6,2},{... | collective-permute-start | bytes 1179656 | tf_op jit(solution)/shard_map/ppermute | solution.py:101
  223.7 0.7 fusion.24
  224.4 2.6 collective-permute-start.21
  227.0 1.1 add.202
  228.1 3.2 %collective-permute-start.9 = (f32[2,56,2048]{2,1,0:T(8,128)}, f32[2,56,2048]{2,1,0:T(8,128)}, u32[]{:S(2)}, u32[]{:S(2)}) collective-permute-start(f32[2,56,2048]{2,1,0:T(8,128)} %add.202), channel_id=1, source_target_pairs={{0,12},{4,0},{8,4},{12,8},{1,13},{5,1},{9,5},{13,9},{2,14},{6,2},{... | collective-permute-start | bytes 2752520 | tf_op jit(solution)/shard_map/ppermute | solution.py:58
  231.3 1.6 collective-permute-done.18
  233.0 0.7 fusion.23
  233.7 2.6 collective-permute-start.22
  236.3 8.6 %collective-permute-done.5 = f32[2,56,2048]{2,1,0:T(8,128)S(1)} collective-permute-done((f32[2,56,2048]{2,1,0:T(8,128)S(1)}, f32[2,56,2048]{2,1,0:T(8,128)S(1)}, u32[]{:S(2)}, u32[]{:S(2)}) %collective-permute-start.5) | collective-permute-done | bytes 917536 | tf_op jit(solution)/shard_map/ppermute | solution.py:57
  245.1 1.5 collective-permute-start.6
  246.7 1.0 pad_maximum_fusion.7
  247.8 0.9 collective-permute-done.9
  248.7 1.3 add.203
  250.0 1.6 collective-permute-start.10
  251.6 6.9 %collective-permute-done.6 = f32[56,2048]{1,0:T(8,128)} collective-permute-done((f32[56,2048]{1,0:T(8,128)S(1)}, f32[56,2048]{1,0:T(8,128)}, u32[]{:S(2)}, u32[]{:S(2)}) %collective-permute-start.6) | collective-permute-done | bytes 458784 | tf_op jit(solution)/shard_map/ppermute | solution.py:66
  258.5 1.1 bitcast_add_fusion.1
  259.6 4.7 %collective-permute-done.10 = f32[56,2048]{1,0:T(8,128)S(1)} collective-permute-done((f32[56,2048]{1,0:T(8,128)S(1)}, f32[56,2048]{1,0:T(8,128)S(1)}, u32[]{:S(2)}, u32[]{:S(2)}) %collective-permute-start.10) | collective-permute-done | bytes 458784 | tf_op jit(solution)/shard_map/ppermute | solution.py:66
  264.4 3.9 %collective-permute-start.19 = (f32[56,1024]{1,0:T(8,128)S(1)}, f32[56,1024]{1,0:T(8,128)S(1)}, u32[]{:S(2)}, u32[]{:S(2)}) collective-permute-start(f32[56,1024]{1,0:T(8,128)S(1)} %get-tuple-element.27), channel_id=1, source_target_pairs={{0,64},{64,0},{1,65},{65,1},{2,66},{66,2},{3,67},{67,3},{4,68},{68... | collective-permute-start | bytes 688136 | tf_op jit(solution)/shard_map/ppermute | solution.py:105
  268.7 5.4 %collective-permute-done.19 = f32[56,1024]{1,0:T(8,128)S(1)} collective-permute-done((f32[56,1024]{1,0:T(8,128)S(1)}, f32[56,1024]{1,0:T(8,128)S(1)}, u32[]{:S(2)}, u32[]{:S(2)}) %collective-permute-start.19) | collective-permute-done | bytes 229408 | tf_op jit(solution)/shard_map/ppermute | solution.py:105
  274.2 2.6 collective-permute-done.20
  276.7 1.0 pad_maximum_fusion.5
  278.0 1.3 maximum_select_fusion
  (66 shorter events, 3.4 us)
Async XLA Ops:
  6.5 71.0 %all-gather.3.cloned.1.call-start = ((), (), s32[]{:S(2)}) async-start(), calls=%async_computation | async-start | bytes 5734400 | tf_op jit(solution)/shard_map/all_gather | solution.py:34
  13.4 4.0 %collective-permute-start = (bf16[8,50,1200]{2,0,1:T(8,128)(2,1)}, bf16[8,50,1200]{2,0,1:T(8,128)(2,1)}, u32[]{:S(2)}, u32[]{:S(2)}) collective-permute-start(bf16[8,50,1200]{2,0,1:T(8,128)(2,1)} %copy.12), channel_id=1, source_target_pairs={{0,1},{1,0},{2,3},{3,2},{4,5},{5,4},{6,7},{7,6},{8,9},{9,8},{10,11... | collective-permute-start | bytes 2880008 | tf_op jit(solution)/shard_map/ppermute | solution.py:31
  13.4 57.6 %collective-permute-start.1 = (bf16[1200,1024]{1,0:T(8,128)(2,1)}, bf16[1200,1024]{1,0:T(8,128)(2,1)}, u32[]{:S(2)}, u32[]{:S(2)}) collective-permute-start(bf16[1200,1024]{1,0:T(8,128)(2,1)} %param.5), channel_id=1, source_target_pairs={{0,64},{64,0},{1,65},{65,1},{2,66},{66,2},{3,67},{67,3},{4,68},{68... | collective-permute-start | bytes 7372808 | tf_op jit(solution)/shard_map/ppermute | solution.py:38
  20.5 108.6 %all-gather.5.cloned.1.call-start = ((), (), s32[]{:S(2)}) async-start(), calls=%async_computation.1 | async-start | bytes 4505600 | tf_op jit(solution)/shard_map/all_gather | solution.py:40
  76.3 8.5 %collective-permute-start.2 = (bf16[1200,2048]{1,0:T(8,128)(2,1)}, bf16[1200,2048]{1,0:T(8,128)(2,1)}, u32[]{:S(2)}, u32[]{:S(2)}) collective-permute-start(bf16[1200,2048]{1,0:T(8,128)(2,1)} %pad_maximum_fusion), channel_id=1, source_target_pairs={{0,1},{1,0},{2,3},{3,2},{4,5},{5,4},{6,7},{7,6},{8,9},{9,8},{10,11... | collective-permute-start | bytes 14745608 | tf_op jit(solution)/shard_map/ppermute | solution.py:41
  91.4 63.5 %collective-permute-start.3 = (f32[2,56,2048]{2,1,0:T(8,128)}, f32[2,56,2048]{2,1,0:T(8,128)}, u32[]{:S(2)}, u32[]{:S(2)}) collective-permute-start(f32[2,56,2048]{2,1,0:T(8,128)} %convolution_bitcast_fusion.9), channel_id=1, source_target_pairs={{0,4},{4,8},{8,12},{12,0},{1,5},{5,9},{9,13},{13,1},{2,6},{6,10},{... | collective-permute-start | bytes 2752520 | tf_op jit(solution)/shard_map/ppermute | solution.py:57
  139.1 31.7 %collective-permute-start.11 = (f32[4,40,2048]{2,1,0:T(8,128)S(1)}, f32[4,40,2048]{2,1,0:T(8,128)S(1)}, u32[]{:S(2)}, u32[]{:S(2)}) collective-permute-start(f32[4,40,2048]{2,1,0:T(8,128)S(1)} %slice.105), channel_id=1, source_target_pairs={{0,2},{2,0},{1,3},{3,1},{4,6},{6,4},{5,7},{7,5},{8,10},{10,8},{9,1... | collective-permute-start | bytes 3932168 | tf_op jit(solution)/shard_map/ppermute | solution.py:83
  145.5 21.9 %collective-permute-start.7 = (f32[2,56,2048]{2,1,0:T(8,128)S(1)}, f32[2,56,2048]{2,1,0:T(8,128)S(1)}, u32[]{:S(2)}, u32[]{:S(2)}) collective-permute-start(f32[2,56,2048]{2,1,0:T(8,128)S(1)} %convolution_bitcast_fusion.5), channel_id=1, source_target_pairs={{0,12},{4,0},{8,4},{12,8},{1,13},{5,1},{9,5},{13,9},{2,14},{6,2},{... | collective-permute-start | bytes 2752520 | tf_op jit(solution)/shard_map/ppermute | solution.py:58
  147.4 7.4 %copy-start.3 = (f32[2,56,2048]{2,1,0:T(8,128)S(1)}, f32[2,56,2048]{2,1,0:T(8,128)}, u32[]{:S(2)}) copy-start(f32[2,56,2048]{2,1,0:T(8,128)} %convolution_bitcast_fusion.8) | copy-start | bytes 2752516
  147.4 55.9 %collective-permute-start.15 = (f32[4,48,2048]{2,1,0:T(8,128)S(1)}, f32[4,48,2048]{2,1,0:T(8,128)S(1)}, u32[]{:S(2)}, u32[]{:S(2)}) collective-permute-start(f32[4,48,2048]{2,1,0:T(8,128)S(1)} %slice.108), channel_id=1, source_target_pairs={{0,2},{2,0},{1,3},{3,1},{4,6},{6,4},{5,7},{7,5},{8,10},{10,8},{9,1... | collective-permute-start | bytes 4718600 | tf_op jit(solution)/shard_map/ppermute | solution.py:83
  154.8 12.6 %copy-start.2 = (f32[2,56,2048]{2,1,0:T(8,128)S(1)}, f32[2,56,2048]{2,1,0:T(8,128)}, u32[]{:S(2)}) copy-start(f32[2,56,2048]{2,1,0:T(8,128)} %convolution_bitcast_fusion.4) | copy-start | bytes 2752516
  156.3 67.2 %collective-permute-start.4 = (f32[2,56,2048]{2,1,0:T(8,128)S(1)}, f32[2,56,2048]{2,1,0:T(8,128)S(1)}, u32[]{:S(2)}, u32[]{:S(2)}) collective-permute-start(f32[2,56,2048]{2,1,0:T(8,128)S(1)} %add.185), channel_id=1, source_target_pairs={{0,4},{4,8},{8,12},{12,0},{1,5},{5,9},{9,13},{13,1},{2,6},{6,10},{... | collective-permute-start | bytes 2752520 | tf_op jit(solution)/shard_map/ppermute | solution.py:57
  167.5 56.8 %collective-permute-start.8 = (f32[2,56,2048]{2,1,0:T(8,128)S(1)}, f32[2,56,2048]{2,1,0:T(8,128)S(1)}, u32[]{:S(2)}, u32[]{:S(2)}) collective-permute-start(f32[2,56,2048]{2,1,0:T(8,128)S(1)} %add.201), channel_id=1, source_target_pairs={{0,12},{4,0},{8,4},{12,8},{1,13},{5,1},{9,5},{13,9},{2,14},{6,2},{... | collective-permute-start | bytes 2752520 | tf_op jit(solution)/shard_map/ppermute | solution.py:58
  171.1 34.5 %collective-permute-start.12 = (f32[40,2048]{1,0:T(8,128)S(1)}, f32[40,2048]{1,0:T(8,128)S(1)}, u32[]{:S(2)}, u32[]{:S(2)}) collective-permute-start(f32[40,2048]{1,0:T(8,128)S(1)} %get-tuple-element.23), channel_id=1, source_target_pairs={{0,4},{4,8},{8,12},{12,0},{1,5},{5,9},{9,13},{13,1},{2,6},{6,10},{... | collective-permute-start | bytes 983048 | tf_op jit(solution)/shard_map/ppermute | solution.py:101
  172.7 33.1 %collective-permute-start.13 = (f32[40,2048]{1,0:T(8,128)S(1)}, f32[40,2048]{1,0:T(8,128)S(1)}, u32[]{:S(2)}, u32[]{:S(2)}) collective-permute-start(f32[40,2048]{1,0:T(8,128)S(1)} %get-tuple-element.25), channel_id=1, source_target_pairs={{0,8},{4,12},{8,0},{12,4},{1,9},{5,13},{9,1},{13,5},{2,10},{6,14},... | collective-permute-start | bytes 983048 | tf_op jit(solution)/shard_map/ppermute | solution.py:101
  203.4 15.8 %collective-permute-start.14 = (f32[40,2048]{1,0:T(8,128)S(1)}, f32[40,2048]{1,0:T(8,128)S(1)}, u32[]{:S(2)}, u32[]{:S(2)}) collective-permute-start(f32[40,2048]{1,0:T(8,128)S(1)} %get-tuple-element.24), channel_id=1, source_target_pairs={{0,12},{4,0},{8,4},{12,8},{1,13},{5,1},{9,5},{13,9},{2,14},{6,2},{... | collective-permute-start | bytes 983048 | tf_op jit(solution)/shard_map/ppermute | solution.py:101
  205.4 18.0 %copy-start.1 = (f32[2,56,2048]{2,1,0:T(8,128)S(1)}, f32[2,56,2048]{2,1,0:T(8,128)}, u32[]{:S(2)}) copy-start(f32[2,56,2048]{2,1,0:T(8,128)} %convolution_bitcast_fusion.7) | copy-start | bytes 2752516
  205.6 22.5 %collective-permute-start.16 = (f32[48,2048]{1,0:T(8,128)S(1)}, f32[48,2048]{1,0:T(8,128)S(1)}, u32[]{:S(2)}, u32[]{:S(2)}) collective-permute-start(f32[48,2048]{1,0:T(8,128)S(1)} %get-tuple-element.20), channel_id=1, source_target_pairs={{0,4},{4,8},{8,12},{12,0},{1,5},{5,9},{9,13},{13,1},{2,6},{6,10},{... | collective-permute-start | bytes 1179656 | tf_op jit(solution)/shard_map/ppermute | solution.py:101
  205.8 25.5 %collective-permute-start.17 = (f32[48,2048]{1,0:T(8,128)S(1)}, f32[48,2048]{1,0:T(8,128)S(1)}, u32[]{:S(2)}, u32[]{:S(2)}) collective-permute-start(f32[48,2048]{1,0:T(8,128)S(1)} %get-tuple-element.22), channel_id=1, source_target_pairs={{0,8},{4,12},{8,0},{12,4},{1,9},{5,13},{9,1},{13,5},{2,10},{6,14},... | collective-permute-start | bytes 1179656 | tf_op jit(solution)/shard_map/ppermute | solution.py:101
  219.2 13.7 %collective-permute-start.18 = (f32[48,2048]{1,0:T(8,128)S(1)}, f32[48,2048]{1,0:T(8,128)S(1)}, u32[]{:S(2)}, u32[]{:S(2)}) collective-permute-start(f32[48,2048]{1,0:T(8,128)S(1)} %get-tuple-element.21), channel_id=1, source_target_pairs={{0,12},{4,0},{8,4},{12,8},{1,13},{5,1},{9,5},{13,9},{2,14},{6,2},{... | collective-permute-start | bytes 1179656 | tf_op jit(solution)/shard_map/ppermute | solution.py:101
  223.6 21.3 %collective-permute-start.5 = (f32[2,56,2048]{2,1,0:T(8,128)S(1)}, f32[2,56,2048]{2,1,0:T(8,128)S(1)}, u32[]{:S(2)}, u32[]{:S(2)}) collective-permute-start(f32[2,56,2048]{2,1,0:T(8,128)S(1)} %add.188), channel_id=1, source_target_pairs={{0,4},{4,8},{8,12},{12,0},{1,5},{5,9},{9,13},{13,1},{2,6},{6,10},{... | collective-permute-start | bytes 2752520 | tf_op jit(solution)/shard_map/ppermute | solution.py:57
  224.4 20.5 %copy-start = (f32[2,56,2048]{2,1,0:T(8,128)S(1)}, f32[2,56,2048]{2,1,0:T(8,128)}, u32[]{:S(2)}) copy-start(f32[2,56,2048]{2,1,0:T(8,128)} %convolution_bitcast_fusion.6) | copy-start | bytes 2752516
  224.4 22.3 %collective-permute-start.21 = (f32[40,1024]{1,0:T(8,128)}, f32[40,1024]{1,0:T(8,128)}, u32[]{:S(2)}, u32[]{:S(2)}) collective-permute-start(f32[40,1024]{1,0:T(8,128)} %get-tuple-element.33), channel_id=1, source_target_pairs={{0,64},{64,0},{1,65},{65,1},{2,66},{66,2},{3,67},{67,3},{4,68},{68... | collective-permute-start | bytes 491528 | tf_op jit(solution)/shard_map/ppermute | solution.py:105
  228.1 20.6 %collective-permute-start.9 = (f32[2,56,2048]{2,1,0:T(8,128)}, f32[2,56,2048]{2,1,0:T(8,128)}, u32[]{:S(2)}, u32[]{:S(2)}) collective-permute-start(f32[2,56,2048]{2,1,0:T(8,128)} %add.202), channel_id=1, source_target_pairs={{0,12},{4,0},{8,4},{12,8},{1,13},{5,1},{9,5},{13,9},{2,14},{6,2},{... | collective-permute-start | bytes 2752520 | tf_op jit(solution)/shard_map/ppermute | solution.py:58
  233.7 12.9 %collective-permute-start.22 = (f32[48,1024]{1,0:T(8,128)}, f32[48,1024]{1,0:T(8,128)}, u32[]{:S(2)}, u32[]{:S(2)}) collective-permute-start(f32[48,1024]{1,0:T(8,128)} %get-tuple-element.31), channel_id=1, source_target_pairs={{0,64},{64,0},{1,65},{65,1},{2,66},{66,2},{3,67},{67,3},{4,68},{68... | collective-permute-start | bytes 589832 | tf_op jit(solution)/shard_map/ppermute | solution.py:105
  245.1 13.4 %collective-permute-start.6 = (f32[56,2048]{1,0:T(8,128)S(1)}, f32[56,2048]{1,0:T(8,128)}, u32[]{:S(2)}, u32[]{:S(2)}) collective-permute-start(f32[56,2048]{1,0:T(8,128)S(1)} %dynamic-slice_bitcast_fusion.7), channel_id=1, source_target_pairs={{0,2},{2,0},{1,3},{3,1},{4,6},{6,4},{5,7},{7,5},{8,10},{10,8},{9,1... | collective-permute-start | bytes 1376264 | tf_op jit(solution)/shard_map/ppermute | solution.py:66
  250.0 14.3 %collective-permute-start.10 = (f32[56,2048]{1,0:T(8,128)S(1)}, f32[56,2048]{1,0:T(8,128)S(1)}, u32[]{:S(2)}, u32[]{:S(2)}) collective-permute-start(f32[56,2048]{1,0:T(8,128)S(1)} %dynamic-slice_bitcast_fusion.6), channel_id=1, source_target_pairs={{0,2},{2,0},{1,3},{3,1},{4,6},{6,4},{5,7},{7,5},{8,10},{10,8},{9,1... | collective-permute-start | bytes 1376264 | tf_op jit(solution)/shard_map/ppermute | solution.py:66
  264.4 9.8 %collective-permute-start.19 = (f32[56,1024]{1,0:T(8,128)S(1)}, f32[56,1024]{1,0:T(8,128)S(1)}, u32[]{:S(2)}, u32[]{:S(2)}) collective-permute-start(f32[56,1024]{1,0:T(8,128)S(1)} %get-tuple-element.27), channel_id=1, source_target_pairs={{0,64},{64,0},{1,65},{65,1},{2,66},{66,2},{3,67},{67,3},{4,68},{68... | collective-permute-start | bytes 688136 | tf_op jit(solution)/shard_map/ppermute | solution.py:105
  268.3 8.4 %collective-permute-start.20 = (f32[56,1024]{1,0:T(8,128)S(1)}, f32[56,1024]{1,0:T(8,128)}, u32[]{:S(2)}, u32[]{:S(2)}) collective-permute-start(f32[56,1024]{1,0:T(8,128)S(1)} %get-tuple-element.29), channel_id=1, source_target_pairs={{0,64},{64,0},{1,65},{65,1},{2,66},{66,2},{3,67},{67,3},{4,68},{68... | collective-permute-start | bytes 688136 | tf_op jit(solution)/shard_map/ppermute | solution.py:105
Sparse Core Ops, SparseCore 0:
  20.7 53.1 all-gather.2
  77.5 46.1 all-gather.4

commit v17 on v12

--- a/solution.py
+++ b/solution.py
@@ -92,14 +92,14 @@
     for hop in range(1, ny):
         to_owner = [(i, (i + hop) % ny) for i in range(ny)]
         late_done = late_done + lax.ppermute(pick(late_sum)(yi + hop), "y", to_owner)
-    pieces = [pair_sum(early[0]), pair_sum(early[1]), late_done]
+    pieces = [pair_sum(jnp.concatenate(early, axis=1)), late_done]
 
     kept = [piece[:, :width] for piece in pieces]
     came = [lax.ppermute(piece[:, width:], "xh", SWAP) for piece in pieces]
 
     def slab_group(parts):
-        early = jnp.concatenate(parts[:2], axis=0).reshape(nz, y_cut, width)
-        late_rows = jnp.concatenate(parts[2:], axis=0).reshape(nz, TB - y_cut, width)
+        early = parts[0].reshape(nz, y_cut, width)
+        late_rows = parts[1].reshape(nz, TB - y_cut, width)
         return jnp.concatenate([early, late_rows], axis=1).reshape(nz * TB, width)
 
     kept, came = slab_group(kept), slab_group(came)

time: 256 us -> 262 us (1.023)
  waiting for transfers between devices: 120 us -> 131 us
  starting transfers between devices: 32.1 us -> 27.3 us
    ppermute x3, waiting for transfers between devices: 19.2 us -> 5.29 us  [ring(): got_ahead = lax.ppermute(acc_ahead, 'y', to_next)]
    ppermute x3, waiting for transfers between devices: 0.9 us -> 12.5 us  [ring(): got_back = lax.ppermute(acc_back, 'y', to_prev)]
    ppermute x1, waiting for transfers between devices: 10 us -> 18.9 us  [local(): late_sum = late_block(xi) + lax.ppermute(late_there, 'xl', SWAP)]
    ppermute x3, starting transfers between devices: 3.59 us -> 0.15 us  [ring(): got_ahead = lax.ppermute(acc_ahead, 'y', to_next)]
    ppermute x3 -> x2, starting transfers between devices: 9.18 us -> 6.06 us  [local(): came = [lax.ppermute(piece[:, width:], 'xh', SWAP) for piece in pieces]]
    ppermute x3, starting transfers between devices: 6.67 us -> 9.75 us  [ring(): got_back = lax.ppermute(acc_back, 'y', to_prev)]
    ppermute x2 -> x1, waiting for transfers between devices: 10.1 us -> 12.5 us  [pair_sum(): return here + lax.ppermute(there, 'xl', SWAP)]
    ppermute x3 -> x2, waiting for transfers between devices: 6.97 us -> 7.29 us  [local(): came = [lax.ppermute(piece[:, width:], 'xh', SWAP) for piece in pieces]]
  transfers between devices with their start and end apart: 20 -> 18, of which waited for: 12 -> 13; matrix products, arithmetic and copies ran while one was open for 31% -> 29% of each run, Pallas kernels for 0% -> 0%
where the time goes in v17:
time: 262 us; the launch traced here: 261 us
  waiting for transfers between devices  131 us (50%)
  matrix products  59.2 us (23%)
  starting transfers between devices  27.3 us (10%)
  local copies, waits for them, and re-layouts  19.3 us (7%)
  between operations  13.8 us (5%)
  other arithmetic  10.2 us (4%)
    ppermute x1, waiting for transfers between devices, local(): lax.ppermute(amplitudes, 'xh', SWAP)  53.7 us
    dot_general x8, matrix products, block(): lax.dot_general(lhs[:, low:high], amp, (((2, 3), (0, 1)), ((), ())), pref...  45.9 us
    ppermute x1, waiting for transfers between devices, local(): late_sum = late_block(xi) + lax.ppermute(late_there, 'xl', SWAP)  18.9 us
    dot_general x2, matrix products, late_block(): lax.dot_general(lhs, amp, (((2, 3), (0, 1)), ((), ())), preferred_element...  13.3 us
    ppermute x1, waiting for transfers between devices, pair_sum(): return here + lax.ppermute(there, 'xl', SWAP)  12.5 us
    ppermute x3, waiting for transfers between devices, ring(): got_back = lax.ppermute(acc_back, 'y', to_prev)  12.5 us
    ppermute x3, waiting for transfers between devices, local(): lax.ppermute(pick(late_sum)(yi + hop), 'y', to_owner)  11.7 us
    ppermute x3, starting transfers between devices, ring(): got_back = lax.ppermute(acc_back, 'y', to_prev)  9.75 us
  transfers between devices with their start and end apart: 18, of which 13 were waited for; matrix products, arithmetic and copies ran while one was open for 29% of the time, Pallas kernels for 0%

profile of v17, /device:TPU:0, one launch (start us, length us, event | category | flops | bytes accessed | tf_op | source)
XLA Modules:
  0.0 261.2 jit_solution(12509123630925964900)
XLA Ops:
  6.5 0.7 dynamic_slice.57
  7.3 1.2 sort.17
  8.6 0.2 fusion.22
  8.9 2.6 reshape.35
  11.4 0.6 gather_fusion.1
  12.1 0.2 broadcast_select_fusion
  12.3 1.1 copy.12
  13.4 0.6 gather_fusion
  14.0 0.2 select_bitcast_fusion
  14.2 2.1 collective-permute-done
  16.3 1.4 copy.35
  17.7 0.1 fusion.4
  17.9 1.6 copy.14
  19.6 3.2 %collective-permute-start.1 = (bf16[1200,1024]{1,0:T(8,128)(2,1)}, bf16[1200,1024]{1,0:T(8,128)(2,1)S(1)}, u32[]{:S(2)}, u32[]{:S(2)}) collective-permute-start(bf16[1200,1024]{1,0:T(8,128)(2,1)} %param.5), channel_id=1, source_target_pairs={{0,64},{64,0},{1,65},{65,1},{2,66},{66,2},{3,67},{67,3},{4,68},{68... | collective-permute-start | bytes 7372808 | tf_op jit(solution)/shard_map/ppermute | solution.py:38
  22.8 0.3 pad_maximum_fusion.1
  23.1 53.7 %collective-permute-done.1 = bf16[1200,1024]{1,0:T(8,128)(2,1)S(1)} collective-permute-done((bf16[1200,1024]{1,0:T(8,128)(2,1)}, bf16[1200,1024]{1,0:T(8,128)(2,1)S(1)}, u32[]{:S(2)}, u32[]{:S(2)}) %collective-permute-start.1) | collective-permute-done | bytes 2457632 | tf_op jit(solution)/shard_map/ppermute | solution.py:38
  76.8 2.7 %pad_maximum_fusion = bf16[1200,2048]{1,0:T(8,128)(2,1)} fusion(bf16[1200,1024]{1,0:T(8,128)(2,1)S(1)} %collective-permute-done.1, bf16[1200,1024]{1,0:T(8,128)(2,1)S(1)} %copy-done), kind=kLoop, calls=%fused_computation.3 | loop fusion | flops 9830400 | bytes 9830400 | tf_op jit(solution)/shard_map/concatenate | solution.py:38
  79.5 1.1 copy.21
  80.7 3.8 %copy.33 = bf16[8,112,2,1200]{3,1,2,0:T(8,128)(2,1)S(1)} copy(bf16[8,112,2,1200]{3,0,2,1:T(8,128)(2,1)} %all-gather.3.cloned.1.call-done) | data formatting | bytes 8601600 | tf_op jit(solution)/shard_map/reshape | solution.py:36
  84.5 0.6 dynamic-slice_bitcast_fusion
  85.1 3.0 %collective-permute-done.2 = bf16[1200,2048]{1,0:T(8,128)(2,1)} collective-permute-done((bf16[1200,2048]{1,0:T(8,128)(2,1)}, bf16[1200,2048]{1,0:T(8,128)(2,1)}, u32[]{:S(2)}, u32[]{:S(2)}) %collective-permute-start.2) | collective-permute-done | bytes 4915232 | tf_op jit(solution)/shard_map/ppermute | solution.py:41
  88.0 6.5 %convolution_bitcast_fusion.5 = f32[2,56,2048]{2,1,0:T(8,128)} fusion(bf16[2,112,2,1200]{3,1,2,0:T(8,128)(2,1)S(1)} %get-tuple-element.15, bf16[1,1200,2048]{2,1,0:T(8,128)(2,1)} %bitcast.5, bf16[1,1200,2048]{2,1,0:T(8,128)(2,1)} %bitcast.4), kind=kOutput, calls=%fused_computation.9 | convolution fusion | flops 1105920000 | bytes 11321344 | tf_op jit(solution)/shard_map/dot_general | solution.py:45
  94.6 3.2 %collective-permute-start.6 = (f32[2,56,2048]{2,1,0:T(8,128)}, f32[2,56,2048]{2,1,0:T(8,128)}, u32[]{:S(2)}, u32[]{:S(2)}) collective-permute-start(f32[2,56,2048]{2,1,0:T(8,128)} %convolution_bitcast_fusion.5), channel_id=1, source_target_pairs={{0,12},{4,0},{8,4},{12,8},{1,13},{5,1},{9,5},{13,9},{2,14},{6,2},{... | collective-permute-start | bytes 2752520 | tf_op jit(solution)/shard_map/ppermute | solution.py:58
  97.8 6.5 %convolution_bitcast_fusion.4 = f32[2,56,2048]{2,1,0:T(8,128)} fusion(bf16[2,112,2,1200]{3,1,2,0:T(8,128)(2,1)S(1)} %get-tuple-element.14, bf16[1,1200,2048]{2,1,0:T(8,128)(2,1)} %bitcast.5, bf16[1,1200,2048]{2,1,0:T(8,128)(2,1)} %bitcast.4), kind=kOutput, calls=%fused_computation.8 | convolution fusion | flops 1105920000 | bytes 11321344 | tf_op jit(solution)/shard_map/dot_general | solution.py:45
  104.3 6.6 %convolution_bitcast_fusion.9 = f32[2,56,2048]{2,1,0:T(8,128)} fusion(bf16[2,112,2,1200]{3,1,2,0:T(8,128)(2,1)S(1)} %get-tuple-element.19, bf16[1,1200,2048]{2,1,0:T(8,128)(2,1)} %bitcast.5, bf16[1,1200,2048]{2,1,0:T(8,128)(2,1)} %bitcast.4), kind=kOutput, calls=%fused_computation.13 | convolution fusion | flops 1105920000 | bytes 11321344 | tf_op jit(solution)/shard_map/dot_general | solution.py:45
  110.9 5.0 %convolution_bitcast_fusion.3 = f32[2,56,2048]{2,1,0:T(8,128)S(1)} fusion(bf16[2,112,2,1200]{3,1,2,0:T(8,128)(2,1)S(1)} %get-tuple-element.19, bf16[1,1200,2048]{2,1,0:T(8,128)(2,1)} %bitcast.5, bf16[1,1200,2048]{2,1,0:T(8,128)(2,1)} %bitcast.4), kind=kOutput, calls=%fused_computation.7 | convolution fusion | flops 1105920000 | bytes 11321344 | tf_op jit(solution)/shard_map/dot_general | solution.py:45
  115.8 6.7 %convolution_bitcast_fusion.8 = f32[2,56,2048]{2,1,0:T(8,128)} fusion(bf16[2,112,2,1200]{3,1,2,0:T(8,128)(2,1)S(1)} %get-tuple-element.18, bf16[1,1200,2048]{2,1,0:T(8,128)(2,1)} %bitcast.5, bf16[1,1200,2048]{2,1,0:T(8,128)(2,1)} %bitcast.4), kind=kOutput, calls=%fused_computation.12 | convolution fusion | flops 1105920000 | bytes 11321344 | tf_op jit(solution)/shard_map/dot_general | solution.py:45
  122.5 4.4 %all-gather.5.cloned.1.call-done = bf16[8,88,2,1200]{3,0,2,1:T(8,128)(2,1)} async-done(((bf16[8,22,2,1200]{3,0,2,1:T(8,128)(2,1)}), bf16[8,88,2,1200]{3,0,2,1:T(8,128)(2,1)}) %all-gather.5.cloned.1.call-update) | async-done | bytes 3379216 | tf_op jit(solution)/shard_map/all_gather | solution.py:40
  126.9 3.2 %copy.22 = bf16[8,88,2,1200]{3,1,2,0:T(8,128)(2,1)S(1)} copy(bf16[8,88,2,1200]{3,0,2,1:T(8,128)(2,1)} %all-gather.5.cloned.1.call-done) | data formatting | bytes 6758400 | tf_op jit(solution)/shard_map/all_gather | solution.py:40
  130.2 1.3 add.169
  131.5 2.8 %collective-permute-start.7 = (f32[2,56,2048]{2,1,0:T(8,128)S(1)}, f32[2,56,2048]{2,1,0:T(8,128)S(1)}, u32[]{:S(2)}, u32[]{:S(2)}) collective-permute-start(f32[2,56,2048]{2,1,0:T(8,128)S(1)} %add.169), channel_id=1, source_target_pairs={{0,12},{4,0},{8,4},{12,8},{1,13},{5,1},{9,5},{13,9},{2,14},{6,2},{... | collective-permute-start | bytes 2752520 | tf_op jit(solution)/shard_map/ppermute | solution.py:58
  134.3 0.2 collective-permute-done.3
  134.5 1.3 add.156
  135.9 6.7 %convolution_bitcast_fusion = f32[4,88,2048]{2,1,0:T(8,128)S(1)} fusion(bf16[4,2,88,2,1200]{4,2,3,1,0:T(8,128)(2,1)S(1)} %bitcast.91, s32[]{:T(128)S(6)} %select_n.120, bf16[1,1200,2048]{2,1,0:T(8,128)(2,1)} %bitcast.5, bf16[1,1200,2048]{2,1,0:T(8,128)(2,1)} %bitcast.4), kind=kOutput, calls=%fused_computation.4 | convolution fusion | flops 3465216000 | bytes 14516228 | tf_op jit(solution)/shard_map/dot_general | solution.py:74
  142.6 1.6 collective-permute-start.10
  144.2 4.9 %convolution_bitcast_fusion.7 = f32[2,56,2048]{2,1,0:T(8,128)S(1)} fusion(bf16[2,112,2,1200]{3,1,2,0:T(8,128)(2,1)S(1)} %get-tuple-element.17, bf16[1,1200,2048]{2,1,0:T(8,128)(2,1)} %bitcast.5, bf16[1,1200,2048]{2,1,0:T(8,128)(2,1)} %bitcast.4), kind=kOutput, calls=%fused_computation.11 | convolution fusion | flops 1105920000 | bytes 11321344 | tf_op jit(solution)/shard_map/dot_general | solution.py:45
  149.0 4.8 %collective-permute-done.7 = f32[2,56,2048]{2,1,0:T(8,128)S(1)} collective-permute-done((f32[2,56,2048]{2,1,0:T(8,128)S(1)}, f32[2,56,2048]{2,1,0:T(8,128)S(1)}, u32[]{:S(2)}, u32[]{:S(2)}) %collective-permute-start.7) | collective-permute-done | bytes 917536 | tf_op jit(solution)/shard_map/ppermute | solution.py:58
  153.8 0.1 add.170
  153.9 3.8 %collective-permute-start.8 = (f32[2,56,2048]{2,1,0:T(8,128)S(1)}, f32[2,56,2048]{2,1,0:T(8,128)S(1)}, u32[]{:S(2)}, u32[]{:S(2)}) collective-permute-start(f32[2,56,2048]{2,1,0:T(8,128)S(1)} %add.170), channel_id=1, source_target_pairs={{0,12},{4,0},{8,4},{12,8},{1,13},{5,1},{9,5},{13,9},{2,14},{6,2},{... | collective-permute-start | bytes 2752520 | tf_op jit(solution)/shard_map/ppermute | solution.py:58
  157.7 0.9 collective-permute-done.4
  158.6 0.1 add.159
  158.8 4.9 %convolution_bitcast_fusion.2 = f32[2,56,2048]{2,1,0:T(8,128)S(1)} fusion(bf16[2,112,2,1200]{3,1,2,0:T(8,128)(2,1)S(1)} %get-tuple-element.16, bf16[1,1200,2048]{2,1,0:T(8,128)(2,1)} %bitcast.5, bf16[1,1200,2048]{2,1,0:T(8,128)(2,1)} %bitcast.4), kind=kOutput, calls=%fused_computation.6 | convolution fusion | flops 1105920000 | bytes 11321344 | tf_op jit(solution)/shard_map/dot_general | solution.py:45
  163.7 4.9 %convolution_bitcast_fusion.6 = f32[2,56,2048]{2,1,0:T(8,128)S(1)} fusion(bf16[2,112,2,1200]{3,1,2,0:T(8,128)(2,1)S(1)} %get-tuple-element.16, bf16[1,1200,2048]{2,1,0:T(8,128)(2,1)} %bitcast.5, bf16[1,1200,2048]{2,1,0:T(8,128)(2,1)} %bitcast.4), kind=kOutput, calls=%fused_computation.10 | convolution fusion | flops 1105920000 | bytes 11321344 | tf_op jit(solution)/shard_map/dot_general | solution.py:45
  168.5 7.7 %collective-permute-done.8 = f32[2,56,2048]{2,1,0:T(8,128)S(1)} collective-permute-done((f32[2,56,2048]{2,1,0:T(8,128)S(1)}, f32[2,56,2048]{2,1,0:T(8,128)S(1)}, u32[]{:S(2)}, u32[]{:S(2)}) %collective-permute-start.8) | collective-permute-done | bytes 917536 | tf_op jit(solution)/shard_map/ppermute | solution.py:58
  176.3 0.1 add.171
  176.4 4.2 %collective-permute-done.5 = f32[2,56,2048]{2,1,0:T(8,128)S(1)} collective-permute-done((f32[2,56,2048]{2,1,0:T(8,128)S(1)}, f32[2,56,2048]{2,1,0:T(8,128)S(1)}, u32[]{:S(2)}, u32[]{:S(2)}) %collective-permute-start.5) | collective-permute-done | bytes 917536 | tf_op jit(solution)/shard_map/ppermute | solution.py:57
  180.6 0.1 add.162
  180.8 1.7 collective-permute-start.9
  182.5 6.6 %convolution_bitcast_fusion.1 = f32[4,88,2048]{2,1,0:T(8,128)S(1)} fusion(bf16[4,2,88,2,1200]{4,2,3,1,0:T(8,128)(2,1)S(1)} %bitcast.92, s32[]{:T(128)S(6)} %select_n.119, bf16[1,1200,2048]{2,1,0:T(8,128)(2,1)} %bitcast.5, bf16[1,1200,2048]{2,1,0:T(8,128)(2,1)} %bitcast.4), kind=kOutput, calls=%fused_computation.5 | convolution fusion | flops 3465216000 | bytes 14516228 | tf_op jit(solution)/shard_map/dot_general | solution.py:74
  189.1 18.9 %collective-permute-done.10 = f32[4,88,2048]{2,1,0:T(8,128)S(1)} collective-permute-done((f32[4,88,2048]{2,1,0:T(8,128)S(1)}, f32[4,88,2048]{2,1,0:T(8,128)S(1)}, u32[]{:S(2)}, u32[]{:S(2)}) %collective-permute-start.10) | collective-permute-done | bytes 2883616 | tf_op jit(solution)/shard_map/ppermute | solution.py:80
  208.0 0.4 add.175
  208.4 0.2 dynamic-slice_bitcast_fusion.8
  208.6 0.6 collective-permute-start.11
  209.2 4.1 %collective-permute-start.12 = (f32[88,2048]{1,0:T(8,128)S(1)}, f32[88,2048]{1,0:T(8,128)S(1)}, u32[]{:S(2)}, u32[]{:S(2)}) collective-permute-start(f32[88,2048]{1,0:T(8,128)S(1)} %get-tuple-element.22), channel_id=1, source_target_pairs={{0,8},{4,12},{8,0},{12,4},{1,9},{5,13},{9,1},{13,5},{2,10},{6,14},... | collective-permute-start | bytes 2162696 | tf_op jit(solution)/shard_map/ppermute | solution.py:94
  213.4 12.5 %collective-permute-done.9 = f32[112,2048]{1,0:T(8,128)S(1)} collective-permute-done((f32[112,2048]{1,0:T(8,128)S(1)}, f32[112,2048]{1,0:T(8,128)S(1)}, u32[]{:S(2)}, u32[]{:S(2)}) %collective-permute-start.9) | collective-permute-done | bytes 917536 | tf_op jit(solution)/shard_map/ppermute | solution.py:66
  225.9 0.1 fusion.9
  226.1 3.1 %collective-permute-start.14 = (f32[112,1024]{1,0:T(8,128)S(1)}, f32[112,1024]{1,0:T(8,128)}, u32[]{:S(2)}, u32[]{:S(2)}) collective-permute-start(f32[112,1024]{1,0:T(8,128)S(1)} %get-tuple-element.24), channel_id=1, source_target_pairs={{0,64},{64,0},{1,65},{65,1},{2,66},{66,2},{3,67},{67,3},{4,68},{68... | collective-permute-start | bytes 1376264 | tf_op jit(solution)/shard_map/ppermute | solution.py:98
  229.1 11.7 %collective-permute-done.12 = f32[88,2048]{1,0:T(8,128)S(1)} collective-permute-done((f32[88,2048]{1,0:T(8,128)S(1)}, f32[88,2048]{1,0:T(8,128)S(1)}, u32[]{:S(2)}, u32[]{:S(2)}) %collective-permute-start.12) | collective-permute-done | bytes 720928 | tf_op jit(solution)/shard_map/ppermute | solution.py:94
  240.8 0.2 fusion.11
  241.1 3.0 %collective-permute-start.15 = (f32[88,1024]{1,0:T(8,128)S(1)}, f32[88,1024]{1,0:T(8,128)S(1)}, u32[]{:S(2)}, u32[]{:S(2)}) collective-permute-start(f32[88,1024]{1,0:T(8,128)S(1)} %get-tuple-element.26), channel_id=1, source_target_pairs={{0,64},{64,0},{1,65},{65,1},{2,66},{66,2},{3,67},{67,3},{4,68},{68... | collective-permute-start | bytes 1081352 | tf_op jit(solution)/shard_map/ppermute | solution.py:98
  244.2 0.1 pad_maximum_fusion.2
  244.4 7.3 %collective-permute-done.15 = f32[88,1024]{1,0:T(8,128)S(1)} collective-permute-done((f32[88,1024]{1,0:T(8,128)S(1)}, f32[88,1024]{1,0:T(8,128)S(1)}, u32[]{:S(2)}, u32[]{:S(2)}) %collective-permute-start.15) | collective-permute-done | bytes 360480 | tf_op jit(solution)/shard_map/ppermute | solution.py:98
  251.7 1.1 reshape.42
  253.0 1.3 maximum_select_fusion
  (37 shorter events, 1.1 us)
Async XLA Ops:
  6.5 74.2 %all-gather.3.cloned.1.call-start = ((), (), s32[]{:S(2)}) async-start(), calls=%async_computation | async-start | bytes 5734400 | tf_op jit(solution)/shard_map/all_gather | solution.py:34
  13.4 3.0 %collective-permute-start = (bf16[8,50,1200]{2,0,1:T(8,128)(2,1)}, bf16[8,50,1200]{2,0,1:T(8,128)(2,1)}, u32[]{:S(2)}, u32[]{:S(2)}) collective-permute-start(bf16[8,50,1200]{2,0,1:T(8,128)(2,1)} %copy.12), channel_id=1, source_target_pairs={{0,1},{1,0},{2,3},{3,2},{4,5},{5,4},{6,7},{7,6},{8,9},{9,8},{10,11... | collective-permute-start | bytes 2880008 | tf_op jit(solution)/shard_map/ppermute | solution.py:31
  19.5 107.4 %all-gather.5.cloned.1.call-start = ((), (), s32[]{:S(2)}) async-start(), calls=%async_computation.1 | async-start | bytes 4505600 | tf_op jit(solution)/shard_map/all_gather | solution.py:40
  19.6 57.2 %copy-start = (bf16[1200,1024]{1,0:T(8,128)(2,1)S(1)}, bf16[1200,1024]{1,0:T(8,128)(2,1)}, u32[]{:S(2)}) copy-start(bf16[1200,1024]{1,0:T(8,128)(2,1)} %param.5) | copy-start | bytes 7372804
  19.6 57.2 %collective-permute-start.1 = (bf16[1200,1024]{1,0:T(8,128)(2,1)}, bf16[1200,1024]{1,0:T(8,128)(2,1)S(1)}, u32[]{:S(2)}, u32[]{:S(2)}) collective-permute-start(bf16[1200,1024]{1,0:T(8,128)(2,1)} %param.5), channel_id=1, source_target_pairs={{0,64},{64,0},{1,65},{65,1},{2,66},{66,2},{3,67},{67,3},{4,68},{68... | collective-permute-start | bytes 7372808 | tf_op jit(solution)/shard_map/ppermute | solution.py:38
  79.5 8.5 %collective-permute-start.2 = (bf16[1200,2048]{1,0:T(8,128)(2,1)}, bf16[1200,2048]{1,0:T(8,128)(2,1)}, u32[]{:S(2)}, u32[]{:S(2)}) collective-permute-start(bf16[1200,2048]{1,0:T(8,128)(2,1)} %pad_maximum_fusion), channel_id=1, source_target_pairs={{0,1},{1,0},{2,3},{3,2},{4,5},{5,4},{6,7},{7,6},{8,9},{9,8},{10,11... | collective-permute-start | bytes 14745608 | tf_op jit(solution)/shard_map/ppermute | solution.py:41
  94.6 35.6 %collective-permute-start.6 = (f32[2,56,2048]{2,1,0:T(8,128)}, f32[2,56,2048]{2,1,0:T(8,128)}, u32[]{:S(2)}, u32[]{:S(2)}) collective-permute-start(f32[2,56,2048]{2,1,0:T(8,128)} %convolution_bitcast_fusion.5), channel_id=1, source_target_pairs={{0,12},{4,0},{8,4},{12,8},{1,13},{5,1},{9,5},{13,9},{2,14},{6,2},{... | collective-permute-start | bytes 2752520 | tf_op jit(solution)/shard_map/ppermute | solution.py:58
  110.9 23.7 %collective-permute-start.3 = (f32[2,56,2048]{2,1,0:T(8,128)}, f32[2,56,2048]{2,1,0:T(8,128)}, u32[]{:S(2)}, u32[]{:S(2)}) collective-permute-start(f32[2,56,2048]{2,1,0:T(8,128)} %convolution_bitcast_fusion.9), channel_id=1, source_target_pairs={{0,4},{4,8},{8,12},{12,0},{1,5},{5,9},{9,13},{13,1},{2,6},{6,10},{... | collective-permute-start | bytes 2752520 | tf_op jit(solution)/shard_map/ppermute | solution.py:57
  126.9 3.3 %copy-start.2 = (f32[2,56,2048]{2,1,0:T(8,128)S(1)}, f32[2,56,2048]{2,1,0:T(8,128)}, u32[]{:S(2)}) copy-start(f32[2,56,2048]{2,1,0:T(8,128)} %convolution_bitcast_fusion.4) | copy-start | bytes 2752516
  126.9 7.6 %copy-start.1 = (f32[2,56,2048]{2,1,0:T(8,128)S(1)}, f32[2,56,2048]{2,1,0:T(8,128)}, u32[]{:S(2)}) copy-start(f32[2,56,2048]{2,1,0:T(8,128)} %convolution_bitcast_fusion.8) | copy-start | bytes 2752516
  131.5 22.3 %collective-permute-start.7 = (f32[2,56,2048]{2,1,0:T(8,128)S(1)}, f32[2,56,2048]{2,1,0:T(8,128)S(1)}, u32[]{:S(2)}, u32[]{:S(2)}) collective-permute-start(f32[2,56,2048]{2,1,0:T(8,128)S(1)} %add.169), channel_id=1, source_target_pairs={{0,12},{4,0},{8,4},{12,8},{1,13},{5,1},{9,5},{13,9},{2,14},{6,2},{... | collective-permute-start | bytes 2752520 | tf_op jit(solution)/shard_map/ppermute | solution.py:58
  135.8 22.7 %collective-permute-start.4 = (f32[2,56,2048]{2,1,0:T(8,128)S(1)}, f32[2,56,2048]{2,1,0:T(8,128)S(1)}, u32[]{:S(2)}, u32[]{:S(2)}) collective-permute-start(f32[2,56,2048]{2,1,0:T(8,128)S(1)} %add.156), channel_id=1, source_target_pairs={{0,4},{4,8},{8,12},{12,0},{1,5},{5,9},{9,13},{13,1},{2,6},{6,10},{... | collective-permute-start | bytes 2752520 | tf_op jit(solution)/shard_map/ppermute | solution.py:57
  142.6 65.4 %collective-permute-start.10 = (f32[4,88,2048]{2,1,0:T(8,128)S(1)}, f32[4,88,2048]{2,1,0:T(8,128)S(1)}, u32[]{:S(2)}, u32[]{:S(2)}) collective-permute-start(f32[4,88,2048]{2,1,0:T(8,128)S(1)} %convolution_bitcast_fusion), channel_id=1, source_target_pairs={{0,2},{2,0},{1,3},{3,1},{4,6},{6,4},{5,7},{7,5},{8,10},{10,8},{9,1... | collective-permute-start | bytes 8650760 | tf_op jit(solution)/shard_map/ppermute | solution.py:80
  153.9 22.4 %collective-permute-start.8 = (f32[2,56,2048]{2,1,0:T(8,128)S(1)}, f32[2,56,2048]{2,1,0:T(8,128)S(1)}, u32[]{:S(2)}, u32[]{:S(2)}) collective-permute-start(f32[2,56,2048]{2,1,0:T(8,128)S(1)} %add.170), channel_id=1, source_target_pairs={{0,12},{4,0},{8,4},{12,8},{1,13},{5,1},{9,5},{13,9},{2,14},{6,2},{... | collective-permute-start | bytes 2752520 | tf_op jit(solution)/shard_map/ppermute | solution.py:58
  158.7 21.9 %collective-permute-start.5 = (f32[2,56,2048]{2,1,0:T(8,128)S(1)}, f32[2,56,2048]{2,1,0:T(8,128)S(1)}, u32[]{:S(2)}, u32[]{:S(2)}) collective-permute-start(f32[2,56,2048]{2,1,0:T(8,128)S(1)} %add.159), channel_id=1, source_target_pairs={{0,4},{4,8},{8,12},{12,0},{1,5},{5,9},{9,13},{13,1},{2,6},{6,10},{... | collective-permute-start | bytes 2752520 | tf_op jit(solution)/shard_map/ppermute | solution.py:57
  180.8 45.1 %collective-permute-start.9 = (f32[112,2048]{1,0:T(8,128)S(1)}, f32[112,2048]{1,0:T(8,128)S(1)}, u32[]{:S(2)}, u32[]{:S(2)}) collective-permute-start(f32[112,2048]{1,0:T(8,128)S(1)} %fusion.6), channel_id=1, source_target_pairs={{0,2},{2,0},{1,3},{3,1},{4,6},{6,4},{5,7},{7,5},{8,10},{10,8},{9,1... | collective-permute-start | bytes 2752520 | tf_op jit(solution)/shard_map/ppermute | solution.py:66
  208.6 20.5 %collective-permute-start.11 = (f32[88,2048]{1,0:T(8,128)S(1)}, f32[88,2048]{1,0:T(8,128)S(1)}, u32[]{:S(2)}, u32[]{:S(2)}) collective-permute-start(f32[88,2048]{1,0:T(8,128)S(1)} %get-tuple-element.20), channel_id=1, source_target_pairs={{0,4},{4,8},{8,12},{12,0},{1,5},{5,9},{9,13},{13,1},{2,6},{6,10},{... | collective-permute-start | bytes 2162696 | tf_op jit(solution)/shard_map/ppermute | solution.py:94
  209.2 31.6 %collective-permute-start.12 = (f32[88,2048]{1,0:T(8,128)S(1)}, f32[88,2048]{1,0:T(8,128)S(1)}, u32[]{:S(2)}, u32[]{:S(2)}) collective-permute-start(f32[88,2048]{1,0:T(8,128)S(1)} %get-tuple-element.22), channel_id=1, source_target_pairs={{0,8},{4,12},{8,0},{12,4},{1,9},{5,13},{9,1},{13,5},{2,10},{6,14},... | collective-permute-start | bytes 2162696 | tf_op jit(solution)/shard_map/ppermute | solution.py:94
  213.3 27.5 %collective-permute-start.13 = (f32[88,2048]{1,0:T(8,128)S(1)}, f32[88,2048]{1,0:T(8,128)S(1)}, u32[]{:S(2)}, u32[]{:S(2)}) collective-permute-start(f32[88,2048]{1,0:T(8,128)S(1)} %get-tuple-element.21), channel_id=1, source_target_pairs={{0,12},{4,0},{8,4},{12,8},{1,13},{5,1},{9,5},{13,9},{2,14},{6,2},{... | collective-permute-start | bytes 2162696 | tf_op jit(solution)/shard_map/ppermute | solution.py:94
  226.1 25.7 %collective-permute-start.14 = (f32[112,1024]{1,0:T(8,128)S(1)}, f32[112,1024]{1,0:T(8,128)}, u32[]{:S(2)}, u32[]{:S(2)}) collective-permute-start(f32[112,1024]{1,0:T(8,128)S(1)} %get-tuple-element.24), channel_id=1, source_target_pairs={{0,64},{64,0},{1,65},{65,1},{2,66},{66,2},{3,67},{67,3},{4,68},{68... | collective-permute-start | bytes 1376264 | tf_op jit(solution)/shard_map/ppermute | solution.py:98
  241.1 10.6 %collective-permute-start.15 = (f32[88,1024]{1,0:T(8,128)S(1)}, f32[88,1024]{1,0:T(8,128)S(1)}, u32[]{:S(2)}, u32[]{:S(2)}) collective-permute-start(f32[88,1024]{1,0:T(8,128)S(1)} %get-tuple-element.26), channel_id=1, source_target_pairs={{0,64},{64,0},{1,65},{65,1},{2,66},{66,2},{3,67},{67,3},{4,68},{68... | collective-permute-start | bytes 1081352 | tf_op jit(solution)/shard_map/ppermute | solution.py:98
Sparse Core Ops, SparseCore 0:
  19.7 54.1 all-gather.2
  80.7 46.1 all-gather.4

commit v18 on v12

--- a/solution.py
+++ b/solution.py
@@ -103,9 +103,8 @@
         return jnp.concatenate([early, late_rows], axis=1).reshape(nz * TB, width)
 
     kept, came = slab_group(kept), slab_group(came)
-    first = jnp.concatenate([kept, came], axis=0)
-    second = jnp.concatenate([came, kept], axis=0)
-    return jnp.where(xh == 0, first, second)
+    both = jnp.concatenate([kept, came, kept], axis=0)
+    return lax.dynamic_slice_in_dim(both, xh * kept.shape[0], 2 * kept.shape[0], 0)
 
 
 def solution(mesh):

time: 256 us -> 257 us (level)
  transfers between devices with their start and end apart: 20 -> 20, of which waited for: 12 -> 12; matrix products, arithmetic and copies ran while one was open for 31% -> 30% of each run, Pallas kernels for 0% -> 0%
where the time goes in v18:
time: 257 us; the launch traced here: 256 us
  waiting for transfers between devices  120 us (47%)
  matrix products  60.9 us (24%)
  starting transfers between devices  32.1 us (12%)
  local copies, waits for them, and re-layouts  18.4 us (7%)
  between operations  13.9 us (5%)
  other arithmetic  10.7 us (4%)
    ppermute x1, waiting for transfers between devices, local(): lax.ppermute(amplitudes, 'xh', SWAP)  53.7 us
    dot_general x8, matrix products, block(): lax.dot_general(lhs[:, low:high], amp, (((2, 3), (0, 1)), ((), ())), pref...  47.7 us
    ppermute x3, waiting for transfers between devices, ring(): got_ahead = lax.ppermute(acc_ahead, 'y', to_next)  19.2 us
    dot_general x2, matrix products, late_block(): lax.dot_general(lhs, amp, (((2, 3), (0, 1)), ((), ())), preferred_element...  13.3 us
    ppermute x3, waiting for transfers between devices, local(): lax.ppermute(pick(late_sum)(yi + hop), 'y', to_owner)  11.1 us
    ppermute x2, waiting for transfers between devices, pair_sum(): return here + lax.ppermute(there, 'xl', SWAP)  10.1 us
    ppermute x1, waiting for transfers between devices, local(): late_sum = late_block(xi) + lax.ppermute(late_there, 'xl', SWAP)  10 us
    ppermute x3, starting transfers between devices, local(): came = [lax.ppermute(piece[:, width:], 'xh', SWAP) for piece in pieces]  9.18 us
  transfers between devices with their start and end apart: 20, of which 12 were waited for; matrix products, arithmetic and copies ran while one was open for 30% of the time, Pallas kernels for 0%

profile of v18, /device:TPU:0, one launch (start us, length us, event | category | flops | bytes accessed | tf_op | source)
XLA Modules:
  0.0 255.8 jit_solution(13949225327920396807)
XLA Ops:
  6.5 0.7 dynamic_slice.66
  7.3 1.2 sort.17
  8.6 0.2 fusion.19
  8.9 2.6 %reshape.35 = bf16[16,50,1200]{2,1,0:T(8,128)(2,1)S(1)} reshape(bf16[800,1200]{1,0:T(8,128)(2,1)} %bitcast.95) | data formatting | bytes 3840000 | tf_op jit(solution)/shard_map/reshape | solution.py:28
  11.4 0.6 gather_fusion.1
  12.1 0.2 broadcast_select_fusion
  12.3 1.1 copy.12
  13.4 0.6 gather_fusion
  14.0 0.2 select_bitcast_fusion
  14.2 2.1 collective-permute-done
  16.3 1.4 copy.35
  17.7 0.1 fusion.6
  17.9 1.6 copy.14
  19.6 3.2 %collective-permute-start.1 = (bf16[1200,1024]{1,0:T(8,128)(2,1)}, bf16[1200,1024]{1,0:T(8,128)(2,1)S(1)}, u32[]{:S(2)}, u32[]{:S(2)}) collective-permute-start(bf16[1200,1024]{1,0:T(8,128)(2,1)} %param.5), channel_id=1, source_target_pairs={{0,64},{64,0},{1,65},{65,1},{2,66},{66,2},{3,67},{67,3},{4,68},{68... | collective-permute-start | bytes 7372808 | tf_op jit(solution)/shard_map/ppermute | solution.py:38
  22.8 0.3 pad_maximum_fusion.1
  23.1 53.7 %collective-permute-done.1 = bf16[1200,1024]{1,0:T(8,128)(2,1)S(1)} collective-permute-done((bf16[1200,1024]{1,0:T(8,128)(2,1)}, bf16[1200,1024]{1,0:T(8,128)(2,1)S(1)}, u32[]{:S(2)}, u32[]{:S(2)}) %collective-permute-start.1) | collective-permute-done | bytes 2457632 | tf_op jit(solution)/shard_map/ppermute | solution.py:38
  76.8 2.7 %pad_maximum_fusion = bf16[1200,2048]{1,0:T(8,128)(2,1)} fusion(bf16[1200,1024]{1,0:T(8,128)(2,1)S(1)} %collective-permute-done.1, bf16[1200,1024]{1,0:T(8,128)(2,1)S(1)} %copy-done), kind=kLoop, calls=%fused_computation.3 | loop fusion | flops 9830400 | bytes 9830400 | tf_op jit(solution)/shard_map/concatenate | solution.py:38
  79.5 1.1 copy.21
  80.7 3.8 %copy.33 = bf16[8,112,2,1200]{3,1,2,0:T(8,128)(2,1)S(1)} copy(bf16[8,112,2,1200]{3,0,2,1:T(8,128)(2,1)} %all-gather.3.cloned.1.call-done) | data formatting | bytes 8601600 | tf_op jit(solution)/shard_map/reshape | solution.py:36
  84.5 0.6 dynamic-slice_bitcast_fusion.3
  85.1 3.0 %collective-permute-done.2 = bf16[1200,2048]{1,0:T(8,128)(2,1)} collective-permute-done((bf16[1200,2048]{1,0:T(8,128)(2,1)}, bf16[1200,2048]{1,0:T(8,128)(2,1)}, u32[]{:S(2)}, u32[]{:S(2)}) %collective-permute-start.2) | collective-permute-done | bytes 4915232 | tf_op jit(solution)/shard_map/ppermute | solution.py:41
  88.0 6.6 %convolution_bitcast_fusion.9 = f32[2,56,2048]{2,1,0:T(8,128)} fusion(bf16[2,112,2,1200]{3,1,2,0:T(8,128)(2,1)S(1)} %get-tuple-element.19, bf16[1,1200,2048]{2,1,0:T(8,128)(2,1)} %bitcast.5, bf16[1,1200,2048]{2,1,0:T(8,128)(2,1)} %bitcast.4), kind=kOutput, calls=%fused_computation.16 | convolution fusion | flops 1105920000 | bytes 11321344 | tf_op jit(solution)/shard_map/dot_general | solution.py:45
  94.6 1.7 collective-permute-start.3
  96.3 6.5 %convolution_bitcast_fusion.5 = f32[2,56,2048]{2,1,0:T(8,128)} fusion(bf16[2,112,2,1200]{3,1,2,0:T(8,128)(2,1)S(1)} %get-tuple-element.16, bf16[1,1200,2048]{2,1,0:T(8,128)(2,1)} %bitcast.5, bf16[1,1200,2048]{2,1,0:T(8,128)(2,1)} %bitcast.4), kind=kOutput, calls=%fused_computation.12 | convolution fusion | flops 1105920000 | bytes 11321344 | tf_op jit(solution)/shard_map/dot_general | solution.py:45
  102.8 1.6 collective-permute-start.7
  104.4 6.6 %convolution_bitcast_fusion.8 = f32[2,56,2048]{2,1,0:T(8,128)} fusion(bf16[2,112,2,1200]{3,1,2,0:T(8,128)(2,1)S(1)} %get-tuple-element.18, bf16[1,1200,2048]{2,1,0:T(8,128)(2,1)} %bitcast.5, bf16[1,1200,2048]{2,1,0:T(8,128)(2,1)} %bitcast.4), kind=kOutput, calls=%fused_computation.15 | convolution fusion | flops 1105920000 | bytes 11321344 | tf_op jit(solution)/shard_map/dot_general | solution.py:45
  111.0 6.6 %convolution_bitcast_fusion.7 = f32[2,56,2048]{2,1,0:T(8,128)} fusion(bf16[2,112,2,1200]{3,1,2,0:T(8,128)(2,1)S(1)} %get-tuple-element.14, bf16[1,1200,2048]{2,1,0:T(8,128)(2,1)} %bitcast.5, bf16[1,1200,2048]{2,1,0:T(8,128)(2,1)} %bitcast.4), kind=kOutput, calls=%fused_computation.14 | convolution fusion | flops 1105920000 | bytes 11321344 | tf_op jit(solution)/shard_map/dot_general | solution.py:45
  117.7 6.6 %convolution_bitcast_fusion.6 = f32[2,56,2048]{2,1,0:T(8,128)} fusion(bf16[2,112,2,1200]{3,1,2,0:T(8,128)(2,1)S(1)} %get-tuple-element.17, bf16[1,1200,2048]{2,1,0:T(8,128)(2,1)} %bitcast.5, bf16[1,1200,2048]{2,1,0:T(8,128)(2,1)} %bitcast.4), kind=kOutput, calls=%fused_computation.13 | convolution fusion | flops 1105920000 | bytes 11321344 | tf_op jit(solution)/shard_map/dot_general | solution.py:45
  124.3 2.7 %all-gather.5.cloned.1.call-done = bf16[8,88,2,1200]{3,0,2,1:T(8,128)(2,1)} async-done(((bf16[8,22,2,1200]{3,0,2,1:T(8,128)(2,1)}), bf16[8,88,2,1200]{3,0,2,1:T(8,128)(2,1)}) %all-gather.5.cloned.1.call-update) | async-done | bytes 3379216 | tf_op jit(solution)/shard_map/all_gather | solution.py:40
  126.9 3.1 %copy.22 = bf16[8,88,2,1200]{3,1,2,0:T(8,128)(2,1)S(1)} copy(bf16[8,88,2,1200]{3,0,2,1:T(8,128)(2,1)} %all-gather.5.cloned.1.call-done) | data formatting | bytes 6758400 | tf_op jit(solution)/shard_map/all_gather | solution.py:40
  130.0 6.7 %convolution_bitcast_fusion = f32[4,88,2048]{2,1,0:T(8,128)S(1)} fusion(bf16[4,2,88,2,1200]{4,2,3,1,0:T(8,128)(2,1)S(1)} %bitcast.93, s32[]{:T(128)S(6)} %select_n.112, bf16[1,1200,2048]{2,1,0:T(8,128)(2,1)} %bitcast.5, bf16[1,1200,2048]{2,1,0:T(8,128)(2,1)} %bitcast.4), kind=kOutput, calls=%fused_computation.4 | convolution fusion | flops 3465216000 | bytes 14516228 | tf_op jit(solution)/shard_map/dot_general | solution.py:74
  136.7 1.5 collective-permute-start.11
  138.3 4.9 %convolution_bitcast_fusion.4 = f32[2,56,2048]{2,1,0:T(8,128)S(1)} fusion(bf16[2,112,2,1200]{3,1,2,0:T(8,128)(2,1)S(1)} %get-tuple-element.15, bf16[1,1200,2048]{2,1,0:T(8,128)(2,1)} %bitcast.5, bf16[1,1200,2048]{2,1,0:T(8,128)(2,1)} %bitcast.4), kind=kOutput, calls=%fused_computation.11 | convolution fusion | flops 1105920000 | bytes 11321344 | tf_op jit(solution)/shard_map/dot_general | solution.py:45
  143.2 1.3 add.164
  144.5 1.6 collective-permute-start.4
  146.1 1.3 add.180
  147.4 1.8 collective-permute-start.8
  149.2 4.9 %convolution_bitcast_fusion.2 = f32[2,56,2048]{2,1,0:T(8,128)S(1)} fusion(bf16[2,112,2,1200]{3,1,2,0:T(8,128)(2,1)S(1)} %get-tuple-element.17, bf16[1,1200,2048]{2,1,0:T(8,128)(2,1)} %bitcast.5, bf16[1,1200,2048]{2,1,0:T(8,128)(2,1)} %bitcast.4), kind=kOutput, calls=%fused_computation.9 | convolution fusion | flops 1105920000 | bytes 11321344 | tf_op jit(solution)/shard_map/dot_general | solution.py:45
  154.1 4.9 %convolution_bitcast_fusion.3 = f32[2,56,2048]{2,1,0:T(8,128)S(1)} fusion(bf16[2,112,2,1200]{3,1,2,0:T(8,128)(2,1)S(1)} %get-tuple-element.19, bf16[1,1200,2048]{2,1,0:T(8,128)(2,1)} %bitcast.5, bf16[1,1200,2048]{2,1,0:T(8,128)(2,1)} %bitcast.4), kind=kOutput, calls=%fused_computation.10 | convolution fusion | flops 1105920000 | bytes 11321344 | tf_op jit(solution)/shard_map/dot_general | solution.py:45
  159.0 8.4 %collective-permute-done.4 = f32[2,56,2048]{2,1,0:T(8,128)S(1)} collective-permute-done((f32[2,56,2048]{2,1,0:T(8,128)S(1)}, f32[2,56,2048]{2,1,0:T(8,128)S(1)}, u32[]{:S(2)}, u32[]{:S(2)}) %collective-permute-start.4) | collective-permute-done | bytes 917536 | tf_op jit(solution)/shard_map/ppermute | solution.py:57
  167.4 0.1 add.167
  167.6 0.3 collective-permute-start.5
  167.9 0.9 collective-permute-done.8
  168.8 0.1 add.181
  168.9 3.3 %collective-permute-start.9 = (f32[2,56,2048]{2,1,0:T(8,128)S(1)}, f32[2,56,2048]{2,1,0:T(8,128)S(1)}, u32[]{:S(2)}, u32[]{:S(2)}) collective-permute-start(f32[2,56,2048]{2,1,0:T(8,128)S(1)} %add.181), channel_id=1, source_target_pairs={{0,12},{4,0},{8,4},{12,8},{1,13},{5,1},{9,5},{13,9},{2,14},{6,2},{... | collective-permute-start | bytes 2752520 | tf_op jit(solution)/shard_map/ppermute | solution.py:58
  172.2 6.6 %convolution_bitcast_fusion.1 = f32[4,88,2048]{2,1,0:T(8,128)S(1)} fusion(bf16[4,2,88,2,1200]{4,2,3,1,0:T(8,128)(2,1)S(1)} %bitcast.94, s32[]{:T(128)S(6)} %select_n.111, bf16[1,1200,2048]{2,1,0:T(8,128)(2,1)} %bitcast.5, bf16[1,1200,2048]{2,1,0:T(8,128)(2,1)} %bitcast.4), kind=kOutput, calls=%fused_computation.5 | convolution fusion | flops 3465216000 | bytes 14516228 | tf_op jit(solution)/shard_map/dot_general | solution.py:74
  178.8 10.8 %collective-permute-done.5 = f32[2,56,2048]{2,1,0:T(8,128)S(1)} collective-permute-done((f32[2,56,2048]{2,1,0:T(8,128)S(1)}, f32[2,56,2048]{2,1,0:T(8,128)S(1)}, u32[]{:S(2)}, u32[]{:S(2)}) %collective-permute-start.5) | collective-permute-done | bytes 917536 | tf_op jit(solution)/shard_map/ppermute | solution.py:57
  189.8 0.6 collective-permute-start.6
  190.6 1.5 collective-permute-start.10
  192.1 10.0 %collective-permute-done.11 = f32[4,88,2048]{2,1,0:T(8,128)S(1)} collective-permute-done((f32[4,88,2048]{2,1,0:T(8,128)S(1)}, f32[4,88,2048]{2,1,0:T(8,128)S(1)}, u32[]{:S(2)}, u32[]{:S(2)}) %collective-permute-start.11) | collective-permute-done | bytes 2883616 | tf_op jit(solution)/shard_map/ppermute | solution.py:80
  202.1 0.4 add.184
  202.6 0.2 dynamic-slice_bitcast_fusion.8
  202.8 1.6 collective-permute-start.12
  204.4 2.7 %collective-permute-start.13 = (f32[88,2048]{1,0:T(8,128)S(1)}, f32[88,2048]{1,0:T(8,128)S(1)}, u32[]{:S(2)}, u32[]{:S(2)}) collective-permute-start(f32[88,2048]{1,0:T(8,128)S(1)} %get-tuple-element.22), channel_id=1, source_target_pairs={{0,8},{4,12},{8,0},{12,4},{1,9},{5,13},{9,1},{13,5},{2,10},{6,14},... | collective-permute-start | bytes 2162696 | tf_op jit(solution)/shard_map/ppermute | solution.py:94
  207.1 1.4 collective-permute-start.14
  208.5 3.4 %collective-permute-done.6 = f32[56,2048]{1,0:T(8,128)S(1)} collective-permute-done((f32[56,2048]{1,0:T(8,128)S(1)}, f32[56,2048]{1,0:T(8,128)S(1)}, u32[]{:S(2)}, u32[]{:S(2)}) %collective-permute-start.6) | collective-permute-done | bytes 458784 | tf_op jit(solution)/shard_map/ppermute | solution.py:66
  212.1 3.1 %collective-permute-start.15 = (f32[56,1024]{1,0:T(8,128)S(1)}, f32[56,1024]{1,0:T(8,128)S(1)}, u32[]{:S(2)}, u32[]{:S(2)}) collective-permute-start(f32[56,1024]{1,0:T(8,128)S(1)} %get-tuple-element.25), channel_id=1, source_target_pairs={{0,64},{64,0},{1,65},{65,1},{2,66},{66,2},{3,67},{67,3},{4,68},{68... | collective-permute-start | bytes 688136 | tf_op jit(solution)/shard_map/ppermute | solution.py:98
  215.1 6.7 %collective-permute-done.10 = f32[56,2048]{1,0:T(8,128)S(1)} collective-permute-done((f32[56,2048]{1,0:T(8,128)S(1)}, f32[56,2048]{1,0:T(8,128)S(1)}, u32[]{:S(2)}, u32[]{:S(2)}) %collective-permute-start.10) | collective-permute-done | bytes 458784 | tf_op jit(solution)/shard_map/ppermute | solution.py:66
  221.9 3.1 %collective-permute-start.16 = (f32[56,1024]{1,0:T(8,128)S(1)}, f32[56,1024]{1,0:T(8,128)S(1)}, u32[]{:S(2)}, u32[]{:S(2)}) collective-permute-start(f32[56,1024]{1,0:T(8,128)S(1)} %get-tuple-element.27), channel_id=1, source_target_pairs={{0,64},{64,0},{1,65},{65,1},{2,66},{66,2},{3,67},{67,3},{4,68},{68... | collective-permute-start | bytes 688136 | tf_op jit(solution)/shard_map/ppermute | solution.py:98
  225.0 11.1 %collective-permute-done.13 = f32[88,2048]{1,0:T(8,128)S(1)} collective-permute-done((f32[88,2048]{1,0:T(8,128)S(1)}, f32[88,2048]{1,0:T(8,128)S(1)}, u32[]{:S(2)}, u32[]{:S(2)}) %collective-permute-start.13) | collective-permute-done | bytes 720928 | tf_op jit(solution)/shard_map/ppermute | solution.py:94
  236.1 0.2 fusion.8
  236.3 3.1 %collective-permute-start.17 = (f32[88,1024]{1,0:T(8,128)S(1)}, f32[88,1024]{1,0:T(8,128)S(1)}, u32[]{:S(2)}, u32[]{:S(2)}) collective-permute-start(f32[88,1024]{1,0:T(8,128)S(1)} %get-tuple-element.23), channel_id=1, source_target_pairs={{0,64},{64,0},{1,65},{65,1},{2,66},{66,2},{3,67},{67,3},{4,68},{68... | collective-permute-start | bytes 1081352 | tf_op jit(solution)/shard_map/ppermute | solution.py:98
  239.8 7.0 %collective-permute-done.17 = f32[88,1024]{1,0:T(8,128)S(1)} collective-permute-done((f32[88,1024]{1,0:T(8,128)S(1)}, f32[88,1024]{1,0:T(8,128)S(1)}, u32[]{:S(2)}, u32[]{:S(2)}) %collective-permute-start.17) | collective-permute-done | bytes 360480 | tf_op jit(solution)/shard_map/ppermute | solution.py:98
  247.1 1.9 fusion.5
  (48 shorter events, 1.4 us)
Async XLA Ops:
  6.5 74.2 %all-gather.3.cloned.1.call-start = ((), (), s32[]{:S(2)}) async-start(), calls=%async_computation | async-start | bytes 5734400 | tf_op jit(solution)/shard_map/all_gather | solution.py:34
  13.4 3.0 %collective-permute-start = (bf16[8,50,1200]{2,0,1:T(8,128)(2,1)}, bf16[8,50,1200]{2,0,1:T(8,128)(2,1)}, u32[]{:S(2)}, u32[]{:S(2)}) collective-permute-start(bf16[8,50,1200]{2,0,1:T(8,128)(2,1)} %copy.12), channel_id=1, source_target_pairs={{0,1},{1,0},{2,3},{3,2},{4,5},{5,4},{6,7},{7,6},{8,9},{9,8},{10,11... | collective-permute-start | bytes 2880008 | tf_op jit(solution)/shard_map/ppermute | solution.py:31
  19.5 107.4 %all-gather.5.cloned.1.call-start = ((), (), s32[]{:S(2)}) async-start(), calls=%async_computation.1 | async-start | bytes 4505600 | tf_op jit(solution)/shard_map/all_gather | solution.py:40
  19.6 57.2 %copy-start = (bf16[1200,1024]{1,0:T(8,128)(2,1)S(1)}, bf16[1200,1024]{1,0:T(8,128)(2,1)}, u32[]{:S(2)}) copy-start(bf16[1200,1024]{1,0:T(8,128)(2,1)} %param.5) | copy-start | bytes 7372804
  19.6 57.2 %collective-permute-start.1 = (bf16[1200,1024]{1,0:T(8,128)(2,1)}, bf16[1200,1024]{1,0:T(8,128)(2,1)S(1)}, u32[]{:S(2)}, u32[]{:S(2)}) collective-permute-start(bf16[1200,1024]{1,0:T(8,128)(2,1)} %param.5), channel_id=1, source_target_pairs={{0,64},{64,0},{1,65},{65,1},{2,66},{66,2},{3,67},{67,3},{4,68},{68... | collective-permute-start | bytes 7372808 | tf_op jit(solution)/shard_map/ppermute | solution.py:38
  79.5 8.5 %collective-permute-start.2 = (bf16[1200,2048]{1,0:T(8,128)(2,1)}, bf16[1200,2048]{1,0:T(8,128)(2,1)}, u32[]{:S(2)}, u32[]{:S(2)}) collective-permute-start(bf16[1200,2048]{1,0:T(8,128)(2,1)} %pad_maximum_fusion), channel_id=1, source_target_pairs={{0,1},{1,0},{2,3},{3,2},{4,5},{5,4},{6,7},{7,6},{8,9},{9,8},{10,11... | collective-permute-start | bytes 14745608 | tf_op jit(solution)/shard_map/ppermute | solution.py:41
  94.6 48.6 %collective-permute-start.3 = (f32[2,56,2048]{2,1,0:T(8,128)}, f32[2,56,2048]{2,1,0:T(8,128)}, u32[]{:S(2)}, u32[]{:S(2)}) collective-permute-start(f32[2,56,2048]{2,1,0:T(8,128)} %convolution_bitcast_fusion.9), channel_id=1, source_target_pairs={{0,4},{4,8},{8,12},{12,0},{1,5},{5,9},{9,13},{13,1},{2,6},{6,10},{... | collective-permute-start | bytes 2752520 | tf_op jit(solution)/shard_map/ppermute | solution.py:57
  102.8 43.2 %collective-permute-start.7 = (f32[2,56,2048]{2,1,0:T(8,128)}, f32[2,56,2048]{2,1,0:T(8,128)}, u32[]{:S(2)}, u32[]{:S(2)}) collective-permute-start(f32[2,56,2048]{2,1,0:T(8,128)} %convolution_bitcast_fusion.5), channel_id=1, source_target_pairs={{0,12},{4,0},{8,4},{12,8},{1,13},{5,1},{9,5},{13,9},{2,14},{6,2},{... | collective-permute-start | bytes 2752520 | tf_op jit(solution)/shard_map/ppermute | solution.py:58
  136.7 65.4 %collective-permute-start.11 = (f32[4,88,2048]{2,1,0:T(8,128)S(1)}, f32[4,88,2048]{2,1,0:T(8,128)S(1)}, u32[]{:S(2)}, u32[]{:S(2)}) collective-permute-start(f32[4,88,2048]{2,1,0:T(8,128)S(1)} %convolution_bitcast_fusion), channel_id=1, source_target_pairs={{0,2},{2,0},{1,3},{3,1},{4,6},{6,4},{5,7},{7,5},{8,10},{10,8},{9,1... | collective-permute-start | bytes 8650760 | tf_op jit(solution)/shard_map/ppermute | solution.py:80
  138.2 5.0 %copy-start.3 = (f32[2,56,2048]{2,1,0:T(8,128)S(1)}, f32[2,56,2048]{2,1,0:T(8,128)}, u32[]{:S(2)}) copy-start(f32[2,56,2048]{2,1,0:T(8,128)} %convolution_bitcast_fusion.8) | copy-start | bytes 2752516
  144.5 22.9 %collective-permute-start.4 = (f32[2,56,2048]{2,1,0:T(8,128)S(1)}, f32[2,56,2048]{2,1,0:T(8,128)S(1)}, u32[]{:S(2)}, u32[]{:S(2)}) collective-permute-start(f32[2,56,2048]{2,1,0:T(8,128)S(1)} %add.164), channel_id=1, source_target_pairs={{0,4},{4,8},{8,12},{12,0},{1,5},{5,9},{9,13},{13,1},{2,6},{6,10},{... | collective-permute-start | bytes 2752520 | tf_op jit(solution)/shard_map/ppermute | solution.py:57
  147.4 21.4 %collective-permute-start.8 = (f32[2,56,2048]{2,1,0:T(8,128)S(1)}, f32[2,56,2048]{2,1,0:T(8,128)S(1)}, u32[]{:S(2)}, u32[]{:S(2)}) collective-permute-start(f32[2,56,2048]{2,1,0:T(8,128)S(1)} %add.180), channel_id=1, source_target_pairs={{0,12},{4,0},{8,4},{12,8},{1,13},{5,1},{9,5},{13,9},{2,14},{6,2},{... | collective-permute-start | bytes 2752520 | tf_op jit(solution)/shard_map/ppermute | solution.py:58
  154.1 13.4 %copy-start.2 = (f32[2,56,2048]{2,1,0:T(8,128)S(1)}, f32[2,56,2048]{2,1,0:T(8,128)}, u32[]{:S(2)}) copy-start(f32[2,56,2048]{2,1,0:T(8,128)} %convolution_bitcast_fusion.7) | copy-start | bytes 2752516
  167.6 22.1 %collective-permute-start.5 = (f32[2,56,2048]{2,1,0:T(8,128)S(1)}, f32[2,56,2048]{2,1,0:T(8,128)S(1)}, u32[]{:S(2)}, u32[]{:S(2)}) collective-permute-start(f32[2,56,2048]{2,1,0:T(8,128)S(1)} %add.167), channel_id=1, source_target_pairs={{0,4},{4,8},{8,12},{12,0},{1,5},{5,9},{9,13},{13,1},{2,6},{6,10},{... | collective-permute-start | bytes 2752520 | tf_op jit(solution)/shard_map/ppermute | solution.py:57
  168.9 20.7 %copy-start.1 = (f32[2,56,2048]{2,1,0:T(8,128)S(1)}, f32[2,56,2048]{2,1,0:T(8,128)}, u32[]{:S(2)}) copy-start(f32[2,56,2048]{2,1,0:T(8,128)} %convolution_bitcast_fusion.6) | copy-start | bytes 2752516
  168.9 21.5 %collective-permute-start.9 = (f32[2,56,2048]{2,1,0:T(8,128)S(1)}, f32[2,56,2048]{2,1,0:T(8,128)S(1)}, u32[]{:S(2)}, u32[]{:S(2)}) collective-permute-start(f32[2,56,2048]{2,1,0:T(8,128)S(1)} %add.181), channel_id=1, source_target_pairs={{0,12},{4,0},{8,4},{12,8},{1,13},{5,1},{9,5},{13,9},{2,14},{6,2},{... | collective-permute-start | bytes 2752520 | tf_op jit(solution)/shard_map/ppermute | solution.py:58
  189.8 22.2 %collective-permute-start.6 = (f32[56,2048]{1,0:T(8,128)S(1)}, f32[56,2048]{1,0:T(8,128)S(1)}, u32[]{:S(2)}, u32[]{:S(2)}) collective-permute-start(f32[56,2048]{1,0:T(8,128)S(1)} %dynamic-slice_bitcast_fusion.10), channel_id=1, source_target_pairs={{0,2},{2,0},{1,3},{3,1},{4,6},{6,4},{5,7},{7,5},{8,10},{10,8},{9,1... | collective-permute-start | bytes 1376264 | tf_op jit(solution)/shard_map/ppermute | solution.py:66
  190.6 31.2 %collective-permute-start.10 = (f32[56,2048]{1,0:T(8,128)S(1)}, f32[56,2048]{1,0:T(8,128)S(1)}, u32[]{:S(2)}, u32[]{:S(2)}) collective-permute-start(f32[56,2048]{1,0:T(8,128)S(1)} %dynamic-slice_bitcast_fusion.9), channel_id=1, source_target_pairs={{0,2},{2,0},{1,3},{3,1},{4,6},{6,4},{5,7},{7,5},{8,10},{10,8},{9,1... | collective-permute-start | bytes 1376264 | tf_op jit(solution)/shard_map/ppermute | solution.py:66
  202.8 22.2 %collective-permute-start.12 = (f32[88,2048]{1,0:T(8,128)S(1)}, f32[88,2048]{1,0:T(8,128)S(1)}, u32[]{:S(2)}, u32[]{:S(2)}) collective-permute-start(f32[88,2048]{1,0:T(8,128)S(1)} %get-tuple-element.20), channel_id=1, source_target_pairs={{0,4},{4,8},{8,12},{12,0},{1,5},{5,9},{9,13},{13,1},{2,6},{6,10},{... | collective-permute-start | bytes 2162696 | tf_op jit(solution)/shard_map/ppermute | solution.py:94
  204.4 31.7 %collective-permute-start.13 = (f32[88,2048]{1,0:T(8,128)S(1)}, f32[88,2048]{1,0:T(8,128)S(1)}, u32[]{:S(2)}, u32[]{:S(2)}) collective-permute-start(f32[88,2048]{1,0:T(8,128)S(1)} %get-tuple-element.22), channel_id=1, source_target_pairs={{0,8},{4,12},{8,0},{12,4},{1,9},{5,13},{9,1},{13,5},{2,10},{6,14},... | collective-permute-start | bytes 2162696 | tf_op jit(solution)/shard_map/ppermute | solution.py:94
  207.1 29.0 %collective-permute-start.14 = (f32[88,2048]{1,0:T(8,128)S(1)}, f32[88,2048]{1,0:T(8,128)S(1)}, u32[]{:S(2)}, u32[]{:S(2)}) collective-permute-start(f32[88,2048]{1,0:T(8,128)S(1)} %get-tuple-element.21), channel_id=1, source_target_pairs={{0,12},{4,0},{8,4},{12,8},{1,13},{5,1},{9,5},{13,9},{2,14},{6,2},{... | collective-permute-start | bytes 2162696 | tf_op jit(solution)/shard_map/ppermute | solution.py:94
  212.1 27.4 %collective-permute-start.15 = (f32[56,1024]{1,0:T(8,128)S(1)}, f32[56,1024]{1,0:T(8,128)S(1)}, u32[]{:S(2)}, u32[]{:S(2)}) collective-permute-start(f32[56,1024]{1,0:T(8,128)S(1)} %get-tuple-element.25), channel_id=1, source_target_pairs={{0,64},{64,0},{1,65},{65,1},{2,66},{66,2},{3,67},{67,3},{4,68},{68... | collective-permute-start | bytes 688136 | tf_op jit(solution)/shard_map/ppermute | solution.py:98
  221.9 17.6 %collective-permute-start.16 = (f32[56,1024]{1,0:T(8,128)S(1)}, f32[56,1024]{1,0:T(8,128)S(1)}, u32[]{:S(2)}, u32[]{:S(2)}) collective-permute-start(f32[56,1024]{1,0:T(8,128)S(1)} %get-tuple-element.27), channel_id=1, source_target_pairs={{0,64},{64,0},{1,65},{65,1},{2,66},{66,2},{3,67},{67,3},{4,68},{68... | collective-permute-start | bytes 688136 | tf_op jit(solution)/shard_map/ppermute | solution.py:98
  236.3 10.5 %collective-permute-start.17 = (f32[88,1024]{1,0:T(8,128)S(1)}, f32[88,1024]{1,0:T(8,128)S(1)}, u32[]{:S(2)}, u32[]{:S(2)}) collective-permute-start(f32[88,1024]{1,0:T(8,128)S(1)} %get-tuple-element.23), channel_id=1, source_target_pairs={{0,64},{64,0},{1,65},{65,1},{2,66},{66,2},{3,67},{67,3},{4,68},{68... | collective-permute-start | bytes 1081352 | tf_op jit(solution)/shard_map/ppermute | solution.py:98
Sparse Core Ops, SparseCore 0:
  19.7 54.1 all-gather.2
  80.7 46.1 all-gather.4

commit v19 on v12

--- a/solution.py
+++ b/solution.py
@@ -35,10 +35,18 @@
     y_rows = gathered.shape[1]
     by_y = gathered.reshape(ny, nxl, y_rows, 2, kc)
 
-    amp = jnp.concatenate([amplitudes, lax.ppermute(amplitudes, "xh", SWAP)], axis=1)
-    late_rows, amp = lax.optimization_barrier((own_owners[:, y_cut:], amp))
+    sibling_own = lax.ppermute(amplitudes, "c", SWAP)
+    partner = lax.ppermute(amplitudes, "xh", SWAP)
+    late_rows, partner = lax.optimization_barrier((own_owners[:, y_cut:], partner))
     gathered_late = lax.all_gather(late_rows, "z", axis=1, tiled=True)
-    amp = jnp.stack([amp, lax.ppermute(amp, "c", SWAP)], axis=0)
+    sibling_partner = lax.ppermute(partner, "c", SWAP)
+    amp = jnp.stack(
+        [
+            jnp.concatenate([amplitudes, partner], axis=1),
+            jnp.concatenate([sibling_own, sibling_partner], axis=1),
+        ],
+        axis=0,
+    )
 
     def block(y_owner, low, high):
         lhs = lax.dynamic_index_in_dim(by_y, y_owner % ny, 0, keepdims=False)

time: 256 us -> 257 us (level)
  matrix products: 60.9 us -> 32.6 us
  waiting for transfers between devices: 120 us -> 140 us
  other arithmetic: 10.1 us -> 17.4 us
    dot_general x8, matrix products: 47.7 us -> 18.9 us  [block(): lax.dot_general(lhs[:, low:high], amp, (((2, 3), (0, 1)), ((), ())), pref...]
    all_gather x1, waiting for transfers between devices: 2.67 us -> 13.1 us  [local(): gathered_late = lax.all_gather(late_rows, 'z', axis=1, tiled=True)]
    another operation x0 -> x2, other arithmetic: none -> 9.96 us  [local(): jnp.stack([jnp.concatenate([amplitudes, partner], axis=1), jnp.concatenat...]
    ppermute x3, waiting for transfers between devices: 19.2 us -> 27.9 us  [ring(): got_ahead = lax.ppermute(acc_ahead, 'y', to_next)]
    ppermute x1, waiting for transfers between devices: 10 us -> 13.3 us  [local(): late_sum = late_block(xi) + lax.ppermute(late_there, 'xl', SWAP)]
    ppermute x2 -> x3, waiting for transfers between devices: 56.6 us -> 53.8 us  [the longest x1 53.7 us: local(): partner = lax.ppermute(amplitudes, 'xh', SWAP)]
    concatenate x1 -> x0, other arithmetic: 2.72 us -> none  [local(): jnp.concatenate([amplitudes, lax.ppermute(amplitudes, 'xh', SWAP)], axis=1)]
  transfers between devices with their start and end apart: 20 -> 21, of which waited for: 12 -> 11; matrix products, arithmetic and copies ran while one was open for 31% -> 22% of each run, Pallas kernels for 0% -> 0%
where the time goes in v19:
time: 257 us; the launch traced here: 256 us
  waiting for transfers between devices  140 us (54%)
  matrix products  32.6 us (13%)
  starting transfers between devices  32 us (12%)
  local copies, waits for them, and re-layouts  20.4 us (8%)
  other arithmetic  17.4 us (7%)
  between operations  13.9 us (5%)
    ppermute x1, waiting for transfers between devices, local(): partner = lax.ppermute(amplitudes, 'xh', SWAP)  53.7 us
    ppermute x3, waiting for transfers between devices, ring(): got_ahead = lax.ppermute(acc_ahead, 'y', to_next)  27.9 us
    dot_general x8, matrix products, block(): lax.dot_general(lhs[:, low:high], amp, (((2, 3), (0, 1)), ((), ())), pref...  18.9 us
    dot_general x2, matrix products, late_block(): lax.dot_general(lhs, amp, (((2, 3), (0, 1)), ((), ())), preferred_element...  13.7 us
    ppermute x1, waiting for transfers between devices, local(): late_sum = late_block(xi) + lax.ppermute(late_there, 'xl', SWAP)  13.3 us
    all_gather x1, waiting for transfers between devices, local(): gathered_late = lax.all_gather(late_rows, 'z', axis=1, tiled=True)  13.1 us
    ppermute x3, waiting for transfers between devices, local(): lax.ppermute(pick(late_sum)(yi + hop), 'y', to_owner)  11.1 us
    ppermute x2, waiting for transfers between devices, pair_sum(): return here + lax.ppermute(there, 'xl', SWAP)  10.1 us
  transfers between devices with their start and end apart: 21, of which 11 were waited for; matrix products, arithmetic and copies ran while one was open for 22% of the time, Pallas kernels for 0%

profile of v19, /device:TPU:0, one launch (start us, length us, event | category | flops | bytes accessed | tf_op | source)
XLA Modules:
  0.0 256.0 jit_solution(6281476353358879118)
XLA Ops:
  6.5 0.7 dynamic_slice.63
  7.3 1.2 sort.17
  8.6 0.2 fusion.17
  8.9 2.6 %reshape.35 = bf16[16,50,1200]{2,1,0:T(8,128)(2,1)S(1)} reshape(bf16[800,1200]{1,0:T(8,128)(2,1)} %bitcast.105) | data formatting | bytes 3840000 | tf_op jit(solution)/shard_map/reshape | solution.py:28
  11.4 0.6 gather_fusion.1
  12.1 0.2 broadcast_select_fusion
  12.3 1.1 copy.12
  13.4 0.6 gather_fusion
  14.0 0.2 select_bitcast_fusion
  14.2 2.1 collective-permute-done
  16.3 1.4 copy.35
  17.9 1.6 copy.14
  19.6 3.2 %collective-permute-start.1 = (bf16[1200,1024]{1,0:T(8,128)(2,1)}, bf16[1200,1024]{1,0:T(8,128)(2,1)}, u32[]{:S(2)}, u32[]{:S(2)}) collective-permute-start(bf16[1200,1024]{1,0:T(8,128)(2,1)} %param.5), channel_id=1, source_target_pairs={{0,64},{64,0},{1,65},{65,1},{2,66},{66,2},{3,67},{67,3},{4,68},{68... | collective-permute-start | bytes 7372808 | tf_op jit(solution)/shard_map/ppermute | solution.py:39
  22.8 0.3 pad_maximum_fusion
  23.1 53.7 %collective-permute-done.1 = bf16[1200,1024]{1,0:T(8,128)(2,1)} collective-permute-done((bf16[1200,1024]{1,0:T(8,128)(2,1)}, bf16[1200,1024]{1,0:T(8,128)(2,1)}, u32[]{:S(2)}, u32[]{:S(2)}) %collective-permute-start.1) | collective-permute-done | bytes 2457632 | tf_op jit(solution)/shard_map/ppermute | solution.py:39
  76.9 1.1 copy.21
  78.1 4.6 %maximum_bitcast_fusion.1 = bf16[1,1200,2048]{2,1,0:T(8,128)(2,1)} fusion(bf16[1200,1024]{1,0:T(8,128)(2,1)} %collective-permute-done.1, bf16[1200,1024]{1,0:T(8,128)(2,1)S(1)} %copy-done), kind=kLoop, calls=%fused_computation.3 | loop fusion | flops 9830400 | bytes 9830400 | tf_op jit(solution)/shard_map/stack | solution.py:43
  82.7 5.4 %maximum_bitcast_fusion.2 = bf16[1,1200,2048]{2,1,0:T(8,128)(2,1)} fusion(bf16[1200,1024]{1,0:T(8,128)(2,1)} %collective-permute-done.3, bf16[1200,1024]{1,0:T(8,128)(2,1)} %collective-permute-done.2), kind=kLoop, calls=%fused_computation.4 | loop fusion | flops 9830400 | bytes 9830400 | tf_op jit(solution)/shard_map/stack | solution.py:43
  88.1 4.3 %copy.33 = bf16[8,112,2,1200]{3,1,2,0:T(8,128)(2,1)S(1)} copy(bf16[8,112,2,1200]{3,0,2,1:T(8,128)(2,1)} %all-gather.3.cloned.1.call-done) | data formatting | bytes 8601600 | tf_op jit(solution)/shard_map/reshape | solution.py:36
  92.4 0.6 dynamic-slice_bitcast_fusion.3
  92.9 0.9 slice-done.4
  93.8 0.2 slice-done.1
  94.1 0.2 slice-done.5
  94.3 2.7 %convolution_bitcast_fusion.9 = f32[2,56,2048]{2,1,0:T(8,128)} fusion(bf16[2,112,2,1200]{3,1,2,0:T(8,128)(2,1)S(1)} %get-tuple-element.19, bf16[1,1200,2048]{2,1,0:T(8,128)(2,1)S(1)} %bitcast.100, bf16[1,1200,2048]{2,1,0:T(8,128)(2,1)S(1)} %bitcast.96), kind=kOutput, calls=%fused_computation.14 | convolution fusion | flops 1105920000 | bytes 11321344 | tf_op jit(solution)/shard_map/dot_general | solution.py:53
  97.1 1.7 collective-permute-start.4
  98.7 2.7 %convolution_bitcast_fusion.5 = f32[2,56,2048]{2,1,0:T(8,128)} fusion(bf16[2,112,2,1200]{3,1,2,0:T(8,128)(2,1)S(1)} %get-tuple-element.16, bf16[1,1200,2048]{2,1,0:T(8,128)(2,1)S(1)} %bitcast.100, bf16[1,1200,2048]{2,1,0:T(8,128)(2,1)S(1)} %bitcast.96), kind=kOutput, calls=%fused_computation.10 | convolution fusion | flops 1105920000 | bytes 11321344 | tf_op jit(solution)/shard_map/dot_general | solution.py:53
  101.4 1.5 collective-permute-start.8
  103.0 2.8 %convolution_bitcast_fusion.8 = f32[2,56,2048]{2,1,0:T(8,128)} fusion(bf16[2,112,2,1200]{3,1,2,0:T(8,128)(2,1)S(1)} %get-tuple-element.18, bf16[1,1200,2048]{2,1,0:T(8,128)(2,1)S(1)} %bitcast.100, bf16[1,1200,2048]{2,1,0:T(8,128)(2,1)S(1)} %bitcast.96), kind=kOutput, calls=%fused_computation.13 | convolution fusion | flops 1105920000 | bytes 11321344 | tf_op jit(solution)/shard_map/dot_general | solution.py:53
  105.7 2.7 %convolution_bitcast_fusion.7 = f32[2,56,2048]{2,1,0:T(8,128)} fusion(bf16[2,112,2,1200]{3,1,2,0:T(8,128)(2,1)S(1)} %get-tuple-element.14, bf16[1,1200,2048]{2,1,0:T(8,128)(2,1)S(1)} %bitcast.100, bf16[1,1200,2048]{2,1,0:T(8,128)(2,1)S(1)} %bitcast.96), kind=kOutput, calls=%fused_computation.12 | convolution fusion | flops 1105920000 | bytes 11321344 | tf_op jit(solution)/shard_map/dot_general | solution.py:53
  108.5 2.7 %convolution_bitcast_fusion.6 = f32[2,56,2048]{2,1,0:T(8,128)} fusion(bf16[2,112,2,1200]{3,1,2,0:T(8,128)(2,1)S(1)} %get-tuple-element.17, bf16[1,1200,2048]{2,1,0:T(8,128)(2,1)S(1)} %bitcast.100, bf16[1,1200,2048]{2,1,0:T(8,128)(2,1)S(1)} %bitcast.96), kind=kOutput, calls=%fused_computation.11 | convolution fusion | flops 1105920000 | bytes 11321344 | tf_op jit(solution)/shard_map/dot_general | solution.py:53
  111.2 13.1 %all-gather.5.cloned.1.call-done = bf16[8,88,2,1200]{3,0,2,1:T(8,128)(2,1)} async-done(((bf16[8,22,2,1200]{3,0,2,1:T(8,128)(2,1)}), bf16[8,88,2,1200]{3,0,2,1:T(8,128)(2,1)}) %all-gather.5.cloned.1.call-update) | async-done | bytes 3379216 | tf_op jit(solution)/shard_map/all_gather | solution.py:41
  124.3 3.3 %copy.22 = bf16[8,88,2,1200]{3,1,2,0:T(8,128)(2,1)S(1)} copy(bf16[8,88,2,1200]{3,0,2,1:T(8,128)(2,1)} %all-gather.5.cloned.1.call-done) | data formatting | bytes 6758400 | tf_op jit(solution)/shard_map/all_gather | solution.py:41
  127.6 9.7 %convolution_bitcast_fusion = f32[4,88,2048]{2,1,0:T(8,128)} fusion(bf16[4,2,88,2,1200]{4,2,3,1,0:T(8,128)(2,1)S(1)} %bitcast.103, s32[]{:T(128)S(6)} %select_n.118, bf16[1,1200,2048]{2,1,0:T(8,128)(2,1)} %maximum_bitcast_fusion.2, bf16[1,1200,2048]{2,1,0:T(8,128)(2,1)} %maximum_bitcast_fusion.1), kind=kOutput, calls=%fused_computation.5 | convolution fusion | flops 3465216000 | bytes 14516228 | tf_op jit(solution)/shard_map/dot_general | solution.py:82
  137.3 1.5 collective-permute-start.12
  138.9 1.8 convolution_bitcast_fusion.4
  140.6 1.3 add.161
  141.9 1.6 collective-permute-start.5
  143.5 1.3 add.177
  144.8 2.0 collective-permute-start.9
  146.9 1.8 convolution_bitcast_fusion.3
  148.6 1.8 convolution_bitcast_fusion.2
  150.4 14.5 %collective-permute-done.5 = f32[2,56,2048]{2,1,0:T(8,128)S(1)} collective-permute-done((f32[2,56,2048]{2,1,0:T(8,128)S(1)}, f32[2,56,2048]{2,1,0:T(8,128)S(1)}, u32[]{:S(2)}, u32[]{:S(2)}) %collective-permute-start.5) | collective-permute-done | bytes 917536 | tf_op jit(solution)/shard_map/ppermute | solution.py:65
  165.0 0.3 collective-permute-start.6
  165.3 1.1 collective-permute-done.9
  166.6 3.0 %collective-permute-start.10 = (f32[2,56,2048]{2,1,0:T(8,128)S(1)}, f32[2,56,2048]{2,1,0:T(8,128)S(1)}, u32[]{:S(2)}, u32[]{:S(2)}) collective-permute-start(f32[2,56,2048]{2,1,0:T(8,128)S(1)} %add.178), channel_id=1, source_target_pairs={{0,12},{4,0},{8,4},{12,8},{1,13},{5,1},{9,5},{13,9},{2,14},{6,2},{... | collective-permute-start | bytes 2752520 | tf_op jit(solution)/shard_map/ppermute | solution.py:66
  169.6 4.0 %convolution_bitcast_fusion.1 = f32[4,88,2048]{2,1,0:T(8,128)S(1)} fusion(bf16[4,2,88,2,1200]{4,2,3,1,0:T(8,128)(2,1)S(1)} %bitcast.104, s32[]{:T(128)S(6)} %select_n.117, bf16[1,1200,2048]{2,1,0:T(8,128)(2,1)S(1)} %bitcast.102, bf16[1,1200,2048]{2,1,0:T(8,128)(2,1)S(1)} %bitcast.98), kind=kOutput, calls=%fused_computation.6 | convolution fusion | flops 3465216000 | bytes 14516228 | tf_op jit(solution)/shard_map/dot_general | solution.py:82
  173.6 13.4 %collective-permute-done.6 = f32[2,56,2048]{2,1,0:T(8,128)S(1)} collective-permute-done((f32[2,56,2048]{2,1,0:T(8,128)S(1)}, f32[2,56,2048]{2,1,0:T(8,128)S(1)}, u32[]{:S(2)}, u32[]{:S(2)}) %collective-permute-start.6) | collective-permute-done | bytes 917536 | tf_op jit(solution)/shard_map/ppermute | solution.py:65
  187.2 0.6 collective-permute-start.7
  188.0 1.6 collective-permute-start.11
  189.6 13.3 %collective-permute-done.12 = f32[4,88,2048]{2,1,0:T(8,128)S(1)} collective-permute-done((f32[4,88,2048]{2,1,0:T(8,128)}, f32[4,88,2048]{2,1,0:T(8,128)S(1)}, u32[]{:S(2)}, u32[]{:S(2)}) %collective-permute-start.12) | collective-permute-done | bytes 2883616 | tf_op jit(solution)/shard_map/ppermute | solution.py:88
  202.9 0.4 add.181
  203.3 0.2 dynamic-slice_bitcast_fusion.8
  203.6 1.6 collective-permute-start.13
  205.1 2.7 %collective-permute-start.14 = (f32[88,2048]{1,0:T(8,128)S(1)}, f32[88,2048]{1,0:T(8,128)S(1)}, u32[]{:S(2)}, u32[]{:S(2)}) collective-permute-start(f32[88,2048]{1,0:T(8,128)S(1)} %get-tuple-element.22), channel_id=1, source_target_pairs={{0,8},{4,12},{8,0},{12,4},{1,9},{5,13},{9,1},{13,5},{2,10},{6,14},... | collective-permute-start | bytes 2162696 | tf_op jit(solution)/shard_map/ppermute | solution.py:102
  207.9 1.4 collective-permute-start.15
  209.3 3.4 %collective-permute-done.7 = f32[56,2048]{1,0:T(8,128)S(1)} collective-permute-done((f32[56,2048]{1,0:T(8,128)S(1)}, f32[56,2048]{1,0:T(8,128)S(1)}, u32[]{:S(2)}, u32[]{:S(2)}) %collective-permute-start.7) | collective-permute-done | bytes 458784 | tf_op jit(solution)/shard_map/ppermute | solution.py:74
  212.9 3.1 %collective-permute-start.16 = (f32[56,1024]{1,0:T(8,128)S(1)}, f32[56,1024]{1,0:T(8,128)S(1)}, u32[]{:S(2)}, u32[]{:S(2)}) collective-permute-start(f32[56,1024]{1,0:T(8,128)S(1)} %get-tuple-element.26), channel_id=1, source_target_pairs={{0,64},{64,0},{1,65},{65,1},{2,66},{66,2},{3,67},{67,3},{4,68},{68... | collective-permute-start | bytes 688136 | tf_op jit(solution)/shard_map/ppermute | solution.py:106
  215.9 6.7 %collective-permute-done.11 = f32[56,2048]{1,0:T(8,128)S(1)} collective-permute-done((f32[56,2048]{1,0:T(8,128)S(1)}, f32[56,2048]{1,0:T(8,128)S(1)}, u32[]{:S(2)}, u32[]{:S(2)}) %collective-permute-start.11) | collective-permute-done | bytes 458784 | tf_op jit(solution)/shard_map/ppermute | solution.py:74
  222.7 3.1 %collective-permute-start.17 = (f32[56,1024]{1,0:T(8,128)S(1)}, f32[56,1024]{1,0:T(8,128)S(1)}, u32[]{:S(2)}, u32[]{:S(2)}) collective-permute-start(f32[56,1024]{1,0:T(8,128)S(1)} %get-tuple-element.28), channel_id=1, source_target_pairs={{0,64},{64,0},{1,65},{65,1},{2,66},{66,2},{3,67},{67,3},{4,68},{68... | collective-permute-start | bytes 688136 | tf_op jit(solution)/shard_map/ppermute | solution.py:106
  225.7 11.1 %collective-permute-done.14 = f32[88,2048]{1,0:T(8,128)S(1)} collective-permute-done((f32[88,2048]{1,0:T(8,128)S(1)}, f32[88,2048]{1,0:T(8,128)S(1)}, u32[]{:S(2)}, u32[]{:S(2)}) %collective-permute-start.14) | collective-permute-done | bytes 720928 | tf_op jit(solution)/shard_map/ppermute | solution.py:102
  236.8 0.2 fusion.6
  237.1 3.1 %collective-permute-start.18 = (f32[88,1024]{1,0:T(8,128)S(1)}, f32[88,1024]{1,0:T(8,128)S(1)}, u32[]{:S(2)}, u32[]{:S(2)}) collective-permute-start(f32[88,1024]{1,0:T(8,128)S(1)} %get-tuple-element.24), channel_id=1, source_target_pairs={{0,64},{64,0},{1,65},{65,1},{2,66},{66,2},{3,67},{67,3},{4,68},{68... | collective-permute-start | bytes 1081352 | tf_op jit(solution)/shard_map/ppermute | solution.py:106
  240.6 7.0 %collective-permute-done.18 = f32[88,1024]{1,0:T(8,128)S(1)} collective-permute-done((f32[88,1024]{1,0:T(8,128)S(1)}, f32[88,1024]{1,0:T(8,128)S(1)}, u32[]{:S(2)}, u32[]{:S(2)}) %collective-permute-start.18) | collective-permute-done | bytes 360480 | tf_op jit(solution)/shard_map/ppermute | solution.py:106
  247.9 1.3 maximum_select_fusion
  (71 shorter events, 1.8 us)
Async XLA Ops:
  6.5 81.5 %all-gather.3.cloned.1.call-start = ((), (), s32[]{:S(2)}) async-start(), calls=%async_computation | async-start | bytes 5734400 | tf_op jit(solution)/shard_map/all_gather | solution.py:34
  13.4 3.0 %collective-permute-start = (bf16[8,50,1200]{2,0,1:T(8,128)(2,1)}, bf16[8,50,1200]{2,0,1:T(8,128)(2,1)}, u32[]{:S(2)}, u32[]{:S(2)}) collective-permute-start(bf16[8,50,1200]{2,0,1:T(8,128)(2,1)} %copy.12), channel_id=1, source_target_pairs={{0,1},{1,0},{2,3},{3,2},{4,5},{5,4},{6,7},{7,6},{8,9},{9,8},{10,11... | collective-permute-start | bytes 2880008 | tf_op jit(solution)/shard_map/ppermute | solution.py:31
  19.5 104.8 %all-gather.5.cloned.1.call-start = ((), (), s32[]{:S(2)}) async-start(), calls=%async_computation.1 | async-start | bytes 4505600 | tf_op jit(solution)/shard_map/all_gather | solution.py:41
  19.6 57.3 %collective-permute-start.1 = (bf16[1200,1024]{1,0:T(8,128)(2,1)}, bf16[1200,1024]{1,0:T(8,128)(2,1)}, u32[]{:S(2)}, u32[]{:S(2)}) collective-permute-start(bf16[1200,1024]{1,0:T(8,128)(2,1)} %param.5), channel_id=1, source_target_pairs={{0,64},{64,0},{1,65},{65,1},{2,66},{66,2},{3,67},{67,3},{4,68},{68... | collective-permute-start | bytes 7372808 | tf_op jit(solution)/shard_map/ppermute | solution.py:39
  22.8 59.9 %collective-permute-start.2 = (bf16[1200,1024]{1,0:T(8,128)(2,1)}, bf16[1200,1024]{1,0:T(8,128)(2,1)}, u32[]{:S(2)}, u32[]{:S(2)}) collective-permute-start(bf16[1200,1024]{1,0:T(8,128)(2,1)} %param.5), channel_id=1, source_target_pairs={{0,1},{1,0},{2,3},{3,2},{4,5},{5,4},{6,7},{7,6},{8,9},{9,8},{10,11... | collective-permute-start | bytes 7372808 | tf_op jit(solution)/shard_map/ppermute | solution.py:38
  23.1 55.0 %copy-start = (bf16[1200,1024]{1,0:T(8,128)(2,1)S(1)}, bf16[1200,1024]{1,0:T(8,128)(2,1)}, u32[]{:S(2)}) copy-start(bf16[1200,1024]{1,0:T(8,128)(2,1)} %param.5) | copy-start | bytes 7372804
  76.9 5.8 %collective-permute-start.3 = (bf16[1200,1024]{1,0:T(8,128)(2,1)}, bf16[1200,1024]{1,0:T(8,128)(2,1)}, u32[]{:S(2)}, u32[]{:S(2)}) collective-permute-start(bf16[1200,1024]{1,0:T(8,128)(2,1)} %collective-permute-done.1), channel_id=1, source_target_pairs={{0,1},{1,0},{2,3},{3,2},{4,5},{5,4},{6,7},{7,6},{8,9},{9,8},{10,11... | collective-permute-start | bytes 7372808 | tf_op jit(solution)/shard_map/ppermute | solution.py:42
  88.1 4.9 %slice-start = ((s8[4915200]{0:T(1024)(128)(4,1)}), s8[4194304]{0:T(1024)(128)(4,1)S(1)}, s32[]{:S(2)}) async-start(s8[4915200]{0:T(1024)(128)(4,1)} %bitcast.95), calls=%async_computation.2 | async-start | bytes 8388608
  88.1 5.8 %slice-start.4 = ((s8[4915200]{0:T(1024)(128)(4,1)}), s8[4194304]{0:T(1024)(128)(4,1)S(1)}, s32[]{:S(2)}) async-start(s8[4915200]{0:T(1024)(128)(4,1)} %bitcast.99), calls=%async_computation.6 | async-start | bytes 8388608
  92.3 1.7 slice-start.1
  92.4 2.0 slice-start.5
  97.1 43.6 %collective-permute-start.4 = (f32[2,56,2048]{2,1,0:T(8,128)}, f32[2,56,2048]{2,1,0:T(8,128)}, u32[]{:S(2)}, u32[]{:S(2)}) collective-permute-start(f32[2,56,2048]{2,1,0:T(8,128)} %convolution_bitcast_fusion.9), channel_id=1, source_target_pairs={{0,4},{4,8},{8,12},{12,0},{1,5},{5,9},{9,13},{13,1},{2,6},{6,10},{... | collective-permute-start | bytes 2752520 | tf_op jit(solution)/shard_map/ppermute | solution.py:65
  101.4 42.1 %collective-permute-start.8 = (f32[2,56,2048]{2,1,0:T(8,128)}, f32[2,56,2048]{2,1,0:T(8,128)}, u32[]{:S(2)}, u32[]{:S(2)}) collective-permute-start(f32[2,56,2048]{2,1,0:T(8,128)} %convolution_bitcast_fusion.5), channel_id=1, source_target_pairs={{0,12},{4,0},{8,4},{12,8},{1,13},{5,1},{9,5},{13,9},{2,14},{6,2},{... | collective-permute-start | bytes 2752520 | tf_op jit(solution)/shard_map/ppermute | solution.py:66
  124.3 14.5 %slice-start.2 = ((s8[4915200]{0:T(1024)(128)(4,1)}), s8[4194304]{0:T(1024)(128)(4,1)S(1)}, s32[]{:S(2)}) async-start(s8[4915200]{0:T(1024)(128)(4,1)} %bitcast.97), calls=%async_computation.4 | async-start | bytes 8388608
  124.3 14.5 %slice-start.6 = ((s8[4915200]{0:T(1024)(128)(4,1)}), s8[4194304]{0:T(1024)(128)(4,1)S(1)}, s32[]{:S(2)}) async-start(s8[4915200]{0:T(1024)(128)(4,1)} %bitcast.101), calls=%async_computation.8 | async-start | bytes 8388608
  127.6 11.2 %slice-start.3 = ((s8[4915200]{0:T(1024)(128)(4,1)}), s8[720896]{0:T(1024)(128)(4,1)S(1)}, s32[]{:S(2)}) async-start(s8[4915200]{0:T(1024)(128)(4,1)} %bitcast.97), calls=%async_computation.5 | async-start | bytes 1441792
  127.6 11.2 %slice-start.7 = ((s8[4915200]{0:T(1024)(128)(4,1)}), s8[720896]{0:T(1024)(128)(4,1)S(1)}, s32[]{:S(2)}) async-start(s8[4915200]{0:T(1024)(128)(4,1)} %bitcast.101), calls=%async_computation.9 | async-start | bytes 1441792
  137.3 65.6 %collective-permute-start.12 = (f32[4,88,2048]{2,1,0:T(8,128)}, f32[4,88,2048]{2,1,0:T(8,128)S(1)}, u32[]{:S(2)}, u32[]{:S(2)}) collective-permute-start(f32[4,88,2048]{2,1,0:T(8,128)} %convolution_bitcast_fusion), channel_id=1, source_target_pairs={{0,2},{2,0},{1,3},{3,1},{4,6},{6,4},{5,7},{7,5},{8,10},{10,8},{9,1... | collective-permute-start | bytes 8650760 | tf_op jit(solution)/shard_map/ppermute | solution.py:88
  138.9 1.8 copy-start.3
  141.9 22.9 %collective-permute-start.5 = (f32[2,56,2048]{2,1,0:T(8,128)S(1)}, f32[2,56,2048]{2,1,0:T(8,128)S(1)}, u32[]{:S(2)}, u32[]{:S(2)}) collective-permute-start(f32[2,56,2048]{2,1,0:T(8,128)S(1)} %add.161), channel_id=1, source_target_pairs={{0,4},{4,8},{8,12},{12,0},{1,5},{5,9},{9,13},{13,1},{2,6},{6,10},{... | collective-permute-start | bytes 2752520 | tf_op jit(solution)/shard_map/ppermute | solution.py:65
  144.8 21.6 %collective-permute-start.9 = (f32[2,56,2048]{2,1,0:T(8,128)S(1)}, f32[2,56,2048]{2,1,0:T(8,128)S(1)}, u32[]{:S(2)}, u32[]{:S(2)}) collective-permute-start(f32[2,56,2048]{2,1,0:T(8,128)S(1)} %add.177), channel_id=1, source_target_pairs={{0,12},{4,0},{8,4},{12,8},{1,13},{5,1},{9,5},{13,9},{2,14},{6,2},{... | collective-permute-start | bytes 2752520 | tf_op jit(solution)/shard_map/ppermute | solution.py:66
  148.6 16.3 %copy-start.2 = (f32[2,56,2048]{2,1,0:T(8,128)S(1)}, f32[2,56,2048]{2,1,0:T(8,128)}, u32[]{:S(2)}) copy-start(f32[2,56,2048]{2,1,0:T(8,128)} %convolution_bitcast_fusion.7) | copy-start | bytes 2752516
  165.0 22.1 %collective-permute-start.6 = (f32[2,56,2048]{2,1,0:T(8,128)S(1)}, f32[2,56,2048]{2,1,0:T(8,128)S(1)}, u32[]{:S(2)}, u32[]{:S(2)}) collective-permute-start(f32[2,56,2048]{2,1,0:T(8,128)S(1)} %add.164), channel_id=1, source_target_pairs={{0,4},{4,8},{8,12},{12,0},{1,5},{5,9},{9,13},{13,1},{2,6},{6,10},{... | collective-permute-start | bytes 2752520 | tf_op jit(solution)/shard_map/ppermute | solution.py:65
  166.6 20.5 %copy-start.1 = (f32[2,56,2048]{2,1,0:T(8,128)S(1)}, f32[2,56,2048]{2,1,0:T(8,128)}, u32[]{:S(2)}) copy-start(f32[2,56,2048]{2,1,0:T(8,128)} %convolution_bitcast_fusion.6) | copy-start | bytes 2752516
  166.6 21.3 %collective-permute-start.10 = (f32[2,56,2048]{2,1,0:T(8,128)S(1)}, f32[2,56,2048]{2,1,0:T(8,128)S(1)}, u32[]{:S(2)}, u32[]{:S(2)}) collective-permute-start(f32[2,56,2048]{2,1,0:T(8,128)S(1)} %add.178), channel_id=1, source_target_pairs={{0,12},{4,0},{8,4},{12,8},{1,13},{5,1},{9,5},{13,9},{2,14},{6,2},{... | collective-permute-start | bytes 2752520 | tf_op jit(solution)/shard_map/ppermute | solution.py:66
  187.2 25.5 %collective-permute-start.7 = (f32[56,2048]{1,0:T(8,128)S(1)}, f32[56,2048]{1,0:T(8,128)S(1)}, u32[]{:S(2)}, u32[]{:S(2)}) collective-permute-start(f32[56,2048]{1,0:T(8,128)S(1)} %dynamic-slice_bitcast_fusion.10), channel_id=1, source_target_pairs={{0,2},{2,0},{1,3},{3,1},{4,6},{6,4},{5,7},{7,5},{8,10},{10,8},{9,1... | collective-permute-start | bytes 1376264 | tf_op jit(solution)/shard_map/ppermute | solution.py:74
  188.0 34.6 %collective-permute-start.11 = (f32[56,2048]{1,0:T(8,128)S(1)}, f32[56,2048]{1,0:T(8,128)S(1)}, u32[]{:S(2)}, u32[]{:S(2)}) collective-permute-start(f32[56,2048]{1,0:T(8,128)S(1)} %dynamic-slice_bitcast_fusion.9), channel_id=1, source_target_pairs={{0,2},{2,0},{1,3},{3,1},{4,6},{6,4},{5,7},{7,5},{8,10},{10,8},{9,1... | collective-permute-start | bytes 1376264 | tf_op jit(solution)/shard_map/ppermute | solution.py:74
  203.6 22.1 %collective-permute-start.13 = (f32[88,2048]{1,0:T(8,128)S(1)}, f32[88,2048]{1,0:T(8,128)S(1)}, u32[]{:S(2)}, u32[]{:S(2)}) collective-permute-start(f32[88,2048]{1,0:T(8,128)S(1)} %get-tuple-element.20), channel_id=1, source_target_pairs={{0,4},{4,8},{8,12},{12,0},{1,5},{5,9},{9,13},{13,1},{2,6},{6,10},{... | collective-permute-start | bytes 2162696 | tf_op jit(solution)/shard_map/ppermute | solution.py:102
  205.1 31.7 %collective-permute-start.14 = (f32[88,2048]{1,0:T(8,128)S(1)}, f32[88,2048]{1,0:T(8,128)S(1)}, u32[]{:S(2)}, u32[]{:S(2)}) collective-permute-start(f32[88,2048]{1,0:T(8,128)S(1)} %get-tuple-element.22), channel_id=1, source_target_pairs={{0,8},{4,12},{8,0},{12,4},{1,9},{5,13},{9,1},{13,5},{2,10},{6,14},... | collective-permute-start | bytes 2162696 | tf_op jit(solution)/shard_map/ppermute | solution.py:102
  207.9 29.0 %collective-permute-start.15 = (f32[88,2048]{1,0:T(8,128)S(1)}, f32[88,2048]{1,0:T(8,128)S(1)}, u32[]{:S(2)}, u32[]{:S(2)}) collective-permute-start(f32[88,2048]{1,0:T(8,128)S(1)} %get-tuple-element.21), channel_id=1, source_target_pairs={{0,12},{4,0},{8,4},{12,8},{1,13},{5,1},{9,5},{13,9},{2,14},{6,2},{... | collective-permute-start | bytes 2162696 | tf_op jit(solution)/shard_map/ppermute | solution.py:102
  212.9 27.4 %collective-permute-start.16 = (f32[56,1024]{1,0:T(8,128)S(1)}, f32[56,1024]{1,0:T(8,128)S(1)}, u32[]{:S(2)}, u32[]{:S(2)}) collective-permute-start(f32[56,1024]{1,0:T(8,128)S(1)} %get-tuple-element.26), channel_id=1, source_target_pairs={{0,64},{64,0},{1,65},{65,1},{2,66},{66,2},{3,67},{67,3},{4,68},{68... | collective-permute-start | bytes 688136 | tf_op jit(solution)/shard_map/ppermute | solution.py:106
  222.7 17.6 %collective-permute-start.17 = (f32[56,1024]{1,0:T(8,128)S(1)}, f32[56,1024]{1,0:T(8,128)S(1)}, u32[]{:S(2)}, u32[]{:S(2)}) collective-permute-start(f32[56,1024]{1,0:T(8,128)S(1)} %get-tuple-element.28), channel_id=1, source_target_pairs={{0,64},{64,0},{1,65},{65,1},{2,66},{66,2},{3,67},{67,3},{4,68},{68... | collective-permute-start | bytes 688136 | tf_op jit(solution)/shard_map/ppermute | solution.py:106
  237.1 10.5 %collective-permute-start.18 = (f32[88,1024]{1,0:T(8,128)S(1)}, f32[88,1024]{1,0:T(8,128)S(1)}, u32[]{:S(2)}, u32[]{:S(2)}) collective-permute-start(f32[88,1024]{1,0:T(8,128)S(1)} %get-tuple-element.24), channel_id=1, source_target_pairs={{0,64},{64,0},{1,65},{65,1},{2,66},{66,2},{3,67},{67,3},{4,68},{68... | collective-permute-start | bytes 1081352 | tf_op jit(solution)/shard_map/ppermute | solution.py:106
Sparse Core Ops, SparseCore 0:
  19.7 54.1 all-gather.2
  78.1 46.1 all-gather.4
